TPU v7x, 32 devices: a whole 2x2x4 slice. The times are simulated.
32 devices in a mesh: grp: 2 (over y), tm: 8 (over z, x), rows: 1, chan: 2 (over core).
Axes of the slice: x: 2, y: 2, z: 4, core: 2. Of those that a mesh axis runs over, the one named last changes fastest.
Arguments:
- frames_in: bfloat16 [64, 1, 64, 512], P(('grp', 'tm'), 'rows'), parts along dimension 0, may hold values from -6 to 6
- in_kernel: bfloat16 [3, 3, 512, 512], P(None, None, None, 'chan'), may hold values from -0.09375 to 0.09375
- out_kernel: bfloat16 [3, 3, 512, 512], P(None, None, 'chan'), may hold values from -0.09375 to 0.09375
- decay_rate: float32 [512], P('chan'), may hold values from 0 to 1, as said below
- frame_keep: float32 [64], P('grp'), parts along dimension 0, may hold values from 0.5 to 1
- out_grad: bfloat16 [64, 1, 64, 512], P(('grp', 'tm'), 'rows'), parts along dimension 0, may hold values from -6 to 6
Outputs:
- mixed: bfloat16 [64, 1, 64, 512], P(('grp', 'tm'), 'rows', None, 'chan'), parts along dimension 0
- grad_in: bfloat16 [64, 1, 64, 512], P(('grp', 'tm'), 'rows', None, 'chan'), parts along dimension 0
- grad_decay: float32 [1024], P(('grp', 'chan')), parts along dimension 0
There are 2 independent parts, one for each index of `grp`. A program takes and returns all parts, laid end to end along the dimension named above; an argument that names none is the same for every part. Nothing has to cross between parts.
Inputs may be any that keep to these rules, and one draw needn't show every extreme that they name: `decay_rate`: every decay factor lies strictly between the bounds.
All inputs are finite; a program needn't handle non-finite values.
Results may differ from a plain program's by a relative error of at most 0.009.
Values may be sent and summed in bfloat16 or wider, within the bound.
No kernel may reach another device: no remote copies, remote signals or barrier semaphores. Data moves between devices by JAX's collectives and lax.ppermute only.
A program may use at most 64 MiB of HBM per device.

v0:
```python
import math

import jax
import jax.numpy as jnp
from jax import lax
from jax.sharding import PartitionSpec as P


def extended_2(cells, sides, width):
    for axis, dim in sides:
        count = lax.axis_size(axis)
        ends = count - 1
        head = lax.slice_in_dim(cells, 0, width, axis=dim)
        tail = lax.slice_in_dim(cells, cells.shape[dim] - width, cells.shape[dim], axis=dim)
        cells = jnp.concatenate(
            [
                lax.ppermute(tail, axis, [(i, (i + 1) % count) for i in range(ends)]),
                cells,
                lax.ppermute(head, axis, [((i + 1) % count, i) for i in range(ends)]),
            ],
            axis=dim,
        )
    return cells


def carried_in(value, axis, join, neutral, backward):
    count, mine = (lax.axis_size(axis), lax.axis_index(axis))
    pieces = jax.tree.map(lambda part: lax.all_gather(part, axis), value)
    if backward:
        pieces = jax.tree.map(lambda part: part[::-1], pieces)
        mine = count - 1 - mine
    so_far = jax.tree.map(
        lambda part, zero: jnp.full_like(part, 0) + jnp.asarray(zero, part.dtype), value, neutral
    )

    def hop(position, so_far):
        longer = join(so_far, jax.tree.map(lambda part: part[position], pieces))
        return jax.tree.map(lambda new, old: jnp.where(position < mine, new, old), longer, so_far)

    return lax.fori_loop(0, count - 1, hop, so_far)


def conv_apply(extended, kernel, transpose):
    padded = jnp.pad(extended, ((0, 0), (0, 0), (1, 1), (0, 0)))
    frame_count = extended.shape[0]
    row_count = extended.shape[1] - 2
    col_count = extended.shape[2]
    channels = extended.shape[3]
    summed = None
    for row_tap in range(3):
        for col_tap in range(3):
            if transpose:
                portion = padded[
                    :,
                    2 - row_tap : 2 - row_tap + row_count,
                    2 - col_tap : 2 - col_tap + col_count,
                    :,
                ]
                term = lax.dot_general(
                    portion.reshape(-1, channels),
                    kernel[row_tap, col_tap],
                    (((1,), (1,)), ((), ())),
                    preferred_element_type=jnp.float32,
                )
            else:
                portion = padded[:, row_tap : row_tap + row_count, col_tap : col_tap + col_count, :]
                term = jnp.dot(
                    portion.reshape(-1, channels),
                    kernel[row_tap, col_tap],
                    preferred_element_type=jnp.float32,
                )
            summed = term if summed is None else summed + term
    return summed.reshape(frame_count, row_count, col_count, -1)


def combine(earlier, later):
    return (later[0] * earlier[0], later[0] * earlier[1] + later[1])


def local(frames_in, in_kernel, out_kernel, decay_rate, frame_keep, out_grad):
    frame_count = frames_in.shape[0]
    row_count = frames_in.shape[1]
    col_count = frames_in.shape[2]
    position = lax.axis_index("tm")
    blocks = lax.axis_size("tm")
    input_ext, cotangent_ext = (
        extended_2(frames_in, (("rows", 1),), 1),
        extended_2(out_grad, (("rows", 1),), 1),
    )
    values = conv_apply(input_ext, in_kernel, False)
    adjoint_in = conv_apply(cotangent_ext, out_kernel, True)
    input_gain = jnp.sqrt(1.0 - decay_rate * decay_rate)
    keep_padded = jnp.concatenate([frame_keep, jnp.zeros((1,), jnp.float32)])
    offset = position * frame_count
    keep_here = lax.dynamic_slice_in_dim(keep_padded, offset, frame_count)
    keep_next = lax.dynamic_slice_in_dim(keep_padded, offset + 1, frame_count)
    decays = keep_here[:, None] * decay_rate[None, :]
    decays_next = keep_next[:, None] * decay_rate[None, :]

    def forward_step(carried, inputs):
        running, product = carried
        factor, current = inputs
        running = factor * running + input_gain * current
        product = product * factor
        return ((running, product), (running, product))

    def backward_step(carried, inputs):
        running, product = carried
        factor, current = inputs
        running = current + factor * running
        product = product * factor
        return ((running, product), (running, product))

    zero_state = jnp.zeros(values.shape[1:], jnp.float32)
    unit_rates = jnp.ones(decay_rate.shape, jnp.float32)
    (end_state, end_product), (local_states, products) = lax.scan(
        forward_step, (zero_state, unit_rates), (decays, values)
    )
    (back_state, back_product), (back_states, back_products) = lax.scan(
        backward_step, (zero_state, unit_rates), (decays_next, adjoint_in), reverse=True
    )
    identity = (unit_rates, zero_state)
    carry_in = carried_in((end_product, end_state), "tm", combine, identity, False)[1]
    carry_back = carried_in((back_product, back_state), "tm", combine, identity, True)[1]
    states = local_states + products[:, None, None, :] * carry_in
    adjoints = back_states + back_products[:, None, None, :] * carry_back
    previous = jnp.concatenate([carry_in[None], states[:-1]], axis=0)
    terms = adjoints * (
        decays[:, None, None, :] * previous - decay_rate * decay_rate / input_gain * values
    )
    total_count = frame_count * blocks * row_count * lax.axis_size("rows") * col_count
    grad_decay = lax.psum(jnp.sum(terms, axis=(0, 1, 2)), ("tm", "rows")) / math.sqrt(total_count)
    state_b = states.astype(jnp.bfloat16)
    adjoint_b = adjoints.astype(jnp.bfloat16)
    state_ext, adjoint_ext = (
        extended_2(state_b, (("rows", 1),), 1),
        extended_2(adjoint_b, (("rows", 1),), 1),
    )
    output_part = conv_apply(state_ext, out_kernel, False)
    input_part = conv_apply(adjoint_ext, in_kernel, True)
    mixed, grad_in = (
        lax.psum_scatter(
            output_part.astype(jnp.bfloat16), "chan", scatter_dimension=3, tiled=True
        ).astype(jnp.float32),
        lax.psum_scatter(
            input_part.astype(jnp.bfloat16), "chan", scatter_dimension=3, tiled=True
        ).astype(jnp.float32),
    )
    return (mixed.astype(jnp.bfloat16), grad_in.astype(jnp.bfloat16), grad_decay)


def solution(mesh):
    placed = (
        P(("grp", "tm"), "rows", None, None),
        P(None, None, None, "chan"),
        P(None, None, "chan", None),
        P("chan"),
        P("grp"),
        P(("grp", "tm"), "rows", None, None),
    )
    return jax.shard_map(
        local,
        mesh=mesh,
        in_specs=placed,
        out_specs=(
            P(("grp", "tm"), "rows", None, "chan"),
            P(("grp", "tm"), "rows", None, "chan"),
            P(("grp", "chan")),
        ),
        check_vma=False,
    )
```

profile of v0, /device:TPU:0, one launch (start us, length us, event | category | flops | bytes accessed | tf_op | source)
XLA Modules:
  0.0 166.2 jit_solution(10950249055028282402)
XLA Ops:
  7.2 0.8 collective-permute-start.2
  8.0 0.7 collective-permute-start
  8.7 0.7 multiply_divide_fusion
  9.4 0.7 pad_maximum_fusion
  10.2 0.7 broadcast_multiply_fusion
  11.0 1.1 select_maximum_fusion
  15.4 0.7 copy-done.3
  16.1 33.0 %all-gather.3 = f32[8,64,256]{2,1,0:T(8,128)S(1)} all-gather(f32[1,64,256]{2,1,0:T(8,128)S(1)} %get-tuple-element.388), channel_id=5, replica_groups=mesh['grp'=2,'tm'=8,'rows'=1,'chan'=2] {'tm'}, dimensions={0}, use_global_device_ids=true | all-gather | bytes 589824 | tf_op jit(solution)/shard_map/all_gather | solution.py:28
  49.1 20.7 %all-gather.5 = f32[8,1,256]{2,1,0:T(1,128)S(1)} all-gather(f32[1,1,256]{2,1,0:T(1,128)S(1)} %bitcast.288), channel_id=4, replica_groups=mesh['grp'=2,'tm'=8,'rows'=1,'chan'=2] {'tm'}, dimensions={0}, use_global_device_ids=true | all-gather | bytes 9216 | tf_op jit(solution)/shard_map/all_gather | solution.py:28
  70.7 1.2 copy-done
  74.5 33.3 %all-gather.1 = f32[8,64,256]{2,1,0:T(8,128)} all-gather(f32[1,64,256]{2,1,0:T(8,128)S(1)} %get-tuple-element.383), channel_id=3, replica_groups=mesh['grp'=2,'tm'=8,'rows'=1,'chan'=2] {'tm'}, dimensions={0}, use_global_device_ids=true | all-gather | bytes 589824 | tf_op jit(solution)/shard_map/all_gather | solution.py:28
  107.8 16.5 %all-gather.4 = f32[8,1,256]{2,1,0:T(1,128)S(1)} all-gather(f32[1,1,256]{2,1,0:T(1,128)S(1)} %bitcast.286), channel_id=2, replica_groups=mesh['grp'=2,'tm'=8,'rows'=1,'chan'=2] {'tm'}, dimensions={0}, use_global_device_ids=true | all-gather | bytes 9216 | tf_op jit(solution)/shard_map/all_gather | solution.py:28
  124.3 6.3 %while.67 = (s32[]{:T(128)}, f32[1,64,256]{2,1,0:T(8,128)S(1)}, s32[]{:T(128)}, f32[8,256]{1,0:T(8,128)S(1)}, f32[8,1,64,256]{3,2,1,0:T(8,128)}, /*index=5*/s32[]{:T(128)}, s32[]{:T(128)}) while((s32[]{:T(128)}, f32[1,64,256]{2,1,0:T(8,128)S(1)}, s32[]{:T(128)}, f32[8,256]{1,0:T(8,128)S(1)}, f32[8,1,64,256]{3,2,1,0:T(8,128)}, ...), condition=%wide.region_3.4_spmd.clone, body=%wide.region_2.3_spmd.clone.sunk | while | flops 65540 | bytes 199785 | solution.py:40
  124.3 0.9 fusion.142
  125.2 0.9 fusion.142
  126.1 0.9 fusion.142
  127.0 0.9 fusion.142
  127.9 0.9 fusion.142
  128.8 0.9 fusion.142
  129.7 0.9 fusion.142
  134.5 1.0 fusion.7
  135.7 1.4 copy-done.2
  138.9 0.9 fusion.6
  139.9 18.9 %psum.7 = f32[256]{0:T(256)S(1)} all-reduce(f32[256]{0:T(256)S(1)} %get-tuple-element.597), channel_id=1, replica_groups=mesh['grp'=2,'tm'=8,'rows'=1,'chan'=2] {'tm','rows'}, use_global_device_ids=true, to_apply=%region_11.12 | all-reduce | flops 256 | bytes 2048 | tf_op jit(solution)/shard_map/psum | solution.py:132
  (139 shorter events, 14.1 us)
Async XLA Ops:
  7.2 5.2 %copy-start.1 = (bf16[3,3,256,512]{3,2,1,0:T(8,128)(2,1)S(1)}, bf16[3,3,256,512]{3,2,1,0:T(8,128)(2,1)}, u32[]{:S(2)}) copy-start(bf16[3,3,256,512]{3,2,1,0:T(8,128)(2,1)} %param.16) | copy-start | bytes 7077892
  7.2 152.2 %reduce-scatter.5.cloned.1.call-start = ((), (), s32[]{:S(2)}) async-start(), calls=%async_computation.3 | async-start | bytes 393216 | tf_op jit(solution)/shard_map/reduce_scatter | solution.py:145
  7.2 3.8 %collective-permute-start.2 = (bf16[4,1,64,512]{3,2,1,0:T(8,128)(2,1)}, bf16[4,1,64,512]{3,2,1,0:T(8,128)(2,1)S(1)}, u32[]{:S(2)}, u32[]{:S(2)}) collective-permute-start(bf16[4,1,64,512]{3,2,1,0:T(8,128)(2,1)} %param.19), channel_id=1, source_target_pairs={} | collective-permute-start | bytes 786440 | tf_op jit(solution)/shard_map/ppermute | solution.py:17
  8.0 62.2 %collective-permute-start = (bf16[4,1,64,512]{3,2,1,0:T(8,128)(2,1)}, bf16[4,1,64,512]{3,2,1,0:T(8,128)(2,1)S(1)}, u32[]{:S(2)}, u32[]{:S(2)}) collective-permute-start(bf16[4,1,64,512]{3,2,1,0:T(8,128)(2,1)} %param.14), channel_id=1, source_target_pairs={} | collective-permute-start | bytes 786440 | tf_op jit(solution)/shard_map/ppermute | solution.py:17
  12.4 1.4 copy-start.5
  14.8 55.4 %copy-start.6 = (bf16[4,1,64,512]{3,2,1,0:T(8,128)(2,1)S(1)}, bf16[4,1,64,512]{3,2,1,0:T(8,128)(2,1)}, u32[]{:S(2)}) copy-start(bf16[4,1,64,512]{3,2,1,0:T(8,128)(2,1)} %param.14) | copy-start | bytes 786436
  15.4 0.7 copy-start.3
  70.2 1.7 %copy-start = (bf16[3,3,512,256]{3,2,1,0:T(8,128)(2,1)S(1)}, bf16[3,3,512,256]{3,2,1,0:T(8,128)(2,1)}, u32[]{:S(2)}) copy-start(bf16[3,3,512,256]{3,2,1,0:T(8,128)(2,1)} %param.15) | copy-start | bytes 7077892
  74.0 56.6 %copy-start.4 = (f32[4,1,64,256]{3,2,1,0:T(8,128)S(1)}, f32[4,1,64,256]{3,2,1,0:T(8,128)}, u32[]{:S(2)}) copy-start(f32[4,1,64,256]{3,2,1,0:T(8,128)} %copy-done.3) | copy-start | bytes 786436
  130.7 1.3 collective-permute-start.3
  131.4 4.1 %collective-permute-start.1 = (bf16[4,1,64,256]{3,2,1,0:T(8,128)(2,1)S(1)}, bf16[4,1,64,256]{3,2,1,0:T(8,128)(2,1)S(1)}, u32[]{:S(2)}, u32[]{:S(2)}) collective-permute-start(bf16[4,1,64,256]{3,2,1,0:T(8,128)(2,1)S(1)} %get-tuple-element.571), channel_id=1, source_target_pairs={} | collective-permute-start | bytes 393224 | tf_op jit(solution)/shard_map/ppermute | solution.py:17
  135.4 1.7 %copy-start.2 = (bf16[3,3,256,512]{3,2,1,0:T(8,128)(2,1)S(1)}, bf16[3,3,256,512]{3,2,1,0:T(8,128)(2,1)}, u32[]{:S(2)}) copy-start(bf16[3,3,256,512]{3,2,1,0:T(8,128)(2,1)} %param.16) | copy-start | bytes 7077892
  135.4 23.9 %reduce-scatter.3.cloned.1.call-start = ((), (), s32[]{:S(2)}) async-start(), calls=%async_computation.2 | async-start | bytes 393216 | tf_op jit(solution)/shard_map/reduce_scatter | solution.py:142
Sparse Core Ops, SparseCore 0:
  135.6 6.1 reduce-scatter.4
  144.7 8.8 reduce-scatter.2
where the time goes:
time: 167 us; the launch traced here: 166 us
  blocking collectives  122 us (73%)
  between operations  14.6 us (9%)
  other arithmetic  10.8 us (6%)
  matrix products  10.2 us (6%)
  local copies, waits for them, and re-layouts  4.77 us (3%)
  starting transfers between devices  2.87 us (2%)
    all_gather x4, blocking collectives, carried_in(): pieces = jax.tree.map(lambda part: lax.all_gather(part, axis), value)  103 us
    psum x1, blocking collectives, local(): lax.psum(jnp.sum(terms, axis=(0, 1, 2)), ('tm', 'rows'))  18.9 us
    select_n x14, other arithmetic, hop(): jnp.where(position < mine, new, old)  6.17 us
    dot_general x18, matrix products, conv_apply(): lax.dot_general(portion.reshape(-1, channels), kernel[row_tap, col_tap],...  5.4 us
    dot_general x18, matrix products, conv_apply(): jnp.dot(portion.reshape(-1, channels), kernel[row_tap, col_tap], preferre...  4.76 us
  transfers between devices with their start and end apart: 6, of which 0 were waited for; matrix products, arithmetic and copies ran while one was open for 8% of the time, Pallas kernels for 0%

commit v1 on v0

v1 whole, which is shorter than its diff:
```python
import math

import jax
import jax.numpy as jnp
from jax import lax
from jax.sharding import PartitionSpec as P


def row_halo(cells):
    count = lax.axis_size("rows")
    if count == 1:
        return None
    ends = count - 1
    head = cells[:, :1]
    tail = cells[:, -1:]
    top = lax.ppermute(tail, "rows", [(i, i + 1) for i in range(ends)])
    bottom = lax.ppermute(head, "rows", [(i + 1, i) for i in range(ends)])
    return top, bottom


def conv_apply(cells, halo, kernel, transpose):
    frame_count, row_count, col_count, channels = cells.shape
    if halo is None and row_count == 1:
        row_taps = (1,)
        extended = cells
    else:
        if halo is None:
            zero = jnp.zeros_like(cells[:, :1])
            halo = (zero, zero)
        row_taps = (0, 1, 2)
        extended = jnp.concatenate([halo[0], cells, halo[1]], axis=1)
    if len(row_taps) == 1:
        extended = jnp.pad(extended, ((0, 0), (1, 1), (0, 0), (0, 0)))
    padded = jnp.pad(extended, ((0, 0), (0, 0), (1, 1), (0, 0)))
    summed = None
    for row_tap in row_taps:
        for col_tap in range(3):
            if transpose:
                portion = padded[
                    :,
                    2 - row_tap : 2 - row_tap + row_count,
                    2 - col_tap : 2 - col_tap + col_count,
                    :,
                ]
                term = lax.dot_general(
                    portion.reshape(-1, channels),
                    kernel[row_tap, col_tap],
                    (((1,), (1,)), ((), ())),
                    preferred_element_type=jnp.float32,
                )
            else:
                portion = padded[:, row_tap : row_tap + row_count, col_tap : col_tap + col_count, :]
                term = jnp.dot(
                    portion.reshape(-1, channels),
                    kernel[row_tap, col_tap],
                    preferred_element_type=jnp.float32,
                )
            summed = term if summed is None else summed + term
    return summed.reshape(frame_count, row_count, col_count, -1)


def combine_packed(earlier, later):
    is_state = lax.broadcasted_iota(jnp.int32, later.shape, 0) > 0
    return later[0:1] * earlier + jnp.where(is_state, later, 0.0)


def exclusive_scan(packed, axis, reverse):
    count = lax.axis_size(axis)
    mine = lax.axis_index(axis)
    rank = count - 1 - mine if reverse else mine
    is_state = lax.broadcasted_iota(jnp.int32, packed.shape, 0) > 0
    excl = jnp.where(is_state, 0.0, 1.0).astype(packed.dtype)
    incl = packed
    step = 1
    while step < count:
        if reverse:
            pairs = [(i, i - step) for i in range(step, count)]
        else:
            pairs = [(i, i + step) for i in range(count - step)]
        got = lax.ppermute(incl, axis, pairs)
        has = rank >= step
        excl = jnp.where(has, combine_packed(got, excl), excl)
        if 2 * step < count:
            incl = jnp.where(has, combine_packed(got, incl), incl)
        step *= 2
    return excl


def all_sum(value, axis):
    count = lax.axis_size(axis)
    if count == 1:
        return value
    if count & (count - 1) == 0:
        step = 1
        while step < count:
            value = value + lax.ppermute(value, axis, [(i, i ^ step) for i in range(count)])
            step *= 2
        return value
    return lax.psum(value, axis)


def chan_sum(cells, halo, kernel, transpose, out_axis_kernel):
    count = lax.axis_size("chan")
    mine = lax.axis_index("chan")
    width = kernel.shape[out_axis_kernel] // count
    if count != 2:
        part = conv_apply(cells, halo, kernel, transpose)
        return lax.psum_scatter(part.astype(jnp.bfloat16), "chan", scatter_dimension=3, tiled=True)
    other_kernel = lax.dynamic_slice_in_dim(kernel, (1 - mine) * width, width, axis=out_axis_kernel)
    own_kernel = lax.dynamic_slice_in_dim(kernel, mine * width, width, axis=out_axis_kernel)
    other = conv_apply(cells, halo, other_kernel, transpose).astype(jnp.bfloat16)
    got = lax.ppermute(other, "chan", [(0, 1), (1, 0)])
    own = conv_apply(cells, halo, own_kernel, transpose)
    return (own + got.astype(jnp.float32)).astype(jnp.bfloat16)


def local(frames_in, in_kernel, out_kernel, decay_rate, frame_keep, out_grad):
    frame_count, row_count, col_count = frames_in.shape[:3]
    channels = decay_rate.shape[0]
    position = lax.axis_index("tm")
    blocks = lax.axis_size("tm")
    values = conv_apply(frames_in, row_halo(frames_in), in_kernel, False)
    adjoint_in = conv_apply(out_grad, row_halo(out_grad), out_kernel, True)
    input_gain = jnp.sqrt(1.0 - decay_rate * decay_rate)
    keep_padded = jnp.concatenate([frame_keep, jnp.zeros((1,), jnp.float32)])
    offset = position * frame_count
    keep_here = lax.dynamic_slice_in_dim(keep_padded, offset, frame_count)
    keep_next = lax.dynamic_slice_in_dim(keep_padded, offset + 1, frame_count)
    decays = keep_here[:, None] * decay_rate[None, :]
    decays_next = keep_next[:, None] * decay_rate[None, :]

    running = None
    product = None
    local_states, products = [], []
    for t in range(frame_count):
        fresh = input_gain * values[t]
        running = fresh if running is None else decays[t] * running + fresh
        product = decays[t] if product is None else product * decays[t]
        local_states.append(running)
        products.append(product)
    running = None
    product = None
    back_states, back_products = [None] * frame_count, [None] * frame_count
    for t in reversed(range(frame_count)):
        running = adjoint_in[t] if running is None else adjoint_in[t] + decays_next[t] * running
        product = decays_next[t] if product is None else product * decays_next[t]
        back_states[t] = running
        back_products[t] = product

    cells = row_count * col_count

    def pack(prod, state):
        return jnp.concatenate([prod[None, :], state.reshape(cells, channels)], axis=0)

    carry_in = exclusive_scan(pack(products[-1], local_states[-1]), "tm", False)[1:]
    carry_back = exclusive_scan(pack(back_products[0], back_states[0]), "tm", True)[1:]
    carry_in = carry_in.reshape(row_count, col_count, channels)
    carry_back = carry_back.reshape(row_count, col_count, channels)

    states = jnp.stack([local_states[t] + products[t] * carry_in for t in range(frame_count)])
    adjoints = jnp.stack([back_states[t] + back_products[t] * carry_back for t in range(frame_count)])
    previous = jnp.concatenate([carry_in[None], states[:-1]], axis=0)
    terms = adjoints * (
        decays[:, None, None, :] * previous - decay_rate * decay_rate / input_gain * values
    )
    total_count = frame_count * blocks * row_count * lax.axis_size("rows") * col_count
    grad_decay = all_sum(all_sum(jnp.sum(terms, axis=(0, 1, 2)), "tm"), "rows") / math.sqrt(total_count)

    state_b = states.astype(jnp.bfloat16)
    adjoint_b = adjoints.astype(jnp.bfloat16)
    mixed = chan_sum(state_b, row_halo(state_b), out_kernel, False, 3)
    grad_in = chan_sum(adjoint_b, row_halo(adjoint_b), in_kernel, True, 2)
    return (mixed, grad_in, grad_decay)


def solution(mesh):
    placed = (
        P(("grp", "tm"), "rows", None, None),
        P(None, None, None, "chan"),
        P(None, None, "chan", None),
        P("chan"),
        P("grp"),
        P(("grp", "tm"), "rows", None, None),
    )
    return jax.shard_map(
        local,
        mesh=mesh,
        in_specs=placed,
        out_specs=(
            P(("grp", "tm"), "rows", None, "chan"),
            P(("grp", "tm"), "rows", None, "chan"),
            P(("grp", "chan")),
        ),
        check_vma=False,
    )
```

time: 167 us -> 66.2 us (0.40)
  blocking collectives: 122 us -> 0 us
  starting transfers between devices: 2.87 us -> 21.2 us
  waiting for transfers between devices: 0.05 us -> 15.6 us
  between operations: 14.6 us -> 1.08 us
  matrix products: 10.2 us -> 12.4 us
    all_gather x4 -> x0, blocking collectives: 103 us -> none  [carried_in(): pieces = jax.tree.map(lambda part: lax.all_gather(part, axis), value)]
    psum x1 -> x0, blocking collectives: 18.9 us -> none  [local(): lax.psum(jnp.sum(terms, axis=(0, 1, 2)), ('tm', 'rows'))]
    ppermute x4 -> x11, starting transfers between devices: 2.79 us -> 21.2 us  [the longest x6 20.5 us: exclusive_scan(): got = lax.ppermute(incl, axis, pairs)]
    ppermute x4 -> x11, waiting for transfers between devices: 0.01 us -> 15.6 us  [the longest x6 9.74 us: exclusive_scan(): got = lax.ppermute(incl, axis, pairs)]
    select_n x14 -> x3, other arithmetic: 6.17 us -> 2.76 us  [the longest x2 2.75 us: exclusive_scan(): incl = jnp.where(has, combine_packed(got, incl), incl)]
    dot_general x18 -> x9, matrix products: 4.76 us -> 7.26 us  [conv_apply(): jnp.dot(portion.reshape(-1, channels), kernel[row_tap, col_tap], preferre...]
    unnamed x17 -> x24, local copies, waits for them, and re-layouts: 3.28 us -> 1.31 us
    mul x8 -> x4, other arithmetic: 0.1 us -> 1.95 us  [the longest x2 1.27 us: local(): product = decays_next[t] if product is None else product * decays_next[t]]
  transfers between devices with their start and end apart: 6 -> 11, of which waited for: 0 -> 5; matrix products, arithmetic and copies ran while one was open for 8% -> 17% of each run, Pallas kernels for 0% -> 0%
where the time goes in v1:
time: 66.2 us; the launch traced here: 65.6 us
  starting transfers between devices  21.2 us (32%)
  waiting for transfers between devices  15.6 us (24%)
  matrix products  12.4 us (19%)
  other arithmetic  11.8 us (18%)
  local copies, waits for them, and re-layouts  3.61 us (5%)
  between operations  1.08 us (2%)
    ppermute x6, starting transfers between devices, exclusive_scan(): got = lax.ppermute(incl, axis, pairs)  20.5 us
    ppermute x6, waiting for transfers between devices, exclusive_scan(): got = lax.ppermute(incl, axis, pairs)  9.74 us
    dot_general x9, matrix products, conv_apply(): jnp.dot(portion.reshape(-1, channels), kernel[row_tap, col_tap], preferre...  7.26 us
    ppermute x3, waiting for transfers between devices, all_sum(): lax.ppermute(value, axis, [(i, i ^ step) for i in range(count)])  5.83 us
    dot_general x9, matrix products, conv_apply(): lax.dot_general(portion.reshape(-1, channels), kernel[row_tap, col_tap],...  5.09 us
    select_n x2, other arithmetic, exclusive_scan(): incl = jnp.where(has, combine_packed(got, incl), incl)  2.75 us
    another operation x3, other arithmetic, local(): jnp.stack([back_states[t] + back_products[t] * carry_back for t in range(...  1.7 us
    convert_element_type x2, other arithmetic, chan_sum(): return (own + got.astype(jnp.float32)).astype(jnp.bfloat16)  1.37 us
  transfers between devices with their start and end apart: 11, of which 5 were waited for; matrix products, arithmetic and copies ran while one was open for 17% of the time, Pallas kernels for 0%

profile of v1, /device:TPU:0, one launch (start us, length us, event | category | flops | bytes accessed | tf_op | source)
XLA Modules:
  0.0 65.6 jit_solution(13289669403497556891)
XLA Ops:
  2.3 1.3 %pad_slice_fusion.1 = (bf16[4,1,64,512]{3,2,1,0:T(8,128)(2,1)S(1)}, bf16[4,1,64,512]{3,2,1,0:T(8,128)(2,1)S(1)}) fusion(bf16[4,1,64,512]{3,2,1,0:T(8,128)(2,1)} %param.11), kind=kLoop, calls=%fused_computation.15 | loop fusion | bytes 786432 | tf_op jit(solution)/shard_map/slice | solution.py:39
  3.6 1.2 %fusion.6 = f32[256,256]{1,0:T(8,128)S(1)} fusion(bf16[256,512]{1,0:T(8,128)(2,1)S(1)} %bitcast.154, bf16[3,3,256,512]{3,2,1,0:T(8,128)(2,1)} %param.8), kind=kOutput, calls=%fused_computation.29 | convolution fusion | flops 67108864 | bytes 786432 | tf_op jit(solution)/shard_map/dot_general | solution.py:45
  4.8 1.3 %convolution_add_fusion.5 = f32[256,256]{1,0:T(8,128)S(1)} fusion(f32[256,256]{1,0:T(8,128)S(1)} %fusion.6, bf16[256,512]{1,0:T(8,128)(2,1)} %bitcast.156, bf16[3,3,256,512]{3,2,1,0:T(8,128)(2,1)} %param.8), kind=kOutput, calls=%fused_computation.5 | convolution fusion | flops 67174400 | bytes 1048576 | tf_op jit(solution)/shard_map/dot_general | solution.py:45
  6.1 1.2 %convolution_add_fusion.4 = f32[256,256]{1,0:T(8,128)S(1)} fusion(f32[256,256]{1,0:T(8,128)S(1)} %convolution_add_fusion.5, bf16[256,512]{1,0:T(8,128)(2,1)S(1)} %bitcast.160, bf16[3,3,256,512]{3,2,1,0:T(8,128)(2,1)} %param.8), kind=kOutput, calls=%fused_computation.4 | convolution fusion | flops 67174400 | bytes 1048576 | tf_op jit(solution)/shard_map/dot_general | solution.py:45
  8.0 1.3 %collective-permute-start.4 = (f32[65,256]{1,0:T(8,128)S(1)}, f32[65,256]{1,0:T(8,128)S(1)}, u32[]{:S(2)}, u32[]{:S(2)}) collective-permute-start(f32[65,256]{1,0:T(8,128)S(1)} %pad_maximum_fusion.3), channel_id=1, source_target_pairs={{2,0},{4,2},{6,4},{8,6},{10,8},{12,10},{14,12},{3,1},{5,3},{7,5},{... | collective-permute-start | bytes 199688 | tf_op jit(solution)/shard_map/ppermute | solution.py:80
  10.8 5.5 %collective-permute-start = (f32[65,256]{1,0:T(8,128)S(1)}, f32[65,256]{1,0:T(8,128)S(1)}, u32[]{:S(2)}, u32[]{:S(2)}) collective-permute-start(f32[65,256]{1,0:T(8,128)S(1)} %pad_maximum_fusion.2), channel_id=1, source_target_pairs={{0,2},{2,4},{4,6},{6,8},{8,10},{10,12},{12,14},{1,3},{3,5},{5,7},{... | collective-permute-start | bytes 199688 | tf_op jit(solution)/shard_map/ppermute | solution.py:80
  16.9 1.4 %collective-permute-done = f32[65,256]{1,0:T(8,128)S(1)} collective-permute-done((f32[65,256]{1,0:T(8,128)S(1)}, f32[65,256]{1,0:T(8,128)S(1)}, u32[]{:S(2)}, u32[]{:S(2)}) %collective-permute-start) | collective-permute-done | bytes 66592 | tf_op jit(solution)/shard_map/ppermute | solution.py:80
  18.9 1.1 %add_select_fusion.5 = (f32[65,256]{1,0:T(8,128)S(1)}, f32[65,256]{1,0:T(8,128)S(1)}, f32[65,256]{1,0:T(8,128)S(1)}, f32[65,256]{1,0:T(8,128)S(1)}) fusion(f32[65,256]{1,0:T(8,128)} %copy-done.5, f32[256]{0:T(256)S(1)} %bitcast.166, pred[65]{0:T(512)(128)(4,1)} %iota_compare_fusion, pred[]{:T(512)S(6)} %ge.20, f32[64,256]{1,0:T(8,128)S(1)} %get-tuple-element.20, ...), kind=kLoop, calls=%fused_computation.71 | loop fusion | flops 282880 | bytes 534859 | tf_op jit(solution)/shard_map/jit(_where)/select_n | solution.py:84
  20.0 6.6 %collective-permute-start.1 = (f32[65,256]{1,0:T(8,128)S(1)}, f32[65,256]{1,0:T(8,128)S(1)}, u32[]{:S(2)}, u32[]{:S(2)}) collective-permute-start(f32[65,256]{1,0:T(8,128)S(1)} %get-tuple-element.41), channel_id=1, source_target_pairs={{0,4},{2,6},{4,8},{6,10},{8,12},{10,14},{1,5},{3,7},{5,9},{7,11},{... | collective-permute-start | bytes 199688 | tf_op jit(solution)/shard_map/ppermute | solution.py:80
  26.6 1.3 %collective-permute-start.5 = (f32[65,256]{1,0:T(8,128)S(1)}, f32[65,256]{1,0:T(8,128)S(1)}, u32[]{:S(2)}, u32[]{:S(2)}) collective-permute-start(f32[65,256]{1,0:T(8,128)S(1)} %get-tuple-element.55), channel_id=1, source_target_pairs={{4,0},{6,2},{8,4},{10,6},{12,8},{14,10},{5,1},{7,3},{9,5},{11,7},{... | collective-permute-start | bytes 199688 | tf_op jit(solution)/shard_map/ppermute | solution.py:80
  27.9 1.3 %fusion.46 = (f32[256]{0:T(256)}, f32[256]{0:T(256)S(1)}, f32[256]{0:T(256)S(1)}) fusion(f32[256]{0:T(256)} %bitcast.184, f32[256]{0:T(256)S(1)} %bitcast.168, f32[256]{0:T(256)S(1)} %bitcast.173, f32[256]{0:T(256)} %bitcast.182), kind=kLoop, calls=%fused_computation.120 | loop fusion | flops 768 | bytes 7168 | tf_op jit(solution)/shard_map/mul | solution.py:146
  29.2 3.7 %collective-permute-done.5 = f32[65,256]{1,0:T(8,128)S(1)} collective-permute-done((f32[65,256]{1,0:T(8,128)S(1)}, f32[65,256]{1,0:T(8,128)S(1)}, u32[]{:S(2)}, u32[]{:S(2)}) %collective-permute-start.5) | collective-permute-done | bytes 66592 | tf_op jit(solution)/shard_map/ppermute | solution.py:80
  33.5 1.7 %add_select_fusion = (f32[65,256]{1,0:T(8,128)}, f32[65,256]{1,0:T(8,128)S(1)}, f32[65,256]{1,0:T(8,128)S(1)}, f32[65,256]{1,0:T(8,128)}) fusion(f32[65,256]{1,0:T(8,128)S(1)} %get-tuple-element.55, f32[65,256]{1,0:T(8,128)} %copy-done.3, f32[256]{0:T(256)S(1)} %bitcast.188, pred[65]{0:T(512)(128)(4,1)} %iota_compare_fusion, pred[]{:T(512)S(6)} %ge.22, ...), kind=kLoop, calls=%fused_computation.66 | loop fusion | flops 266240 | bytes 669763 | tf_op jit(solution)/shard_map/jit(_where)/select_n | solution.py:84
  35.2 4.5 %collective-permute-start.2 = (f32[65,256]{1,0:T(8,128)}, f32[65,256]{1,0:T(8,128)S(1)}, u32[]{:S(2)}, u32[]{:S(2)}) collective-permute-start(f32[65,256]{1,0:T(8,128)} %get-tuple-element.64), channel_id=1, source_target_pairs={{0,8},{2,10},{4,12},{6,14},{1,9},{3,11},{5,13},{7,15},{16,24},{18,... | collective-permute-start | bytes 199688 | tf_op jit(solution)/shard_map/ppermute | solution.py:80
  39.7 1.3 %collective-permute-start.6 = (f32[65,256]{1,0:T(8,128)}, f32[65,256]{1,0:T(8,128)S(1)}, u32[]{:S(2)}, u32[]{:S(2)}) collective-permute-start(f32[65,256]{1,0:T(8,128)} %get-tuple-element.35), channel_id=1, source_target_pairs={{8,0},{10,2},{12,4},{14,6},{9,1},{11,3},{13,5},{15,7},{24,16},{26,... | collective-permute-start | bytes 199688 | tf_op jit(solution)/shard_map/ppermute | solution.py:80
  42.4 4.7 %collective-permute-done.6 = f32[65,256]{1,0:T(8,128)S(1)} collective-permute-done((f32[65,256]{1,0:T(8,128)}, f32[65,256]{1,0:T(8,128)S(1)}, u32[]{:S(2)}, u32[]{:S(2)}) %collective-permute-start.6) | collective-permute-done | bytes 66592 | tf_op jit(solution)/shard_map/ppermute | solution.py:80
  49.4 1.1 %fusion.20 = f32[256,256]{1,0:T(8,128)S(1)} fusion(bf16[256,256]{1,0:T(8,128)(2,1)S(1)} %bitcast.152, bf16[3,3,256,512]{3,2,1,0:T(8,128)(2,1)} %param.8, s32[]{:T(128)S(6)} %add.218, s32[]{:T(128)S(6)} %select_n.129), kind=kOutput, calls=%fused_computation.54 | convolution fusion | flops 33554432 | bytes 524296 | tf_op jit(solution)/shard_map/dot_general | solution.py:53
  50.5 1.1 %fusion.21 = f32[256,256]{1,0:T(8,128)S(1)} fusion(bf16[256,256]{1,0:T(8,128)(2,1)S(1)} %bitcast.153, bf16[3,3,256,512]{3,2,1,0:T(8,128)(2,1)} %param.8, s32[]{:T(128)S(6)} %add.218, s32[]{:T(128)S(6)} %select_n.128), kind=kOutput, calls=%fused_computation.58 | convolution fusion | flops 33554432 | bytes 524296 | tf_op jit(solution)/shard_map/dot_general | solution.py:53
  52.8 1.1 %convolution_add_fusion.7 = f32[256,256]{1,0:T(8,128)S(1)} fusion(f32[256,256]{1,0:T(8,128)S(1)} %fusion.20, bf16[256,256]{1,0:T(8,128)(2,1)S(1)} %bitcast.142, bf16[3,3,256,512]{3,2,1,0:T(8,128)(2,1)} %param.8, s32[]{:T(128)S(6)} %add.218, s32[]{:T(128)S(6)} %select_n.129), kind=kOutput, calls=%fused_computation.7 | convolution fusion | flops 33619968 | bytes 786440 | tf_op jit(solution)/shard_map/dot_general | solution.py:53
  53.9 1.1 %fusion = bf16[256,256]{1,0:T(8,128)(2,1)S(1)} fusion(f32[256,256]{1,0:T(8,128)S(1)} %convolution_add_fusion.7, bf16[256,256]{1,0:T(8,128)(2,1)S(1)} %bitcast.146, bf16[3,3,256,512]{3,2,1,0:T(8,128)(2,1)} %param.8, s32[]{:T(128)S(6)} %add.218, s32[]{:T(128)S(6)} %add.222, s32[]{:T(128)S(6)} %select_n.129), kind=kOutput, calls=%fused_computation.12 | convolution fusion | flops 33685504 | bytes 655372 | tf_op jit(solution)/shard_map/dot_general | solution.py:53
  55.6 1.1 %convolution_add_fusion.9 = f32[256,256]{1,0:T(8,128)S(1)} fusion(f32[256,256]{1,0:T(8,128)S(1)} %fusion.21, bf16[256,256]{1,0:T(8,128)(2,1)S(1)} %bitcast.143, bf16[3,3,256,512]{3,2,1,0:T(8,128)(2,1)} %param.8, s32[]{:T(128)S(6)} %add.218, s32[]{:T(128)S(6)} %select_n.128), kind=kOutput, calls=%fused_computation.9 | convolution fusion | flops 33619968 | bytes 786440 | tf_op jit(solution)/shard_map/dot_general | solution.py:53
  56.7 2.5 %collective-permute-done.9 = f32[256]{0:T(256)S(1)} collective-permute-done((f32[256]{0:T(256)S(1)}, f32[256]{0:T(256)S(1)}, u32[]{:S(2)}, u32[]{:S(2)}) %collective-permute-start.9) | collective-permute-done | bytes 1056 | tf_op jit(solution)/shard_map/ppermute | solution.py:96
  59.2 1.1 %convolution_add_fusion.8 = f32[256,256]{1,0:T(8,128)S(1)} fusion(f32[256,256]{1,0:T(8,128)S(1)} %convolution_add_fusion.9, bf16[256,256]{1,0:T(8,128)(2,1)S(1)} %bitcast.147, bf16[3,3,256,512]{3,2,1,0:T(8,128)(2,1)} %param.8, s32[]{:T(128)S(6)} %add.218, s32[]{:T(128)S(6)} %add.222, s32[]{:T(128)S(6)} %select_n.128), kind=kOutput, calls=%fused_computation.8 | convolution fusion | flops 33619968 | bytes 786444 | tf_op jit(solution)/shard_map/dot_general | solution.py:53
  60.3 3.4 %collective-permute-done.10 = f32[256]{0:T(256)S(1)} collective-permute-done((f32[256]{0:T(256)S(1)}, f32[256]{0:T(256)S(1)}, u32[]{:S(2)}, u32[]{:S(2)}) %collective-permute-start.10) | collective-permute-done | bytes 1056 | tf_op jit(solution)/shard_map/ppermute | solution.py:96
  (78 shorter events, 12.9 us)
Async XLA Ops:
  0.6 8.7 %copy-start.11 = (f32[256]{0:T(256)S(1)}, f32[256]{0:T(256)}, u32[]{:S(2)}) copy-start(f32[256]{0:T(256)} %param.9) | copy-start | bytes 3076
  0.6 9.3 %copy-start = (bf16[4,1,64,512]{3,2,1,0:T(8,128)(2,1)S(1)}, bf16[4,1,64,512]{3,2,1,0:T(8,128)(2,1)}, u32[]{:S(2)}) copy-start(bf16[4,1,64,512]{3,2,1,0:T(8,128)(2,1)} %param.6) | copy-start | bytes 786436
  2.3 7.6 %copy-start.8 = (f32[1,256]{1,0:T(1,128)}, f32[1,256]{1,0:T(1,128)S(1)}, u32[]{:S(2)}) copy-start(f32[1,256]{1,0:T(1,128)S(1)} %get-tuple-element.46) | copy-start | bytes 3076
  2.3 7.6 %copy-start.9 = (f32[1,256]{1,0:T(1,128)}, f32[1,256]{1,0:T(1,128)S(1)}, u32[]{:S(2)}) copy-start(f32[1,256]{1,0:T(1,128)S(1)} %get-tuple-element.48) | copy-start | bytes 3076
  2.3 7.8 %copy-start.1 = (bf16[3,3,512,256]{3,2,1,0:T(8,128)(2,1)S(1)}, bf16[3,3,512,256]{3,2,1,0:T(8,128)(2,1)}, u32[]{:S(2)}) copy-start(bf16[3,3,512,256]{3,2,1,0:T(8,128)(2,1)} %param.7) | copy-start | bytes 7077892
  8.0 8.9 %collective-permute-start.4 = (f32[65,256]{1,0:T(8,128)S(1)}, f32[65,256]{1,0:T(8,128)S(1)}, u32[]{:S(2)}, u32[]{:S(2)}) collective-permute-start(f32[65,256]{1,0:T(8,128)S(1)} %pad_maximum_fusion.3), channel_id=1, source_target_pairs={{2,0},{4,2},{6,4},{8,6},{10,8},{12,10},{14,12},{3,1},{5,3},{7,5},{... | collective-permute-start | bytes 199688 | tf_op jit(solution)/shard_map/ppermute | solution.py:80
  9.9 0.9 %copy-start.6 = (f32[1,256]{1,0:T(1,128)}, f32[1,256]{1,0:T(1,128)S(1)}, u32[]{:S(2)}) copy-start(f32[1,256]{1,0:T(1,128)S(1)} %get-tuple-element.50) | copy-start | bytes 3076
  9.9 0.9 %copy-start.7 = (f32[1,256]{1,0:T(1,128)}, f32[1,256]{1,0:T(1,128)S(1)}, u32[]{:S(2)}) copy-start(f32[1,256]{1,0:T(1,128)S(1)} %get-tuple-element.52) | copy-start | bytes 3076
  10.8 7.4 %collective-permute-start = (f32[65,256]{1,0:T(8,128)S(1)}, f32[65,256]{1,0:T(8,128)S(1)}, u32[]{:S(2)}, u32[]{:S(2)}) collective-permute-start(f32[65,256]{1,0:T(8,128)S(1)} %pad_maximum_fusion.2), channel_id=1, source_target_pairs={{0,2},{2,4},{4,6},{6,8},{8,10},{10,12},{12,14},{1,3},{3,5},{5,7},{... | collective-permute-start | bytes 199688 | tf_op jit(solution)/shard_map/ppermute | solution.py:80
  16.9 1.4 %copy-start.4 = (f32[65,256]{1,0:T(8,128)}, f32[65,256]{1,0:T(8,128)S(1)}, u32[]{:S(2)}) copy-start(f32[65,256]{1,0:T(8,128)S(1)} %collective-permute-done.4) | copy-start | bytes 199684
  18.3 0.6 copy-start.5
  20.0 9.2 %collective-permute-start.1 = (f32[65,256]{1,0:T(8,128)S(1)}, f32[65,256]{1,0:T(8,128)S(1)}, u32[]{:S(2)}, u32[]{:S(2)}) collective-permute-start(f32[65,256]{1,0:T(8,128)S(1)} %get-tuple-element.41), channel_id=1, source_target_pairs={{0,4},{2,6},{4,8},{6,10},{8,12},{10,14},{1,5},{3,7},{5,9},{7,11},{... | collective-permute-start | bytes 199688 | tf_op jit(solution)/shard_map/ppermute | solution.py:80
  26.6 6.2 %collective-permute-start.5 = (f32[65,256]{1,0:T(8,128)S(1)}, f32[65,256]{1,0:T(8,128)S(1)}, u32[]{:S(2)}, u32[]{:S(2)}) collective-permute-start(f32[65,256]{1,0:T(8,128)S(1)} %get-tuple-element.55), channel_id=1, source_target_pairs={{4,0},{6,2},{8,4},{10,6},{12,8},{14,10},{5,1},{7,3},{9,5},{11,7},{... | collective-permute-start | bytes 199688 | tf_op jit(solution)/shard_map/ppermute | solution.py:80
  29.2 3.7 %copy-start.2 = (f32[65,256]{1,0:T(8,128)}, f32[65,256]{1,0:T(8,128)S(1)}, u32[]{:S(2)}) copy-start(f32[65,256]{1,0:T(8,128)S(1)} %collective-permute-done.1) | copy-start | bytes 199684
  32.9 0.6 copy-start.3
  35.2 7.2 %collective-permute-start.2 = (f32[65,256]{1,0:T(8,128)}, f32[65,256]{1,0:T(8,128)S(1)}, u32[]{:S(2)}, u32[]{:S(2)}) collective-permute-start(f32[65,256]{1,0:T(8,128)} %get-tuple-element.64), channel_id=1, source_target_pairs={{0,8},{2,10},{4,12},{6,14},{1,9},{3,11},{5,13},{7,15},{16,24},{18,... | collective-permute-start | bytes 199688 | tf_op jit(solution)/shard_map/ppermute | solution.py:80
  39.7 7.4 %collective-permute-start.6 = (f32[65,256]{1,0:T(8,128)}, f32[65,256]{1,0:T(8,128)S(1)}, u32[]{:S(2)}, u32[]{:S(2)}) collective-permute-start(f32[65,256]{1,0:T(8,128)} %get-tuple-element.35), channel_id=1, source_target_pairs={{8,0},{10,2},{12,4},{14,6},{9,1},{11,3},{13,5},{15,7},{24,16},{26,... | collective-permute-start | bytes 199688 | tf_op jit(solution)/shard_map/ppermute | solution.py:80
  48.7 2.9 %copy-start.10 = (f32[256]{0:T(256)S(1)}, f32[256]{0:T(256)}, u32[]{:S(2)}) copy-start(f32[256]{0:T(256)} %get-tuple-element.56) | copy-start | bytes 3076
  51.7 3.9 %collective-permute-start.8 = (f32[256]{0:T(256)S(1)}, f32[256]{0:T(256)S(1)}, u32[]{:S(2)}, u32[]{:S(2)}) collective-permute-start(f32[256]{0:T(256)S(1)} %fusion.3), channel_id=1, source_target_pairs={{0,2},{2,0},{4,6},{6,4},{8,10},{10,8},{12,14},{14,12},{1,3},{3,1},... | collective-permute-start | bytes 3080 | tf_op jit(solution)/shard_map/ppermute | solution.py:96
  52.3 11.9 %collective-permute-start.7 = (bf16[4,1,64,256]{3,2,1,0:T(8,128)(2,1)S(1)}, bf16[4,1,64,256]{3,2,1,0:T(8,128)(2,1)S(1)}, u32[]{:S(2)}, u32[]{:S(2)}) collective-permute-start(bf16[4,1,64,256]{3,2,1,0:T(8,128)(2,1)S(1)} %bitcast.163), channel_id=1, source_target_pairs={{0,1},{1,0},{2,3},{3,2},{4,5},{5,4},{6,7},{7,6},{8,9},{9,8},{10,11... | collective-permute-start | bytes 393224 | tf_op jit(solution)/shard_map/ppermute | solution.py:112
  55.0 9.9 %collective-permute-start.3 = (bf16[4,1,64,256]{3,2,1,0:T(8,128)(2,1)S(1)}, bf16[4,1,64,256]{3,2,1,0:T(8,128)(2,1)S(1)}, u32[]{:S(2)}, u32[]{:S(2)}) collective-permute-start(bf16[4,1,64,256]{3,2,1,0:T(8,128)(2,1)S(1)} %bitcast.164), channel_id=1, source_target_pairs={{0,1},{1,0},{2,3},{3,2},{4,5},{5,4},{6,7},{7,6},{8,9},{9,8},{10,11... | collective-permute-start | bytes 393224 | tf_op jit(solution)/shard_map/ppermute | solution.py:112
  55.6 3.6 %collective-permute-start.9 = (f32[256]{0:T(256)S(1)}, f32[256]{0:T(256)S(1)}, u32[]{:S(2)}, u32[]{:S(2)}) collective-permute-start(f32[256]{0:T(256)S(1)} %add.215), channel_id=1, source_target_pairs={{0,4},{2,6},{4,0},{6,2},{8,12},{10,14},{12,8},{14,10},{1,5},{3,7},... | collective-permute-start | bytes 3080 | tf_op jit(solution)/shard_map/ppermute | solution.py:96
  59.2 4.5 %collective-permute-start.10 = (f32[256]{0:T(256)S(1)}, f32[256]{0:T(256)S(1)}, u32[]{:S(2)}, u32[]{:S(2)}) collective-permute-start(f32[256]{0:T(256)S(1)} %add.216), channel_id=1, source_target_pairs={{0,8},{2,10},{4,12},{6,14},{8,0},{10,2},{12,4},{14,6},{1,9},{3,11}... | collective-permute-start | bytes 3080 | tf_op jit(solution)/shard_map/ppermute | solution.py:96

commit v2 on v1

v2 whole, which is shorter than its diff:
```python
import math

import jax
import jax.numpy as jnp
from jax import lax
from jax.sharding import PartitionSpec as P


def row_halo(cells):
    count = lax.axis_size("rows")
    if count == 1:
        return None
    ends = count - 1
    head = cells[:, :1]
    tail = cells[:, -1:]
    top = lax.ppermute(tail, "rows", [(i, i + 1) for i in range(ends)])
    bottom = lax.ppermute(head, "rows", [(i + 1, i) for i in range(ends)])
    return top, bottom


def row_taps_of(halo, row_count):
    return (1,) if halo is None and row_count == 1 else (0, 1, 2)


def prep_kernel(kernel, transpose, row_taps):
    if transpose:
        flipped = kernel[::-1, ::-1]
        taps = jnp.stack([flipped[a] for a in row_taps])
        taps = jnp.swapaxes(taps, 2, 3)
    else:
        taps = jnp.stack([kernel[a] for a in row_taps])
    return lax.optimization_barrier(taps)


def conv_apply(cells, halo, taps, row_taps):
    frame_count, row_count, col_count, channels = cells.shape
    if len(row_taps) == 1:
        extended = jnp.pad(cells, ((0, 0), (1, 1), (0, 0), (0, 0)))
    else:
        if halo is None:
            zero = jnp.zeros_like(cells[:, :1])
            halo = (zero, zero)
        extended = jnp.concatenate([halo[0], cells, halo[1]], axis=1)
    padded = jnp.pad(extended, ((0, 0), (0, 0), (1, 1), (0, 0)))
    summed = None
    for index, row_tap in enumerate(row_taps):
        for col_tap in range(3):
            portion = padded[:, row_tap : row_tap + row_count, col_tap : col_tap + col_count, :]
            term = jnp.dot(
                portion.reshape(-1, channels),
                taps[index, col_tap],
                preferred_element_type=jnp.float32,
            )
            summed = term if summed is None else summed + term
    return summed.reshape(frame_count, row_count, col_count, -1)


def all_sum(value, axis):
    count = lax.axis_size(axis)
    if count == 1:
        return value
    if count & (count - 1) == 0:
        step = 1
        while step < count:
            value = value + lax.ppermute(value, axis, [(i, i ^ step) for i in range(count)])
            step *= 2
        return value
    return lax.psum(value, axis)


def chan_sum(cells, halo, taps, row_taps):
    count = lax.axis_size("chan")
    mine = lax.axis_index("chan")
    width = taps.shape[3] // count
    if count != 2:
        part = conv_apply(cells, halo, taps, row_taps)
        return lax.psum_scatter(part.astype(jnp.bfloat16), "chan", scatter_dimension=3, tiled=True)
    other_taps = lax.dynamic_slice_in_dim(taps, (1 - mine) * width, width, axis=3)
    own_taps = lax.dynamic_slice_in_dim(taps, mine * width, width, axis=3)
    other = conv_apply(cells, halo, other_taps, row_taps).astype(jnp.bfloat16)
    got = lax.ppermute(other, "chan", [(0, 1), (1, 0)])
    own = conv_apply(cells, halo, own_taps, row_taps)
    return (own + got.astype(jnp.float32)).astype(jnp.bfloat16)


def block_carries(fwd_end, bwd_start, fwd_prod, bwd_prod, axis):
    count = lax.axis_size(axis)
    mine = lax.axis_index(axis)
    received = {}
    for step in range(1, count):
        message = jnp.where(mine + step < count, fwd_end, bwd_start)
        received[step] = lax.ppermute(message, axis, [(i, (i + step) % count) for i in range(count)])
    carry_in = jnp.zeros_like(fwd_end)
    for step in reversed(range(1, count)):
        source = mine - step
        factor = lax.dynamic_index_in_dim(fwd_prod, jnp.maximum(source, 0), 0, keepdims=False)
        carry_in = jnp.where(source >= 0, received[step], 0.0) + factor * carry_in
    carry_back = jnp.zeros_like(bwd_start)
    for step in reversed(range(1, count)):
        source = mine + step
        factor = lax.dynamic_index_in_dim(bwd_prod, jnp.minimum(source, count - 1), 0, keepdims=False)
        carry_back = jnp.where(source < count, received[count - step], 0.0) + factor * carry_back
    return carry_in, carry_back


def local(frames_in, in_kernel, out_kernel, decay_rate, frame_keep, out_grad):
    frame_count, row_count, col_count = frames_in.shape[:3]
    position = lax.axis_index("tm")
    blocks = lax.axis_size("tm")
    in_halo = row_halo(frames_in)
    grad_halo = row_halo(out_grad)
    row_taps = row_taps_of(in_halo, row_count)
    values = conv_apply(frames_in, in_halo, prep_kernel(in_kernel, False, row_taps), row_taps)
    adjoint_in = conv_apply(out_grad, grad_halo, prep_kernel(out_kernel, True, row_taps), row_taps)
    input_gain = jnp.sqrt(1.0 - decay_rate * decay_rate)
    keep_padded = jnp.concatenate([frame_keep, jnp.zeros((1,), jnp.float32)])
    offset = position * frame_count
    keep_here = lax.dynamic_slice_in_dim(keep_padded, offset, frame_count)
    keep_next = lax.dynamic_slice_in_dim(keep_padded, offset + 1, frame_count)
    decays = keep_here[:, None] * decay_rate[None, :]
    decays_next = keep_next[:, None] * decay_rate[None, :]

    running = None
    product = None
    local_states, products = [], []
    for t in range(frame_count):
        fresh = input_gain * values[t]
        running = fresh if running is None else decays[t] * running + fresh
        product = decays[t] if product is None else product * decays[t]
        local_states.append(running)
        products.append(product)
    running = None
    product = None
    back_states, back_products = [None] * frame_count, [None] * frame_count
    for t in reversed(range(frame_count)):
        running = adjoint_in[t] if running is None else adjoint_in[t] + decays_next[t] * running
        product = decays_next[t] if product is None else product * decays_next[t]
        back_states[t] = running
        back_products[t] = product

    all_decays = (frame_keep[:, None] * decay_rate[None, :]).reshape(blocks, frame_count, -1)
    all_next = (keep_padded[1:, None] * decay_rate[None, :]).reshape(blocks, frame_count, -1)
    fwd_prod = all_decays[:, 0]
    for t in range(1, frame_count):
        fwd_prod = fwd_prod * all_decays[:, t]
    bwd_prod = all_next[:, frame_count - 1]
    for t in reversed(range(frame_count - 1)):
        bwd_prod = bwd_prod * all_next[:, t]
    carry_in, carry_back = block_carries(local_states[-1], back_states[0], fwd_prod, bwd_prod, "tm")

    states = jnp.stack([local_states[t] + products[t] * carry_in for t in range(frame_count)])
    adjoints = jnp.stack([back_states[t] + back_products[t] * carry_back for t in range(frame_count)])
    previous = jnp.concatenate([carry_in[None], states[:-1]], axis=0)
    terms = adjoints * (
        decays[:, None, None, :] * previous - decay_rate * decay_rate / input_gain * values
    )
    total_count = frame_count * blocks * row_count * lax.axis_size("rows") * col_count
    grad_decay = all_sum(all_sum(jnp.sum(terms, axis=(0, 1, 2)), "tm"), "rows") / math.sqrt(total_count)

    state_b = states.astype(jnp.bfloat16)
    adjoint_b = adjoints.astype(jnp.bfloat16)
    mixed = chan_sum(state_b, row_halo(state_b), prep_kernel(out_kernel, False, row_taps), row_taps)
    grad_in = chan_sum(adjoint_b, row_halo(adjoint_b), prep_kernel(in_kernel, True, row_taps), row_taps)
    return (mixed, grad_in, grad_decay)


def solution(mesh):
    placed = (
        P(("grp", "tm"), "rows", None, None),
        P(None, None, None, "chan"),
        P(None, None, "chan", None),
        P("chan"),
        P("grp"),
        P(("grp", "tm"), "rows", None, None),
    )
    return jax.shard_map(
        local,
        mesh=mesh,
        in_specs=placed,
        out_specs=(
            P(("grp", "tm"), "rows", None, "chan"),
            P(("grp", "tm"), "rows", None, "chan"),
            P(("grp", "chan")),
        ),
        check_vma=False,
    )
```

time: 66.2 us -> 51.9 us (0.78)
  starting transfers between devices: 21.2 us -> 13.6 us
  matrix products: 12.4 us -> 4.93 us
  local copies, waits for them, and re-layouts: 3.61 us -> 9.78 us
  other arithmetic: 11.8 us -> 6.74 us
    ppermute x6 -> x7, starting transfers between devices: 20.5 us -> 12.9 us  [block_carries(): lax.ppermute(message, axis, [(i, (i + step) % count) for i in range(count)])]
    dot_general x18, matrix products: 12.4 us -> 4.93 us  [conv_apply(): jnp.dot(portion.reshape(-1, channels), taps[index, col_tap], preferred_el...]
    ppermute x6 -> x7, waiting for transfers between devices: 9.74 us -> 6.27 us  [block_carries(): lax.ppermute(message, axis, [(i, (i + step) % count) for i in range(count)])]
    ppermute x3, waiting for transfers between devices: 5.83 us -> 9.19 us  [all_sum(): lax.ppermute(value, axis, [(i, i ^ step) for i in range(count)])]
    slice x2 -> x4, local copies, waits for them, and re-layouts: 0.16 us -> 2.8 us  [conv_apply(): padded[:, row_tap:row_tap + row_count, col_tap:col_tap + col_count, :]]
    slice x9 -> x4, local copies, waits for them, and re-layouts: 2.06 us -> 4.25 us  [the longest x1 1.24 us: local(): keep_padded[1:, None] * decay_rate[None, :]]
    mul x0 -> x2, local copies, waits for them, and re-layouts: none -> 2.03 us  [the longest x1 1.32 us: local(): frame_keep[:, None] * decay_rate[None, :]]
    select_n x3 -> x2, other arithmetic: 2.76 us -> 0.8 us  [block_carries(): message = jnp.where(mine + step < count, fwd_end, bwd_start)]
  transfers between devices with their start and end apart: 11 -> 12, of which waited for: 5 -> 5; matrix products, arithmetic and copies ran while one was open for 17% -> 17% of each run, Pallas kernels for 0% -> 0%
where the time goes in v2:
time: 51.9 us; the launch traced here: 51.6 us
  waiting for transfers between devices  15.5 us (30%)
  starting transfers between devices  13.6 us (26%)
  local copies, waits for them, and re-layouts  9.78 us (19%)
  other arithmetic  6.74 us (13%)
  matrix products  4.93 us (9%)
  between operations  1.07 us (2%)
    ppermute x7, starting transfers between devices, block_carries(): lax.ppermute(message, axis, [(i, (i + step) % count) for i in range(count)])  12.9 us
    ppermute x3, waiting for transfers between devices, all_sum(): lax.ppermute(value, axis, [(i, i ^ step) for i in range(count)])  9.19 us
    ppermute x7, waiting for transfers between devices, block_carries(): lax.ppermute(message, axis, [(i, (i + step) % count) for i in range(count)])  6.27 us
    dot_general x18, matrix products, conv_apply(): jnp.dot(portion.reshape(-1, channels), taps[index, col_tap], preferred_el...  4.93 us
    slice x4, local copies, waits for them, and re-layouts, conv_apply(): padded[:, row_tap:row_tap + row_count, col_tap:col_tap + col_count, :]  2.8 us
    convert_element_type x2, other arithmetic, chan_sum(): return (own + got.astype(jnp.float32)).astype(jnp.bfloat16)  1.37 us
    mul x1, local copies, waits for them, and re-layouts, local(): frame_keep[:, None] * decay_rate[None, :]  1.32 us
    slice x1, local copies, waits for them, and re-layouts, local(): keep_padded[1:, None] * decay_rate[None, :]  1.24 us
  transfers between devices with their start and end apart: 12, of which 5 were waited for; matrix products, arithmetic and copies ran while one was open for 17% of the time, Pallas kernels for 0%

profile of v2, /device:TPU:0, one launch (start us, length us, event | category | flops | bytes accessed | tf_op | source)
XLA Modules:
  0.0 51.6 jit_solution(5626355559471688107)
XLA Ops:
  0.6 1.2 %slice.198 = bf16[1,3,512,256]{3,2,1,0:T(8,128)(2,1)S(1)} slice(bf16[3,3,512,256]{3,2,1,0:T(8,128)(2,1)} %param.7), slice={[1:2], [0:3], [0:512], [0:256]} | slice | bytes 1572864 | tf_op jit(solution)/shard_map/slice | solution.py:31
  1.9 1.9 %pad_slice_fusion.3 = (bf16[4,1,64,512]{3,2,1,0:T(8,128)(2,1)}, bf16[4,1,64,512]{3,2,1,0:T(8,128)(2,1)S(1)}) fusion(bf16[4,1,64,512]{3,2,1,0:T(8,128)(2,1)} %param.6), kind=kLoop, calls=%fused_computation.17 | loop fusion | bytes 786432 | tf_op jit(solution)/shard_map/slice | solution.py:48
  3.8 1.2 %slice.212 = bf16[1,3,256,512]{3,2,1,0:T(8,128)(2,1)S(1)} slice(bf16[3,3,256,512]{3,2,1,0:T(8,128)(2,1)} %param.8), slice={[1:2], [0:3], [0:256], [0:512]} | slice | bytes 1572864 | tf_op jit(solution)/shard_map/slice | solution.py:28
  5.1 0.8 %pad_slice_fusion.1 = (bf16[4,1,64,512]{3,2,1,0:T(8,128)(2,1)}, bf16[4,1,64,512]{3,2,1,0:T(8,128)(2,1)S(1)}) fusion(bf16[4,1,64,512]{3,2,1,0:T(8,128)(2,1)S(1)} %copy-done.1), kind=kLoop, calls=%fused_computation.15 | loop fusion | bytes 786432 | tf_op jit(solution)/shard_map/slice | solution.py:48
  8.2 1.2 %convolution_add_fusion.10 = f32[256,256]{1,0:T(8,128)S(1)} fusion(f32[256,256]{1,0:T(8,128)S(1)} %convolution_add_fusion.11, bf16[256,512]{1,0:T(8,128)(2,1)} %bitcast.218, bf16[1,3,512,256]{3,2,1,0:T(8,128)(2,1)S(1)} %slice.198), kind=kOutput, calls=%fused_computation.10 | convolution fusion | flops 67174400 | bytes 1048576 | tf_op jit(solution)/shard_map/dot_general | solution.py:49
  10.3 0.7 %select_bitcast_fusion.5 = (f32[1,64,256]{2,1,0:T(8,128)}, f32[1,64,256]{2,1,0:T(8,128)}, f32[1,64,256]{2,1,0:T(8,128)}, f32[1,64,256]{2,1,0:T(8,128)}, f32[1,64,256]{2,1,0:T(8,128)}, /*index=5*/f32[1,64,256]{2,1,0:T(8,128)}) fusion(f32[64,256]{1,0:T(8,128)S(1)} %get-tuple-element.21, f32[64,256]{1,0:T(8,128)S(1)} %get-tuple-element.19, pred[]{:T(512)S(6)} %lt.74, ...), kind=kLoop, calls=%fused_computation.89 | loop fusion | flops 98304 | bytes 524294 | tf_op jit(solution)/shard_map/jit(_where)/select_n | solution.py:91
  11.0 3.0 %collective-permute-start.1 = (f32[1,64,256]{2,1,0:T(8,128)}, f32[1,64,256]{2,1,0:T(8,128)S(1)}, u32[]{:S(2)}, u32[]{:S(2)}) collective-permute-start(f32[1,64,256]{2,1,0:T(8,128)} %get-tuple-element.36), channel_id=1, source_target_pairs={{0,4},{2,6},{4,8},{6,10},{8,12},{10,14},{12,0},{14,2},{1,5},{3,7},... | collective-permute-start | bytes 196616 | tf_op jit(solution)/shard_map/ppermute | solution.py:92
  14.1 2.5 %collective-permute-start.2 = (f32[1,64,256]{2,1,0:T(8,128)}, f32[1,64,256]{2,1,0:T(8,128)S(1)}, u32[]{:S(2)}, u32[]{:S(2)}) collective-permute-start(f32[1,64,256]{2,1,0:T(8,128)} %get-tuple-element.41), channel_id=1, source_target_pairs={{0,6},{2,8},{4,10},{6,12},{8,14},{10,0},{12,2},{14,4},{1,7},{3,9},... | collective-permute-start | bytes 196616 | tf_op jit(solution)/shard_map/ppermute | solution.py:92
  16.6 1.2 %collective-permute-start.3 = (f32[1,64,256]{2,1,0:T(8,128)}, f32[1,64,256]{2,1,0:T(8,128)S(1)}, u32[]{:S(2)}, u32[]{:S(2)}) collective-permute-start(f32[1,64,256]{2,1,0:T(8,128)} %get-tuple-element.40), channel_id=1, source_target_pairs={{0,8},{2,10},{4,12},{6,14},{8,0},{10,2},{12,4},{14,6},{1,9},{3,11}... | collective-permute-start | bytes 196616 | tf_op jit(solution)/shard_map/ppermute | solution.py:92
  17.8 2.7 %collective-permute-start.4 = (f32[1,64,256]{2,1,0:T(8,128)}, f32[1,64,256]{2,1,0:T(8,128)S(1)}, u32[]{:S(2)}, u32[]{:S(2)}) collective-permute-start(f32[1,64,256]{2,1,0:T(8,128)} %get-tuple-element.39), channel_id=1, source_target_pairs={{0,10},{2,12},{4,14},{6,0},{8,2},{10,4},{12,6},{14,8},{1,11},{3,13... | collective-permute-start | bytes 196616 | tf_op jit(solution)/shard_map/ppermute | solution.py:92
  20.5 1.3 %collective-permute-start.5 = (f32[1,64,256]{2,1,0:T(8,128)}, f32[1,64,256]{2,1,0:T(8,128)S(1)}, u32[]{:S(2)}, u32[]{:S(2)}) collective-permute-start(f32[1,64,256]{2,1,0:T(8,128)} %get-tuple-element.38), channel_id=1, source_target_pairs={{0,12},{2,14},{4,0},{6,2},{8,4},{10,6},{12,8},{14,10},{1,13},{3,15... | collective-permute-start | bytes 196616 | tf_op jit(solution)/shard_map/ppermute | solution.py:92
  21.8 1.2 %slice.238 = f32[32]{0:T(128)} slice(f32[33]{0:T(128)} %copy-done.10), slice={[1:33]} | slice | bytes 256 | tf_op jit(solution)/shard_map/slice | solution.py:142
  23.1 1.3 %mul.533 = f32[8,4]{1,0:T(8,128)} reshape(f32[32]{0:T(128)} %param.10) | data formatting | bytes 256 | tf_op jit(solution)/shard_map/mul | solution.py:141
  24.5 0.7 %mul.577 = f32[8,4]{1,0:T(8,128)S(1)} reshape(f32[32]{0:T(128)} %slice.238) | data formatting | bytes 256 | tf_op jit(solution)/shard_map/mul | solution.py:142
  25.2 0.7 %fusion.37 = (f32[256]{0:T(256)S(1)}, f32[256]{0:T(256)S(1)}, f32[256]{0:T(256)S(1)}) fusion(f32[256]{0:T(256)} %bitcast.241, f32[256]{0:T(256)S(1)} %bitcast.228, f32[256]{0:T(256)} %bitcast.232, f32[256]{0:T(256)} %bitcast.239), kind=kLoop, calls=%fused_computation.135 | loop fusion | flops 768 | bytes 7168 | tf_op jit(solution)/shard_map/mul | solution.py:137
  25.9 0.7 %fusion.44 = (f32[256]{0:T(256)S(1)}, f32[256]{0:T(256)S(1)}, f32[256]{0:T(256)S(1)}) fusion(f32[256]{0:T(256)} %bitcast.235, f32[256]{0:T(256)S(1)} %bitcast.225, f32[256]{0:T(256)} %bitcast.230, f32[256]{0:T(256)} %bitcast.237), kind=kLoop, calls=%fused_computation.139 | loop fusion | flops 768 | bytes 7168 | tf_op jit(solution)/shard_map/mul | solution.py:129
  26.6 0.8 %broadcast_multiply_fusion = (f32[8,4,256]{2,1,0:T(4,128)S(1)}, f32[8,4,256]{2,1,0:T(4,128)S(1)}) fusion(f32[8,4]{1,0:T(8,128)S(1)} %mul.577, f32[256]{0:T(256)} %param.9, f32[8,4]{1,0:T(8,128)} %mul.533), kind=kLoop, calls=%fused_computation.92 | loop fusion | flops 16384 | bytes 66816 | tf_op jit(solution)/shard_map/mul | solution.py:142
  27.5 1.4 %collective-permute-start.6 = (f32[1,64,256]{2,1,0:T(8,128)}, f32[1,64,256]{2,1,0:T(8,128)S(1)}, u32[]{:S(2)}, u32[]{:S(2)}) collective-permute-start(f32[1,64,256]{2,1,0:T(8,128)} %get-tuple-element.37), channel_id=1, source_target_pairs={{0,14},{2,0},{4,2},{6,4},{8,6},{10,8},{12,10},{14,12},{1,15},{3,1}... | collective-permute-start | bytes 196616 | tf_op jit(solution)/shard_map/ppermute | solution.py:92
  29.6 2.4 %collective-permute-done.6 = f32[1,64,256]{2,1,0:T(8,128)S(1)} collective-permute-done((f32[1,64,256]{2,1,0:T(8,128)}, f32[1,64,256]{2,1,0:T(8,128)S(1)}, u32[]{:S(2)}, u32[]{:S(2)}) %collective-permute-start.6) | collective-permute-done | bytes 65568 | tf_op jit(solution)/shard_map/ppermute | solution.py:92
  32.0 3.9 %collective-permute-done = f32[1,64,256]{2,1,0:T(8,128)S(1)} collective-permute-done((f32[1,64,256]{2,1,0:T(8,128)S(1)}, f32[1,64,256]{2,1,0:T(8,128)S(1)}, u32[]{:S(2)}, u32[]{:S(2)}) %collective-permute-start) | collective-permute-done | bytes 65568 | tf_op jit(solution)/shard_map/ppermute | solution.py:92
  35.9 0.7 %fusion.15 = (f32[1,1,64,256]{3,2,1,0:T(8,128)S(1)}, f32[1,1,64,256]{3,2,1,0:T(8,128)S(1)}, f32[1,1,64,256]{3,2,1,0:T(8,128)S(1)}) fusion(f32[1,64,256]{2,1,0:T(8,128)S(1)} %get-tuple-element.4, f32[256]{0:T(256)S(1)} %get-tuple-element.6, f32[64,256]{1,0:T(8,128)S(1)} %get-tuple-element.20, f32[256]{0:T(256)S(1)} %bitcast.229, ...), kind=kLoop, calls=%fused_computation.71 | loop fusion | flops 131072 | bytes 462848 | tf_op jit(solution)/shard_map/stack | solution.py:152
  40.0 1.6 %collective-permute-done.9 = f32[256]{0:T(256)S(1)} collective-permute-done((f32[256]{0:T(256)S(1)}, f32[256]{0:T(256)S(1)}, u32[]{:S(2)}, u32[]{:S(2)}) %collective-permute-start.9) | collective-permute-done | bytes 1056 | tf_op jit(solution)/shard_map/ppermute | solution.py:65
  41.8 3.4 %collective-permute-done.10 = f32[256]{0:T(256)S(1)} collective-permute-done((f32[256]{0:T(256)S(1)}, f32[256]{0:T(256)S(1)}, u32[]{:S(2)}, u32[]{:S(2)}) %collective-permute-start.10) | collective-permute-done | bytes 1056 | tf_op jit(solution)/shard_map/ppermute | solution.py:65
  45.4 4.3 %collective-permute-done.11 = f32[256]{0:T(256)S(1)} collective-permute-done((f32[256]{0:T(256)S(1)}, f32[256]{0:T(256)S(1)}, u32[]{:S(2)}, u32[]{:S(2)}) %collective-permute-start.11) | collective-permute-done | bytes 1056 | tf_op jit(solution)/shard_map/ppermute | solution.py:65
  (80 shorter events, 9.6 us)
Async XLA Ops:
  1.8 3.2 %copy-start.1 = (bf16[4,1,64,512]{3,2,1,0:T(8,128)(2,1)S(1)}, bf16[4,1,64,512]{3,2,1,0:T(8,128)(2,1)}, u32[]{:S(2)}) copy-start(bf16[4,1,64,512]{3,2,1,0:T(8,128)(2,1)} %param.11) | copy-start | bytes 786436
  1.8 4.0 %copy-start.3 = (f32[256]{0:T(256)S(1)}, f32[256]{0:T(256)}, u32[]{:S(2)}) copy-start(f32[256]{0:T(256)} %param.9) | copy-start | bytes 3076
  1.9 4.6 %copy-start.11 = (f32[32]{0:T(128)S(1)}, f32[32]{0:T(128)}, u32[]{:S(2)}) copy-start(f32[32]{0:T(128)} %param.10) | copy-start | bytes 388
  3.8 4.2 %copy-start = (bf16[4,1,64,512]{3,2,1,0:T(8,128)(2,1)S(1)}, bf16[4,1,64,512]{3,2,1,0:T(8,128)(2,1)}, u32[]{:S(2)}) copy-start(bf16[4,1,64,512]{3,2,1,0:T(8,128)(2,1)} %param.6) | copy-start | bytes 786436
  6.5 0.5 %copy-start.10 = (f32[33]{0:T(128)}, f32[33]{0:T(128)S(1)}, u32[]{:S(2)}) copy-start(f32[33]{0:T(128)S(1)} %pad_maximum_fusion.2) | copy-start | bytes 400
  7.7 2.5 %copy-start.5 = (f32[1,256]{1,0:T(1,128)}, f32[1,256]{1,0:T(1,128)S(1)}, u32[]{:S(2)}) copy-start(f32[1,256]{1,0:T(1,128)S(1)} %get-tuple-element.74) | copy-start | bytes 3076
  7.7 2.5 %copy-start.6 = (f32[1,256]{1,0:T(1,128)}, f32[1,256]{1,0:T(1,128)S(1)}, u32[]{:S(2)}) copy-start(f32[1,256]{1,0:T(1,128)S(1)} %get-tuple-element.76) | copy-start | bytes 3076
  7.7 2.5 %copy-start.7 = (f32[1,256]{1,0:T(1,128)}, f32[1,256]{1,0:T(1,128)S(1)}, u32[]{:S(2)}) copy-start(f32[1,256]{1,0:T(1,128)S(1)} %get-tuple-element.58) | copy-start | bytes 3076
  7.7 2.5 %copy-start.8 = (f32[1,256]{1,0:T(1,128)}, f32[1,256]{1,0:T(1,128)S(1)}, u32[]{:S(2)}) copy-start(f32[1,256]{1,0:T(1,128)S(1)} %get-tuple-element.60) | copy-start | bytes 3076
  7.7 2.2 %copy-start.2 = (bf16[4,1,64,512]{3,2,1,0:T(8,128)(2,1)S(1)}, bf16[4,1,64,512]{3,2,1,0:T(8,128)(2,1)}, u32[]{:S(2)}) copy-start(bf16[4,1,64,512]{3,2,1,0:T(8,128)(2,1)} %get-tuple-element.25) | copy-start | bytes 786436
  11.0 16.4 %collective-permute-start.1 = (f32[1,64,256]{2,1,0:T(8,128)}, f32[1,64,256]{2,1,0:T(8,128)S(1)}, u32[]{:S(2)}, u32[]{:S(2)}) collective-permute-start(f32[1,64,256]{2,1,0:T(8,128)} %get-tuple-element.36), channel_id=1, source_target_pairs={{0,4},{2,6},{4,8},{6,10},{8,12},{10,14},{12,0},{14,2},{1,5},{3,7},... | collective-permute-start | bytes 196616 | tf_op jit(solution)/shard_map/ppermute | solution.py:92
  14.1 14.8 %collective-permute-start.2 = (f32[1,64,256]{2,1,0:T(8,128)}, f32[1,64,256]{2,1,0:T(8,128)S(1)}, u32[]{:S(2)}, u32[]{:S(2)}) collective-permute-start(f32[1,64,256]{2,1,0:T(8,128)} %get-tuple-element.41), channel_id=1, source_target_pairs={{0,6},{2,8},{4,10},{6,12},{8,14},{10,0},{12,2},{14,4},{1,7},{3,9},... | collective-permute-start | bytes 196616 | tf_op jit(solution)/shard_map/ppermute | solution.py:92
  16.6 13.0 %collective-permute-start.3 = (f32[1,64,256]{2,1,0:T(8,128)}, f32[1,64,256]{2,1,0:T(8,128)S(1)}, u32[]{:S(2)}, u32[]{:S(2)}) collective-permute-start(f32[1,64,256]{2,1,0:T(8,128)} %get-tuple-element.40), channel_id=1, source_target_pairs={{0,8},{2,10},{4,12},{6,14},{8,0},{10,2},{12,4},{14,6},{1,9},{3,11}... | collective-permute-start | bytes 196616 | tf_op jit(solution)/shard_map/ppermute | solution.py:92
  17.8 11.8 %collective-permute-start.4 = (f32[1,64,256]{2,1,0:T(8,128)}, f32[1,64,256]{2,1,0:T(8,128)S(1)}, u32[]{:S(2)}, u32[]{:S(2)}) collective-permute-start(f32[1,64,256]{2,1,0:T(8,128)} %get-tuple-element.39), channel_id=1, source_target_pairs={{0,10},{2,12},{4,14},{6,0},{8,2},{10,4},{12,6},{14,8},{1,11},{3,13... | collective-permute-start | bytes 196616 | tf_op jit(solution)/shard_map/ppermute | solution.py:92
  20.5 9.1 %collective-permute-start.5 = (f32[1,64,256]{2,1,0:T(8,128)}, f32[1,64,256]{2,1,0:T(8,128)S(1)}, u32[]{:S(2)}, u32[]{:S(2)}) collective-permute-start(f32[1,64,256]{2,1,0:T(8,128)} %get-tuple-element.38), channel_id=1, source_target_pairs={{0,12},{2,14},{4,0},{6,2},{8,4},{10,6},{12,8},{14,10},{1,13},{3,15... | collective-permute-start | bytes 196616 | tf_op jit(solution)/shard_map/ppermute | solution.py:92
  24.5 12.8 %copy-start.4 = (f32[1,256]{1,0:T(1,128)S(1)}, f32[1,256]{1,0:T(1,128)}, u32[]{:S(2)}) copy-start(f32[1,256]{1,0:T(1,128)} %get-tuple-element.73) | copy-start | bytes 3076
  27.5 4.5 %collective-permute-start.6 = (f32[1,64,256]{2,1,0:T(8,128)}, f32[1,64,256]{2,1,0:T(8,128)S(1)}, u32[]{:S(2)}, u32[]{:S(2)}) collective-permute-start(f32[1,64,256]{2,1,0:T(8,128)} %get-tuple-element.37), channel_id=1, source_target_pairs={{0,14},{2,0},{4,2},{6,4},{8,6},{10,8},{12,10},{14,12},{1,15},{3,1}... | collective-permute-start | bytes 196616 | tf_op jit(solution)/shard_map/ppermute | solution.py:92
  28.9 7.0 %collective-permute-start = (f32[1,64,256]{2,1,0:T(8,128)S(1)}, f32[1,64,256]{2,1,0:T(8,128)S(1)}, u32[]{:S(2)}, u32[]{:S(2)}) collective-permute-start(f32[1,64,256]{2,1,0:T(8,128)S(1)} %get-tuple-element.18), channel_id=1, source_target_pairs={{0,2},{2,4},{4,6},{6,8},{8,10},{10,12},{12,14},{14,0},{1,3},{3,5},... | collective-permute-start | bytes 196616 | tf_op jit(solution)/shard_map/ppermute | solution.py:92
  36.7 1.1 %copy-start.9 = (f32[256]{0:T(256)S(1)}, f32[256]{0:T(256)}, u32[]{:S(2)}) copy-start(f32[256]{0:T(256)} %get-tuple-element.65) | copy-start | bytes 3076
  37.9 3.6 %collective-permute-start.9 = (f32[256]{0:T(256)S(1)}, f32[256]{0:T(256)S(1)}, u32[]{:S(2)}, u32[]{:S(2)}) collective-permute-start(f32[256]{0:T(256)S(1)} %fusion.5), channel_id=1, source_target_pairs={{0,2},{2,0},{4,6},{6,4},{8,10},{10,8},{12,14},{14,12},{1,3},{3,1},... | collective-permute-start | bytes 3080 | tf_op jit(solution)/shard_map/ppermute | solution.py:65
  38.5 11.7 %collective-permute-start.8 = (bf16[4,1,64,256]{3,2,1,0:T(8,128)(2,1)S(1)}, bf16[4,1,64,256]{3,2,1,0:T(8,128)(2,1)S(1)}, u32[]{:S(2)}, u32[]{:S(2)}) collective-permute-start(bf16[4,1,64,256]{3,2,1,0:T(8,128)(2,1)S(1)} %bitcast.222), channel_id=1, source_target_pairs={{0,1},{1,0},{2,3},{3,2},{4,5},{5,4},{6,7},{7,6},{8,9},{9,8},{10,11... | collective-permute-start | bytes 393224 | tf_op jit(solution)/shard_map/ppermute | solution.py:81
  39.5 11.4 %collective-permute-start.7 = (bf16[4,1,64,256]{3,2,1,0:T(8,128)(2,1)S(1)}, bf16[4,1,64,256]{3,2,1,0:T(8,128)(2,1)S(1)}, u32[]{:S(2)}, u32[]{:S(2)}) collective-permute-start(bf16[4,1,64,256]{3,2,1,0:T(8,128)(2,1)S(1)} %bitcast.223), channel_id=1, source_target_pairs={{0,1},{1,0},{2,3},{3,2},{4,5},{5,4},{6,7},{7,6},{8,9},{9,8},{10,11... | collective-permute-start | bytes 393224 | tf_op jit(solution)/shard_map/ppermute | solution.py:81
  41.6 3.6 %collective-permute-start.10 = (f32[256]{0:T(256)S(1)}, f32[256]{0:T(256)S(1)}, u32[]{:S(2)}, u32[]{:S(2)}) collective-permute-start(f32[256]{0:T(256)S(1)} %add.319), channel_id=1, source_target_pairs={{0,4},{2,6},{4,0},{6,2},{8,12},{10,14},{12,8},{14,10},{1,5},{3,7},... | collective-permute-start | bytes 3080 | tf_op jit(solution)/shard_map/ppermute | solution.py:65
  45.1 4.5 %collective-permute-start.11 = (f32[256]{0:T(256)S(1)}, f32[256]{0:T(256)S(1)}, u32[]{:S(2)}, u32[]{:S(2)}) collective-permute-start(f32[256]{0:T(256)S(1)} %add.320), channel_id=1, source_target_pairs={{0,8},{2,10},{4,12},{6,14},{8,0},{10,2},{12,4},{14,6},{1,9},{3,11}... | collective-permute-start | bytes 3080 | tf_op jit(solution)/shard_map/ppermute | solution.py:65

commit v3 on v2

--- a/solution.py
+++ b/solution.py
@@ -59,13 +59,17 @@
     count = lax.axis_size(axis)
     if count == 1:
         return value
-    if count & (count - 1) == 0:
-        step = 1
-        while step < count:
-            value = value + lax.ppermute(value, axis, [(i, i ^ step) for i in range(count)])
-            step *= 2
-        return value
-    return lax.psum(value, axis)
+    mine = lax.axis_index(axis)
+    got = [value] + [
+        lax.ppermute(value, axis, [(i, (i + step) % count) for i in range(count)])
+        for step in range(1, count)
+    ]
+    stacked = jnp.stack(got)
+    ordered = jnp.take(stacked, (mine - jnp.arange(count)) % count, axis=0)
+    total = ordered[0]
+    for index in range(1, count):
+        total = total + ordered[index]
+    return total
 
 
 def chan_sum(cells, halo, taps, row_taps):

time: 51.9 us -> 56.2 us (1.083)
  starting transfers between devices: 13.6 us -> 23.1 us
  waiting for transfers between devices: 15.5 us -> 7.59 us
  other arithmetic: 6.74 us -> 8.69 us
  local copies, waits for them, and re-layouts: 9.78 us -> 10.4 us
    ppermute x3 -> x7, starting transfers between devices: 0.07 us -> 9.75 us  [all_sum(): lax.ppermute(value, axis, [(i, (i + step) % count) for i in range(count)])]
    ppermute x3 -> x7, waiting for transfers between devices: 9.19 us -> 1.32 us  [all_sum(): lax.ppermute(value, axis, [(i, (i + step) % count) for i in range(count)])]
    another operation x2, other arithmetic: 0.11 us -> 0.79 us
    gather x0 -> x1, other arithmetic: none -> 0.61 us  [all_sum(): ordered = jnp.take(stacked, (mine - jnp.arange(count)) % count, axis=0)]
    select_n x0 -> x2, other arithmetic: none -> 0.6 us  [all_sum(): ordered = jnp.take(stacked, (mine - jnp.arange(count)) % count, axis=0)]
  transfers between devices with their start and end apart: 12 -> 16, of which waited for: 5 -> 3; matrix products, arithmetic and copies ran while one was open for 17% -> 20% of each run, Pallas kernels for 0% -> 0%
where the time goes in v3:
time: 56.2 us; the launch traced here: 55.9 us
  starting transfers between devices  23.1 us (41%)
  local copies, waits for them, and re-layouts  10.4 us (19%)
  other arithmetic  8.69 us (15%)
  waiting for transfers between devices  7.59 us (14%)
  matrix products  4.92 us (9%)
  between operations  1.09 us (2%)
    ppermute x7, starting transfers between devices, block_carries(): lax.ppermute(message, axis, [(i, (i + step) % count) for i in range(count)])  12.8 us
    ppermute x7, starting transfers between devices, all_sum(): lax.ppermute(value, axis, [(i, (i + step) % count) for i in range(count)])  9.75 us
    ppermute x7, waiting for transfers between devices, block_carries(): lax.ppermute(message, axis, [(i, (i + step) % count) for i in range(count)])  6.26 us
    dot_general x18, matrix products, conv_apply(): jnp.dot(portion.reshape(-1, channels), taps[index, col_tap], preferred_el...  4.92 us
    slice x4, local copies, waits for them, and re-layouts, conv_apply(): padded[:, row_tap:row_tap + row_count, col_tap:col_tap + col_count, :]  2.81 us
    convert_element_type x2, other arithmetic, chan_sum(): return (own + got.astype(jnp.float32)).astype(jnp.bfloat16)  1.37 us
    ppermute x7, waiting for transfers between devices, all_sum(): lax.ppermute(value, axis, [(i, (i + step) % count) for i in range(count)])  1.32 us
    mul x1, local copies, waits for them, and re-layouts, local(): frame_keep[:, None] * decay_rate[None, :]  1.32 us
  transfers between devices with their start and end apart: 16, of which 3 were waited for; matrix products, arithmetic and copies ran while one was open for 20% of the time, Pallas kernels for 0%

profile of v3, /device:TPU:0, one launch (start us, length us, event | category | flops | bytes accessed | tf_op | source)
XLA Modules:
  0.0 55.9 jit_solution(4470607616035188992)
XLA Ops:
  0.6 1.2 %slice.222 = bf16[1,3,512,256]{3,2,1,0:T(8,128)(2,1)S(1)} slice(bf16[3,3,512,256]{3,2,1,0:T(8,128)(2,1)} %param.7), slice={[1:2], [0:3], [0:512], [0:256]} | slice | bytes 1572864 | tf_op jit(solution)/shard_map/slice | solution.py:31
  1.9 1.9 %pad_slice_fusion.3 = (bf16[4,1,64,512]{3,2,1,0:T(8,128)(2,1)}, bf16[4,1,64,512]{3,2,1,0:T(8,128)(2,1)S(1)}) fusion(bf16[4,1,64,512]{3,2,1,0:T(8,128)(2,1)} %param.6), kind=kLoop, calls=%fused_computation.18 | loop fusion | bytes 786432 | tf_op jit(solution)/shard_map/slice | solution.py:48
  3.7 1.2 %slice.236 = bf16[1,3,256,512]{3,2,1,0:T(8,128)(2,1)S(1)} slice(bf16[3,3,256,512]{3,2,1,0:T(8,128)(2,1)} %param.8), slice={[1:2], [0:3], [0:256], [0:512]} | slice | bytes 1572864 | tf_op jit(solution)/shard_map/slice | solution.py:28
  5.0 0.8 %pad_slice_fusion.1 = (bf16[4,1,64,512]{3,2,1,0:T(8,128)(2,1)}, bf16[4,1,64,512]{3,2,1,0:T(8,128)(2,1)S(1)}) fusion(bf16[4,1,64,512]{3,2,1,0:T(8,128)(2,1)S(1)} %copy-done.1), kind=kLoop, calls=%fused_computation.16 | loop fusion | bytes 786432 | tf_op jit(solution)/shard_map/slice | solution.py:48
  8.2 1.2 %convolution_add_fusion.10 = f32[256,256]{1,0:T(8,128)S(1)} fusion(f32[256,256]{1,0:T(8,128)S(1)} %convolution_add_fusion.11, bf16[256,512]{1,0:T(8,128)(2,1)} %bitcast.231, bf16[1,3,512,256]{3,2,1,0:T(8,128)(2,1)S(1)} %slice.222), kind=kOutput, calls=%fused_computation.11 | convolution fusion | flops 67174400 | bytes 1048576 | tf_op jit(solution)/shard_map/dot_general | solution.py:49
  10.3 0.8 %select_bitcast_fusion.5 = (f32[1,64,256]{2,1,0:T(8,128)}, f32[1,64,256]{2,1,0:T(8,128)}, f32[1,64,256]{2,1,0:T(8,128)}, f32[1,64,256]{2,1,0:T(8,128)}, f32[1,64,256]{2,1,0:T(8,128)}, /*index=5*/f32[1,64,256]{2,1,0:T(8,128)}) fusion(f32[64,256]{1,0:T(8,128)S(1)} %get-tuple-element.21, f32[64,256]{1,0:T(8,128)S(1)} %get-tuple-element.19, pred[]{:T(512)S(6)} %lt.97, ...), kind=kLoop, calls=%fused_computation.90 | loop fusion | flops 98304 | bytes 524294 | tf_op jit(solution)/shard_map/jit(_where)/select_n | solution.py:95
  11.1 3.0 %collective-permute-start.1 = (f32[1,64,256]{2,1,0:T(8,128)}, f32[1,64,256]{2,1,0:T(8,128)S(1)}, u32[]{:S(2)}, u32[]{:S(2)}) collective-permute-start(f32[1,64,256]{2,1,0:T(8,128)} %get-tuple-element.36), channel_id=1, source_target_pairs={{0,4},{2,6},{4,8},{6,10},{8,12},{10,14},{12,0},{14,2},{1,5},{3,7},... | collective-permute-start | bytes 196616 | tf_op jit(solution)/shard_map/ppermute | solution.py:96
  14.1 2.5 %collective-permute-start.2 = (f32[1,64,256]{2,1,0:T(8,128)}, f32[1,64,256]{2,1,0:T(8,128)S(1)}, u32[]{:S(2)}, u32[]{:S(2)}) collective-permute-start(f32[1,64,256]{2,1,0:T(8,128)} %get-tuple-element.41), channel_id=1, source_target_pairs={{0,6},{2,8},{4,10},{6,12},{8,14},{10,0},{12,2},{14,4},{1,7},{3,9},... | collective-permute-start | bytes 196616 | tf_op jit(solution)/shard_map/ppermute | solution.py:96
  16.6 1.2 %collective-permute-start.3 = (f32[1,64,256]{2,1,0:T(8,128)}, f32[1,64,256]{2,1,0:T(8,128)S(1)}, u32[]{:S(2)}, u32[]{:S(2)}) collective-permute-start(f32[1,64,256]{2,1,0:T(8,128)} %get-tuple-element.40), channel_id=1, source_target_pairs={{0,8},{2,10},{4,12},{6,14},{8,0},{10,2},{12,4},{14,6},{1,9},{3,11}... | collective-permute-start | bytes 196616 | tf_op jit(solution)/shard_map/ppermute | solution.py:96
  17.9 2.7 %collective-permute-start.4 = (f32[1,64,256]{2,1,0:T(8,128)}, f32[1,64,256]{2,1,0:T(8,128)S(1)}, u32[]{:S(2)}, u32[]{:S(2)}) collective-permute-start(f32[1,64,256]{2,1,0:T(8,128)} %get-tuple-element.39), channel_id=1, source_target_pairs={{0,10},{2,12},{4,14},{6,0},{8,2},{10,4},{12,6},{14,8},{1,11},{3,13... | collective-permute-start | bytes 196616 | tf_op jit(solution)/shard_map/ppermute | solution.py:96
  20.5 1.3 %collective-permute-start.5 = (f32[1,64,256]{2,1,0:T(8,128)}, f32[1,64,256]{2,1,0:T(8,128)S(1)}, u32[]{:S(2)}, u32[]{:S(2)}) collective-permute-start(f32[1,64,256]{2,1,0:T(8,128)} %get-tuple-element.38), channel_id=1, source_target_pairs={{0,12},{2,14},{4,0},{6,2},{8,4},{10,6},{12,8},{14,10},{1,13},{3,15... | collective-permute-start | bytes 196616 | tf_op jit(solution)/shard_map/ppermute | solution.py:96
  21.9 1.3 %slice.262 = f32[32]{0:T(128)} slice(f32[33]{0:T(128)} %copy-done.9), slice={[1:33]} | slice | bytes 256 | tf_op jit(solution)/shard_map/slice | solution.py:146
  23.2 1.3 %mul.533 = f32[8,4]{1,0:T(8,128)} reshape(f32[32]{0:T(128)} %param.10) | data formatting | bytes 256 | tf_op jit(solution)/shard_map/mul | solution.py:145
  25.1 0.8 %mul.577 = f32[8,4]{1,0:T(8,128)S(1)} reshape(f32[32]{0:T(128)} %slice.262) | data formatting | bytes 256 | tf_op jit(solution)/shard_map/mul | solution.py:146
  27.2 0.8 %broadcast_multiply_fusion = (f32[8,4,256]{2,1,0:T(4,128)S(1)}, f32[8,4,256]{2,1,0:T(4,128)S(1)}) fusion(f32[8,4]{1,0:T(8,128)S(1)} %mul.577, f32[256]{0:T(256)} %param.9, f32[8,4]{1,0:T(8,128)} %mul.533), kind=kLoop, calls=%fused_computation.93 | loop fusion | flops 16384 | bytes 66816 | tf_op jit(solution)/shard_map/mul | solution.py:146
  28.7 1.4 %collective-permute-start.6 = (f32[1,64,256]{2,1,0:T(8,128)}, f32[1,64,256]{2,1,0:T(8,128)S(1)}, u32[]{:S(2)}, u32[]{:S(2)}) collective-permute-start(f32[1,64,256]{2,1,0:T(8,128)} %get-tuple-element.37), channel_id=1, source_target_pairs={{0,14},{2,0},{4,2},{6,4},{8,6},{10,8},{12,10},{14,12},{1,15},{3,1}... | collective-permute-start | bytes 196616 | tf_op jit(solution)/shard_map/ppermute | solution.py:96
  30.8 2.4 %collective-permute-done.6 = f32[1,64,256]{2,1,0:T(8,128)S(1)} collective-permute-done((f32[1,64,256]{2,1,0:T(8,128)}, f32[1,64,256]{2,1,0:T(8,128)S(1)}, u32[]{:S(2)}, u32[]{:S(2)}) %collective-permute-start.6) | collective-permute-done | bytes 65568 | tf_op jit(solution)/shard_map/ppermute | solution.py:96
  33.2 3.9 %collective-permute-done = f32[1,64,256]{2,1,0:T(8,128)S(1)} collective-permute-done((f32[1,64,256]{2,1,0:T(8,128)S(1)}, f32[1,64,256]{2,1,0:T(8,128)S(1)}, u32[]{:S(2)}, u32[]{:S(2)}) %collective-permute-start) | collective-permute-done | bytes 65568 | tf_op jit(solution)/shard_map/ppermute | solution.py:96
  37.9 0.8 %fusion.42 = (bf16[1,1,64,256]{3,2,1,0:T(8,128)(2,1)S(1)}, f32[1,1,64,256]{3,2,1,0:T(8,128)S(1)}, f32[1,64,256]{2,1,0:T(8,128)S(1)}) fusion(f32[256]{0:T(256)} %bitcast.242, f32[256,256]{1,0:T(8,128)S(1)} %convolution_add_fusion.10, f32[256]{0:T(256)S(1)} %get-tuple-element.66, f32[256]{0:T(256)S(1)} %bitcast.255, ...), kind=kLoop, calls=%fused_computation.158 | loop fusion | flops 393216 | bytes 697351 | tf_op jit(solution)/shard_map/convert
  38.9 1.3 %collective-permute-start.11 = (f32[256]{0:T(256)S(1)}, f32[256]{0:T(256)S(1)}, u32[]{:S(2)}, u32[]{:S(2)}) collective-permute-start(f32[256]{0:T(256)S(1)} %fusion.5), channel_id=1, source_target_pairs={{0,6},{2,8},{4,10},{6,12},{8,14},{10,0},{12,2},{14,4},{1,7},{3,9},... | collective-permute-start | bytes 3080 | tf_op jit(solution)/shard_map/ppermute | solution.py:64
  40.2 3.9 %collective-permute-start.12 = (f32[256]{0:T(256)S(1)}, f32[256]{0:T(256)S(1)}, u32[]{:S(2)}, u32[]{:S(2)}) collective-permute-start(f32[256]{0:T(256)S(1)} %fusion.5), channel_id=1, source_target_pairs={{0,8},{2,10},{4,12},{6,14},{8,0},{10,2},{12,4},{14,6},{1,9},{3,11}... | collective-permute-start | bytes 3080 | tf_op jit(solution)/shard_map/ppermute | solution.py:64
  46.7 3.0 %collective-permute-start.14 = (f32[256]{0:T(256)S(1)}, f32[256]{0:T(256)S(1)}, u32[]{:S(2)}, u32[]{:S(2)}) collective-permute-start(f32[256]{0:T(256)S(1)} %fusion.5), channel_id=1, source_target_pairs={{0,12},{2,14},{4,0},{6,2},{8,4},{10,6},{12,8},{14,10},{1,13},{3,15... | collective-permute-start | bytes 3080 | tf_op jit(solution)/shard_map/ppermute | solution.py:64
  49.7 1.5 %collective-permute-start.15 = (f32[256]{0:T(256)S(1)}, f32[256]{0:T(256)S(1)}, u32[]{:S(2)}, u32[]{:S(2)}) collective-permute-start(f32[256]{0:T(256)S(1)} %fusion.5), channel_id=1, source_target_pairs={{0,14},{2,0},{4,2},{6,4},{8,6},{10,8},{12,10},{14,12},{1,15},{3,1}... | collective-permute-start | bytes 3080 | tf_op jit(solution)/shard_map/ppermute | solution.py:64
  51.9 1.3 %collective-permute-done.15 = f32[256]{0:T(256)S(1)} collective-permute-done((f32[256]{0:T(256)S(1)}, f32[256]{0:T(256)S(1)}, u32[]{:S(2)}, u32[]{:S(2)}) %collective-permute-start.15) | collective-permute-done | bytes 1056 | tf_op jit(solution)/shard_map/ppermute | solution.py:64
  (90 shorter events, 13.5 us)
Async XLA Ops:
  1.8 3.2 %copy-start.1 = (bf16[4,1,64,512]{3,2,1,0:T(8,128)(2,1)S(1)}, bf16[4,1,64,512]{3,2,1,0:T(8,128)(2,1)}, u32[]{:S(2)}) copy-start(bf16[4,1,64,512]{3,2,1,0:T(8,128)(2,1)} %param.11) | copy-start | bytes 786436
  1.8 4.0 %copy-start.3 = (f32[256]{0:T(256)S(1)}, f32[256]{0:T(256)}, u32[]{:S(2)}) copy-start(f32[256]{0:T(256)} %param.9) | copy-start | bytes 3076
  1.9 4.6 %copy-start.10 = (f32[32]{0:T(128)S(1)}, f32[32]{0:T(128)}, u32[]{:S(2)}) copy-start(f32[32]{0:T(128)} %param.10) | copy-start | bytes 388
  3.7 4.3 %copy-start = (bf16[4,1,64,512]{3,2,1,0:T(8,128)(2,1)S(1)}, bf16[4,1,64,512]{3,2,1,0:T(8,128)(2,1)}, u32[]{:S(2)}) copy-start(bf16[4,1,64,512]{3,2,1,0:T(8,128)(2,1)} %param.6) | copy-start | bytes 786436
  7.7 2.5 %copy-start.5 = (f32[1,256]{1,0:T(1,128)}, f32[1,256]{1,0:T(1,128)S(1)}, u32[]{:S(2)}) copy-start(f32[1,256]{1,0:T(1,128)S(1)} %get-tuple-element.76) | copy-start | bytes 3076
  7.7 2.5 %copy-start.6 = (f32[1,256]{1,0:T(1,128)}, f32[1,256]{1,0:T(1,128)S(1)}, u32[]{:S(2)}) copy-start(f32[1,256]{1,0:T(1,128)S(1)} %get-tuple-element.58) | copy-start | bytes 3076
  7.8 2.5 %copy-start.7 = (f32[1,256]{1,0:T(1,128)}, f32[1,256]{1,0:T(1,128)S(1)}, u32[]{:S(2)}) copy-start(f32[1,256]{1,0:T(1,128)S(1)} %get-tuple-element.60) | copy-start | bytes 3076
  11.1 17.6 %collective-permute-start.1 = (f32[1,64,256]{2,1,0:T(8,128)}, f32[1,64,256]{2,1,0:T(8,128)S(1)}, u32[]{:S(2)}, u32[]{:S(2)}) collective-permute-start(f32[1,64,256]{2,1,0:T(8,128)} %get-tuple-element.36), channel_id=1, source_target_pairs={{0,4},{2,6},{4,8},{6,10},{8,12},{10,14},{12,0},{14,2},{1,5},{3,7},... | collective-permute-start | bytes 196616 | tf_op jit(solution)/shard_map/ppermute | solution.py:96
  14.1 16.0 %collective-permute-start.2 = (f32[1,64,256]{2,1,0:T(8,128)}, f32[1,64,256]{2,1,0:T(8,128)S(1)}, u32[]{:S(2)}, u32[]{:S(2)}) collective-permute-start(f32[1,64,256]{2,1,0:T(8,128)} %get-tuple-element.41), channel_id=1, source_target_pairs={{0,6},{2,8},{4,10},{6,12},{8,14},{10,0},{12,2},{14,4},{1,7},{3,9},... | collective-permute-start | bytes 196616 | tf_op jit(solution)/shard_map/ppermute | solution.py:96
  16.6 14.1 %collective-permute-start.3 = (f32[1,64,256]{2,1,0:T(8,128)}, f32[1,64,256]{2,1,0:T(8,128)S(1)}, u32[]{:S(2)}, u32[]{:S(2)}) collective-permute-start(f32[1,64,256]{2,1,0:T(8,128)} %get-tuple-element.40), channel_id=1, source_target_pairs={{0,8},{2,10},{4,12},{6,14},{8,0},{10,2},{12,4},{14,6},{1,9},{3,11}... | collective-permute-start | bytes 196616 | tf_op jit(solution)/shard_map/ppermute | solution.py:96
  17.9 12.9 %collective-permute-start.4 = (f32[1,64,256]{2,1,0:T(8,128)}, f32[1,64,256]{2,1,0:T(8,128)S(1)}, u32[]{:S(2)}, u32[]{:S(2)}) collective-permute-start(f32[1,64,256]{2,1,0:T(8,128)} %get-tuple-element.39), channel_id=1, source_target_pairs={{0,10},{2,12},{4,14},{6,0},{8,2},{10,4},{12,6},{14,8},{1,11},{3,13... | collective-permute-start | bytes 196616 | tf_op jit(solution)/shard_map/ppermute | solution.py:96
  20.5 10.2 %collective-permute-start.5 = (f32[1,64,256]{2,1,0:T(8,128)}, f32[1,64,256]{2,1,0:T(8,128)S(1)}, u32[]{:S(2)}, u32[]{:S(2)}) collective-permute-start(f32[1,64,256]{2,1,0:T(8,128)} %get-tuple-element.38), channel_id=1, source_target_pairs={{0,12},{2,14},{4,0},{6,2},{8,4},{10,6},{12,8},{14,10},{1,13},{3,15... | collective-permute-start | bytes 196616 | tf_op jit(solution)/shard_map/ppermute | solution.py:96
  25.1 13.6 %copy-start.8 = (f32[256]{0:T(256)S(1)}, f32[256]{0:T(256)}, u32[]{:S(2)}) copy-start(f32[256]{0:T(256)} %get-tuple-element.65) | copy-start | bytes 3076
  28.7 4.5 %collective-permute-start.6 = (f32[1,64,256]{2,1,0:T(8,128)}, f32[1,64,256]{2,1,0:T(8,128)S(1)}, u32[]{:S(2)}, u32[]{:S(2)}) collective-permute-start(f32[1,64,256]{2,1,0:T(8,128)} %get-tuple-element.37), channel_id=1, source_target_pairs={{0,14},{2,0},{4,2},{6,4},{8,6},{10,8},{12,10},{14,12},{1,15},{3,1}... | collective-permute-start | bytes 196616 | tf_op jit(solution)/shard_map/ppermute | solution.py:96
  30.1 7.0 %collective-permute-start = (f32[1,64,256]{2,1,0:T(8,128)S(1)}, f32[1,64,256]{2,1,0:T(8,128)S(1)}, u32[]{:S(2)}, u32[]{:S(2)}) collective-permute-start(f32[1,64,256]{2,1,0:T(8,128)S(1)} %get-tuple-element.18), channel_id=1, source_target_pairs={{0,2},{2,4},{4,6},{6,8},{8,10},{10,12},{12,14},{14,0},{1,3},{3,5},... | collective-permute-start | bytes 196616 | tf_op jit(solution)/shard_map/ppermute | solution.py:96
  38.8 7.9 %collective-permute-start.9 = (f32[256]{0:T(256)S(1)}, f32[256]{0:T(256)S(1)}, u32[]{:S(2)}, u32[]{:S(2)}) collective-permute-start(f32[256]{0:T(256)S(1)} %fusion.5), channel_id=1, source_target_pairs={{0,2},{2,4},{4,6},{6,8},{8,10},{10,12},{12,14},{14,0},{1,3},{3,5},... | collective-permute-start | bytes 3080 | tf_op jit(solution)/shard_map/ppermute | solution.py:64
  38.8 10.8 %collective-permute-start.10 = (f32[256]{0:T(256)S(1)}, f32[256]{0:T(256)S(1)}, u32[]{:S(2)}, u32[]{:S(2)}) collective-permute-start(f32[256]{0:T(256)S(1)} %fusion.5), channel_id=1, source_target_pairs={{0,4},{2,6},{4,8},{6,10},{8,12},{10,14},{12,0},{14,2},{1,5},{3,7},... | collective-permute-start | bytes 3080 | tf_op jit(solution)/shard_map/ppermute | solution.py:64
  38.9 12.4 %collective-permute-start.11 = (f32[256]{0:T(256)S(1)}, f32[256]{0:T(256)S(1)}, u32[]{:S(2)}, u32[]{:S(2)}) collective-permute-start(f32[256]{0:T(256)S(1)} %fusion.5), channel_id=1, source_target_pairs={{0,6},{2,8},{4,10},{6,12},{8,14},{10,0},{12,2},{14,4},{1,7},{3,9},... | collective-permute-start | bytes 3080 | tf_op jit(solution)/shard_map/ppermute | solution.py:64
  40.2 11.2 %collective-permute-start.12 = (f32[256]{0:T(256)S(1)}, f32[256]{0:T(256)S(1)}, u32[]{:S(2)}, u32[]{:S(2)}) collective-permute-start(f32[256]{0:T(256)S(1)} %fusion.5), channel_id=1, source_target_pairs={{0,8},{2,10},{4,12},{6,14},{8,0},{10,2},{12,4},{14,6},{1,9},{3,11}... | collective-permute-start | bytes 3080 | tf_op jit(solution)/shard_map/ppermute | solution.py:64
  44.1 7.8 %collective-permute-start.13 = (f32[256]{0:T(256)S(1)}, f32[256]{0:T(256)S(1)}, u32[]{:S(2)}, u32[]{:S(2)}) collective-permute-start(f32[256]{0:T(256)S(1)} %fusion.5), channel_id=1, source_target_pairs={{0,10},{2,12},{4,14},{6,0},{8,2},{10,4},{12,6},{14,8},{1,11},{3,13... | collective-permute-start | bytes 3080 | tf_op jit(solution)/shard_map/ppermute | solution.py:64
  46.7 5.2 %collective-permute-start.14 = (f32[256]{0:T(256)S(1)}, f32[256]{0:T(256)S(1)}, u32[]{:S(2)}, u32[]{:S(2)}) collective-permute-start(f32[256]{0:T(256)S(1)} %fusion.5), channel_id=1, source_target_pairs={{0,12},{2,14},{4,0},{6,2},{8,4},{10,6},{12,8},{14,10},{1,13},{3,15... | collective-permute-start | bytes 3080 | tf_op jit(solution)/shard_map/ppermute | solution.py:64
  49.7 3.6 %collective-permute-start.15 = (f32[256]{0:T(256)S(1)}, f32[256]{0:T(256)S(1)}, u32[]{:S(2)}, u32[]{:S(2)}) collective-permute-start(f32[256]{0:T(256)S(1)} %fusion.5), channel_id=1, source_target_pairs={{0,14},{2,0},{4,2},{6,4},{8,6},{10,8},{12,10},{14,12},{1,15},{3,1}... | collective-permute-start | bytes 3080 | tf_op jit(solution)/shard_map/ppermute | solution.py:64
  51.3 3.1 %collective-permute-start.8 = (bf16[4,1,64,256]{3,2,1,0:T(8,128)(2,1)S(1)}, bf16[4,1,64,256]{3,2,1,0:T(8,128)(2,1)S(1)}, u32[]{:S(2)}, u32[]{:S(2)}) collective-permute-start(bf16[4,1,64,256]{3,2,1,0:T(8,128)(2,1)S(1)} %bitcast.233), channel_id=1, source_target_pairs={{0,1},{1,0},{2,3},{3,2},{4,5},{5,4},{6,7},{7,6},{8,9},{9,8},{10,11... | collective-permute-start | bytes 393224 | tf_op jit(solution)/shard_map/ppermute | solution.py:85
  51.4 3.7 %collective-permute-start.7 = (bf16[4,1,64,256]{3,2,1,0:T(8,128)(2,1)S(1)}, bf16[4,1,64,256]{3,2,1,0:T(8,128)(2,1)S(1)}, u32[]{:S(2)}, u32[]{:S(2)}) collective-permute-start(bf16[4,1,64,256]{3,2,1,0:T(8,128)(2,1)S(1)} %bitcast.234), channel_id=1, source_target_pairs={{0,1},{1,0},{2,3},{3,2},{4,5},{5,4},{6,7},{7,6},{8,9},{9,8},{10,11... | collective-permute-start | bytes 393224 | tf_op jit(solution)/shard_map/ppermute | solution.py:85
  (3 other events, 5.2 us)

commit v4 on v2

--- a/solution.py
+++ b/solution.py
@@ -86,10 +86,13 @@
 def block_carries(fwd_end, bwd_start, fwd_prod, bwd_prod, axis):
     count = lax.axis_size(axis)
     mine = lax.axis_index(axis)
-    received = {}
-    for step in range(1, count):
-        message = jnp.where(mine + step < count, fwd_end, bwd_start)
-        received[step] = lax.ppermute(message, axis, [(i, (i + step) % count) for i in range(count)])
+    later = (lax.broadcasted_iota(jnp.int32, (count,) + (1,) * fwd_end.ndim, 0) > mine)
+    outgoing = jnp.where(later, fwd_end[None], bwd_start[None])
+    incoming = lax.all_to_all(outgoing, axis, 0, 0, tiled=True)
+    received = {
+        step: lax.dynamic_index_in_dim(incoming, (mine - step) % count, 0, keepdims=False)
+        for step in range(1, count)
+    }
     carry_in = jnp.zeros_like(fwd_end)
     for step in reversed(range(1, count)):
         source = mine - step

time: 51.9 us -> 51.1 us (0.985)
  local copies, waits for them, and re-layouts: 9.78 us -> 5.67 us
  starting transfers between devices: 13.6 us -> 10.3 us
  other arithmetic: 6.74 us -> 9.87 us
  waiting for transfers between devices: 15.5 us -> 17.7 us
  matrix products: 4.93 us -> 5.88 us
    ppermute x7 -> x0, starting transfers between devices: 12.9 us -> none  [block_carries(): lax.ppermute(message, axis, [(i, (i + step) % count) for i in range(count)])]
    all_to_all x0 -> x1, waiting for transfers between devices: none -> 10.8 us  [block_carries(): incoming = lax.all_to_all(outgoing, axis, 0, 0, tiled=True)]
    all_to_all x0 -> x1, starting transfers between devices: none -> 7.25 us  [block_carries(): incoming = lax.all_to_all(outgoing, axis, 0, 0, tiled=True)]
    ppermute x7 -> x0, waiting for transfers between devices: 6.27 us -> none  [block_carries(): lax.ppermute(message, axis, [(i, (i + step) % count) for i in range(count)])]
    ppermute x3, starting transfers between devices: 0.07 us -> 2.43 us  [all_sum(): lax.ppermute(value, axis, [(i, i ^ step) for i in range(count)])]
    ppermute x3, waiting for transfers between devices: 9.19 us -> 6.85 us  [all_sum(): lax.ppermute(value, axis, [(i, i ^ step) for i in range(count)])]
    add x0 -> x3, other arithmetic: none -> 1.38 us  [the longest x1 0.66 us: local(): running = fresh if running is None else decays[t] * running + fresh]
    mul x1, local copies, waits for them, and re-layouts: 1.32 us -> 0.08 us  [local(): frame_keep[:, None] * decay_rate[None, :]]
  transfers between devices with their start and end apart: 12 -> 6, of which waited for: 5 -> 4; matrix products, arithmetic and copies ran while one was open for 17% -> 13% of each run, Pallas kernels for 0% -> 0%
where the time goes in v4:
time: 51.1 us; the launch traced here: 50.6 us
  waiting for transfers between devices  17.7 us (35%)
  starting transfers between devices  10.3 us (20%)
  other arithmetic  9.87 us (19%)
  matrix products  5.88 us (12%)
  local copies, waits for them, and re-layouts  5.67 us (11%)
  between operations  1.26 us (2%)
    all_to_all x1, waiting for transfers between devices, block_carries(): incoming = lax.all_to_all(outgoing, axis, 0, 0, tiled=True)  10.8 us
    all_to_all x1, starting transfers between devices, block_carries(): incoming = lax.all_to_all(outgoing, axis, 0, 0, tiled=True)  7.25 us
    ppermute x3, waiting for transfers between devices, all_sum(): lax.ppermute(value, axis, [(i, i ^ step) for i in range(count)])  6.85 us
    dot_general x18, matrix products, conv_apply(): jnp.dot(portion.reshape(-1, channels), taps[index, col_tap], preferred_el...  5.88 us
    ppermute x3, starting transfers between devices, all_sum(): lax.ppermute(value, axis, [(i, i ^ step) for i in range(count)])  2.43 us
    slice x4, local copies, waits for them, and re-layouts, conv_apply(): padded[:, row_tap:row_tap + row_count, col_tap:col_tap + col_count, :]  1.72 us
    convert_element_type x2, other arithmetic, chan_sum(): return (own + got.astype(jnp.float32)).astype(jnp.bfloat16)  1.37 us
    slice x1, local copies, waits for them, and re-layouts, prep_kernel(): taps = jnp.stack([flipped[a] for a in row_taps])  1.23 us
  transfers between devices with their start and end apart: 6, of which 4 were waited for; matrix products, arithmetic and copies ran while one was open for 13% of the time, Pallas kernels for 0%

profile of v4, /device:TPU:0, one launch (start us, length us, event | category | flops | bytes accessed | tf_op | source)
XLA Modules:
  0.0 50.6 jit_solution(4797849052155577532)
XLA Ops:
  1.2 1.2 %slice.212 = bf16[1,3,256,512]{3,2,1,0:T(8,128)(2,1)S(1)} slice(bf16[3,3,256,512]{3,2,1,0:T(8,128)(2,1)} %param.8), slice={[1:2], [0:3], [0:256], [0:512]} | slice | bytes 1572864 | tf_op jit(solution)/shard_map/slice | solution.py:28
  2.5 0.8 %pad_slice_fusion.1 = (bf16[4,1,64,512]{3,2,1,0:T(8,128)(2,1)}, bf16[4,1,64,512]{3,2,1,0:T(8,128)(2,1)S(1)}) fusion(bf16[4,1,64,512]{3,2,1,0:T(8,128)(2,1)S(1)} %copy-done), kind=kLoop, calls=%fused_computation.15 | loop fusion | bytes 786432 | tf_op jit(solution)/shard_map/slice | solution.py:48
  3.3 1.2 %slice.198 = bf16[1,3,512,256]{3,2,1,0:T(8,128)(2,1)S(1)} slice(bf16[3,3,512,256]{3,2,1,0:T(8,128)(2,1)} %param.7), slice={[1:2], [0:3], [0:512], [0:256]} | slice | bytes 1572864 | tf_op jit(solution)/shard_map/slice | solution.py:31
  4.5 0.8 %pad_slice_fusion.3 = (bf16[4,1,64,512]{3,2,1,0:T(8,128)(2,1)}, bf16[4,1,64,512]{3,2,1,0:T(8,128)(2,1)S(1)}) fusion(bf16[4,1,64,512]{3,2,1,0:T(8,128)(2,1)S(1)} %copy-done.1), kind=kLoop, calls=%fused_computation.17 | loop fusion | bytes 786432 | tf_op jit(solution)/shard_map/slice | solution.py:48
  5.3 0.6 %multiply_divide_fusion = (f32[256]{0:T(256)}, f32[256]{0:T(256)S(1)}) fusion(f32[256]{0:T(256)S(1)} %copy-done.4), kind=kLoop, calls=%fused_computation.143 | loop fusion | flops 768 | bytes 3072 | tf_op jit(solution)/shard_map/div | solution.py:158
  6.6 0.6 %fusion.61 = (f32[1,256]{1,0:T(1,128)}, f32[1,256]{1,0:T(1,128)S(1)}, f32[1,256]{1,0:T(1,128)S(1)}, f32[1,256]{1,0:T(1,128)S(1)}, f32[1,256]{1,0:T(1,128)S(1)}, ...) fusion(f32[4,256]{1,0:T(4,128)S(1)} %get-tuple-element.62, f32[4,256]{1,0:T(4,128)S(1)} %get-tuple-element.63), kind=kLoop, calls=%fused_computation.152 | loop fusion | bytes 16384 | tf_op jit(solution)/shard_map/slice | solution.py:140
  7.8 1.2 %convolution_add_fusion.8 = f32[256,256]{1,0:T(8,128)S(1)} fusion(f32[256,256]{1,0:T(8,128)S(1)} %convolution_add_fusion.9, bf16[256,512]{1,0:T(8,128)(2,1)} %bitcast.257, bf16[1,3,512,256]{2,3,1,0:T(8,128)(2,1)S(1)} %reverse_bitcast_fusion.1), kind=kOutput, calls=%fused_computation.8 | convolution fusion | flops 67174400 | bytes 1048576 | tf_op jit(solution)/shard_map/dot_general | solution.py:49
  9.3 1.2 %convolution_add_fusion.11 = f32[256,256]{1,0:T(8,128)S(1)} fusion(f32[256,256]{1,0:T(8,128)S(1)} %fusion.3, bf16[256,512]{1,0:T(8,128)(2,1)} %bitcast.254, bf16[1,3,512,256]{3,2,1,0:T(8,128)(2,1)S(1)} %slice.198), kind=kOutput, calls=%fused_computation.11 | convolution fusion | flops 67174400 | bytes 1048576 | tf_op jit(solution)/shard_map/dot_general | solution.py:49
  10.7 0.6 %slice_add_fusion.2 = (f32[64,256]{1,0:T(8,128)S(1)}, f32[64,256]{1,0:T(8,128)}) fusion(f32[256,256]{1,0:T(8,128)S(1)} %convolution_add_fusion.8, f32[256]{0:T(256)S(1)} %bitcast.291, f32[256]{0:T(256)S(1)} %bitcast.264, f32[256]{0:T(256)S(1)} %bitcast.289), kind=kLoop, calls=%fused_computation.59 | loop fusion | flops 98304 | bytes 396288 | tf_op jit(solution)/shard_map/add | solution.py:139
  11.4 0.7 %fusion.10 = (f32[64,256]{1,0:T(8,128)S(1)}, f32[64,256]{1,0:T(8,128)}) fusion(f32[256,256]{1,0:T(8,128)S(1)} %convolution_add_fusion.10, f32[256]{0:T(256)S(1)} %bitcast.285, f32[256]{0:T(256)S(1)} %get-tuple-element.59, f32[256]{0:T(256)S(1)} %bitcast.261, f32[256]{0:T(256)S(1)} %bitcast.287), kind=kLoop, calls=%fused_computation.61 | loop fusion | flops 163840 | bytes 397312 | tf_op jit(solution)/shard_map/add | solution.py:131
  12.1 0.9 %broadcast_select_fusion = f32[8,1,64,256]{3,2,1,0:T(8,128)} fusion(f32[64,256]{1,0:T(8,128)S(1)} %get-tuple-element.18, f32[64,256]{1,0:T(8,128)S(1)} %get-tuple-element.20, pred[8]{0:T(512)(128)(4,1)S(1)} %copy-done.16), kind=kLoop, calls=%fused_computation.39 | loop fusion | flops 131072 | bytes 655368 | tf_op jit(solution)/shard_map/jit(_where)/select_n | solution.py:90
  12.9 7.2 %all-to-all-start = ((f32[8,1,64,256]{3,2,1,0:T(8,128)}), f32[8,1,64,256]{3,2,1,0:T(8,128)S(1)}, u32[]{:S(2)}, u32[]{:S(2)}) async-start(f32[8,1,64,256]{3,2,1,0:T(8,128)} %broadcast_select_fusion), calls=%async_computation | async-start | bytes 1048576 | tf_op jit(solution)/shard_map/all_to_all | solution.py:91
  20.4 0.7 %broadcast_multiply_fusion = (f32[8,4,256]{2,1,0:T(4,128)}, f32[8,4,256]{2,1,0:T(4,128)}) fusion(f32[8,4]{1,0:T(8,128)S(1)} %mul.636, f32[256]{0:T(256)S(1)} %copy-done.5, f32[8,4]{1,0:T(8,128)S(1)} %mul.592), kind=kLoop, calls=%fused_computation.103 | loop fusion | flops 16384 | bytes 66816 | tf_op jit(solution)/shard_map/mul | solution.py:145
  21.4 1.0 %slice_multiply_fusion.4 = (f32[8,1,256]{2,1,0:T(1,128)S(1)}, f32[8,1,256]{2,1,0:T(1,128)S(1)}) fusion(f32[8,4,256]{2,1,0:T(4,128)} %get-tuple-element.60, f32[8,4,256]{2,1,0:T(4,128)} %get-tuple-element.61), kind=kLoop, calls=%fused_computation.131 | loop fusion | flops 12288 | bytes 81920 | tf_op jit(solution)/shard_map/mul | solution.py:151
  22.5 0.7 %fusion.54 = (f32[256]{0:T(256)S(1)}, f32[256]{0:T(256)S(1)}, f32[256]{0:T(256)S(1)}) fusion(f32[256]{0:T(256)} %bitcast.292, f32[256]{0:T(256)S(1)} %bitcast.265, f32[256]{0:T(256)} %bitcast.283, f32[256]{0:T(256)} %bitcast.290), kind=kLoop, calls=%fused_computation.147 | loop fusion | flops 768 | bytes 7168 | tf_op jit(solution)/shard_map/mul | solution.py:140
  23.2 0.7 %fusion.59 = (f32[256]{0:T(256)S(1)}, f32[256]{0:T(256)S(1)}, f32[256]{0:T(256)S(1)}) fusion(f32[256]{0:T(256)} %bitcast.286, f32[256]{0:T(256)S(1)} %bitcast.262, f32[256]{0:T(256)} %bitcast.281, f32[256]{0:T(256)} %bitcast.288), kind=kLoop, calls=%fused_computation.151 | loop fusion | flops 768 | bytes 7168 | tf_op jit(solution)/shard_map/mul | solution.py:132
  23.9 10.8 %all-to-all-done = f32[8,1,64,256]{3,2,1,0:T(8,128)S(1)} async-done(((f32[8,1,64,256]{3,2,1,0:T(8,128)}), f32[8,1,64,256]{3,2,1,0:T(8,128)S(1)}, u32[]{:S(2)}, u32[]{:S(2)}) %all-to-all-start) | async-done | bytes 524320 | tf_op jit(solution)/shard_map/all_to_all | solution.py:91
  34.7 0.9 %add_bitcast_fusion.2 = (f32[1,1,64,256]{3,2,1,0:T(8,128)S(1)}, f32[1,1,64,256]{3,2,1,0:T(8,128)S(1)}, f32[1,1,64,256]{3,2,1,0:T(8,128)S(1)}) fusion(f32[64,256]{1,0:T(8,128)S(1)} %get-tuple-element.4, f32[256]{0:T(256)S(1)} %get-tuple-element.6, f32[64,256]{1,0:T(8,128)} %get-tuple-element.19, f32[256]{0:T(256)S(1)} %bitcast.266, ...), kind=kLoop, calls=%fused_computation.96 | loop fusion | flops 131072 | bytes 462848 | tf_op jit(solution)/shard_map/stack | solution.py:155
  37.0 1.5 %collective-permute-start.2 = (f32[256]{0:T(256)S(1)}, f32[256]{0:T(256)S(1)}, u32[]{:S(2)}, u32[]{:S(2)}) collective-permute-start(f32[256]{0:T(256)S(1)} %fusion.5), channel_id=1, source_target_pairs={{0,2},{2,0},{4,6},{6,4},{8,10},{10,8},{12,14},{14,12},{1,3},{3,1},... | collective-permute-start | bytes 3080 | tf_op jit(solution)/shard_map/ppermute | solution.py:65
  40.7 0.8 %collective-permute-start.3 = (f32[256]{0:T(256)S(1)}, f32[256]{0:T(256)S(1)}, u32[]{:S(2)}, u32[]{:S(2)}) collective-permute-start(f32[256]{0:T(256)S(1)} %add.409), channel_id=1, source_target_pairs={{0,4},{2,6},{4,0},{6,2},{8,12},{10,14},{12,8},{14,10},{1,5},{3,7},... | collective-permute-start | bytes 3080 | tf_op jit(solution)/shard_map/ppermute | solution.py:65
  41.6 2.6 %collective-permute-done.3 = f32[256]{0:T(256)S(1)} collective-permute-done((f32[256]{0:T(256)S(1)}, f32[256]{0:T(256)S(1)}, u32[]{:S(2)}, u32[]{:S(2)}) %collective-permute-start.3) | collective-permute-done | bytes 1056 | tf_op jit(solution)/shard_map/ppermute | solution.py:65
  44.6 4.1 %collective-permute-done.4 = f32[256]{0:T(256)S(1)} collective-permute-done((f32[256]{0:T(256)S(1)}, f32[256]{0:T(256)S(1)}, u32[]{:S(2)}, u32[]{:S(2)}) %collective-permute-start.4) | collective-permute-done | bytes 1056 | tf_op jit(solution)/shard_map/ppermute | solution.py:65
  49.3 0.7 %add_convert_fusion = bf16[4,1,64,256]{3,2,1,0:T(8,128)(2,1)} fusion(f32[4,1,64,256]{3,2,1,0:T(8,128)S(1)} %bitcast.255, bf16[4,1,64,256]{3,2,1,0:T(8,128)(2,1)S(1)} %collective-permute-done.1), kind=kLoop, calls=%fused_computation.37 | loop fusion | flops 196608 | bytes 524288 | tf_op jit(solution)/shard_map/convert_element_type | solution.py:83
  50.0 0.7 %add_convert_fusion.1 = bf16[4,1,64,256]{3,2,1,0:T(8,128)(2,1)} fusion(f32[4,1,64,256]{3,2,1,0:T(8,128)S(1)} %bitcast.258, bf16[4,1,64,256]{3,2,1,0:T(8,128)(2,1)S(1)} %collective-permute-done), kind=kLoop, calls=%fused_computation.38 | loop fusion | flops 196608 | bytes 524288 | tf_op jit(solution)/shard_map/convert_element_type | solution.py:83
  (81 shorter events, 7.2 us)
Async XLA Ops:
  0.6 1.9 %copy-start = (bf16[4,1,64,512]{3,2,1,0:T(8,128)(2,1)S(1)}, bf16[4,1,64,512]{3,2,1,0:T(8,128)(2,1)}, u32[]{:S(2)}) copy-start(bf16[4,1,64,512]{3,2,1,0:T(8,128)(2,1)} %param.11) | copy-start | bytes 786436
  1.2 3.3 %copy-start.1 = (bf16[4,1,64,512]{3,2,1,0:T(8,128)(2,1)S(1)}, bf16[4,1,64,512]{3,2,1,0:T(8,128)(2,1)}, u32[]{:S(2)}) copy-start(bf16[4,1,64,512]{3,2,1,0:T(8,128)(2,1)} %param.6) | copy-start | bytes 786436
  2.4 2.9 %copy-start.4 = (f32[256]{0:T(256)S(1)}, f32[256]{0:T(256)}, u32[]{:S(2)}) copy-start(f32[256]{0:T(256)} %param.9) | copy-start | bytes 3076
  2.4 3.5 %copy-start.14 = (f32[32]{0:T(128)S(1)}, f32[32]{0:T(128)}, u32[]{:S(2)}) copy-start(f32[32]{0:T(128)} %param.10) | copy-start | bytes 388
  6.0 0.5 %copy-start.12 = (f32[33]{0:T(128)}, f32[33]{0:T(128)S(1)}, u32[]{:S(2)}) copy-start(f32[33]{0:T(128)S(1)} %pad_maximum_fusion.2) | copy-start | bytes 400
  7.2 3.5 %copy-start.9 = (f32[1,256]{1,0:T(1,128)}, f32[1,256]{1,0:T(1,128)S(1)}, u32[]{:S(2)}) copy-start(f32[1,256]{1,0:T(1,128)S(1)} %get-tuple-element.51) | copy-start | bytes 3076
  7.2 3.5 %copy-start.10 = (f32[1,256]{1,0:T(1,128)}, f32[1,256]{1,0:T(1,128)S(1)}, u32[]{:S(2)}) copy-start(f32[1,256]{1,0:T(1,128)S(1)} %get-tuple-element.53) | copy-start | bytes 3076
  7.2 4.2 %copy-start.7 = (f32[1,256]{1,0:T(1,128)}, f32[1,256]{1,0:T(1,128)S(1)}, u32[]{:S(2)}) copy-start(f32[1,256]{1,0:T(1,128)S(1)} %get-tuple-element.66) | copy-start | bytes 3076
  7.2 4.2 %copy-start.8 = (f32[1,256]{1,0:T(1,128)}, f32[1,256]{1,0:T(1,128)S(1)}, u32[]{:S(2)}) copy-start(f32[1,256]{1,0:T(1,128)S(1)} %get-tuple-element.68) | copy-start | bytes 3076
  7.2 3.2 %copy-start.2 = (bf16[4,1,64,512]{3,2,1,0:T(8,128)(2,1)S(1)}, bf16[4,1,64,512]{3,2,1,0:T(8,128)(2,1)}, u32[]{:S(2)}) copy-start(bf16[4,1,64,512]{3,2,1,0:T(8,128)(2,1)} %get-tuple-element.26) | copy-start | bytes 786436
  7.8 4.3 %copy-start.16 = (pred[8]{0:T(512)(128)(4,1)S(1)}, pred[8]{0:T(512)(128)(4,1)}, u32[]{:S(2)}) copy-start(pred[8]{0:T(512)(128)(4,1)} %iota_compare_fusion) | copy-start | bytes 28
  9.2 10.9 %copy-start.13 = (f32[33]{0:T(128)S(1)}, f32[33]{0:T(128)}, u32[]{:S(2)}) copy-start(f32[33]{0:T(128)} %copy-done.12) | copy-start | bytes 400
  9.3 11.0 %copy-start.15 = (f32[32]{0:T(128)S(1)}, f32[32]{0:T(128)}, u32[]{:S(2)}) copy-start(f32[32]{0:T(128)} %param.10) | copy-start | bytes 388
  9.3 11.2 %copy-start.5 = (f32[256]{0:T(256)S(1)}, f32[256]{0:T(256)}, u32[]{:S(2)}) copy-start(f32[256]{0:T(256)} %param.9) | copy-start | bytes 3076
  12.9 21.7 %all-to-all-start = ((f32[8,1,64,256]{3,2,1,0:T(8,128)}), f32[8,1,64,256]{3,2,1,0:T(8,128)S(1)}, u32[]{:S(2)}, u32[]{:S(2)}) async-start(f32[8,1,64,256]{3,2,1,0:T(8,128)} %broadcast_select_fusion), calls=%async_computation | async-start | bytes 1048576 | tf_op jit(solution)/shard_map/all_to_all | solution.py:91
  21.2 15.0 %copy-start.6 = (f32[1,256]{1,0:T(1,128)S(1)}, f32[1,256]{1,0:T(1,128)}, u32[]{:S(2)}) copy-start(f32[1,256]{1,0:T(1,128)} %get-tuple-element.69) | copy-start | bytes 3076
  21.2 15.1 %copy-start.3 = (f32[64,256]{1,0:T(8,128)S(1)}, f32[64,256]{1,0:T(8,128)}, u32[]{:S(2)}) copy-start(f32[64,256]{1,0:T(8,128)} %get-tuple-element.21) | copy-start | bytes 196612
  36.0 1.0 %copy-start.11 = (f32[256]{0:T(256)S(1)}, f32[256]{0:T(256)}, u32[]{:S(2)}) copy-start(f32[256]{0:T(256)} %get-tuple-element.58) | copy-start | bytes 3076
  37.0 3.6 %collective-permute-start.2 = (f32[256]{0:T(256)S(1)}, f32[256]{0:T(256)S(1)}, u32[]{:S(2)}, u32[]{:S(2)}) collective-permute-start(f32[256]{0:T(256)S(1)} %fusion.5), channel_id=1, source_target_pairs={{0,2},{2,0},{4,6},{6,4},{8,10},{10,8},{12,14},{14,12},{1,3},{3,1},... | collective-permute-start | bytes 3080 | tf_op jit(solution)/shard_map/ppermute | solution.py:65
  39.0 10.3 %collective-permute-start.1 = (bf16[4,1,64,256]{3,2,1,0:T(8,128)(2,1)S(1)}, bf16[4,1,64,256]{3,2,1,0:T(8,128)(2,1)S(1)}, u32[]{:S(2)}, u32[]{:S(2)}) collective-permute-start(bf16[4,1,64,256]{3,2,1,0:T(8,128)(2,1)S(1)} %bitcast.259), channel_id=1, source_target_pairs={{0,1},{1,0},{2,3},{3,2},{4,5},{5,4},{6,7},{7,6},{8,9},{9,8},{10,11... | collective-permute-start | bytes 393224 | tf_op jit(solution)/shard_map/ppermute | solution.py:81
  40.0 10.0 %collective-permute-start = (bf16[4,1,64,256]{3,2,1,0:T(8,128)(2,1)S(1)}, bf16[4,1,64,256]{3,2,1,0:T(8,128)(2,1)S(1)}, u32[]{:S(2)}, u32[]{:S(2)}) collective-permute-start(bf16[4,1,64,256]{3,2,1,0:T(8,128)(2,1)S(1)} %bitcast.260), channel_id=1, source_target_pairs={{0,1},{1,0},{2,3},{3,2},{4,5},{5,4},{6,7},{7,6},{8,9},{9,8},{10,11... | collective-permute-start | bytes 393224 | tf_op jit(solution)/shard_map/ppermute | solution.py:81
  40.7 3.6 %collective-permute-start.3 = (f32[256]{0:T(256)S(1)}, f32[256]{0:T(256)S(1)}, u32[]{:S(2)}, u32[]{:S(2)}) collective-permute-start(f32[256]{0:T(256)S(1)} %add.409), channel_id=1, source_target_pairs={{0,4},{2,6},{4,0},{6,2},{8,12},{10,14},{12,8},{14,10},{1,5},{3,7},... | collective-permute-start | bytes 3080 | tf_op jit(solution)/shard_map/ppermute | solution.py:65
  44.2 4.5 %collective-permute-start.4 = (f32[256]{0:T(256)S(1)}, f32[256]{0:T(256)S(1)}, u32[]{:S(2)}, u32[]{:S(2)}) collective-permute-start(f32[256]{0:T(256)S(1)} %add.410), channel_id=1, source_target_pairs={{0,8},{2,10},{4,12},{6,14},{8,0},{10,2},{12,4},{14,6},{1,9},{3,11}... | collective-permute-start | bytes 3080 | tf_op jit(solution)/shard_map/ppermute | solution.py:65

commit v5 on v2

--- a/solution.py
+++ b/solution.py
@@ -86,6 +86,8 @@
 def block_carries(fwd_end, bwd_start, fwd_prod, bwd_prod, axis):
     count = lax.axis_size(axis)
     mine = lax.axis_index(axis)
+    if count % 2 == 0 and count > 2:
+        return paired_carries(fwd_end, bwd_start, fwd_prod, bwd_prod, axis)
     received = {}
     for step in range(1, count):
         message = jnp.where(mine + step < count, fwd_end, bwd_start)
@@ -100,6 +102,41 @@
         source = mine + step
         factor = lax.dynamic_index_in_dim(bwd_prod, jnp.minimum(source, count - 1), 0, keepdims=False)
         carry_back = jnp.where(source < count, received[count - step], 0.0) + factor * carry_back
+    return carry_in, carry_back
+
+
+def paired_carries(fwd_end, bwd_start, fwd_prod, bwd_prod, axis):
+    count = lax.axis_size(axis)
+    pairs_count = count // 2
+    mine = lax.axis_index(axis)
+    upper = mine % 2 == 1
+    pair = mine // 2
+    swap = [(i, i ^ 1) for i in range(count)]
+
+    def pick(table, index):
+        return lax.dynamic_index_in_dim(table, jnp.clip(index, 0, table.shape[0] - 1), 0, keepdims=False)
+
+    partner = lax.ppermute(jnp.where(upper, bwd_start, fwd_end), axis, swap)
+    aggregate = jnp.where(
+        upper,
+        fwd_end + pick(fwd_prod, mine) * partner,
+        bwd_start + pick(bwd_prod, mine) * partner,
+    )
+    pair_fwd = fwd_prod[1::2] * fwd_prod[0::2]
+    pair_bwd = bwd_prod[0::2] * bwd_prod[1::2]
+    received = {}
+    for step in range(1, pairs_count):
+        links = [(2 * z + 1, 2 * (z + step) + 1) for z in range(pairs_count - step)]
+        links += [(2 * z, 2 * (z - step)) for z in range(step, pairs_count)]
+        received[step] = lax.ppermute(aggregate, axis, links)
+    outer = jnp.zeros_like(aggregate)
+    for step in reversed(range(1, pairs_count)):
+        valid = jnp.where(upper, pair - step >= 0, pair + step < pairs_count)
+        factor = jnp.where(upper, pick(pair_fwd, pair - step), pick(pair_bwd, pair + step))
+        outer = jnp.where(valid, received[step], 0.0) + factor * outer
+    other = lax.ppermute(outer, axis, swap)
+    carry_in = jnp.where(upper, partner + pick(fwd_prod, mine - 1) * outer, other)
+    carry_back = jnp.where(upper, other, partner + pick(bwd_prod, mine + 1) * outer)
     return carry_in, carry_back
 
 

time: 51.9 us -> 47.1 us (0.908)
  local copies, waits for them, and re-layouts: 9.78 us -> 6.97 us
  other arithmetic: 6.74 us -> 4.6 us
  waiting for transfers between devices: 15.5 us -> 16.3 us
  starting transfers between devices: 13.6 us -> 12.9 us
    ppermute x7 -> x5, waiting for transfers between devices: 6.27 us -> 10.9 us  [the longest x3 7.91 us: paired_carries(): received[step] = lax.ppermute(aggregate, axis, links)]
    ppermute x7 -> x5, starting transfers between devices: 12.9 us -> 8.31 us  [the longest x3 3.88 us: paired_carries(): received[step] = lax.ppermute(aggregate, axis, links)]
    ppermute x3, starting transfers between devices: 0.07 us -> 3.93 us  [all_sum(): lax.ppermute(value, axis, [(i, i ^ step) for i in range(count)])]
    ppermute x3, waiting for transfers between devices: 9.19 us -> 5.36 us  [all_sum(): lax.ppermute(value, axis, [(i, i ^ step) for i in range(count)])]
    mul x1, local copies, waits for them, and re-layouts: 1.32 us -> 0.08 us  [local(): frame_keep[:, None] * decay_rate[None, :]]
    slice x1, local copies, waits for them, and re-layouts: 1.24 us -> 0.07 us  [local(): keep_padded[1:, None] * decay_rate[None, :]]
    select_n x2 -> x3, other arithmetic: 0.8 us -> 0.09 us  [the longest x1 0.05 us: paired_carries(): partner = lax.ppermute(jnp.where(upper, bwd_start, fwd_end), axis, swap)]
    another operation x3, other arithmetic: 0.79 us -> 0.09 us  [local(): jnp.stack([back_states[t] + back_products[t] * carry_back for t in range(...]
  transfers between devices with their start and end apart: 12 -> 10, of which waited for: 5 -> 8; matrix products, arithmetic and copies ran while one was open for 17% -> 11% of each run, Pallas kernels for 0% -> 0%
where the time goes in v5:
time: 47.1 us; the launch traced here: 46.8 us
  waiting for transfers between devices  16.3 us (35%)
  starting transfers between devices  12.9 us (27%)
  local copies, waits for them, and re-layouts  6.97 us (15%)
  matrix products  4.93 us (10%)
  other arithmetic  4.6 us (10%)
  between operations  1.2 us (3%)
    ppermute x3, waiting for transfers between devices, paired_carries(): received[step] = lax.ppermute(aggregate, axis, links)  7.91 us
    ppermute x3, waiting for transfers between devices, all_sum(): lax.ppermute(value, axis, [(i, i ^ step) for i in range(count)])  5.36 us
    dot_general x18, matrix products, conv_apply(): jnp.dot(portion.reshape(-1, channels), taps[index, col_tap], preferred_el...  4.93 us
    ppermute x3, starting transfers between devices, all_sum(): lax.ppermute(value, axis, [(i, i ^ step) for i in range(count)])  3.93 us
    ppermute x3, starting transfers between devices, paired_carries(): received[step] = lax.ppermute(aggregate, axis, links)  3.88 us
    ppermute x1, starting transfers between devices, paired_carries(): partner = lax.ppermute(jnp.where(upper, bwd_start, fwd_end), axis, swap)  2.99 us
    ppermute x1, waiting for transfers between devices, paired_carries(): other = lax.ppermute(outer, axis, swap)  2.83 us
    slice x4, local copies, waits for them, and re-layouts, conv_apply(): padded[:, row_tap:row_tap + row_count, col_tap:col_tap + col_count, :]  2.82 us
  transfers between devices with their start and end apart: 10, of which 8 were waited for; matrix products, arithmetic and copies ran while one was open for 11% of the time, Pallas kernels for 0%

profile of v5, /device:TPU:0, one launch (start us, length us, event | category | flops | bytes accessed | tf_op | source)
XLA Modules:
  0.0 46.8 jit_solution(16743043986386669855)
XLA Ops:
  0.6 1.2 %slice.210 = bf16[1,3,512,256]{3,2,1,0:T(8,128)(2,1)S(1)} slice(bf16[3,3,512,256]{3,2,1,0:T(8,128)(2,1)} %param.7), slice={[1:2], [0:3], [0:512], [0:256]} | slice | bytes 1572864 | tf_op jit(solution)/shard_map/slice | solution.py:31
  1.9 1.9 %pad_slice_fusion.3 = (bf16[4,1,64,512]{3,2,1,0:T(8,128)(2,1)}, bf16[4,1,64,512]{3,2,1,0:T(8,128)(2,1)S(1)}) fusion(bf16[4,1,64,512]{3,2,1,0:T(8,128)(2,1)} %param.6), kind=kLoop, calls=%fused_computation.17 | loop fusion | bytes 786432 | tf_op jit(solution)/shard_map/slice | solution.py:48
  3.8 1.2 %slice.218 = bf16[1,3,256,512]{3,2,1,0:T(8,128)(2,1)S(1)} slice(bf16[3,3,256,512]{3,2,1,0:T(8,128)(2,1)} %param.8), slice={[1:2], [0:3], [0:256], [0:512]} | slice | bytes 1572864 | tf_op jit(solution)/shard_map/slice | solution.py:28
  5.1 0.8 %pad_slice_fusion.1 = (bf16[4,1,64,512]{3,2,1,0:T(8,128)(2,1)}, bf16[4,1,64,512]{3,2,1,0:T(8,128)(2,1)S(1)}) fusion(bf16[4,1,64,512]{3,2,1,0:T(8,128)(2,1)S(1)} %copy-done.1), kind=kLoop, calls=%fused_computation.15 | loop fusion | bytes 786432 | tf_op jit(solution)/shard_map/slice | solution.py:48
  5.9 0.6 %multiply_divide_fusion = (f32[256]{0:T(256)}, f32[256]{0:T(256)S(1)}) fusion(f32[256]{0:T(256)S(1)} %copy-done.3), kind=kLoop, calls=%fused_computation.129 | loop fusion | flops 768 | bytes 3072 | tf_op jit(solution)/shard_map/div | solution.py:192
  7.2 0.6 %fusion.47 = (f32[1,256]{1,0:T(1,128)}, f32[1,256]{1,0:T(1,128)S(1)}, f32[1,256]{1,0:T(1,128)S(1)}, f32[1,256]{1,0:T(1,128)S(1)}, f32[1,256]{1,0:T(1,128)}, /*in...) fusion(f32[4,256]{1,0:T(4,128)S(1)} %get-tuple-element.57, f32[4,256]{1,0:T(4,128)S(1)} %get-tuple-element.58), kind=kLoop, calls=%fused_computation.137 | loop fusion | bytes 16384 | tf_op jit(solution)/shard_map/slice | solution.py:174
  8.3 1.2 %convolution_add_fusion.10 = f32[256,256]{1,0:T(8,128)S(1)} fusion(f32[256,256]{1,0:T(8,128)S(1)} %convolution_add_fusion.11, bf16[256,512]{1,0:T(8,128)(2,1)} %bitcast.211, bf16[1,3,512,256]{3,2,1,0:T(8,128)(2,1)S(1)} %slice.210), kind=kOutput, calls=%fused_computation.10 | convolution fusion | flops 67174400 | bytes 1048576 | tf_op jit(solution)/shard_map/dot_general | solution.py:49
  10.5 3.0 %collective-permute-start = (f32[1,64,256]{2,1,0:T(8,128)S(1)}, f32[1,64,256]{2,1,0:T(8,128)S(1)}, u32[]{:S(2)}, u32[]{:S(2)}) collective-permute-start(f32[1,64,256]{2,1,0:T(8,128)S(1)} %get-tuple-element.18), channel_id=1, source_target_pairs={{0,2},{2,0},{4,6},{6,4},{8,10},{10,8},{12,14},{14,12},{1,3},{3,1},... | collective-permute-start | bytes 196616 | tf_op jit(solution)/shard_map/ppermute | solution.py:119
  14.1 0.7 %fusion.37 = (f32[256]{0:T(256)S(1)}, f32[256]{0:T(256)S(1)}, f32[256]{0:T(256)S(1)}) fusion(f32[256]{0:T(256)} %bitcast.235, f32[256]{0:T(256)S(1)} %bitcast.222, f32[256]{0:T(256)S(1)} %bitcast.224, f32[256]{0:T(256)} %bitcast.233), kind=kLoop, calls=%fused_computation.132 | loop fusion | flops 768 | bytes 7168 | tf_op jit(solution)/shard_map/mul | solution.py:174
  14.8 0.7 %fusion.44 = (f32[256]{0:T(256)S(1)}, f32[256]{0:T(256)S(1)}, f32[256]{0:T(256)S(1)}) fusion(f32[256]{0:T(256)} %bitcast.229, f32[256]{0:T(256)S(1)} %bitcast.219, f32[256]{0:T(256)S(1)} %bitcast.226, f32[256]{0:T(256)} %bitcast.231), kind=kLoop, calls=%fused_computation.136 | loop fusion | flops 768 | bytes 7168 | tf_op jit(solution)/shard_map/mul | solution.py:166
  15.7 1.3 %collective-permute-start.1 = (f32[1,64,256]{2,1,0:T(8,128)S(1)}, f32[1,64,256]{2,1,0:T(8,128)S(1)}, u32[]{:S(2)}, u32[]{:S(2)}) collective-permute-start(f32[1,64,256]{2,1,0:T(8,128)S(1)} %fusion.18), channel_id=1, source_target_pairs={{2,6},{6,10},{10,14},{4,0},{8,4},{12,8},{3,7},{7,11},{11,15},{5,1}... | collective-permute-start | bytes 196616 | tf_op jit(solution)/shard_map/ppermute | solution.py:131
  17.0 1.3 %collective-permute-start.2 = (f32[1,64,256]{2,1,0:T(8,128)S(1)}, f32[1,64,256]{2,1,0:T(8,128)S(1)}, u32[]{:S(2)}, u32[]{:S(2)}) collective-permute-start(f32[1,64,256]{2,1,0:T(8,128)S(1)} %fusion.18), channel_id=1, source_target_pairs={{2,10},{6,14},{8,0},{12,4},{3,11},{7,15},{9,1},{13,5},{18,26},{22,... | collective-permute-start | bytes 196616 | tf_op jit(solution)/shard_map/ppermute | solution.py:131
  18.3 1.3 %collective-permute-start.3 = (f32[1,64,256]{2,1,0:T(8,128)S(1)}, f32[1,64,256]{2,1,0:T(8,128)S(1)}, u32[]{:S(2)}, u32[]{:S(2)}) collective-permute-start(f32[1,64,256]{2,1,0:T(8,128)S(1)} %fusion.18), channel_id=1, source_target_pairs={{2,14},{12,0},{3,15},{13,1},{18,30},{28,16},{19,31},{29,17}} | collective-permute-start | bytes 196616 | tf_op jit(solution)/shard_map/ppermute | solution.py:131
  19.6 2.3 %collective-permute-done.1 = f32[1,64,256]{2,1,0:T(8,128)S(1)} collective-permute-done((f32[1,64,256]{2,1,0:T(8,128)S(1)}, f32[1,64,256]{2,1,0:T(8,128)S(1)}, u32[]{:S(2)}, u32[]{:S(2)}) %collective-permute-start.1) | collective-permute-done | bytes 65568 | tf_op jit(solution)/shard_map/ppermute | solution.py:131
  22.0 4.6 %collective-permute-done.2 = f32[1,64,256]{2,1,0:T(8,128)S(1)} collective-permute-done((f32[1,64,256]{2,1,0:T(8,128)S(1)}, f32[1,64,256]{2,1,0:T(8,128)S(1)}, u32[]{:S(2)}, u32[]{:S(2)}) %collective-permute-start.2) | collective-permute-done | bytes 65568 | tf_op jit(solution)/shard_map/ppermute | solution.py:131
  26.6 1.0 %collective-permute-done.3 = f32[1,64,256]{2,1,0:T(8,128)S(1)} collective-permute-done((f32[1,64,256]{2,1,0:T(8,128)S(1)}, f32[1,64,256]{2,1,0:T(8,128)S(1)}, u32[]{:S(2)}, u32[]{:S(2)}) %collective-permute-start.3) | collective-permute-done | bytes 65568 | tf_op jit(solution)/shard_map/ppermute | solution.py:131
  27.6 1.4 %collective-permute-start.4 = (f32[1,64,256]{2,1,0:T(8,128)S(1)}, f32[1,64,256]{2,1,0:T(8,128)S(1)}, u32[]{:S(2)}, u32[]{:S(2)}) collective-permute-start(f32[1,64,256]{2,1,0:T(8,128)S(1)} %multiply_add_fusion), channel_id=1, source_target_pairs={{0,2},{2,0},{4,6},{6,4},{8,10},{10,8},{12,14},{14,12},{1,3},{3,1},... | collective-permute-start | bytes 196616 | tf_op jit(solution)/shard_map/ppermute | solution.py:137
  29.1 2.8 %collective-permute-done.4 = f32[1,64,256]{2,1,0:T(8,128)S(1)} collective-permute-done((f32[1,64,256]{2,1,0:T(8,128)S(1)}, f32[1,64,256]{2,1,0:T(8,128)S(1)}, u32[]{:S(2)}, u32[]{:S(2)}) %collective-permute-start.4) | collective-permute-done | bytes 65568 | tf_op jit(solution)/shard_map/ppermute | solution.py:137
  33.2 1.4 %collective-permute-start.7 = (f32[256]{0:T(256)S(1)}, f32[256]{0:T(256)S(1)}, u32[]{:S(2)}, u32[]{:S(2)}) collective-permute-start(f32[256]{0:T(256)S(1)} %fusion.5), channel_id=1, source_target_pairs={{0,2},{2,0},{4,6},{6,4},{8,10},{10,8},{12,14},{14,12},{1,3},{3,1},... | collective-permute-start | bytes 3080 | tf_op jit(solution)/shard_map/ppermute | solution.py:65
  37.0 3.4 %collective-permute-done.8 = f32[256]{0:T(256)S(1)} collective-permute-done((f32[256]{0:T(256)S(1)}, f32[256]{0:T(256)S(1)}, u32[]{:S(2)}, u32[]{:S(2)}) %collective-permute-start.8) | collective-permute-done | bytes 1056 | tf_op jit(solution)/shard_map/ppermute | solution.py:65
  40.4 2.5 %collective-permute-start.9 = (f32[256]{0:T(256)S(1)}, f32[256]{0:T(256)S(1)}, u32[]{:S(2)}, u32[]{:S(2)}) collective-permute-start(f32[256]{0:T(256)S(1)} %add.255), channel_id=1, source_target_pairs={{0,8},{2,10},{4,12},{6,14},{8,0},{10,2},{12,4},{14,6},{1,9},{3,11}... | collective-permute-start | bytes 3080 | tf_op jit(solution)/shard_map/ppermute | solution.py:65
  43.1 1.8 %collective-permute-done.9 = f32[256]{0:T(256)S(1)} collective-permute-done((f32[256]{0:T(256)S(1)}, f32[256]{0:T(256)S(1)}, u32[]{:S(2)}, u32[]{:S(2)}) %collective-permute-start.9) | collective-permute-done | bytes 1056 | tf_op jit(solution)/shard_map/ppermute | solution.py:65
  45.5 0.7 %add_convert_fusion = bf16[4,1,64,256]{3,2,1,0:T(8,128)(2,1)} fusion(f32[4,1,64,256]{3,2,1,0:T(8,128)S(1)} %bitcast.209, bf16[4,1,64,256]{3,2,1,0:T(8,128)(2,1)S(1)} %collective-permute-done.6), kind=kLoop, calls=%fused_computation.37 | loop fusion | flops 196608 | bytes 524288 | tf_op jit(solution)/shard_map/convert_element_type | solution.py:83
  46.1 0.7 %add_convert_fusion.1 = bf16[4,1,64,256]{3,2,1,0:T(8,128)(2,1)} fusion(f32[4,1,64,256]{3,2,1,0:T(8,128)S(1)} %bitcast.212, bf16[4,1,64,256]{3,2,1,0:T(8,128)(2,1)S(1)} %collective-permute-done.5), kind=kLoop, calls=%fused_computation.38 | loop fusion | flops 196608 | bytes 524288 | tf_op jit(solution)/shard_map/convert_element_type | solution.py:83
  (96 shorter events, 7.3 us)
Async XLA Ops:
  1.8 3.2 %copy-start.1 = (bf16[4,1,64,512]{3,2,1,0:T(8,128)(2,1)S(1)}, bf16[4,1,64,512]{3,2,1,0:T(8,128)(2,1)}, u32[]{:S(2)}) copy-start(bf16[4,1,64,512]{3,2,1,0:T(8,128)(2,1)} %param.11) | copy-start | bytes 786436
  1.8 4.0 %copy-start.3 = (f32[256]{0:T(256)S(1)}, f32[256]{0:T(256)}, u32[]{:S(2)}) copy-start(f32[256]{0:T(256)} %param.9) | copy-start | bytes 3076
  1.9 4.6 %copy-start.14 = (f32[32]{0:T(128)S(1)}, f32[32]{0:T(128)}, u32[]{:S(2)}) copy-start(f32[32]{0:T(128)} %param.10) | copy-start | bytes 388
  3.8 4.3 %copy-start = (bf16[4,1,64,512]{3,2,1,0:T(8,128)(2,1)S(1)}, bf16[4,1,64,512]{3,2,1,0:T(8,128)(2,1)}, u32[]{:S(2)}) copy-start(bf16[4,1,64,512]{3,2,1,0:T(8,128)(2,1)} %param.6) | copy-start | bytes 786436
  7.8 2.6 %copy-start.8 = (f32[1,256]{1,0:T(1,128)}, f32[1,256]{1,0:T(1,128)S(1)}, u32[]{:S(2)}) copy-start(f32[1,256]{1,0:T(1,128)S(1)} %get-tuple-element.64) | copy-start | bytes 3076
  7.8 2.6 %copy-start.9 = (f32[1,256]{1,0:T(1,128)}, f32[1,256]{1,0:T(1,128)S(1)}, u32[]{:S(2)}) copy-start(f32[1,256]{1,0:T(1,128)S(1)} %get-tuple-element.48) | copy-start | bytes 3076
  7.8 2.6 %copy-start.10 = (f32[1,256]{1,0:T(1,128)}, f32[1,256]{1,0:T(1,128)S(1)}, u32[]{:S(2)}) copy-start(f32[1,256]{1,0:T(1,128)S(1)} %get-tuple-element.50) | copy-start | bytes 3076
  7.8 2.7 %copy-start.7 = (f32[1,256]{1,0:T(1,128)}, f32[1,256]{1,0:T(1,128)S(1)}, u32[]{:S(2)}) copy-start(f32[1,256]{1,0:T(1,128)S(1)} %get-tuple-element.62) | copy-start | bytes 3076
  7.8 2.3 %copy-start.2 = (bf16[4,1,64,512]{3,2,1,0:T(8,128)(2,1)S(1)}, bf16[4,1,64,512]{3,2,1,0:T(8,128)(2,1)}, u32[]{:S(2)}) copy-start(bf16[4,1,64,512]{3,2,1,0:T(8,128)(2,1)} %get-tuple-element.25) | copy-start | bytes 786436
  8.3 5.2 %copy-start.13 = (f32[33]{0:T(128)S(1)}, f32[33]{0:T(128)}, u32[]{:S(2)}) copy-start(f32[33]{0:T(128)} %copy-done.12) | copy-start | bytes 400
  8.3 5.2 %copy-start.15 = (f32[32]{0:T(128)S(1)}, f32[32]{0:T(128)}, u32[]{:S(2)}) copy-start(f32[32]{0:T(128)} %param.10) | copy-start | bytes 388
  8.3 5.5 %copy-start.4 = (f32[256]{0:T(256)S(1)}, f32[256]{0:T(256)}, u32[]{:S(2)}) copy-start(f32[256]{0:T(256)} %param.9) | copy-start | bytes 3076
  8.3 5.8 %copy-start.5 = (f32[1,256]{1,0:T(1,128)S(1)}, f32[1,256]{1,0:T(1,128)}, u32[]{:S(2)}) copy-start(f32[1,256]{1,0:T(1,128)} %get-tuple-element.47) | copy-start | bytes 3076
  8.3 6.5 %copy-start.6 = (f32[1,256]{1,0:T(1,128)S(1)}, f32[1,256]{1,0:T(1,128)}, u32[]{:S(2)}) copy-start(f32[1,256]{1,0:T(1,128)} %get-tuple-element.61) | copy-start | bytes 3076
  10.5 5.2 %collective-permute-start = (f32[1,64,256]{2,1,0:T(8,128)S(1)}, f32[1,64,256]{2,1,0:T(8,128)S(1)}, u32[]{:S(2)}, u32[]{:S(2)}) collective-permute-start(f32[1,64,256]{2,1,0:T(8,128)S(1)} %get-tuple-element.18), channel_id=1, source_target_pairs={{0,2},{2,0},{4,6},{6,4},{8,10},{10,8},{12,14},{14,12},{1,3},{3,1},... | collective-permute-start | bytes 196616 | tf_op jit(solution)/shard_map/ppermute | solution.py:119
  15.7 6.3 %collective-permute-start.1 = (f32[1,64,256]{2,1,0:T(8,128)S(1)}, f32[1,64,256]{2,1,0:T(8,128)S(1)}, u32[]{:S(2)}, u32[]{:S(2)}) collective-permute-start(f32[1,64,256]{2,1,0:T(8,128)S(1)} %fusion.18), channel_id=1, source_target_pairs={{2,6},{6,10},{10,14},{4,0},{8,4},{12,8},{3,7},{7,11},{11,15},{5,1}... | collective-permute-start | bytes 196616 | tf_op jit(solution)/shard_map/ppermute | solution.py:131
  17.0 9.6 %collective-permute-start.2 = (f32[1,64,256]{2,1,0:T(8,128)S(1)}, f32[1,64,256]{2,1,0:T(8,128)S(1)}, u32[]{:S(2)}, u32[]{:S(2)}) collective-permute-start(f32[1,64,256]{2,1,0:T(8,128)S(1)} %fusion.18), channel_id=1, source_target_pairs={{2,10},{6,14},{8,0},{12,4},{3,11},{7,15},{9,1},{13,5},{18,26},{22,... | collective-permute-start | bytes 196616 | tf_op jit(solution)/shard_map/ppermute | solution.py:131
  18.3 9.2 %collective-permute-start.3 = (f32[1,64,256]{2,1,0:T(8,128)S(1)}, f32[1,64,256]{2,1,0:T(8,128)S(1)}, u32[]{:S(2)}, u32[]{:S(2)}) collective-permute-start(f32[1,64,256]{2,1,0:T(8,128)S(1)} %fusion.18), channel_id=1, source_target_pairs={{2,14},{12,0},{3,15},{13,1},{18,30},{28,16},{19,31},{29,17}} | collective-permute-start | bytes 196616 | tf_op jit(solution)/shard_map/ppermute | solution.py:131
  27.6 4.3 %collective-permute-start.4 = (f32[1,64,256]{2,1,0:T(8,128)S(1)}, f32[1,64,256]{2,1,0:T(8,128)S(1)}, u32[]{:S(2)}, u32[]{:S(2)}) collective-permute-start(f32[1,64,256]{2,1,0:T(8,128)S(1)} %multiply_add_fusion), channel_id=1, source_target_pairs={{0,2},{2,0},{4,6},{6,4},{8,10},{10,8},{12,14},{14,12},{1,3},{3,1},... | collective-permute-start | bytes 196616 | tf_op jit(solution)/shard_map/ppermute | solution.py:137
  33.2 3.6 %collective-permute-start.7 = (f32[256]{0:T(256)S(1)}, f32[256]{0:T(256)S(1)}, u32[]{:S(2)}, u32[]{:S(2)}) collective-permute-start(f32[256]{0:T(256)S(1)} %fusion.5), channel_id=1, source_target_pairs={{0,2},{2,0},{4,6},{6,4},{8,10},{10,8},{12,14},{14,12},{1,3},{3,1},... | collective-permute-start | bytes 3080 | tf_op jit(solution)/shard_map/ppermute | solution.py:65
  35.1 10.3 %collective-permute-start.6 = (bf16[4,1,64,256]{3,2,1,0:T(8,128)(2,1)S(1)}, bf16[4,1,64,256]{3,2,1,0:T(8,128)(2,1)S(1)}, u32[]{:S(2)}, u32[]{:S(2)}) collective-permute-start(bf16[4,1,64,256]{3,2,1,0:T(8,128)(2,1)S(1)} %bitcast.214), channel_id=1, source_target_pairs={{0,1},{1,0},{2,3},{3,2},{4,5},{5,4},{6,7},{7,6},{8,9},{9,8},{10,11... | collective-permute-start | bytes 393224 | tf_op jit(solution)/shard_map/ppermute | solution.py:81
  36.1 10.1 %collective-permute-start.5 = (bf16[4,1,64,256]{3,2,1,0:T(8,128)(2,1)S(1)}, bf16[4,1,64,256]{3,2,1,0:T(8,128)(2,1)S(1)}, u32[]{:S(2)}, u32[]{:S(2)}) collective-permute-start(bf16[4,1,64,256]{3,2,1,0:T(8,128)(2,1)S(1)} %bitcast.215), channel_id=1, source_target_pairs={{0,1},{1,0},{2,3},{3,2},{4,5},{5,4},{6,7},{7,6},{8,9},{9,8},{10,11... | collective-permute-start | bytes 393224 | tf_op jit(solution)/shard_map/ppermute | solution.py:81
  36.8 3.6 %collective-permute-start.8 = (f32[256]{0:T(256)S(1)}, f32[256]{0:T(256)S(1)}, u32[]{:S(2)}, u32[]{:S(2)}) collective-permute-start(f32[256]{0:T(256)S(1)} %add.254), channel_id=1, source_target_pairs={{0,4},{2,6},{4,0},{6,2},{8,12},{10,14},{12,8},{14,10},{1,5},{3,7},... | collective-permute-start | bytes 3080 | tf_op jit(solution)/shard_map/ppermute | solution.py:65
  40.4 4.5 %collective-permute-start.9 = (f32[256]{0:T(256)S(1)}, f32[256]{0:T(256)S(1)}, u32[]{:S(2)}, u32[]{:S(2)}) collective-permute-start(f32[256]{0:T(256)S(1)} %add.255), channel_id=1, source_target_pairs={{0,8},{2,10},{4,12},{6,14},{8,0},{10,2},{12,4},{14,6},{1,9},{3,11}... | collective-permute-start | bytes 3080 | tf_op jit(solution)/shard_map/ppermute | solution.py:65
  (2 other events, 1.7 us)

commit v6 on v5

--- a/solution.py
+++ b/solution.py
@@ -59,13 +59,12 @@
     count = lax.axis_size(axis)
     if count == 1:
         return value
-    if count & (count - 1) == 0:
-        step = 1
-        while step < count:
-            value = value + lax.ppermute(value, axis, [(i, i ^ step) for i in range(count)])
-            step *= 2
-        return value
-    return lax.psum(value, axis)
+    outgoing = jnp.broadcast_to(value[None], (count,) + value.shape)
+    incoming = lax.all_to_all(outgoing, axis, 0, 0, tiled=True)
+    total = incoming[0]
+    for index in range(1, count):
+        total = total + incoming[index]
+    return total
 
 
 def chan_sum(cells, halo, taps, row_taps):

time: 47.1 us -> 49.6 us (1.053)
  starting transfers between devices: 12.9 us -> 15.2 us
  waiting for transfers between devices: 16.3 us -> 15 us
  matrix products: 4.93 us -> 5.66 us
  local copies, waits for them, and re-layouts: 6.97 us -> 7.58 us
    all_to_all x0 -> x1, starting transfers between devices: none -> 6.25 us  [all_sum(): incoming = lax.all_to_all(outgoing, axis, 0, 0, tiled=True)]
    ppermute x3 -> x0, waiting for transfers between devices: 5.36 us -> none  [all_sum(): lax.ppermute(value, axis, [(i, i ^ step) for i in range(count)])]
    all_to_all x0 -> x1, waiting for transfers between devices: none -> 4.11 us  [all_sum(): incoming = lax.all_to_all(outgoing, axis, 0, 0, tiled=True)]
    ppermute x3 -> x0, starting transfers between devices: 3.93 us -> none  [all_sum(): lax.ppermute(value, axis, [(i, i ^ step) for i in range(count)])]
    dot_general x18, matrix products: 4.93 us -> 5.66 us  [conv_apply(): jnp.dot(portion.reshape(-1, channels), taps[index, col_tap], preferred_el...]
    broadcast_in_dim x0 -> x1, local copies, waits for them, and re-layouts: none -> 0.61 us  [all_sum(): outgoing = jnp.broadcast_to(value[None], (count,) + value.shape)]
  transfers between devices with their start and end apart: 10 -> 8, of which waited for: 8 -> 6; matrix products, arithmetic and copies ran while one was open for 11% -> 10% of each run, Pallas kernels for 0% -> 0%
where the time goes in v6:
time: 49.6 us; the launch traced here: 49.2 us
  starting transfers between devices  15.2 us (31%)
  waiting for transfers between devices  15 us (30%)
  local copies, waits for them, and re-layouts  7.58 us (15%)
  matrix products  5.66 us (11%)
  other arithmetic  4.6 us (9%)
  between operations  1.2 us (2%)
    ppermute x3, waiting for transfers between devices, paired_carries(): received[step] = lax.ppermute(aggregate, axis, links)  7.91 us
    all_to_all x1, starting transfers between devices, all_sum(): incoming = lax.all_to_all(outgoing, axis, 0, 0, tiled=True)  6.25 us
    dot_general x18, matrix products, conv_apply(): jnp.dot(portion.reshape(-1, channels), taps[index, col_tap], preferred_el...  5.66 us
    all_to_all x1, waiting for transfers between devices, all_sum(): incoming = lax.all_to_all(outgoing, axis, 0, 0, tiled=True)  4.11 us
    ppermute x3, starting transfers between devices, paired_carries(): received[step] = lax.ppermute(aggregate, axis, links)  3.88 us
    ppermute x1, starting transfers between devices, paired_carries(): partner = lax.ppermute(jnp.where(upper, bwd_start, fwd_end), axis, swap)  2.99 us
    ppermute x1, waiting for transfers between devices, paired_carries(): other = lax.ppermute(outer, axis, swap)  2.83 us
    slice x4, local copies, waits for them, and re-layouts, conv_apply(): padded[:, row_tap:row_tap + row_count, col_tap:col_tap + col_count, :]  2.82 us
  transfers between devices with their start and end apart: 8, of which 6 were waited for; matrix products, arithmetic and copies ran while one was open for 10% of the time, Pallas kernels for 0%

profile of v6, /device:TPU:0, one launch (start us, length us, event | category | flops | bytes accessed | tf_op | source)
XLA Modules:
  0.0 49.2 jit_solution(236417141385201721)
XLA Ops:
  0.6 1.2 %slice.242 = bf16[1,3,512,256]{3,2,1,0:T(8,128)(2,1)S(1)} slice(bf16[3,3,512,256]{3,2,1,0:T(8,128)(2,1)} %param.7), slice={[1:2], [0:3], [0:512], [0:256]} | slice | bytes 1572864 | tf_op jit(solution)/shard_map/slice | solution.py:31
  1.9 1.9 %pad_slice_fusion.3 = (bf16[4,1,64,512]{3,2,1,0:T(8,128)(2,1)}, bf16[4,1,64,512]{3,2,1,0:T(8,128)(2,1)S(1)}) fusion(bf16[4,1,64,512]{3,2,1,0:T(8,128)(2,1)} %param.6), kind=kLoop, calls=%fused_computation.17 | loop fusion | bytes 786432 | tf_op jit(solution)/shard_map/slice | solution.py:48
  3.8 1.2 %slice.250 = bf16[1,3,256,512]{3,2,1,0:T(8,128)(2,1)S(1)} slice(bf16[3,3,256,512]{3,2,1,0:T(8,128)(2,1)} %param.8), slice={[1:2], [0:3], [0:256], [0:512]} | slice | bytes 1572864 | tf_op jit(solution)/shard_map/slice | solution.py:28
  5.1 0.8 %pad_slice_fusion.1 = (bf16[4,1,64,512]{3,2,1,0:T(8,128)(2,1)}, bf16[4,1,64,512]{3,2,1,0:T(8,128)(2,1)S(1)}) fusion(bf16[4,1,64,512]{3,2,1,0:T(8,128)(2,1)S(1)} %copy-done.2), kind=kLoop, calls=%fused_computation.15 | loop fusion | bytes 786432 | tf_op jit(solution)/shard_map/slice | solution.py:48
  5.9 0.6 %multiply_divide_fusion = (f32[256]{0:T(256)}, f32[256]{0:T(256)S(1)}) fusion(f32[256]{0:T(256)S(1)} %copy-done.4), kind=kLoop, calls=%fused_computation.136 | loop fusion | flops 768 | bytes 3072 | tf_op jit(solution)/shard_map/div | solution.py:191
  7.2 0.6 %fusion.48 = (f32[1,256]{1,0:T(1,128)}, f32[1,256]{1,0:T(1,128)S(1)}, f32[1,256]{1,0:T(1,128)S(1)}, f32[1,256]{1,0:T(1,128)S(1)}, f32[1,256]{1,0:T(1,128)}, /*in...) fusion(f32[4,256]{1,0:T(4,128)S(1)} %get-tuple-element.57, f32[4,256]{1,0:T(4,128)S(1)} %get-tuple-element.58), kind=kLoop, calls=%fused_computation.144 | loop fusion | bytes 16384 | tf_op jit(solution)/shard_map/slice | solution.py:173
  8.3 1.2 %convolution_add_fusion.10 = f32[256,256]{1,0:T(8,128)S(1)} fusion(f32[256,256]{1,0:T(8,128)S(1)} %convolution_add_fusion.11, bf16[256,512]{1,0:T(8,128)(2,1)} %bitcast.211, bf16[1,3,512,256]{3,2,1,0:T(8,128)(2,1)S(1)} %slice.242), kind=kOutput, calls=%fused_computation.10 | convolution fusion | flops 67174400 | bytes 1048576 | tf_op jit(solution)/shard_map/dot_general | solution.py:49
  10.5 3.0 %collective-permute-start = (f32[1,64,256]{2,1,0:T(8,128)S(1)}, f32[1,64,256]{2,1,0:T(8,128)S(1)}, u32[]{:S(2)}, u32[]{:S(2)}) collective-permute-start(f32[1,64,256]{2,1,0:T(8,128)S(1)} %get-tuple-element.18), channel_id=1, source_target_pairs={{0,2},{2,0},{4,6},{6,4},{8,10},{10,8},{12,14},{14,12},{1,3},{3,1},... | collective-permute-start | bytes 196616 | tf_op jit(solution)/shard_map/ppermute | solution.py:118
  14.1 0.7 %fusion.38 = (f32[256]{0:T(256)S(1)}, f32[256]{0:T(256)S(1)}, f32[256]{0:T(256)S(1)}) fusion(f32[256]{0:T(256)} %bitcast.236, f32[256]{0:T(256)S(1)} %bitcast.223, f32[256]{0:T(256)S(1)} %bitcast.225, f32[256]{0:T(256)} %bitcast.234), kind=kLoop, calls=%fused_computation.139 | loop fusion | flops 768 | bytes 7168 | tf_op jit(solution)/shard_map/mul | solution.py:173
  14.8 0.7 %fusion.45 = (f32[256]{0:T(256)S(1)}, f32[256]{0:T(256)S(1)}, f32[256]{0:T(256)S(1)}) fusion(f32[256]{0:T(256)} %bitcast.230, f32[256]{0:T(256)S(1)} %bitcast.220, f32[256]{0:T(256)S(1)} %bitcast.227, f32[256]{0:T(256)} %bitcast.232), kind=kLoop, calls=%fused_computation.143 | loop fusion | flops 768 | bytes 7168 | tf_op jit(solution)/shard_map/mul | solution.py:165
  15.7 1.3 %collective-permute-start.1 = (f32[1,64,256]{2,1,0:T(8,128)S(1)}, f32[1,64,256]{2,1,0:T(8,128)S(1)}, u32[]{:S(2)}, u32[]{:S(2)}) collective-permute-start(f32[1,64,256]{2,1,0:T(8,128)S(1)} %fusion.18), channel_id=1, source_target_pairs={{2,6},{6,10},{10,14},{4,0},{8,4},{12,8},{3,7},{7,11},{11,15},{5,1}... | collective-permute-start | bytes 196616 | tf_op jit(solution)/shard_map/ppermute | solution.py:130
  17.0 1.3 %collective-permute-start.2 = (f32[1,64,256]{2,1,0:T(8,128)S(1)}, f32[1,64,256]{2,1,0:T(8,128)S(1)}, u32[]{:S(2)}, u32[]{:S(2)}) collective-permute-start(f32[1,64,256]{2,1,0:T(8,128)S(1)} %fusion.18), channel_id=1, source_target_pairs={{2,10},{6,14},{8,0},{12,4},{3,11},{7,15},{9,1},{13,5},{18,26},{22,... | collective-permute-start | bytes 196616 | tf_op jit(solution)/shard_map/ppermute | solution.py:130
  18.3 1.3 %collective-permute-start.3 = (f32[1,64,256]{2,1,0:T(8,128)S(1)}, f32[1,64,256]{2,1,0:T(8,128)S(1)}, u32[]{:S(2)}, u32[]{:S(2)}) collective-permute-start(f32[1,64,256]{2,1,0:T(8,128)S(1)} %fusion.18), channel_id=1, source_target_pairs={{2,14},{12,0},{3,15},{13,1},{18,30},{28,16},{19,31},{29,17}} | collective-permute-start | bytes 196616 | tf_op jit(solution)/shard_map/ppermute | solution.py:130
  19.6 2.3 %collective-permute-done.1 = f32[1,64,256]{2,1,0:T(8,128)S(1)} collective-permute-done((f32[1,64,256]{2,1,0:T(8,128)S(1)}, f32[1,64,256]{2,1,0:T(8,128)S(1)}, u32[]{:S(2)}, u32[]{:S(2)}) %collective-permute-start.1) | collective-permute-done | bytes 65568 | tf_op jit(solution)/shard_map/ppermute | solution.py:130
  22.0 4.6 %collective-permute-done.2 = f32[1,64,256]{2,1,0:T(8,128)S(1)} collective-permute-done((f32[1,64,256]{2,1,0:T(8,128)S(1)}, f32[1,64,256]{2,1,0:T(8,128)S(1)}, u32[]{:S(2)}, u32[]{:S(2)}) %collective-permute-start.2) | collective-permute-done | bytes 65568 | tf_op jit(solution)/shard_map/ppermute | solution.py:130
  26.6 1.0 %collective-permute-done.3 = f32[1,64,256]{2,1,0:T(8,128)S(1)} collective-permute-done((f32[1,64,256]{2,1,0:T(8,128)S(1)}, f32[1,64,256]{2,1,0:T(8,128)S(1)}, u32[]{:S(2)}, u32[]{:S(2)}) %collective-permute-start.3) | collective-permute-done | bytes 65568 | tf_op jit(solution)/shard_map/ppermute | solution.py:130
  27.6 1.4 %collective-permute-start.4 = (f32[1,64,256]{2,1,0:T(8,128)S(1)}, f32[1,64,256]{2,1,0:T(8,128)S(1)}, u32[]{:S(2)}, u32[]{:S(2)}) collective-permute-start(f32[1,64,256]{2,1,0:T(8,128)S(1)} %multiply_add_fusion), channel_id=1, source_target_pairs={{0,2},{2,0},{4,6},{6,4},{8,10},{10,8},{12,14},{14,12},{1,3},{3,1},... | collective-permute-start | bytes 196616 | tf_op jit(solution)/shard_map/ppermute | solution.py:136
  29.1 2.8 %collective-permute-done.4 = f32[1,64,256]{2,1,0:T(8,128)S(1)} collective-permute-done((f32[1,64,256]{2,1,0:T(8,128)S(1)}, f32[1,64,256]{2,1,0:T(8,128)S(1)}, u32[]{:S(2)}, u32[]{:S(2)}) %collective-permute-start.4) | collective-permute-done | bytes 65568 | tf_op jit(solution)/shard_map/ppermute | solution.py:136
  32.7 0.9 %fusion.8 = f32[256,256]{1,0:T(8,128)} fusion(bf16[256,256]{1,0:T(8,128)(2,1)S(1)} %bitcast.200, bf16[1,3,256,512]{3,2,1,0:T(8,128)(2,1)S(1)} %slice.250, s32[]{:T(128)S(6)} %select_n.153), kind=kOutput, calls=%fused_computation.50 | convolution fusion | flops 33554432 | bytes 524292 | tf_op jit(solution)/shard_map/dot_general | solution.py:49
  33.9 0.6 %broadcast_in_dim.11 = f32[8,1,256]{2,1,0:T(1,128)} broadcast(f32[256]{0:T(256)S(1)} %fusion.5), dimensions={2} | broadcast | bytes 9216 | tf_op jit(solution)/shard_map/broadcast_in_dim | solution.py:62
  34.5 6.3 %all-to-all-start = ((f32[8,1,256]{2,1,0:T(1,128)}), f32[8,1,256]{2,1,0:T(1,128)S(1)}, u32[]{:S(2)}, u32[]{:S(2)}) async-start(f32[8,1,256]{2,1,0:T(1,128)} %broadcast_in_dim.11), calls=%async_computation | async-start | bytes 16384 | tf_op jit(solution)/shard_map/all_to_all | solution.py:63
  43.2 4.1 %all-to-all-done = f32[8,1,256]{2,1,0:T(1,128)S(1)} async-done(((f32[8,1,256]{2,1,0:T(1,128)}), f32[8,1,256]{2,1,0:T(1,128)S(1)}, u32[]{:S(2)}, u32[]{:S(2)}) %all-to-all-start) | async-done | bytes 8224 | tf_op jit(solution)/shard_map/all_to_all | solution.py:63
  47.9 0.7 %add_convert_fusion = bf16[4,1,64,256]{3,2,1,0:T(8,128)(2,1)} fusion(f32[4,1,64,256]{3,2,1,0:T(8,128)S(1)} %bitcast.212, bf16[4,1,64,256]{3,2,1,0:T(8,128)(2,1)S(1)} %collective-permute-done.6), kind=kLoop, calls=%fused_computation.37 | loop fusion | flops 196608 | bytes 524288 | tf_op jit(solution)/shard_map/convert_element_type | solution.py:82
  48.6 0.7 %add_convert_fusion.1 = bf16[4,1,64,256]{3,2,1,0:T(8,128)(2,1)} fusion(f32[4,1,64,256]{3,2,1,0:T(8,128)S(1)} %bitcast.213, bf16[4,1,64,256]{3,2,1,0:T(8,128)(2,1)S(1)} %collective-permute-done.5), kind=kLoop, calls=%fused_computation.38 | loop fusion | flops 196608 | bytes 524288 | tf_op jit(solution)/shard_map/convert_element_type | solution.py:82
  (93 shorter events, 6.9 us)
Async XLA Ops:
  1.8 3.2 %copy-start.2 = (bf16[4,1,64,512]{3,2,1,0:T(8,128)(2,1)S(1)}, bf16[4,1,64,512]{3,2,1,0:T(8,128)(2,1)}, u32[]{:S(2)}) copy-start(bf16[4,1,64,512]{3,2,1,0:T(8,128)(2,1)} %param.11) | copy-start | bytes 786436
  1.8 4.0 %copy-start.4 = (f32[256]{0:T(256)S(1)}, f32[256]{0:T(256)}, u32[]{:S(2)}) copy-start(f32[256]{0:T(256)} %param.9) | copy-start | bytes 3076
  1.9 4.6 %copy-start.15 = (f32[32]{0:T(128)S(1)}, f32[32]{0:T(128)}, u32[]{:S(2)}) copy-start(f32[32]{0:T(128)} %param.10) | copy-start | bytes 388
  3.8 4.3 %copy-start.1 = (bf16[4,1,64,512]{3,2,1,0:T(8,128)(2,1)S(1)}, bf16[4,1,64,512]{3,2,1,0:T(8,128)(2,1)}, u32[]{:S(2)}) copy-start(bf16[4,1,64,512]{3,2,1,0:T(8,128)(2,1)} %param.6) | copy-start | bytes 786436
  7.8 2.6 %copy-start.9 = (f32[1,256]{1,0:T(1,128)}, f32[1,256]{1,0:T(1,128)S(1)}, u32[]{:S(2)}) copy-start(f32[1,256]{1,0:T(1,128)S(1)} %get-tuple-element.64) | copy-start | bytes 3076
  7.8 2.6 %copy-start.10 = (f32[1,256]{1,0:T(1,128)}, f32[1,256]{1,0:T(1,128)S(1)}, u32[]{:S(2)}) copy-start(f32[1,256]{1,0:T(1,128)S(1)} %get-tuple-element.48) | copy-start | bytes 3076
  7.8 2.6 %copy-start.11 = (f32[1,256]{1,0:T(1,128)}, f32[1,256]{1,0:T(1,128)S(1)}, u32[]{:S(2)}) copy-start(f32[1,256]{1,0:T(1,128)S(1)} %get-tuple-element.50) | copy-start | bytes 3076
  7.8 2.7 %copy-start.8 = (f32[1,256]{1,0:T(1,128)}, f32[1,256]{1,0:T(1,128)S(1)}, u32[]{:S(2)}) copy-start(f32[1,256]{1,0:T(1,128)S(1)} %get-tuple-element.62) | copy-start | bytes 3076
  7.8 2.3 %copy-start.3 = (bf16[4,1,64,512]{3,2,1,0:T(8,128)(2,1)S(1)}, bf16[4,1,64,512]{3,2,1,0:T(8,128)(2,1)}, u32[]{:S(2)}) copy-start(bf16[4,1,64,512]{3,2,1,0:T(8,128)(2,1)} %get-tuple-element.25) | copy-start | bytes 786436
  8.3 5.2 %copy-start.14 = (f32[33]{0:T(128)S(1)}, f32[33]{0:T(128)}, u32[]{:S(2)}) copy-start(f32[33]{0:T(128)} %copy-done.13) | copy-start | bytes 400
  8.3 5.2 %copy-start.16 = (f32[32]{0:T(128)S(1)}, f32[32]{0:T(128)}, u32[]{:S(2)}) copy-start(f32[32]{0:T(128)} %param.10) | copy-start | bytes 388
  8.3 5.5 %copy-start.5 = (f32[256]{0:T(256)S(1)}, f32[256]{0:T(256)}, u32[]{:S(2)}) copy-start(f32[256]{0:T(256)} %param.9) | copy-start | bytes 3076
  8.3 5.8 %copy-start.6 = (f32[1,256]{1,0:T(1,128)S(1)}, f32[1,256]{1,0:T(1,128)}, u32[]{:S(2)}) copy-start(f32[1,256]{1,0:T(1,128)} %get-tuple-element.47) | copy-start | bytes 3076
  8.3 6.5 %copy-start.7 = (f32[1,256]{1,0:T(1,128)S(1)}, f32[1,256]{1,0:T(1,128)}, u32[]{:S(2)}) copy-start(f32[1,256]{1,0:T(1,128)} %get-tuple-element.61) | copy-start | bytes 3076
  10.5 5.2 %collective-permute-start = (f32[1,64,256]{2,1,0:T(8,128)S(1)}, f32[1,64,256]{2,1,0:T(8,128)S(1)}, u32[]{:S(2)}, u32[]{:S(2)}) collective-permute-start(f32[1,64,256]{2,1,0:T(8,128)S(1)} %get-tuple-element.18), channel_id=1, source_target_pairs={{0,2},{2,0},{4,6},{6,4},{8,10},{10,8},{12,14},{14,12},{1,3},{3,1},... | collective-permute-start | bytes 196616 | tf_op jit(solution)/shard_map/ppermute | solution.py:118
  15.7 6.3 %collective-permute-start.1 = (f32[1,64,256]{2,1,0:T(8,128)S(1)}, f32[1,64,256]{2,1,0:T(8,128)S(1)}, u32[]{:S(2)}, u32[]{:S(2)}) collective-permute-start(f32[1,64,256]{2,1,0:T(8,128)S(1)} %fusion.18), channel_id=1, source_target_pairs={{2,6},{6,10},{10,14},{4,0},{8,4},{12,8},{3,7},{7,11},{11,15},{5,1}... | collective-permute-start | bytes 196616 | tf_op jit(solution)/shard_map/ppermute | solution.py:130
  17.0 9.6 %collective-permute-start.2 = (f32[1,64,256]{2,1,0:T(8,128)S(1)}, f32[1,64,256]{2,1,0:T(8,128)S(1)}, u32[]{:S(2)}, u32[]{:S(2)}) collective-permute-start(f32[1,64,256]{2,1,0:T(8,128)S(1)} %fusion.18), channel_id=1, source_target_pairs={{2,10},{6,14},{8,0},{12,4},{3,11},{7,15},{9,1},{13,5},{18,26},{22,... | collective-permute-start | bytes 196616 | tf_op jit(solution)/shard_map/ppermute | solution.py:130
  18.3 9.2 %collective-permute-start.3 = (f32[1,64,256]{2,1,0:T(8,128)S(1)}, f32[1,64,256]{2,1,0:T(8,128)S(1)}, u32[]{:S(2)}, u32[]{:S(2)}) collective-permute-start(f32[1,64,256]{2,1,0:T(8,128)S(1)} %fusion.18), channel_id=1, source_target_pairs={{2,14},{12,0},{3,15},{13,1},{18,30},{28,16},{19,31},{29,17}} | collective-permute-start | bytes 196616 | tf_op jit(solution)/shard_map/ppermute | solution.py:130
  27.6 4.3 %collective-permute-start.4 = (f32[1,64,256]{2,1,0:T(8,128)S(1)}, f32[1,64,256]{2,1,0:T(8,128)S(1)}, u32[]{:S(2)}, u32[]{:S(2)}) collective-permute-start(f32[1,64,256]{2,1,0:T(8,128)S(1)} %multiply_add_fusion), channel_id=1, source_target_pairs={{0,2},{2,0},{4,6},{6,4},{8,10},{10,8},{12,14},{14,12},{1,3},{3,1},... | collective-permute-start | bytes 196616 | tf_op jit(solution)/shard_map/ppermute | solution.py:136
  32.0 1.8 %copy-start.12 = (f32[256]{0:T(256)S(1)}, f32[256]{0:T(256)}, u32[]{:S(2)}) copy-start(f32[256]{0:T(256)} %get-tuple-element.55) | copy-start | bytes 3076
  34.5 12.8 %all-to-all-start = ((f32[8,1,256]{2,1,0:T(1,128)}), f32[8,1,256]{2,1,0:T(1,128)S(1)}, u32[]{:S(2)}, u32[]{:S(2)}) async-start(f32[8,1,256]{2,1,0:T(1,128)} %broadcast_in_dim.11), calls=%async_computation | async-start | bytes 16384 | tf_op jit(solution)/shard_map/all_to_all | solution.py:63
  40.8 1.0 %copy-start = (f32[256,256]{1,0:T(8,128)S(1)}, f32[256,256]{1,0:T(8,128)}, u32[]{:S(2)}) copy-start(f32[256,256]{1,0:T(8,128)} %fusion.8) | copy-start | bytes 786436
  41.3 6.6 %collective-permute-start.6 = (bf16[4,1,64,256]{3,2,1,0:T(8,128)(2,1)S(1)}, bf16[4,1,64,256]{3,2,1,0:T(8,128)(2,1)S(1)}, u32[]{:S(2)}, u32[]{:S(2)}) collective-permute-start(bf16[4,1,64,256]{3,2,1,0:T(8,128)(2,1)S(1)} %bitcast.215), channel_id=1, source_target_pairs={{0,1},{1,0},{2,3},{3,2},{4,5},{5,4},{6,7},{7,6},{8,9},{9,8},{10,11... | collective-permute-start | bytes 393224 | tf_op jit(solution)/shard_map/ppermute | solution.py:80
  42.2 6.3 %collective-permute-start.5 = (bf16[4,1,64,256]{3,2,1,0:T(8,128)(2,1)S(1)}, bf16[4,1,64,256]{3,2,1,0:T(8,128)(2,1)S(1)}, u32[]{:S(2)}, u32[]{:S(2)}) collective-permute-start(bf16[4,1,64,256]{3,2,1,0:T(8,128)(2,1)S(1)} %bitcast.216), channel_id=1, source_target_pairs={{0,1},{1,0},{2,3},{3,2},{4,5},{5,4},{6,7},{7,6},{8,9},{9,8},{10,11... | collective-permute-start | bytes 393224 | tf_op jit(solution)/shard_map/ppermute | solution.py:80
  (1 other events, 0.6 us)

commit v7 on v2

--- a/solution.py
+++ b/solution.py
@@ -83,30 +83,59 @@
     return (own + got.astype(jnp.float32)).astype(jnp.bfloat16)
 
 
-def block_carries(fwd_end, bwd_start, fwd_prod, bwd_prod, axis):
-    count = lax.axis_size(axis)
-    mine = lax.axis_index(axis)
+def cyclic_carries(fwd_end, bwd_start, fwd_prod, bwd_prod, axis, index, count, route):
     received = {}
     for step in range(1, count):
-        message = jnp.where(mine + step < count, fwd_end, bwd_start)
-        received[step] = lax.ppermute(message, axis, [(i, (i + step) % count) for i in range(count)])
+        message = jnp.where(index + step < count, fwd_end, bwd_start)
+        received[step] = lax.ppermute(message, axis, route(step))
     carry_in = jnp.zeros_like(fwd_end)
     for step in reversed(range(1, count)):
-        source = mine - step
+        source = index - step
         factor = lax.dynamic_index_in_dim(fwd_prod, jnp.maximum(source, 0), 0, keepdims=False)
         carry_in = jnp.where(source >= 0, received[step], 0.0) + factor * carry_in
     carry_back = jnp.zeros_like(bwd_start)
     for step in reversed(range(1, count)):
-        source = mine + step
+        source = index + step
         factor = lax.dynamic_index_in_dim(bwd_prod, jnp.minimum(source, count - 1), 0, keepdims=False)
         carry_back = jnp.where(source < count, received[count - step], 0.0) + factor * carry_back
     return carry_in, carry_back
+
+
+def group_sum(value, axis, index, count, route):
+    if count == 1:
+        return value
+    if count & (count - 1):
+        return None
+    step = 1
+    while step < count:
+        value = value + lax.ppermute(value, axis, route(step))
+        step *= 2
+    return value
 
 
 def local(frames_in, in_kernel, out_kernel, decay_rate, frame_keep, out_grad):
     frame_count, row_count, col_count = frames_in.shape[:3]
     position = lax.axis_index("tm")
     blocks = lax.axis_size("tm")
+    width = 2 if blocks % 2 == 0 else 1
+    groups = blocks // width
+    group = position // width
+    upper = position % width == 1
+    if width == 2:
+        swap = [(i, i ^ 1) for i in range(blocks)]
+        other_frames = lax.ppermute(frames_in, "tm", swap)
+        other_grad = lax.ppermute(out_grad, "tm", swap)
+        frames_in = jnp.where(
+            upper,
+            jnp.concatenate([other_frames, frames_in]),
+            jnp.concatenate([frames_in, other_frames]),
+        )
+        out_grad = jnp.where(
+            upper,
+            jnp.concatenate([other_grad, out_grad]),
+            jnp.concatenate([out_grad, other_grad]),
+        )
+    span = frame_count * width
     in_halo = row_halo(frames_in)
     grad_halo = row_halo(out_grad)
     row_taps = row_taps_of(in_halo, row_count)
@@ -114,16 +143,16 @@
     adjoint_in = conv_apply(out_grad, grad_halo, prep_kernel(out_kernel, True, row_taps), row_taps)
     input_gain = jnp.sqrt(1.0 - decay_rate * decay_rate)
     keep_padded = jnp.concatenate([frame_keep, jnp.zeros((1,), jnp.float32)])
-    offset = position * frame_count
-    keep_here = lax.dynamic_slice_in_dim(keep_padded, offset, frame_count)
-    keep_next = lax.dynamic_slice_in_dim(keep_padded, offset + 1, frame_count)
+    offset = group * span
+    keep_here = lax.dynamic_slice_in_dim(keep_padded, offset, span)
+    keep_next = lax.dynamic_slice_in_dim(keep_padded, offset + 1, span)
     decays = keep_here[:, None] * decay_rate[None, :]
     decays_next = keep_next[:, None] * decay_rate[None, :]
 
     running = None
     product = None
     local_states, products = [], []
-    for t in range(frame_count):
+    for t in range(span):
         fresh = input_gain * values[t]
         running = fresh if running is None else decays[t] * running + fresh
         product = decays[t] if product is None else product * decays[t]
@@ -131,32 +160,49 @@
         products.append(product)
     running = None
     product = None
-    back_states, back_products = [None] * frame_count, [None] * frame_count
-    for t in reversed(range(frame_count)):
+    back_states, back_products = [None] * span, [None] * span
+    for t in reversed(range(span)):
         running = adjoint_in[t] if running is None else adjoint_in[t] + decays_next[t] * running
         product = decays_next[t] if product is None else product * decays_next[t]
         back_states[t] = running
         back_products[t] = product
 
-    all_decays = (frame_keep[:, None] * decay_rate[None, :]).reshape(blocks, frame_count, -1)
-    all_next = (keep_padded[1:, None] * decay_rate[None, :]).reshape(blocks, frame_count, -1)
+    all_decays = (frame_keep[:, None] * decay_rate[None, :]).reshape(groups, span, -1)
+    all_next = (keep_padded[1:, None] * decay_rate[None, :]).reshape(groups, span, -1)
     fwd_prod = all_decays[:, 0]
-    for t in range(1, frame_count):
+    for t in range(1, span):
         fwd_prod = fwd_prod * all_decays[:, t]
-    bwd_prod = all_next[:, frame_count - 1]
-    for t in reversed(range(frame_count - 1)):
+    bwd_prod = all_next[:, span - 1]
+    for t in reversed(range(span - 1)):
         bwd_prod = bwd_prod * all_next[:, t]
-    carry_in, carry_back = block_carries(local_states[-1], back_states[0], fwd_prod, bwd_prod, "tm")
-
-    states = jnp.stack([local_states[t] + products[t] * carry_in for t in range(frame_count)])
-    adjoints = jnp.stack([back_states[t] + back_products[t] * carry_back for t in range(frame_count)])
+
+    def route(step, cyclic=True):
+        return [
+            (width * z + x, width * ((z + step) % groups if cyclic else z ^ step) + x)
+            for z in range(groups)
+            for x in range(width)
+        ]
+
+    carry_in, carry_back = cyclic_carries(
+        local_states[-1], back_states[0], fwd_prod, bwd_prod, "tm", group, groups, route
+    )
+
+    states = jnp.stack([local_states[t] + products[t] * carry_in for t in range(span)])
+    adjoints = jnp.stack([back_states[t] + back_products[t] * carry_back for t in range(span)])
     previous = jnp.concatenate([carry_in[None], states[:-1]], axis=0)
     terms = adjoints * (
         decays[:, None, None, :] * previous - decay_rate * decay_rate / input_gain * values
     )
     total_count = frame_count * blocks * row_count * lax.axis_size("rows") * col_count
-    grad_decay = all_sum(all_sum(jnp.sum(terms, axis=(0, 1, 2)), "tm"), "rows") / math.sqrt(total_count)
-
+    partial = jnp.sum(terms, axis=(0, 1, 2))
+    summed = group_sum(partial, "tm", group, groups, lambda step: route(step, False))
+    if summed is None:
+        summed = lax.psum(partial, "tm") / width
+    grad_decay = all_sum(summed, "rows") / math.sqrt(total_count)
+
+    if width == 2:
+        states = jnp.where(upper, states[frame_count:], states[:frame_count])
+        adjoints = jnp.where(upper, adjoints[frame_count:], adjoints[:frame_count])
     state_b = states.astype(jnp.bfloat16)
     adjoint_b = adjoints.astype(jnp.bfloat16)
     mixed = chan_sum(state_b, row_halo(state_b), prep_kernel(out_kernel, False, row_taps), row_taps)

time: 51.9 us -> 42.2 us (0.81)
  local copies, waits for them, and re-layouts: 9.78 us -> 4.06 us
  starting transfers between devices: 13.6 us -> 11.4 us
  other arithmetic: 6.74 us -> 5.13 us
  matrix products: 4.93 us -> 4.39 us
    slice x4, local copies, waits for them, and re-layouts: 2.8 us -> 0.54 us  [conv_apply(): padded[:, row_tap:row_tap + row_count, col_tap:col_tap + col_count, :]]
    ppermute x10 -> x7, starting transfers between devices: 12.9 us -> 11.3 us  [the longest x3 5.88 us: cyclic_carries(): received[step] = lax.ppermute(message, axis, route(step))]
    slice x1, local copies, waits for them, and re-layouts: 1.24 us -> 0.07 us  [local(): keep_padded[1:, None] * decay_rate[None, :]]
    select_n x2 -> x3, other arithmetic: 0.8 us -> 1.64 us  [the longest x1 1.52 us: local(): jnp.where(upper, jnp.concatenate([other_frames, frames_in]), jnp.concaten...]
    another operation x3 -> x1, other arithmetic: 0.79 us -> 0.02 us  [local(): jnp.stack([back_states[t] + back_products[t] * carry_back for t in range(...]
    mul x1, other arithmetic: 0.71 us -> 0.01 us  [local(): product = decays_next[t] if product is None else product * decays_next[t]]
    mul x1, other arithmetic: 0.77 us -> 0.08 us  [local(): keep_padded[1:, None] * decay_rate[None, :]]
    mul x1, other arithmetic: 0.69 us -> 0.01 us  [local(): product = decays[t] if product is None else product * decays[t]]
  transfers between devices with their start and end apart: 12 -> 9, of which waited for: 5 -> 7; matrix products, arithmetic and copies ran while one was open for 17% -> 16% of each run, Pallas kernels for 0% -> 0%
where the time goes in v7:
time: 42.2 us; the launch traced here: 42 us
  waiting for transfers between devices  15.9 us (38%)
  starting transfers between devices  11.4 us (27%)
  other arithmetic  5.13 us (12%)
  matrix products  4.39 us (10%)
  local copies, waits for them, and re-layouts  4.06 us (10%)
  between operations  1.1 us (3%)
    ppermute x3, starting transfers between devices, cyclic_carries(): received[step] = lax.ppermute(message, axis, route(step))  5.88 us
    ppermute x2, waiting for transfers between devices, group_sum(): value = value + lax.ppermute(value, axis, route(step))  5.22 us
    ppermute x1, waiting for transfers between devices, local(): other_grad = lax.ppermute(out_grad, 'tm', swap)  4.79 us
    dot_general x18, matrix products, conv_apply(): jnp.dot(portion.reshape(-1, channels), taps[index, col_tap], preferred_el...  4.39 us
    ppermute x3, waiting for transfers between devices, cyclic_carries(): received[step] = lax.ppermute(message, axis, route(step))  3.17 us
    ppermute x1, starting transfers between devices, local(): other_frames = lax.ppermute(frames_in, 'tm', swap)  3 us
    ppermute x1, waiting for transfers between devices, local(): other_frames = lax.ppermute(frames_in, 'tm', swap)  2.71 us
    ppermute x2, starting transfers between devices, group_sum(): value = value + lax.ppermute(value, axis, route(step))  2.33 us
  transfers between devices with their start and end apart: 9, of which 7 were waited for; matrix products, arithmetic and copies ran while one was open for 16% of the time, Pallas kernels for 0%

profile of v7, /device:TPU:0, one launch (start us, length us, event | category | flops | bytes accessed | tf_op | source)
XLA Modules:
  0.0 42.0 jit_solution(406508313799870582)
XLA Ops:
  0.6 3.0 %collective-permute-start = (bf16[4,1,64,512]{3,2,1,0:T(8,128)(2,1)}, bf16[4,1,64,512]{3,2,1,0:T(8,128)(2,1)}, u32[]{:S(2)}, u32[]{:S(2)}) collective-permute-start(bf16[4,1,64,512]{3,2,1,0:T(8,128)(2,1)} %param.6), channel_id=1, source_target_pairs={{0,2},{2,0},{4,6},{6,4},{8,10},{10,8},{12,14},{14,12},{1,3},{3,1},... | collective-permute-start | bytes 786440 | tf_op jit(solution)/shard_map/ppermute | solution.py:126
  3.7 0.7 %mul.853 = f32[4,8]{1,0:T(4,128)S(1)} reshape(f32[32]{0:T(128)} %param.10) | data formatting | bytes 256 | tf_op jit(solution)/shard_map/mul | solution.py:170
  4.5 0.7 %pad_maximum_fusion = f32[33]{0:T(128)S(1)} fusion(f32[1]{0:T(128)} %constant.67.clone.1, f32[32]{0:T(128)} %param.10), kind=kLoop, calls=%fused_computation.176 | loop fusion | flops 33 | bytes 264 | tf_op jit(solution)/shard_map/concatenate | solution.py:145
  5.2 1.2 %slice.316 = bf16[1,3,256,512]{3,2,1,0:T(8,128)(2,1)S(1)} slice(bf16[3,3,256,512]{3,2,1,0:T(8,128)(2,1)} %param.8), slice={[1:2], [0:3], [0:256], [0:512]} | slice | bytes 1572864 | tf_op jit(solution)/shard_map/slice | solution.py:28
  6.5 1.2 %slice.298 = bf16[1,3,512,256]{3,2,1,0:T(8,128)(2,1)S(1)} slice(bf16[3,3,512,256]{3,2,1,0:T(8,128)(2,1)} %param.7), slice={[1:2], [0:3], [0:512], [0:256]} | slice | bytes 1572864 | tf_op jit(solution)/shard_map/slice | solution.py:31
  8.4 2.7 %collective-permute-done = bf16[4,1,64,512]{3,2,1,0:T(8,128)(2,1)} collective-permute-done((bf16[4,1,64,512]{3,2,1,0:T(8,128)(2,1)}, bf16[4,1,64,512]{3,2,1,0:T(8,128)(2,1)}, u32[]{:S(2)}, u32[]{:S(2)}) %collective-permute-start) | collective-permute-done | bytes 262176 | tf_op jit(solution)/shard_map/ppermute | solution.py:126
  11.1 4.8 %collective-permute-done.1 = bf16[4,1,64,512]{3,2,1,0:T(8,128)(2,1)} collective-permute-done((bf16[4,1,64,512]{3,2,1,0:T(8,128)(2,1)}, bf16[4,1,64,512]{3,2,1,0:T(8,128)(2,1)}, u32[]{:S(2)}, u32[]{:S(2)}) %collective-permute-start.1) | collective-permute-done | bytes 262176 | tf_op jit(solution)/shard_map/ppermute | solution.py:127
  15.9 1.5 %maximum_select_fusion = (bf16[8,1,64,512]{3,2,1,0:T(8,128)(2,1)S(1)}, bf16[8,1,64,512]{3,2,1,0:T(8,128)(2,1)S(1)}) fusion(bf16[4,1,64,512]{3,2,1,0:T(8,128)(2,1)S(1)} %copy-done, bf16[4,1,64,512]{3,2,1,0:T(8,128)(2,1)} %collective-permute-done, pred[]{:T(512)S(6)} %eq.5, bf16[4,1,64,512]{3,2,1,0:T(8,128)(2,1)} %collective-permute-done.1, ...), kind=kLoop, calls=%fused_computation.24 | loop fusion | flops 1572864 | bytes 2097153 | tf_op jit(solution)/shard_map/jit(_where)/select_n | solution.py:128
  17.9 0.3 fusion.4
  18.2 0.3 convolution_add_fusion.1
  18.5 0.3 convolution_add_fusion
  19.9 1.9 %collective-permute-start.2 = (f32[1,64,256]{2,1,0:T(8,128)S(1)}, f32[1,64,256]{2,1,0:T(8,128)S(1)}, u32[]{:S(2)}, u32[]{:S(2)}) collective-permute-start(f32[1,64,256]{2,1,0:T(8,128)S(1)} %get-tuple-element.50), channel_id=1, source_target_pairs={{0,4},{2,6},{4,8},{6,10},{8,12},{10,14},{12,0},{14,2},{1,5},{3,7},... | collective-permute-start | bytes 196616 | tf_op jit(solution)/shard_map/ppermute | solution.py:90
  21.8 2.7 %collective-permute-start.3 = (f32[1,64,256]{2,1,0:T(8,128)S(1)}, f32[1,64,256]{2,1,0:T(8,128)S(1)}, u32[]{:S(2)}, u32[]{:S(2)}) collective-permute-start(f32[1,64,256]{2,1,0:T(8,128)S(1)} %get-tuple-element.69), channel_id=1, source_target_pairs={{0,8},{2,10},{4,12},{6,14},{8,0},{10,2},{12,4},{14,6},{1,9},{3,11}... | collective-permute-start | bytes 196616 | tf_op jit(solution)/shard_map/ppermute | solution.py:90
  24.4 1.4 %collective-permute-start.4 = (f32[1,64,256]{2,1,0:T(8,128)S(1)}, f32[1,64,256]{2,1,0:T(8,128)S(1)}, u32[]{:S(2)}, u32[]{:S(2)}) collective-permute-start(f32[1,64,256]{2,1,0:T(8,128)S(1)} %get-tuple-element.70), channel_id=1, source_target_pairs={{0,12},{2,14},{4,0},{6,2},{8,4},{10,6},{12,8},{14,10},{1,13},{3,15... | collective-permute-start | bytes 196616 | tf_op jit(solution)/shard_map/ppermute | solution.py:90
  25.8 1.0 %collective-permute-done.2 = f32[1,64,256]{2,1,0:T(8,128)S(1)} collective-permute-done((f32[1,64,256]{2,1,0:T(8,128)S(1)}, f32[1,64,256]{2,1,0:T(8,128)S(1)}, u32[]{:S(2)}, u32[]{:S(2)}) %collective-permute-start.2) | collective-permute-done | bytes 65568 | tf_op jit(solution)/shard_map/ppermute | solution.py:90
  26.8 1.9 %collective-permute-done.3 = f32[1,64,256]{2,1,0:T(8,128)S(1)} collective-permute-done((f32[1,64,256]{2,1,0:T(8,128)S(1)}, f32[1,64,256]{2,1,0:T(8,128)S(1)}, u32[]{:S(2)}, u32[]{:S(2)}) %collective-permute-start.3) | collective-permute-done | bytes 65568 | tf_op jit(solution)/shard_map/ppermute | solution.py:90
  28.7 0.3 collective-permute-done.4
  32.0 0.9 %collective-permute-start.7 = (f32[256]{0:T(256)S(1)}, f32[256]{0:T(256)S(1)}, u32[]{:S(2)}, u32[]{:S(2)}) collective-permute-start(f32[256]{0:T(256)S(1)} %fusion.3), channel_id=1, source_target_pairs={{0,4},{2,6},{4,0},{6,2},{8,12},{10,14},{12,8},{14,10},{1,5},{3,7},... | collective-permute-start | bytes 3080 | tf_op jit(solution)/shard_map/ppermute | solution.py:111
  33.1 2.5 %collective-permute-done.7 = f32[256]{0:T(256)S(1)} collective-permute-done((f32[256]{0:T(256)S(1)}, f32[256]{0:T(256)S(1)}, u32[]{:S(2)}, u32[]{:S(2)}) %collective-permute-start.7) | collective-permute-done | bytes 1056 | tf_op jit(solution)/shard_map/ppermute | solution.py:111
  35.6 1.4 %collective-permute-start.8 = (f32[256]{0:T(256)S(1)}, f32[256]{0:T(256)S(1)}, u32[]{:S(2)}, u32[]{:S(2)}) collective-permute-start(f32[256]{0:T(256)S(1)} %add.342), channel_id=1, source_target_pairs={{0,8},{2,10},{4,12},{6,14},{8,0},{10,2},{12,4},{14,6},{1,9},{3,11}... | collective-permute-start | bytes 3080 | tf_op jit(solution)/shard_map/ppermute | solution.py:111
  37.3 2.7 %collective-permute-done.8 = f32[256]{0:T(256)S(1)} collective-permute-done((f32[256]{0:T(256)S(1)}, f32[256]{0:T(256)S(1)}, u32[]{:S(2)}, u32[]{:S(2)}) %collective-permute-start.8) | collective-permute-done | bytes 1056 | tf_op jit(solution)/shard_map/ppermute | solution.py:111
  40.1 0.6 %add_multiply_fusion = f32[256]{0:T(256)} fusion(f32[256]{0:T(256)S(1)} %add.342, f32[256]{0:T(256)S(1)} %collective-permute-done.8), kind=kLoop, calls=%fused_computation.173 | loop fusion | flops 512 | bytes 3072 | tf_op jit(solution)/shard_map/div | solution.py:201
  40.6 0.7 %add_convert_fusion.1 = bf16[4,1,64,256]{3,2,1,0:T(8,128)(2,1)} fusion(f32[4,1,64,256]{3,2,1,0:T(8,128)S(1)} %bitcast.282, bf16[4,1,64,256]{3,2,1,0:T(8,128)(2,1)S(1)} %collective-permute-done.5), kind=kLoop, calls=%fused_computation.43 | loop fusion | flops 196608 | bytes 524288 | tf_op jit(solution)/shard_map/convert_element_type | solution.py:83
  41.3 0.7 %add_convert_fusion = bf16[4,1,64,256]{3,2,1,0:T(8,128)(2,1)} fusion(f32[4,1,64,256]{3,2,1,0:T(8,128)S(1)} %bitcast.283, bf16[4,1,64,256]{3,2,1,0:T(8,128)(2,1)S(1)} %collective-permute-done.6), kind=kLoop, calls=%fused_computation.42 | loop fusion | flops 196608 | bytes 524288 | tf_op jit(solution)/shard_map/convert_element_type | solution.py:83
  (65 shorter events, 5.5 us)
Async XLA Ops:
  0.6 10.5 %collective-permute-start = (bf16[4,1,64,512]{3,2,1,0:T(8,128)(2,1)}, bf16[4,1,64,512]{3,2,1,0:T(8,128)(2,1)}, u32[]{:S(2)}, u32[]{:S(2)}) collective-permute-start(bf16[4,1,64,512]{3,2,1,0:T(8,128)(2,1)} %param.6), channel_id=1, source_target_pairs={{0,2},{2,0},{4,6},{6,4},{8,10},{10,8},{12,14},{14,12},{1,3},{3,1},... | collective-permute-start | bytes 786440 | tf_op jit(solution)/shard_map/ppermute | solution.py:126
  3.6 12.2 %collective-permute-start.1 = (bf16[4,1,64,512]{3,2,1,0:T(8,128)(2,1)}, bf16[4,1,64,512]{3,2,1,0:T(8,128)(2,1)}, u32[]{:S(2)}, u32[]{:S(2)}) collective-permute-start(bf16[4,1,64,512]{3,2,1,0:T(8,128)(2,1)} %param.11), channel_id=1, source_target_pairs={{0,2},{2,0},{4,6},{6,4},{8,10},{10,8},{12,14},{14,12},{1,3},{3,1},... | collective-permute-start | bytes 786440 | tf_op jit(solution)/shard_map/ppermute | solution.py:127
  6.4 1.3 %copy-start.1 = (f32[256]{0:T(256)S(1)}, f32[256]{0:T(256)}, u32[]{:S(2)}) copy-start(f32[256]{0:T(256)} %param.9) | copy-start | bytes 3076
  6.4 9.4 %copy-start = (bf16[4,1,64,512]{3,2,1,0:T(8,128)(2,1)S(1)}, bf16[4,1,64,512]{3,2,1,0:T(8,128)(2,1)}, u32[]{:S(2)}) copy-start(bf16[4,1,64,512]{3,2,1,0:T(8,128)(2,1)} %param.6) | copy-start | bytes 786436
  19.9 6.9 %collective-permute-start.2 = (f32[1,64,256]{2,1,0:T(8,128)S(1)}, f32[1,64,256]{2,1,0:T(8,128)S(1)}, u32[]{:S(2)}, u32[]{:S(2)}) collective-permute-start(f32[1,64,256]{2,1,0:T(8,128)S(1)} %get-tuple-element.50), channel_id=1, source_target_pairs={{0,4},{2,6},{4,8},{6,10},{8,12},{10,14},{12,0},{14,2},{1,5},{3,7},... | collective-permute-start | bytes 196616 | tf_op jit(solution)/shard_map/ppermute | solution.py:90
  21.8 6.9 %collective-permute-start.3 = (f32[1,64,256]{2,1,0:T(8,128)S(1)}, f32[1,64,256]{2,1,0:T(8,128)S(1)}, u32[]{:S(2)}, u32[]{:S(2)}) collective-permute-start(f32[1,64,256]{2,1,0:T(8,128)S(1)} %get-tuple-element.69), channel_id=1, source_target_pairs={{0,8},{2,10},{4,12},{6,14},{8,0},{10,2},{12,4},{14,6},{1,9},{3,11}... | collective-permute-start | bytes 196616 | tf_op jit(solution)/shard_map/ppermute | solution.py:90
  24.4 4.5 %collective-permute-start.4 = (f32[1,64,256]{2,1,0:T(8,128)S(1)}, f32[1,64,256]{2,1,0:T(8,128)S(1)}, u32[]{:S(2)}, u32[]{:S(2)}) collective-permute-start(f32[1,64,256]{2,1,0:T(8,128)S(1)} %get-tuple-element.70), channel_id=1, source_target_pairs={{0,12},{2,14},{4,0},{6,2},{8,4},{10,6},{12,8},{14,10},{1,13},{3,15... | collective-permute-start | bytes 196616 | tf_op jit(solution)/shard_map/ppermute | solution.py:90
  31.2 9.4 %collective-permute-start.5 = (bf16[4,1,64,256]{3,2,1,0:T(8,128)(2,1)S(1)}, bf16[4,1,64,256]{3,2,1,0:T(8,128)(2,1)S(1)}, u32[]{:S(2)}, u32[]{:S(2)}) collective-permute-start(bf16[4,1,64,256]{3,2,1,0:T(8,128)(2,1)S(1)} %bitcast.284), channel_id=1, source_target_pairs={{0,1},{1,0},{2,3},{3,2},{4,5},{5,4},{6,7},{7,6},{8,9},{9,8},{10,11... | collective-permute-start | bytes 393224 | tf_op jit(solution)/shard_map/ppermute | solution.py:81
  32.0 3.6 %collective-permute-start.7 = (f32[256]{0:T(256)S(1)}, f32[256]{0:T(256)S(1)}, u32[]{:S(2)}, u32[]{:S(2)}) collective-permute-start(f32[256]{0:T(256)S(1)} %fusion.3), channel_id=1, source_target_pairs={{0,4},{2,6},{4,0},{6,2},{8,12},{10,14},{12,8},{14,10},{1,5},{3,7},... | collective-permute-start | bytes 3080 | tf_op jit(solution)/shard_map/ppermute | solution.py:111
  35.6 4.5 %collective-permute-start.8 = (f32[256]{0:T(256)S(1)}, f32[256]{0:T(256)S(1)}, u32[]{:S(2)}, u32[]{:S(2)}) collective-permute-start(f32[256]{0:T(256)S(1)} %add.342), channel_id=1, source_target_pairs={{0,8},{2,10},{4,12},{6,14},{8,0},{10,2},{12,4},{14,6},{1,9},{3,11}... | collective-permute-start | bytes 3080 | tf_op jit(solution)/shard_map/ppermute | solution.py:111
  37.2 4.1 %collective-permute-start.6 = (bf16[4,1,64,256]{3,2,1,0:T(8,128)(2,1)S(1)}, bf16[4,1,64,256]{3,2,1,0:T(8,128)(2,1)S(1)}, u32[]{:S(2)}, u32[]{:S(2)}) collective-permute-start(bf16[4,1,64,256]{3,2,1,0:T(8,128)(2,1)S(1)} %bitcast.285), channel_id=1, source_target_pairs={{0,1},{1,0},{2,3},{3,2},{4,5},{5,4},{6,7},{7,6},{8,9},{9,8},{10,11... | collective-permute-start | bytes 393224 | tf_op jit(solution)/shard_map/ppermute | solution.py:81

commit v8 on v7

--- a/solution.py
+++ b/solution.py
@@ -123,8 +123,15 @@
     upper = position % width == 1
     if width == 2:
         swap = [(i, i ^ 1) for i in range(blocks)]
-        other_frames = lax.ppermute(frames_in, "tm", swap)
-        other_grad = lax.ppermute(out_grad, "tm", swap)
+        if lax.axis_size("chan") == 2:
+            first = lax.axis_index("chan") == 0
+            got = lax.ppermute(jnp.where(first, frames_in, out_grad), "tm", swap)
+            traded = lax.ppermute(got, "chan", [(0, 1), (1, 0)])
+            other_frames = jnp.where(first, got, traded)
+            other_grad = jnp.where(first, traded, got)
+        else:
+            other_frames = lax.ppermute(frames_in, "tm", swap)
+            other_grad = lax.ppermute(out_grad, "tm", swap)
         frames_in = jnp.where(
             upper,
             jnp.concatenate([other_frames, frames_in]),

time: 42.2 us -> 41.6 us (0.986)
  waiting for transfers between devices: 15.9 us -> 11 us
  other arithmetic: 5.13 us -> 8.75 us
  starting transfers between devices: 11.4 us -> 11.9 us
    ppermute x2, waiting for transfers between devices: 7.5 us -> 2.8 us  [the longest x1 1.85 us: local(): traded = lax.ppermute(got, 'chan', [(0, 1), (1, 0)])]
    select_n x0 -> x2, other arithmetic: none -> 2.77 us  [the longest x1 1.71 us: local(): got = lax.ppermute(jnp.where(first, frames_in, out_grad), 'tm', swap)]
    ppermute x2, starting transfers between devices: 2.33 us -> 2.97 us  [group_sum(): value = value + lax.ppermute(value, axis, route(step))]
    ppermute x2, waiting for transfers between devices: 5.22 us -> 4.58 us  [group_sum(): value = value + lax.ppermute(value, axis, route(step))]
    mul x1, other arithmetic: 0.01 us -> 0.61 us  [local(): product = decays_next[t] if product is None else product * decays_next[t]]
    div x1, other arithmetic: 0.01 us -> 0.58 us  [local(): decay_rate * decay_rate / input_gain * values]
    ppermute x3, waiting for transfers between devices: 3.17 us -> 3.59 us  [cyclic_carries(): received[step] = lax.ppermute(message, axis, route(step))]
  transfers between devices with their start and end apart: 9 -> 9, of which waited for: 7 -> 7; matrix products, arithmetic and copies ran while one was open for 16% -> 19% of each run, Pallas kernels for 0% -> 0%
where the time goes in v8:
time: 41.6 us; the launch traced here: 41.3 us
  starting transfers between devices  11.9 us (29%)
  waiting for transfers between devices  11 us (26%)
  other arithmetic  8.75 us (21%)
  matrix products  4.39 us (11%)
  local copies, waits for them, and re-layouts  4.05 us (10%)
  between operations  1.17 us (3%)
    ppermute x3, starting transfers between devices, cyclic_carries(): received[step] = lax.ppermute(message, axis, route(step))  5.88 us
    ppermute x2, waiting for transfers between devices, group_sum(): value = value + lax.ppermute(value, axis, route(step))  4.58 us
    dot_general x18, matrix products, conv_apply(): jnp.dot(portion.reshape(-1, channels), taps[index, col_tap], preferred_el...  4.39 us
    ppermute x3, waiting for transfers between devices, cyclic_carries(): received[step] = lax.ppermute(message, axis, route(step))  3.59 us
    ppermute x2, starting transfers between devices, group_sum(): value = value + lax.ppermute(value, axis, route(step))  2.97 us
    ppermute x1, starting transfers between devices, local(): got = lax.ppermute(jnp.where(first, frames_in, out_grad), 'tm', swap)  2.94 us
    ppermute x1, waiting for transfers between devices, local(): traded = lax.ppermute(got, 'chan', [(0, 1), (1, 0)])  1.85 us
    select_n x1, other arithmetic, local(): got = lax.ppermute(jnp.where(first, frames_in, out_grad), 'tm', swap)  1.71 us
  transfers between devices with their start and end apart: 9, of which 7 were waited for; matrix products, arithmetic and copies ran while one was open for 19% of the time, Pallas kernels for 0%

profile of v8, /device:TPU:0, one launch (start us, length us, event | category | flops | bytes accessed | tf_op | source)
XLA Modules:
  0.0 41.3 jit_solution(10325890209196450027)
XLA Ops:
  0.6 1.7 %broadcast_select_fusion.2 = bf16[4,1,64,512]{3,2,1,0:T(8,128)(2,1)} fusion(bf16[4,1,64,512]{3,2,1,0:T(8,128)(2,1)} %param.6, bf16[4,1,64,512]{3,2,1,0:T(8,128)(2,1)} %param.11, pred[]{:T(512)S(6)} %eq.9), kind=kLoop, calls=%fused_computation.46 | loop fusion | flops 131072 | bytes 786433 | tf_op jit(solution)/shard_map/jit(_where)/select_n | solution.py:128
  2.3 2.9 %collective-permute-start = (bf16[4,1,64,512]{3,2,1,0:T(8,128)(2,1)}, bf16[4,1,64,512]{3,2,1,0:T(8,128)(2,1)}, u32[]{:S(2)}, u32[]{:S(2)}) collective-permute-start(bf16[4,1,64,512]{3,2,1,0:T(8,128)(2,1)} %broadcast_select_fusion.2), channel_id=1, source_target_pairs={{0,2},{2,0},{4,6},{6,4},{8,10},{10,8},{12,14},{14,12},{1,3},{3,1},... | collective-permute-start | bytes 786440 | tf_op jit(solution)/shard_map/ppermute | solution.py:128
  5.3 0.7 %mul.853 = f32[4,8]{1,0:T(4,128)S(1)} reshape(f32[32]{0:T(128)} %param.10) | data formatting | bytes 256 | tf_op jit(solution)/shard_map/mul | solution.py:177
  6.0 0.7 %pad_maximum_fusion = f32[33]{0:T(128)S(1)} fusion(f32[1]{0:T(128)} %constant.67.clone.1, f32[32]{0:T(128)} %param.10), kind=kLoop, calls=%fused_computation.179 | loop fusion | flops 33 | bytes 264 | tf_op jit(solution)/shard_map/concatenate | solution.py:152
  6.8 1.2 %slice.316 = bf16[1,3,256,512]{3,2,1,0:T(8,128)(2,1)S(1)} slice(bf16[3,3,256,512]{3,2,1,0:T(8,128)(2,1)} %param.8), slice={[1:2], [0:3], [0:256], [0:512]} | slice | bytes 1572864 | tf_op jit(solution)/shard_map/slice | solution.py:28
  8.0 1.2 %slice.298 = bf16[1,3,512,256]{3,2,1,0:T(8,128)(2,1)S(1)} slice(bf16[3,3,512,256]{3,2,1,0:T(8,128)(2,1)} %param.7), slice={[1:2], [0:3], [0:512], [0:256]} | slice | bytes 1572864 | tf_op jit(solution)/shard_map/slice | solution.py:31
  9.2 0.6 %multiply_divide_fusion = (f32[256]{0:T(256)}, f32[256]{0:T(256)S(1)}) fusion(f32[256]{0:T(256)S(1)} %copy-done.1), kind=kLoop, calls=%fused_computation.178 | loop fusion | flops 768 | bytes 3072 | tf_op jit(solution)/shard_map/div | solution.py:201
  10.2 0.6 %fusion.64 = (f32[256]{0:T(256)}, f32[256]{0:T(256)}, f32[256]{0:T(256)}, f32[256]{0:T(256)}, f32[256]{0:T(256)}, /*index=5*/f32[256]{0:T(256)}, f32[256]{0:T(256)}) fusion(f32[256]{0:T(256)S(1)} %bitcast.314, f32[256]{0:T(256)S(1)} %bitcast.292, f32[256]{0:T(256)S(1)} %bitcast.312, f32[256]{0:T(256)S(1)} %bitcast.289, f32[256]{0:T(256)S(1)} %bitcast.310, ...), kind=kLoop, calls=%fused_computation.180 | loop fusion | flops 1792 | bytes 15360 | tf_op jit(solution)/shard_map/mul | solution.py:173
  11.0 0.9 %collective-permute-done = bf16[4,1,64,512]{3,2,1,0:T(8,128)(2,1)} collective-permute-done((bf16[4,1,64,512]{3,2,1,0:T(8,128)(2,1)}, bf16[4,1,64,512]{3,2,1,0:T(8,128)(2,1)}, u32[]{:S(2)}, u32[]{:S(2)}) %collective-permute-start) | collective-permute-done | bytes 262176 | tf_op jit(solution)/shard_map/ppermute | solution.py:128
  11.9 1.9 %collective-permute-done.1 = bf16[4,1,64,512]{3,2,1,0:T(8,128)(2,1)} collective-permute-done((bf16[4,1,64,512]{3,2,1,0:T(8,128)(2,1)}, bf16[4,1,64,512]{3,2,1,0:T(8,128)(2,1)}, u32[]{:S(2)}, u32[]{:S(2)}) %collective-permute-start.1) | collective-permute-done | bytes 262176 | tf_op jit(solution)/shard_map/ppermute | solution.py:129
  13.8 1.1 %broadcast_select_fusion.1 = (bf16[4,1,64,512]{3,2,1,0:T(8,128)(2,1)S(1)}, bf16[4,1,64,512]{3,2,1,0:T(8,128)(2,1)S(1)}) fusion(bf16[4,1,64,512]{3,2,1,0:T(8,128)(2,1)} %collective-permute-done, bf16[4,1,64,512]{3,2,1,0:T(8,128)(2,1)} %collective-permute-done.1, pred[]{:T(512)S(6)} %eq.9), kind=kLoop, calls=%fused_computation.45 | loop fusion | flops 262144 | bytes 1048577 | tf_op jit(solution)/shard_map/jit(_where)/select_n | solution.py:130
  14.9 1.2 %maximum_select_fusion = (bf16[8,1,64,512]{3,2,1,0:T(8,128)(2,1)S(1)}, bf16[8,1,64,512]{3,2,1,0:T(8,128)(2,1)S(1)}) fusion(bf16[4,1,64,512]{3,2,1,0:T(8,128)(2,1)S(1)} %copy-done, bf16[4,1,64,512]{3,2,1,0:T(8,128)(2,1)S(1)} %get-tuple-element.61, pred[]{:T(512)S(6)} %eq.8, bf16[4,1,64,512]{3,2,1,0:T(8,128)(2,1)S(1)} %get-tuple-element.62, ...), kind=kLoop, calls=%fused_computation.24 | loop fusion | flops 1572864 | bytes 2097153 | tf_op jit(solution)/shard_map/jit(_where)/select_n | solution.py:135
  18.6 1.9 %collective-permute-start.2 = (f32[1,64,256]{2,1,0:T(8,128)S(1)}, f32[1,64,256]{2,1,0:T(8,128)S(1)}, u32[]{:S(2)}, u32[]{:S(2)}) collective-permute-start(f32[1,64,256]{2,1,0:T(8,128)S(1)} %get-tuple-element.50), channel_id=1, source_target_pairs={{0,4},{2,6},{4,8},{6,10},{8,12},{10,14},{12,0},{14,2},{1,5},{3,7},... | collective-permute-start | bytes 196616 | tf_op jit(solution)/shard_map/ppermute | solution.py:90
  20.5 2.7 %collective-permute-start.3 = (f32[1,64,256]{2,1,0:T(8,128)S(1)}, f32[1,64,256]{2,1,0:T(8,128)S(1)}, u32[]{:S(2)}, u32[]{:S(2)}) collective-permute-start(f32[1,64,256]{2,1,0:T(8,128)S(1)} %get-tuple-element.71), channel_id=1, source_target_pairs={{0,8},{2,10},{4,12},{6,14},{8,0},{10,2},{12,4},{14,6},{1,9},{3,11}... | collective-permute-start | bytes 196616 | tf_op jit(solution)/shard_map/ppermute | solution.py:90
  23.1 1.3 %collective-permute-start.4 = (f32[1,64,256]{2,1,0:T(8,128)S(1)}, f32[1,64,256]{2,1,0:T(8,128)S(1)}, u32[]{:S(2)}, u32[]{:S(2)}) collective-permute-start(f32[1,64,256]{2,1,0:T(8,128)S(1)} %get-tuple-element.72), channel_id=1, source_target_pairs={{0,12},{2,14},{4,0},{6,2},{8,4},{10,6},{12,8},{14,10},{1,13},{3,15... | collective-permute-start | bytes 196616 | tf_op jit(solution)/shard_map/ppermute | solution.py:90
  24.5 0.5 %collective-permute-done.2 = f32[1,64,256]{2,1,0:T(8,128)S(1)} collective-permute-done((f32[1,64,256]{2,1,0:T(8,128)S(1)}, f32[1,64,256]{2,1,0:T(8,128)S(1)}, u32[]{:S(2)}, u32[]{:S(2)}) %collective-permute-start.2) | collective-permute-done | bytes 65568 | tf_op jit(solution)/shard_map/ppermute | solution.py:90
  25.0 2.8 %collective-permute-done.3 = f32[1,64,256]{2,1,0:T(8,128)S(1)} collective-permute-done((f32[1,64,256]{2,1,0:T(8,128)S(1)}, f32[1,64,256]{2,1,0:T(8,128)S(1)}, u32[]{:S(2)}, u32[]{:S(2)}) %collective-permute-start.3) | collective-permute-done | bytes 65568 | tf_op jit(solution)/shard_map/ppermute | solution.py:90
  31.2 1.6 %collective-permute-start.7 = (f32[256]{0:T(256)S(1)}, f32[256]{0:T(256)S(1)}, u32[]{:S(2)}, u32[]{:S(2)}) collective-permute-start(f32[256]{0:T(256)S(1)} %fusion.3), channel_id=1, source_target_pairs={{0,4},{2,6},{4,0},{6,2},{8,12},{10,14},{12,8},{14,10},{1,5},{3,7},... | collective-permute-start | bytes 3080 | tf_op jit(solution)/shard_map/ppermute | solution.py:111
  33.1 1.7 %collective-permute-done.7 = f32[256]{0:T(256)S(1)} collective-permute-done((f32[256]{0:T(256)S(1)}, f32[256]{0:T(256)S(1)}, u32[]{:S(2)}, u32[]{:S(2)}) %collective-permute-start.7) | collective-permute-done | bytes 1056 | tf_op jit(solution)/shard_map/ppermute | solution.py:111
  34.9 1.3 %collective-permute-start.8 = (f32[256]{0:T(256)S(1)}, f32[256]{0:T(256)S(1)}, u32[]{:S(2)}, u32[]{:S(2)}) collective-permute-start(f32[256]{0:T(256)S(1)} %add.342), channel_id=1, source_target_pairs={{0,8},{2,10},{4,12},{6,14},{8,0},{10,2},{12,4},{14,6},{1,9},{3,11}... | collective-permute-start | bytes 3080 | tf_op jit(solution)/shard_map/ppermute | solution.py:111
  36.5 2.8 %collective-permute-done.8 = f32[256]{0:T(256)S(1)} collective-permute-done((f32[256]{0:T(256)S(1)}, f32[256]{0:T(256)S(1)}, u32[]{:S(2)}, u32[]{:S(2)}) %collective-permute-start.8) | collective-permute-done | bytes 1056 | tf_op jit(solution)/shard_map/ppermute | solution.py:111
  39.3 0.6 %add_multiply_fusion = f32[256]{0:T(256)} fusion(f32[256]{0:T(256)S(1)} %add.342, f32[256]{0:T(256)S(1)} %collective-permute-done.8), kind=kLoop, calls=%fused_computation.176 | loop fusion | flops 512 | bytes 3072 | tf_op jit(solution)/shard_map/div | solution.py:208
  39.9 0.7 %add_convert_fusion.1 = bf16[4,1,64,256]{3,2,1,0:T(8,128)(2,1)} fusion(f32[4,1,64,256]{3,2,1,0:T(8,128)S(1)} %bitcast.282, bf16[4,1,64,256]{3,2,1,0:T(8,128)(2,1)S(1)} %collective-permute-done.5), kind=kLoop, calls=%fused_computation.43 | loop fusion | flops 196608 | bytes 524288 | tf_op jit(solution)/shard_map/convert_element_type | solution.py:83
  40.6 0.7 %add_convert_fusion = bf16[4,1,64,256]{3,2,1,0:T(8,128)(2,1)} fusion(f32[4,1,64,256]{3,2,1,0:T(8,128)S(1)} %bitcast.283, bf16[4,1,64,256]{3,2,1,0:T(8,128)(2,1)S(1)} %collective-permute-done.6), kind=kLoop, calls=%fused_computation.42 | loop fusion | flops 196608 | bytes 524288 | tf_op jit(solution)/shard_map/convert_element_type | solution.py:83
  (83 shorter events, 6.7 us)
Async XLA Ops:
  2.3 9.6 %collective-permute-start = (bf16[4,1,64,512]{3,2,1,0:T(8,128)(2,1)}, bf16[4,1,64,512]{3,2,1,0:T(8,128)(2,1)}, u32[]{:S(2)}, u32[]{:S(2)}) collective-permute-start(bf16[4,1,64,512]{3,2,1,0:T(8,128)(2,1)} %broadcast_select_fusion.2), channel_id=1, source_target_pairs={{0,2},{2,0},{4,6},{6,4},{8,10},{10,8},{12,14},{14,12},{1,3},{3,1},... | collective-permute-start | bytes 786440 | tf_op jit(solution)/shard_map/ppermute | solution.py:128
  7.9 1.3 %copy-start.1 = (f32[256]{0:T(256)S(1)}, f32[256]{0:T(256)}, u32[]{:S(2)}) copy-start(f32[256]{0:T(256)} %param.9) | copy-start | bytes 3076
  9.2 5.6 %copy-start = (bf16[4,1,64,512]{3,2,1,0:T(8,128)(2,1)S(1)}, bf16[4,1,64,512]{3,2,1,0:T(8,128)(2,1)}, u32[]{:S(2)}) copy-start(bf16[4,1,64,512]{3,2,1,0:T(8,128)(2,1)} %param.6) | copy-start | bytes 786436
  11.9 1.9 %collective-permute-start.1 = (bf16[4,1,64,512]{3,2,1,0:T(8,128)(2,1)}, bf16[4,1,64,512]{3,2,1,0:T(8,128)(2,1)}, u32[]{:S(2)}, u32[]{:S(2)}) collective-permute-start(bf16[4,1,64,512]{3,2,1,0:T(8,128)(2,1)} %collective-permute-done), channel_id=1, source_target_pairs={{0,1},{1,0},{2,3},{3,2},{4,5},{5,4},{6,7},{7,6},{8,9},{9,8},{10,11... | collective-permute-start | bytes 786440 | tf_op jit(solution)/shard_map/ppermute | solution.py:129
  18.2 9.9 %copy-start.9 = (f32[256]{0:T(256)S(1)}, f32[256]{0:T(256)}, u32[]{:S(2)}) copy-start(f32[256]{0:T(256)} %get-tuple-element.36) | copy-start | bytes 3076
  18.6 6.4 %collective-permute-start.2 = (f32[1,64,256]{2,1,0:T(8,128)S(1)}, f32[1,64,256]{2,1,0:T(8,128)S(1)}, u32[]{:S(2)}, u32[]{:S(2)}) collective-permute-start(f32[1,64,256]{2,1,0:T(8,128)S(1)} %get-tuple-element.50), channel_id=1, source_target_pairs={{0,4},{2,6},{4,8},{6,10},{8,12},{10,14},{12,0},{14,2},{1,5},{3,7},... | collective-permute-start | bytes 196616 | tf_op jit(solution)/shard_map/ppermute | solution.py:90
  20.5 7.3 %collective-permute-start.3 = (f32[1,64,256]{2,1,0:T(8,128)S(1)}, f32[1,64,256]{2,1,0:T(8,128)S(1)}, u32[]{:S(2)}, u32[]{:S(2)}) collective-permute-start(f32[1,64,256]{2,1,0:T(8,128)S(1)} %get-tuple-element.71), channel_id=1, source_target_pairs={{0,8},{2,10},{4,12},{6,14},{8,0},{10,2},{12,4},{14,6},{1,9},{3,11}... | collective-permute-start | bytes 196616 | tf_op jit(solution)/shard_map/ppermute | solution.py:90
  23.1 4.9 %collective-permute-start.4 = (f32[1,64,256]{2,1,0:T(8,128)S(1)}, f32[1,64,256]{2,1,0:T(8,128)S(1)}, u32[]{:S(2)}, u32[]{:S(2)}) collective-permute-start(f32[1,64,256]{2,1,0:T(8,128)S(1)} %get-tuple-element.72), channel_id=1, source_target_pairs={{0,12},{2,14},{4,0},{6,2},{8,4},{10,6},{12,8},{14,10},{1,13},{3,15... | collective-permute-start | bytes 196616 | tf_op jit(solution)/shard_map/ppermute | solution.py:90
  28.2 0.7 %copy-start.8 = (f32[256]{0:T(256)S(1)}, f32[256]{0:T(256)}, u32[]{:S(2)}) copy-start(f32[256]{0:T(256)} %get-tuple-element.37) | copy-start | bytes 3076
  28.2 0.7 %copy-start.7 = (f32[256]{0:T(256)S(1)}, f32[256]{0:T(256)}, u32[]{:S(2)}) copy-start(f32[256]{0:T(256)} %get-tuple-element.38) | copy-start | bytes 3076
  28.3 0.7 %copy-start.6 = (f32[256]{0:T(256)S(1)}, f32[256]{0:T(256)}, u32[]{:S(2)}) copy-start(f32[256]{0:T(256)} %get-tuple-element.39) | copy-start | bytes 3076
  28.3 0.7 %copy-start.5 = (f32[256]{0:T(256)S(1)}, f32[256]{0:T(256)}, u32[]{:S(2)}) copy-start(f32[256]{0:T(256)} %get-tuple-element.40) | copy-start | bytes 3076
  28.3 0.7 %copy-start.4 = (f32[256]{0:T(256)S(1)}, f32[256]{0:T(256)}, u32[]{:S(2)}) copy-start(f32[256]{0:T(256)} %get-tuple-element.41) | copy-start | bytes 3076
  28.4 0.7 %copy-start.3 = (f32[256]{0:T(256)S(1)}, f32[256]{0:T(256)}, u32[]{:S(2)}) copy-start(f32[256]{0:T(256)} %get-tuple-element.42) | copy-start | bytes 3076
  30.3 0.8 %copy-start.2 = (f32[256]{0:T(256)S(1)}, f32[256]{0:T(256)}, u32[]{:S(2)}) copy-start(f32[256]{0:T(256)} %get-tuple-element.95) | copy-start | bytes 3076
  30.5 9.4 %collective-permute-start.5 = (bf16[4,1,64,256]{3,2,1,0:T(8,128)(2,1)S(1)}, bf16[4,1,64,256]{3,2,1,0:T(8,128)(2,1)S(1)}, u32[]{:S(2)}, u32[]{:S(2)}) collective-permute-start(bf16[4,1,64,256]{3,2,1,0:T(8,128)(2,1)S(1)} %bitcast.284), channel_id=1, source_target_pairs={{0,1},{1,0},{2,3},{3,2},{4,5},{5,4},{6,7},{7,6},{8,9},{9,8},{10,11... | collective-permute-start | bytes 393224 | tf_op jit(solution)/shard_map/ppermute | solution.py:81
  31.2 3.6 %collective-permute-start.7 = (f32[256]{0:T(256)S(1)}, f32[256]{0:T(256)S(1)}, u32[]{:S(2)}, u32[]{:S(2)}) collective-permute-start(f32[256]{0:T(256)S(1)} %fusion.3), channel_id=1, source_target_pairs={{0,4},{2,6},{4,0},{6,2},{8,12},{10,14},{12,8},{14,10},{1,5},{3,7},... | collective-permute-start | bytes 3080 | tf_op jit(solution)/shard_map/ppermute | solution.py:111
  34.9 4.5 %collective-permute-start.8 = (f32[256]{0:T(256)S(1)}, f32[256]{0:T(256)S(1)}, u32[]{:S(2)}, u32[]{:S(2)}) collective-permute-start(f32[256]{0:T(256)S(1)} %add.342), channel_id=1, source_target_pairs={{0,8},{2,10},{4,12},{6,14},{8,0},{10,2},{12,4},{14,6},{1,9},{3,11}... | collective-permute-start | bytes 3080 | tf_op jit(solution)/shard_map/ppermute | solution.py:111
  36.4 4.2 %collective-permute-start.6 = (bf16[4,1,64,256]{3,2,1,0:T(8,128)(2,1)S(1)}, bf16[4,1,64,256]{3,2,1,0:T(8,128)(2,1)S(1)}, u32[]{:S(2)}, u32[]{:S(2)}) collective-permute-start(bf16[4,1,64,256]{3,2,1,0:T(8,128)(2,1)S(1)} %bitcast.285), channel_id=1, source_target_pairs={{0,1},{1,0},{2,3},{3,2},{4,5},{5,4},{6,7},{7,6},{8,9},{9,8},{10,11... | collective-permute-start | bytes 393224 | tf_op jit(solution)/shard_map/ppermute | solution.py:81

commit v9 on v8

--- a/solution.py
+++ b/solution.py
@@ -132,22 +132,21 @@
         else:
             other_frames = lax.ppermute(frames_in, "tm", swap)
             other_grad = lax.ppermute(out_grad, "tm", swap)
-        frames_in = jnp.where(
-            upper,
-            jnp.concatenate([other_frames, frames_in]),
-            jnp.concatenate([frames_in, other_frames]),
-        )
-        out_grad = jnp.where(
-            upper,
-            jnp.concatenate([other_grad, out_grad]),
-            jnp.concatenate([out_grad, other_grad]),
-        )
+        frame_blocks = [jnp.where(upper, other_frames, frames_in), jnp.where(upper, frames_in, other_frames)]
+        grad_blocks = [jnp.where(upper, other_grad, out_grad), jnp.where(upper, out_grad, other_grad)]
+    else:
+        frame_blocks = [frames_in]
+        grad_blocks = [out_grad]
     span = frame_count * width
-    in_halo = row_halo(frames_in)
-    grad_halo = row_halo(out_grad)
-    row_taps = row_taps_of(in_halo, row_count)
-    values = conv_apply(frames_in, in_halo, prep_kernel(in_kernel, False, row_taps), row_taps)
-    adjoint_in = conv_apply(out_grad, grad_halo, prep_kernel(out_kernel, True, row_taps), row_taps)
+    row_taps = row_taps_of(row_halo(frames_in), row_count)
+    in_taps = prep_kernel(in_kernel, False, row_taps)
+    adjoint_taps = prep_kernel(out_kernel, True, row_taps)
+    values = jnp.concatenate(
+        [conv_apply(block, row_halo(block), in_taps, row_taps) for block in frame_blocks]
+    )
+    adjoint_in = jnp.concatenate(
+        [conv_apply(block, row_halo(block), adjoint_taps, row_taps) for block in grad_blocks]
+    )
     input_gain = jnp.sqrt(1.0 - decay_rate * decay_rate)
     keep_padded = jnp.concatenate([frame_keep, jnp.zeros((1,), jnp.float32)])
     offset = group * span

time: 41.6 us -> 40.9 us (0.983)
  waiting for transfers between devices: 11 us -> 13.2 us
  other arithmetic: 8.75 us -> 6.98 us
  starting transfers between devices: 11.9 us -> 10.4 us
  matrix products: 4.39 us -> 5.41 us
  local copies, waits for them, and re-layouts: 4.05 us -> 3.47 us
    ppermute x3, waiting for transfers between devices: 3.59 us -> 5.38 us  [cyclic_carries(): received[step] = lax.ppermute(message, axis, route(step))]
    ppermute x1, waiting for transfers between devices: 0.94 us -> 2.18 us  [local(): got = lax.ppermute(jnp.where(first, frames_in, out_grad), 'tm', swap)]
    select_n x2 -> x1, other arithmetic: 2.29 us -> 1.18 us  [local(): jnp.where(upper, other_frames, frames_in)]
    ppermute x2, starting transfers between devices: 2.97 us -> 1.93 us  [group_sum(): value = value + lax.ppermute(value, axis, route(step))]
    dot_general x18 -> x24, matrix products: 4.39 us -> 5.41 us  [conv_apply(): jnp.dot(portion.reshape(-1, channels), taps[index, col_tap], preferred_el...]
    ppermute x3, starting transfers between devices: 5.88 us -> 4.93 us  [cyclic_carries(): received[step] = lax.ppermute(message, axis, route(step))]
    ppermute x2, waiting for transfers between devices: 4.58 us -> 3.78 us  [group_sum(): value = value + lax.ppermute(value, axis, route(step))]
    concatenate x1, other arithmetic: 0.73 us -> 0.07 us  [local(): keep_padded = jnp.concatenate([frame_keep, jnp.zeros((1,), jnp.float32)])]
  transfers between devices with their start and end apart: 9 -> 9, of which waited for: 7 -> 7; matrix products, arithmetic and copies ran while one was open for 19% -> 18% of each run, Pallas kernels for 0% -> 0%
where the time goes in v9:
time: 40.9 us; the launch traced here: 40.7 us
  waiting for transfers between devices  13.2 us (32%)
  starting transfers between devices  10.4 us (25%)
  other arithmetic  6.98 us (17%)
  matrix products  5.41 us (13%)
  local copies, waits for them, and re-layouts  3.47 us (8%)
  between operations  1.2 us (3%)
    dot_general x24, matrix products, conv_apply(): jnp.dot(portion.reshape(-1, channels), taps[index, col_tap], preferred_el...  5.41 us
    ppermute x3, waiting for transfers between devices, cyclic_carries(): received[step] = lax.ppermute(message, axis, route(step))  5.38 us
    ppermute x3, starting transfers between devices, cyclic_carries(): received[step] = lax.ppermute(message, axis, route(step))  4.93 us
    ppermute x2, waiting for transfers between devices, group_sum(): value = value + lax.ppermute(value, axis, route(step))  3.78 us
    ppermute x1, starting transfers between devices, local(): got = lax.ppermute(jnp.where(first, frames_in, out_grad), 'tm', swap)  2.94 us
    ppermute x1, waiting for transfers between devices, local(): got = lax.ppermute(jnp.where(first, frames_in, out_grad), 'tm', swap)  2.18 us
    ppermute x2, starting transfers between devices, group_sum(): value = value + lax.ppermute(value, axis, route(step))  1.93 us
    ppermute x1, waiting for transfers between devices, local(): traded = lax.ppermute(got, 'chan', [(0, 1), (1, 0)])  1.85 us
  transfers between devices with their start and end apart: 9, of which 7 were waited for; matrix products, arithmetic and copies ran while one was open for 18% of the time, Pallas kernels for 0%

profile of v9, /device:TPU:0, one launch (start us, length us, event | category | flops | bytes accessed | tf_op | source)
XLA Modules:
  0.0 40.7 jit_solution(3816712684724273747)
XLA Ops:
  0.6 1.7 %broadcast_select_fusion.2 = bf16[4,1,64,512]{3,2,1,0:T(8,128)(2,1)} fusion(bf16[4,1,64,512]{3,2,1,0:T(8,128)(2,1)} %param.6, bf16[4,1,64,512]{3,2,1,0:T(8,128)(2,1)} %param.11, pred[]{:T(512)S(6)} %eq.9), kind=kLoop, calls=%fused_computation.50 | loop fusion | flops 131072 | bytes 786433 | tf_op jit(solution)/shard_map/jit(_where)/select_n | solution.py:128
  2.3 2.9 %collective-permute-start = (bf16[4,1,64,512]{3,2,1,0:T(8,128)(2,1)}, bf16[4,1,64,512]{3,2,1,0:T(8,128)(2,1)}, u32[]{:S(2)}, u32[]{:S(2)}) collective-permute-start(bf16[4,1,64,512]{3,2,1,0:T(8,128)(2,1)} %broadcast_select_fusion.2), channel_id=1, source_target_pairs={{0,2},{2,0},{4,6},{6,4},{8,10},{10,8},{12,14},{14,12},{1,3},{3,1},... | collective-permute-start | bytes 786440 | tf_op jit(solution)/shard_map/ppermute | solution.py:128
  5.3 1.2 %slice.320 = bf16[1,3,512,256]{3,2,1,0:T(8,128)(2,1)S(1)} slice(bf16[3,3,512,256]{3,2,1,0:T(8,128)(2,1)} %param.7), slice={[1:2], [0:3], [0:512], [0:256]} | slice | bytes 1572864 | tf_op jit(solution)/shard_map/slice | solution.py:31
  6.5 1.2 %slice.340 = bf16[1,3,256,512]{3,2,1,0:T(8,128)(2,1)S(1)} slice(bf16[3,3,256,512]{3,2,1,0:T(8,128)(2,1)} %param.8), slice={[1:2], [0:3], [0:256], [0:512]} | slice | bytes 1572864 | tf_op jit(solution)/shard_map/slice | solution.py:28
  8.0 0.6 %multiply_divide_fusion = (f32[256]{0:T(256)}, f32[256]{0:T(256)S(1)}) fusion(f32[256]{0:T(256)S(1)} %copy-done.1), kind=kLoop, calls=%fused_computation.190 | loop fusion | flops 768 | bytes 3072 | tf_op jit(solution)/shard_map/div | solution.py:200
  9.0 0.6 %fusion.67 = (f32[256]{0:T(256)}, f32[256]{0:T(256)}, f32[256]{0:T(256)}, f32[256]{0:T(256)}, f32[256]{0:T(256)}, /*index=5*/f32[256]{0:T(256)}, f32[256]{0:T(256)}) fusion(f32[256]{0:T(256)S(1)} %bitcast.338, f32[256]{0:T(256)S(1)} %bitcast.325, f32[256]{0:T(256)S(1)} %bitcast.336, f32[256]{0:T(256)S(1)} %bitcast.322, f32[256]{0:T(256)S(1)} %bitcast.334, ...), kind=kLoop, calls=%fused_computation.192 | loop fusion | flops 1792 | bytes 15360 | tf_op jit(solution)/shard_map/mul | solution.py:172
  9.7 2.2 %collective-permute-done = bf16[4,1,64,512]{3,2,1,0:T(8,128)(2,1)} collective-permute-done((bf16[4,1,64,512]{3,2,1,0:T(8,128)(2,1)}, bf16[4,1,64,512]{3,2,1,0:T(8,128)(2,1)}, u32[]{:S(2)}, u32[]{:S(2)}) %collective-permute-start) | collective-permute-done | bytes 262176 | tf_op jit(solution)/shard_map/ppermute | solution.py:128
  11.9 1.9 %collective-permute-done.1 = bf16[4,1,64,512]{3,2,1,0:T(8,128)(2,1)} collective-permute-done((bf16[4,1,64,512]{3,2,1,0:T(8,128)(2,1)}, bf16[4,1,64,512]{3,2,1,0:T(8,128)(2,1)}, u32[]{:S(2)}, u32[]{:S(2)}) %collective-permute-start.1) | collective-permute-done | bytes 262176 | tf_op jit(solution)/shard_map/ppermute | solution.py:129
  13.8 1.2 %broadcast_select_fusion.6 = (bf16[4,1,64,512]{3,2,1,0:T(8,128)(2,1)S(1)}, bf16[4,1,64,512]{3,2,1,0:T(8,128)(2,1)S(1)}, bf16[4,1,64,512]{3,2,1,0:T(8,128)(2,1)S(1)}, bf16[4,1,64,512]{3,2,1,0:T(8,128)(2,1)S(1)}) fusion(bf16[4,1,64,512]{3,2,1,0:T(8,128)(2,1)S(1)} %copy-done, pred[]{:T(512)S(6)} %eq.8, bf16[4,1,64,512]{3,2,1,0:T(8,128)(2,1)} %collective-permute-done, ...), kind=kLoop, calls=%fused_computation.54 | loop fusion | flops 786432 | bytes 2097154 | tf_op jit(solution)/shard_map/jit(_where)/select_n | solution.py:135
  17.4 0.3 convolution_add_fusion.9
  17.6 0.3 convolution_add_fusion.8
  18.6 2.9 %collective-permute-start.3 = (f32[1,64,256]{2,1,0:T(8,128)S(1)}, f32[1,64,256]{2,1,0:T(8,128)S(1)}, u32[]{:S(2)}, u32[]{:S(2)}) collective-permute-start(f32[1,64,256]{2,1,0:T(8,128)S(1)} %get-tuple-element.79), channel_id=1, source_target_pairs={{0,8},{2,10},{4,12},{6,14},{8,0},{10,2},{12,4},{14,6},{1,9},{3,11}... | collective-permute-start | bytes 196616 | tf_op jit(solution)/shard_map/ppermute | solution.py:90
  21.5 1.3 %collective-permute-start.4 = (f32[1,64,256]{2,1,0:T(8,128)S(1)}, f32[1,64,256]{2,1,0:T(8,128)S(1)}, u32[]{:S(2)}, u32[]{:S(2)}) collective-permute-start(f32[1,64,256]{2,1,0:T(8,128)S(1)} %get-tuple-element.80), channel_id=1, source_target_pairs={{0,12},{2,14},{4,0},{6,2},{8,4},{10,6},{12,8},{14,10},{1,13},{3,15... | collective-permute-start | bytes 196616 | tf_op jit(solution)/shard_map/ppermute | solution.py:90
  22.9 0.7 %collective-permute-start.2 = (f32[1,64,256]{2,1,0:T(8,128)S(1)}, f32[1,64,256]{2,1,0:T(8,128)S(1)}, u32[]{:S(2)}, u32[]{:S(2)}) collective-permute-start(f32[1,64,256]{2,1,0:T(8,128)S(1)} %get-tuple-element.50), channel_id=1, source_target_pairs={{0,4},{2,6},{4,8},{6,10},{8,12},{10,14},{12,0},{14,2},{1,5},{3,7},... | collective-permute-start | bytes 196616 | tf_op jit(solution)/shard_map/ppermute | solution.py:90
  23.6 1.4 %collective-permute-done.3 = f32[1,64,256]{2,1,0:T(8,128)S(1)} collective-permute-done((f32[1,64,256]{2,1,0:T(8,128)S(1)}, f32[1,64,256]{2,1,0:T(8,128)S(1)}, u32[]{:S(2)}, u32[]{:S(2)}) %collective-permute-start.3) | collective-permute-done | bytes 65568 | tf_op jit(solution)/shard_map/ppermute | solution.py:90
  24.9 0.9 %collective-permute-done.4 = f32[1,64,256]{2,1,0:T(8,128)S(1)} collective-permute-done((f32[1,64,256]{2,1,0:T(8,128)S(1)}, f32[1,64,256]{2,1,0:T(8,128)S(1)}, u32[]{:S(2)}, u32[]{:S(2)}) %collective-permute-start.4) | collective-permute-done | bytes 65568 | tf_op jit(solution)/shard_map/ppermute | solution.py:90
  25.8 3.1 %collective-permute-done.2 = f32[1,64,256]{2,1,0:T(8,128)S(1)} collective-permute-done((f32[1,64,256]{2,1,0:T(8,128)S(1)}, f32[1,64,256]{2,1,0:T(8,128)S(1)}, u32[]{:S(2)}, u32[]{:S(2)}) %collective-permute-start.2) | collective-permute-done | bytes 65568 | tf_op jit(solution)/shard_map/ppermute | solution.py:90
  32.1 0.6 %collective-permute-start.5 = (bf16[4,1,64,256]{3,2,1,0:T(8,128)(2,1)S(1)}, bf16[4,1,64,256]{3,2,1,0:T(8,128)(2,1)S(1)}, u32[]{:S(2)}, u32[]{:S(2)}) collective-permute-start(bf16[4,1,64,256]{3,2,1,0:T(8,128)(2,1)S(1)} %bitcast.309), channel_id=1, source_target_pairs={{0,1},{1,0},{2,3},{3,2},{4,5},{5,4},{6,7},{7,6},{8,9},{9,8},{10,11... | collective-permute-start | bytes 393224 | tf_op jit(solution)/shard_map/ppermute | solution.py:81
  32.9 1.4 %collective-permute-done.7 = f32[256]{0:T(256)S(1)} collective-permute-done((f32[256]{0:T(256)S(1)}, f32[256]{0:T(256)S(1)}, u32[]{:S(2)}, u32[]{:S(2)}) %collective-permute-start.7) | collective-permute-done | bytes 1056 | tf_op jit(solution)/shard_map/ppermute | solution.py:111
  34.3 1.9 %collective-permute-start.8 = (f32[256]{0:T(256)S(1)}, f32[256]{0:T(256)S(1)}, u32[]{:S(2)}, u32[]{:S(2)}) collective-permute-start(f32[256]{0:T(256)S(1)} %add.366), channel_id=1, source_target_pairs={{0,8},{2,10},{4,12},{6,14},{8,0},{10,2},{12,4},{14,6},{1,9},{3,11}... | collective-permute-start | bytes 3080 | tf_op jit(solution)/shard_map/ppermute | solution.py:111
  36.3 2.4 %collective-permute-done.8 = f32[256]{0:T(256)S(1)} collective-permute-done((f32[256]{0:T(256)S(1)}, f32[256]{0:T(256)S(1)}, u32[]{:S(2)}, u32[]{:S(2)}) %collective-permute-start.8) | collective-permute-done | bytes 1056 | tf_op jit(solution)/shard_map/ppermute | solution.py:111
  38.8 0.6 %add_multiply_fusion = f32[256]{0:T(256)} fusion(f32[256]{0:T(256)S(1)} %add.366, f32[256]{0:T(256)S(1)} %collective-permute-done.8), kind=kLoop, calls=%fused_computation.188 | loop fusion | flops 512 | bytes 3072 | tf_op jit(solution)/shard_map/div | solution.py:207
  39.3 0.7 %add_convert_fusion = bf16[4,1,64,256]{3,2,1,0:T(8,128)(2,1)} fusion(f32[4,1,64,256]{3,2,1,0:T(8,128)S(1)} %bitcast.298, bf16[4,1,64,256]{3,2,1,0:T(8,128)(2,1)S(1)} %collective-permute-done.6), kind=kLoop, calls=%fused_computation.46 | loop fusion | flops 196608 | bytes 524288 | tf_op jit(solution)/shard_map/convert_element_type | solution.py:83
  40.0 0.7 %add_convert_fusion.1 = bf16[4,1,64,256]{3,2,1,0:T(8,128)(2,1)} fusion(f32[4,1,64,256]{3,2,1,0:T(8,128)S(1)} %bitcast.299, bf16[4,1,64,256]{3,2,1,0:T(8,128)(2,1)S(1)} %collective-permute-done.5), kind=kLoop, calls=%fused_computation.47 | loop fusion | flops 196608 | bytes 524288 | tf_op jit(solution)/shard_map/convert_element_type | solution.py:83
  (89 shorter events, 7.0 us)
Async XLA Ops:
  2.3 9.6 %collective-permute-start = (bf16[4,1,64,512]{3,2,1,0:T(8,128)(2,1)}, bf16[4,1,64,512]{3,2,1,0:T(8,128)(2,1)}, u32[]{:S(2)}, u32[]{:S(2)}) collective-permute-start(bf16[4,1,64,512]{3,2,1,0:T(8,128)(2,1)} %broadcast_select_fusion.2), channel_id=1, source_target_pairs={{0,2},{2,0},{4,6},{6,4},{8,10},{10,8},{12,14},{14,12},{1,3},{3,1},... | collective-permute-start | bytes 786440 | tf_op jit(solution)/shard_map/ppermute | solution.py:128
  5.3 2.5 %copy-start.10 = (f32[32]{0:T(128)S(1)}, f32[32]{0:T(128)}, u32[]{:S(2)}) copy-start(f32[32]{0:T(128)} %param.10) | copy-start | bytes 388
  5.3 2.7 %copy-start.1 = (f32[256]{0:T(256)S(1)}, f32[256]{0:T(256)}, u32[]{:S(2)}) copy-start(f32[256]{0:T(256)} %param.9) | copy-start | bytes 3076
  6.5 7.3 %copy-start = (bf16[4,1,64,512]{3,2,1,0:T(8,128)(2,1)S(1)}, bf16[4,1,64,512]{3,2,1,0:T(8,128)(2,1)}, u32[]{:S(2)}) copy-start(bf16[4,1,64,512]{3,2,1,0:T(8,128)(2,1)} %param.6) | copy-start | bytes 786436
  11.9 1.9 %collective-permute-start.1 = (bf16[4,1,64,512]{3,2,1,0:T(8,128)(2,1)}, bf16[4,1,64,512]{3,2,1,0:T(8,128)(2,1)}, u32[]{:S(2)}, u32[]{:S(2)}) collective-permute-start(bf16[4,1,64,512]{3,2,1,0:T(8,128)(2,1)} %collective-permute-done), channel_id=1, source_target_pairs={{0,1},{1,0},{2,3},{3,2},{4,5},{5,4},{6,7},{7,6},{8,9},{9,8},{10,11... | collective-permute-start | bytes 786440 | tf_op jit(solution)/shard_map/ppermute | solution.py:129
  17.6 11.3 %copy-start.9 = (f32[256]{0:T(256)S(1)}, f32[256]{0:T(256)}, u32[]{:S(2)}) copy-start(f32[256]{0:T(256)} %get-tuple-element.36) | copy-start | bytes 3076
  17.9 11.1 %copy-start.8 = (f32[256]{0:T(256)S(1)}, f32[256]{0:T(256)}, u32[]{:S(2)}) copy-start(f32[256]{0:T(256)} %get-tuple-element.37) | copy-start | bytes 3076
  17.9 11.1 %copy-start.7 = (f32[256]{0:T(256)S(1)}, f32[256]{0:T(256)}, u32[]{:S(2)}) copy-start(f32[256]{0:T(256)} %get-tuple-element.38) | copy-start | bytes 3076
  17.9 11.2 %copy-start.6 = (f32[256]{0:T(256)S(1)}, f32[256]{0:T(256)}, u32[]{:S(2)}) copy-start(f32[256]{0:T(256)} %get-tuple-element.39) | copy-start | bytes 3076
  18.2 10.9 %copy-start.5 = (f32[256]{0:T(256)S(1)}, f32[256]{0:T(256)}, u32[]{:S(2)}) copy-start(f32[256]{0:T(256)} %get-tuple-element.40) | copy-start | bytes 3076
  18.2 10.9 %copy-start.4 = (f32[256]{0:T(256)S(1)}, f32[256]{0:T(256)}, u32[]{:S(2)}) copy-start(f32[256]{0:T(256)} %get-tuple-element.41) | copy-start | bytes 3076
  18.2 11.0 %copy-start.3 = (f32[256]{0:T(256)S(1)}, f32[256]{0:T(256)}, u32[]{:S(2)}) copy-start(f32[256]{0:T(256)} %get-tuple-element.42) | copy-start | bytes 3076
  18.6 6.3 %collective-permute-start.3 = (f32[1,64,256]{2,1,0:T(8,128)S(1)}, f32[1,64,256]{2,1,0:T(8,128)S(1)}, u32[]{:S(2)}, u32[]{:S(2)}) collective-permute-start(f32[1,64,256]{2,1,0:T(8,128)S(1)} %get-tuple-element.79), channel_id=1, source_target_pairs={{0,8},{2,10},{4,12},{6,14},{8,0},{10,2},{12,4},{14,6},{1,9},{3,11}... | collective-permute-start | bytes 196616 | tf_op jit(solution)/shard_map/ppermute | solution.py:90
  21.5 4.3 %collective-permute-start.4 = (f32[1,64,256]{2,1,0:T(8,128)S(1)}, f32[1,64,256]{2,1,0:T(8,128)S(1)}, u32[]{:S(2)}, u32[]{:S(2)}) collective-permute-start(f32[1,64,256]{2,1,0:T(8,128)S(1)} %get-tuple-element.80), channel_id=1, source_target_pairs={{0,12},{2,14},{4,0},{6,2},{8,4},{10,6},{12,8},{14,10},{1,13},{3,15... | collective-permute-start | bytes 196616 | tf_op jit(solution)/shard_map/ppermute | solution.py:90
  22.9 6.1 %collective-permute-start.2 = (f32[1,64,256]{2,1,0:T(8,128)S(1)}, f32[1,64,256]{2,1,0:T(8,128)S(1)}, u32[]{:S(2)}, u32[]{:S(2)}) collective-permute-start(f32[1,64,256]{2,1,0:T(8,128)S(1)} %get-tuple-element.50), channel_id=1, source_target_pairs={{0,4},{2,6},{4,8},{6,10},{8,12},{10,14},{12,0},{14,2},{1,5},{3,7},... | collective-permute-start | bytes 196616 | tf_op jit(solution)/shard_map/ppermute | solution.py:90
  29.3 1.2 %copy-start.2 = (f32[256]{0:T(256)S(1)}, f32[256]{0:T(256)}, u32[]{:S(2)}) copy-start(f32[256]{0:T(256)} %get-tuple-element.103) | copy-start | bytes 3076
  30.7 3.6 %collective-permute-start.7 = (f32[256]{0:T(256)S(1)}, f32[256]{0:T(256)S(1)}, u32[]{:S(2)}, u32[]{:S(2)}) collective-permute-start(f32[256]{0:T(256)S(1)} %fusion.4), channel_id=1, source_target_pairs={{0,4},{2,6},{4,0},{6,2},{8,12},{10,14},{12,8},{14,10},{1,5},{3,7},... | collective-permute-start | bytes 3080 | tf_op jit(solution)/shard_map/ppermute | solution.py:111
  31.2 8.1 %collective-permute-start.6 = (bf16[4,1,64,256]{3,2,1,0:T(8,128)(2,1)S(1)}, bf16[4,1,64,256]{3,2,1,0:T(8,128)(2,1)S(1)}, u32[]{:S(2)}, u32[]{:S(2)}) collective-permute-start(bf16[4,1,64,256]{3,2,1,0:T(8,128)(2,1)S(1)} %bitcast.308), channel_id=1, source_target_pairs={{0,1},{1,0},{2,3},{3,2},{4,5},{5,4},{6,7},{7,6},{8,9},{9,8},{10,11... | collective-permute-start | bytes 393224 | tf_op jit(solution)/shard_map/ppermute | solution.py:81
  32.1 7.9 %collective-permute-start.5 = (bf16[4,1,64,256]{3,2,1,0:T(8,128)(2,1)S(1)}, bf16[4,1,64,256]{3,2,1,0:T(8,128)(2,1)S(1)}, u32[]{:S(2)}, u32[]{:S(2)}) collective-permute-start(bf16[4,1,64,256]{3,2,1,0:T(8,128)(2,1)S(1)} %bitcast.309), channel_id=1, source_target_pairs={{0,1},{1,0},{2,3},{3,2},{4,5},{5,4},{6,7},{7,6},{8,9},{9,8},{10,11... | collective-permute-start | bytes 393224 | tf_op jit(solution)/shard_map/ppermute | solution.py:81
  34.3 4.5 %collective-permute-start.8 = (f32[256]{0:T(256)S(1)}, f32[256]{0:T(256)S(1)}, u32[]{:S(2)}, u32[]{:S(2)}) collective-permute-start(f32[256]{0:T(256)S(1)} %add.366), channel_id=1, source_target_pairs={{0,8},{2,10},{4,12},{6,14},{8,0},{10,2},{12,4},{14,6},{1,9},{3,11}... | collective-permute-start | bytes 3080 | tf_op jit(solution)/shard_map/ppermute | solution.py:111

commit v10 on v9

--- a/solution.py
+++ b/solution.py
@@ -68,19 +68,28 @@
     return lax.psum(value, axis)
 
 
-def chan_sum(cells, halo, taps, row_taps):
+def chan_sums(jobs):
     count = lax.axis_size("chan")
     mine = lax.axis_index("chan")
-    width = taps.shape[3] // count
     if count != 2:
-        part = conv_apply(cells, halo, taps, row_taps)
-        return lax.psum_scatter(part.astype(jnp.bfloat16), "chan", scatter_dimension=3, tiled=True)
-    other_taps = lax.dynamic_slice_in_dim(taps, (1 - mine) * width, width, axis=3)
-    own_taps = lax.dynamic_slice_in_dim(taps, mine * width, width, axis=3)
-    other = conv_apply(cells, halo, other_taps, row_taps).astype(jnp.bfloat16)
-    got = lax.ppermute(other, "chan", [(0, 1), (1, 0)])
-    own = conv_apply(cells, halo, own_taps, row_taps)
-    return (own + got.astype(jnp.float32)).astype(jnp.bfloat16)
+        return [
+            lax.psum_scatter(
+                conv_apply(*job).astype(jnp.bfloat16), "chan", scatter_dimension=3, tiled=True
+            )
+            for job in jobs
+        ]
+    width = jobs[0][2].shape[3] // count
+    others = []
+    for cells, halo, taps, row_taps in jobs:
+        other_taps = lax.dynamic_slice_in_dim(taps, (1 - mine) * width, width, axis=3)
+        others.append(conv_apply(cells, halo, other_taps, row_taps).astype(jnp.bfloat16))
+    got = lax.ppermute(jnp.stack(others), "chan", [(0, 1), (1, 0)])
+    results = []
+    for index, (cells, halo, taps, row_taps) in enumerate(jobs):
+        own_taps = lax.dynamic_slice_in_dim(taps, mine * width, width, axis=3)
+        own = conv_apply(cells, halo, own_taps, row_taps)
+        results.append((own + got[index].astype(jnp.float32)).astype(jnp.bfloat16))
+    return results
 
 
 def cyclic_carries(fwd_end, bwd_start, fwd_prod, bwd_prod, axis, index, count, route):
@@ -211,8 +220,12 @@
         adjoints = jnp.where(upper, adjoints[frame_count:], adjoints[:frame_count])
     state_b = states.astype(jnp.bfloat16)
     adjoint_b = adjoints.astype(jnp.bfloat16)
-    mixed = chan_sum(state_b, row_halo(state_b), prep_kernel(out_kernel, False, row_taps), row_taps)
-    grad_in = chan_sum(adjoint_b, row_halo(adjoint_b), prep_kernel(in_kernel, True, row_taps), row_taps)
+    mixed, grad_in = chan_sums(
+        [
+            (state_b, row_halo(state_b), prep_kernel(out_kernel, False, row_taps), row_taps),
+            (adjoint_b, row_halo(adjoint_b), prep_kernel(in_kernel, True, row_taps), row_taps),
+        ]
+    )
     return (mixed, grad_in, grad_decay)
 
 

time: 40.9 us -> 40.9 us (level)
  waiting for transfers between devices: 13.2 us -> 13.8 us
  starting transfers between devices: 10.4 us -> 9.82 us
    unnamed x13 -> x14, other arithmetic: 0.28 us -> 0.96 us
    convert_element_type x2 -> x1, other arithmetic: 1.37 us -> 0.69 us  [chan_sums(): results.append((own + got[index].astype(jnp.float32)).astype(jnp.bfloat16))]
    ppermute x2, waiting for transfers between devices: 3.78 us -> 4.34 us  [group_sum(): value = value + lax.ppermute(value, axis, route(step))]
    ppermute x2 -> x1, starting transfers between devices: 0.63 us -> 0.07 us  [chan_sums(): got = lax.ppermute(jnp.stack(others), 'chan', [(0, 1), (1, 0)])]
  transfers between devices with their start and end apart: 9 -> 8, of which waited for: 7 -> 7; matrix products, arithmetic and copies ran while one was open for 18% -> 16% of each run, Pallas kernels for 0% -> 0%
where the time goes in v10:
time: 40.9 us; the launch traced here: 40.7 us
  waiting for transfers between devices  13.8 us (34%)
  starting transfers between devices  9.82 us (24%)
  other arithmetic  6.99 us (17%)
  matrix products  5.42 us (13%)
  local copies, waits for them, and re-layouts  3.47 us (8%)
  between operations  1.21 us (3%)
    dot_general x24, matrix products, conv_apply(): jnp.dot(portion.reshape(-1, channels), taps[index, col_tap], preferred_el...  5.42 us
    ppermute x3, waiting for transfers between devices, cyclic_carries(): received[step] = lax.ppermute(message, axis, route(step))  5.4 us
    ppermute x3, starting transfers between devices, cyclic_carries(): received[step] = lax.ppermute(message, axis, route(step))  4.93 us
    ppermute x2, waiting for transfers between devices, group_sum(): value = value + lax.ppermute(value, axis, route(step))  4.34 us
    ppermute x1, starting transfers between devices, local(): got = lax.ppermute(jnp.where(first, frames_in, out_grad), 'tm', swap)  2.94 us
    ppermute x1, waiting for transfers between devices, local(): got = lax.ppermute(jnp.where(first, frames_in, out_grad), 'tm', swap)  2.19 us
    ppermute x2, starting transfers between devices, group_sum(): value = value + lax.ppermute(value, axis, route(step))  1.88 us
    ppermute x1, waiting for transfers between devices, local(): traded = lax.ppermute(got, 'chan', [(0, 1), (1, 0)])  1.85 us
  transfers between devices with their start and end apart: 8, of which 7 were waited for; matrix products, arithmetic and copies ran while one was open for 16% of the time, Pallas kernels for 0%

profile of v10, /device:TPU:0, one launch (start us, length us, event | category | flops | bytes accessed | tf_op | source)
XLA Modules:
  0.0 40.7 jit_solution(10899785575819206176)
XLA Ops:
  0.6 1.7 %broadcast_select_fusion.2 = bf16[4,1,64,512]{3,2,1,0:T(8,128)(2,1)} fusion(bf16[4,1,64,512]{3,2,1,0:T(8,128)(2,1)} %param.6, bf16[4,1,64,512]{3,2,1,0:T(8,128)(2,1)} %param.11, pred[]{:T(512)S(6)} %eq.9), kind=kLoop, calls=%fused_computation.53 | loop fusion | flops 131072 | bytes 786433 | tf_op jit(solution)/shard_map/jit(_where)/select_n | solution.py:137
  2.3 2.9 %collective-permute-start = (bf16[4,1,64,512]{3,2,1,0:T(8,128)(2,1)}, bf16[4,1,64,512]{3,2,1,0:T(8,128)(2,1)}, u32[]{:S(2)}, u32[]{:S(2)}) collective-permute-start(bf16[4,1,64,512]{3,2,1,0:T(8,128)(2,1)} %broadcast_select_fusion.2), channel_id=1, source_target_pairs={{0,2},{2,0},{4,6},{6,4},{8,10},{10,8},{12,14},{14,12},{1,3},{3,1},... | collective-permute-start | bytes 786440 | tf_op jit(solution)/shard_map/ppermute | solution.py:137
  5.3 1.2 %slice.326 = bf16[1,3,512,256]{3,2,1,0:T(8,128)(2,1)S(1)} slice(bf16[3,3,512,256]{3,2,1,0:T(8,128)(2,1)} %param.7), slice={[1:2], [0:3], [0:512], [0:256]} | slice | bytes 1572864 | tf_op jit(solution)/shard_map/slice | solution.py:31
  6.5 1.2 %slice.346 = bf16[1,3,256,512]{3,2,1,0:T(8,128)(2,1)S(1)} slice(bf16[3,3,256,512]{3,2,1,0:T(8,128)(2,1)} %param.8), slice={[1:2], [0:3], [0:256], [0:512]} | slice | bytes 1572864 | tf_op jit(solution)/shard_map/slice | solution.py:28
  8.0 0.6 %multiply_divide_fusion = (f32[256]{0:T(256)}, f32[256]{0:T(256)S(1)}) fusion(f32[256]{0:T(256)S(1)} %copy-done.1), kind=kLoop, calls=%fused_computation.196 | loop fusion | flops 768 | bytes 3072 | tf_op jit(solution)/shard_map/div | solution.py:209
  9.0 0.6 %fusion.70 = (f32[256]{0:T(256)}, f32[256]{0:T(256)}, f32[256]{0:T(256)}, f32[256]{0:T(256)}, f32[256]{0:T(256)}, /*index=5*/f32[256]{0:T(256)}, f32[256]{0:T(256)}) fusion(f32[256]{0:T(256)S(1)} %bitcast.344, f32[256]{0:T(256)S(1)} %bitcast.331, f32[256]{0:T(256)S(1)} %bitcast.342, f32[256]{0:T(256)S(1)} %bitcast.328, f32[256]{0:T(256)S(1)} %bitcast.340, ...), kind=kLoop, calls=%fused_computation.198 | loop fusion | flops 1792 | bytes 15360 | tf_op jit(solution)/shard_map/mul | solution.py:181
  9.7 2.2 %collective-permute-done = bf16[4,1,64,512]{3,2,1,0:T(8,128)(2,1)} collective-permute-done((bf16[4,1,64,512]{3,2,1,0:T(8,128)(2,1)}, bf16[4,1,64,512]{3,2,1,0:T(8,128)(2,1)}, u32[]{:S(2)}, u32[]{:S(2)}) %collective-permute-start) | collective-permute-done | bytes 262176 | tf_op jit(solution)/shard_map/ppermute | solution.py:137
  11.9 1.9 %collective-permute-done.1 = bf16[4,1,64,512]{3,2,1,0:T(8,128)(2,1)} collective-permute-done((bf16[4,1,64,512]{3,2,1,0:T(8,128)(2,1)}, bf16[4,1,64,512]{3,2,1,0:T(8,128)(2,1)}, u32[]{:S(2)}, u32[]{:S(2)}) %collective-permute-start.1) | collective-permute-done | bytes 262176 | tf_op jit(solution)/shard_map/ppermute | solution.py:138
  13.8 1.2 %broadcast_select_fusion.6 = (bf16[4,1,64,512]{3,2,1,0:T(8,128)(2,1)S(1)}, bf16[4,1,64,512]{3,2,1,0:T(8,128)(2,1)S(1)}, bf16[4,1,64,512]{3,2,1,0:T(8,128)(2,1)S(1)}, bf16[4,1,64,512]{3,2,1,0:T(8,128)(2,1)S(1)}) fusion(bf16[4,1,64,512]{3,2,1,0:T(8,128)(2,1)S(1)} %copy-done, pred[]{:T(512)S(6)} %eq.8, bf16[4,1,64,512]{3,2,1,0:T(8,128)(2,1)} %collective-permute-done, ...), kind=kLoop, calls=%fused_computation.57 | loop fusion | flops 786432 | bytes 2097154 | tf_op jit(solution)/shard_map/jit(_where)/select_n | solution.py:144
  17.3 0.3 convolution_add_fusion.9
  17.6 0.3 convolution_add_fusion.8
  17.9 0.3 convolution_add_fusion.11
  18.6 2.9 %collective-permute-start.3 = (f32[1,64,256]{2,1,0:T(8,128)S(1)}, f32[1,64,256]{2,1,0:T(8,128)S(1)}, u32[]{:S(2)}, u32[]{:S(2)}) collective-permute-start(f32[1,64,256]{2,1,0:T(8,128)S(1)} %get-tuple-element.82), channel_id=1, source_target_pairs={{0,8},{2,10},{4,12},{6,14},{8,0},{10,2},{12,4},{14,6},{1,9},{3,11}... | collective-permute-start | bytes 196616 | tf_op jit(solution)/shard_map/ppermute | solution.py:99
  21.5 1.4 %collective-permute-start.4 = (f32[1,64,256]{2,1,0:T(8,128)S(1)}, f32[1,64,256]{2,1,0:T(8,128)S(1)}, u32[]{:S(2)}, u32[]{:S(2)}) collective-permute-start(f32[1,64,256]{2,1,0:T(8,128)S(1)} %get-tuple-element.83), channel_id=1, source_target_pairs={{0,12},{2,14},{4,0},{6,2},{8,4},{10,6},{12,8},{14,10},{1,13},{3,15... | collective-permute-start | bytes 196616 | tf_op jit(solution)/shard_map/ppermute | solution.py:99
  22.9 0.7 %collective-permute-start.2 = (f32[1,64,256]{2,1,0:T(8,128)S(1)}, f32[1,64,256]{2,1,0:T(8,128)S(1)}, u32[]{:S(2)}, u32[]{:S(2)}) collective-permute-start(f32[1,64,256]{2,1,0:T(8,128)S(1)} %get-tuple-element.53), channel_id=1, source_target_pairs={{0,4},{2,6},{4,8},{6,10},{8,12},{10,14},{12,0},{14,2},{1,5},{3,7},... | collective-permute-start | bytes 196616 | tf_op jit(solution)/shard_map/ppermute | solution.py:99
  23.6 1.3 %collective-permute-done.3 = f32[1,64,256]{2,1,0:T(8,128)S(1)} collective-permute-done((f32[1,64,256]{2,1,0:T(8,128)S(1)}, f32[1,64,256]{2,1,0:T(8,128)S(1)}, u32[]{:S(2)}, u32[]{:S(2)}) %collective-permute-start.3) | collective-permute-done | bytes 65568 | tf_op jit(solution)/shard_map/ppermute | solution.py:99
  24.8 1.0 %collective-permute-done.4 = f32[1,64,256]{2,1,0:T(8,128)S(1)} collective-permute-done((f32[1,64,256]{2,1,0:T(8,128)S(1)}, f32[1,64,256]{2,1,0:T(8,128)S(1)}, u32[]{:S(2)}, u32[]{:S(2)}) %collective-permute-start.4) | collective-permute-done | bytes 65568 | tf_op jit(solution)/shard_map/ppermute | solution.py:99
  25.8 3.2 %collective-permute-done.2 = f32[1,64,256]{2,1,0:T(8,128)S(1)} collective-permute-done((f32[1,64,256]{2,1,0:T(8,128)S(1)}, f32[1,64,256]{2,1,0:T(8,128)S(1)}, u32[]{:S(2)}, u32[]{:S(2)}) %collective-permute-start.2) | collective-permute-done | bytes 65568 | tf_op jit(solution)/shard_map/ppermute | solution.py:99
  32.4 1.9 %collective-permute-done.6 = f32[256]{0:T(256)S(1)} collective-permute-done((f32[256]{0:T(256)S(1)}, f32[256]{0:T(256)S(1)}, u32[]{:S(2)}, u32[]{:S(2)}) %collective-permute-start.6) | collective-permute-done | bytes 1056 | tf_op jit(solution)/shard_map/ppermute | solution.py:120
  34.3 1.8 %collective-permute-start.7 = (f32[256]{0:T(256)S(1)}, f32[256]{0:T(256)S(1)}, u32[]{:S(2)}, u32[]{:S(2)}) collective-permute-start(f32[256]{0:T(256)S(1)} %add.382), channel_id=1, source_target_pairs={{0,8},{2,10},{4,12},{6,14},{8,0},{10,2},{12,4},{14,6},{1,9},{3,11}... | collective-permute-start | bytes 3080 | tf_op jit(solution)/shard_map/ppermute | solution.py:120
  36.3 2.5 %collective-permute-done.7 = f32[256]{0:T(256)S(1)} collective-permute-done((f32[256]{0:T(256)S(1)}, f32[256]{0:T(256)S(1)}, u32[]{:S(2)}, u32[]{:S(2)}) %collective-permute-start.7) | collective-permute-done | bytes 1056 | tf_op jit(solution)/shard_map/ppermute | solution.py:120
  38.8 0.6 %add_multiply_fusion = f32[256]{0:T(256)} fusion(f32[256]{0:T(256)S(1)} %add.382, f32[256]{0:T(256)S(1)} %collective-permute-done.7), kind=kLoop, calls=%fused_computation.194 | loop fusion | flops 512 | bytes 3072 | tf_op jit(solution)/shard_map/div | solution.py:216
  39.3 0.7 %fusion.7 = bf16[4,1,64,256]{3,2,1,0:T(8,128)(2,1)} fusion(f32[4,1,64,256]{3,2,1,0:T(8,128)S(1)} %bitcast.304, bf16[2,4,1,64,256]{4,3,1,2,0:T(8,128)(2,1)S(1)} %collective-permute-done.5), kind=kLoop, calls=%fused_computation.48 | loop fusion | flops 196608 | bytes 524288 | tf_op jit(solution)/shard_map/convert_element_type | solution.py:91
  40.0 0.7 %fusion.13 = bf16[4,1,64,256]{3,2,1,0:T(8,128)(2,1)} fusion(f32[4,1,64,256]{3,2,0,1:T(8,128)S(1)} %bitcast.305, bf16[2,4,1,64,256]{4,3,1,2,0:T(8,128)(2,1)S(1)} %collective-permute-done.5), kind=kLoop, calls=%fused_computation.62 | loop fusion | flops 196608 | bytes 524288
  (88 shorter events, 6.8 us)
Async XLA Ops:
  2.3 9.6 %collective-permute-start = (bf16[4,1,64,512]{3,2,1,0:T(8,128)(2,1)}, bf16[4,1,64,512]{3,2,1,0:T(8,128)(2,1)}, u32[]{:S(2)}, u32[]{:S(2)}) collective-permute-start(bf16[4,1,64,512]{3,2,1,0:T(8,128)(2,1)} %broadcast_select_fusion.2), channel_id=1, source_target_pairs={{0,2},{2,0},{4,6},{6,4},{8,10},{10,8},{12,14},{14,12},{1,3},{3,1},... | collective-permute-start | bytes 786440 | tf_op jit(solution)/shard_map/ppermute | solution.py:137
  5.3 2.5 %copy-start.10 = (f32[32]{0:T(128)S(1)}, f32[32]{0:T(128)}, u32[]{:S(2)}) copy-start(f32[32]{0:T(128)} %param.10) | copy-start | bytes 388
  5.3 2.7 %copy-start.1 = (f32[256]{0:T(256)S(1)}, f32[256]{0:T(256)}, u32[]{:S(2)}) copy-start(f32[256]{0:T(256)} %param.9) | copy-start | bytes 3076
  6.5 7.3 %copy-start = (bf16[4,1,64,512]{3,2,1,0:T(8,128)(2,1)S(1)}, bf16[4,1,64,512]{3,2,1,0:T(8,128)(2,1)}, u32[]{:S(2)}) copy-start(bf16[4,1,64,512]{3,2,1,0:T(8,128)(2,1)} %param.6) | copy-start | bytes 786436
  11.9 1.9 %collective-permute-start.1 = (bf16[4,1,64,512]{3,2,1,0:T(8,128)(2,1)}, bf16[4,1,64,512]{3,2,1,0:T(8,128)(2,1)}, u32[]{:S(2)}, u32[]{:S(2)}) collective-permute-start(bf16[4,1,64,512]{3,2,1,0:T(8,128)(2,1)} %collective-permute-done), channel_id=1, source_target_pairs={{0,1},{1,0},{2,3},{3,2},{4,5},{5,4},{6,7},{7,6},{8,9},{9,8},{10,11... | collective-permute-start | bytes 786440 | tf_op jit(solution)/shard_map/ppermute | solution.py:138
  17.6 11.3 %copy-start.9 = (f32[256]{0:T(256)S(1)}, f32[256]{0:T(256)}, u32[]{:S(2)}) copy-start(f32[256]{0:T(256)} %get-tuple-element.39) | copy-start | bytes 3076
  17.9 11.1 %copy-start.8 = (f32[256]{0:T(256)S(1)}, f32[256]{0:T(256)}, u32[]{:S(2)}) copy-start(f32[256]{0:T(256)} %get-tuple-element.40) | copy-start | bytes 3076
  17.9 11.1 %copy-start.7 = (f32[256]{0:T(256)S(1)}, f32[256]{0:T(256)}, u32[]{:S(2)}) copy-start(f32[256]{0:T(256)} %get-tuple-element.41) | copy-start | bytes 3076
  17.9 11.2 %copy-start.6 = (f32[256]{0:T(256)S(1)}, f32[256]{0:T(256)}, u32[]{:S(2)}) copy-start(f32[256]{0:T(256)} %get-tuple-element.42) | copy-start | bytes 3076
  18.2 10.9 %copy-start.5 = (f32[256]{0:T(256)S(1)}, f32[256]{0:T(256)}, u32[]{:S(2)}) copy-start(f32[256]{0:T(256)} %get-tuple-element.43) | copy-start | bytes 3076
  18.2 10.9 %copy-start.4 = (f32[256]{0:T(256)S(1)}, f32[256]{0:T(256)}, u32[]{:S(2)}) copy-start(f32[256]{0:T(256)} %get-tuple-element.44) | copy-start | bytes 3076
  18.2 11.0 %copy-start.3 = (f32[256]{0:T(256)S(1)}, f32[256]{0:T(256)}, u32[]{:S(2)}) copy-start(f32[256]{0:T(256)} %get-tuple-element.45) | copy-start | bytes 3076
  18.6 6.2 %collective-permute-start.3 = (f32[1,64,256]{2,1,0:T(8,128)S(1)}, f32[1,64,256]{2,1,0:T(8,128)S(1)}, u32[]{:S(2)}, u32[]{:S(2)}) collective-permute-start(f32[1,64,256]{2,1,0:T(8,128)S(1)} %get-tuple-element.82), channel_id=1, source_target_pairs={{0,8},{2,10},{4,12},{6,14},{8,0},{10,2},{12,4},{14,6},{1,9},{3,11}... | collective-permute-start | bytes 196616 | tf_op jit(solution)/shard_map/ppermute | solution.py:99
  21.5 4.3 %collective-permute-start.4 = (f32[1,64,256]{2,1,0:T(8,128)S(1)}, f32[1,64,256]{2,1,0:T(8,128)S(1)}, u32[]{:S(2)}, u32[]{:S(2)}) collective-permute-start(f32[1,64,256]{2,1,0:T(8,128)S(1)} %get-tuple-element.83), channel_id=1, source_target_pairs={{0,12},{2,14},{4,0},{6,2},{8,4},{10,6},{12,8},{14,10},{1,13},{3,15... | collective-permute-start | bytes 196616 | tf_op jit(solution)/shard_map/ppermute | solution.py:99
  22.9 6.1 %collective-permute-start.2 = (f32[1,64,256]{2,1,0:T(8,128)S(1)}, f32[1,64,256]{2,1,0:T(8,128)S(1)}, u32[]{:S(2)}, u32[]{:S(2)}) collective-permute-start(f32[1,64,256]{2,1,0:T(8,128)S(1)} %get-tuple-element.53), channel_id=1, source_target_pairs={{0,4},{2,6},{4,8},{6,10},{8,12},{10,14},{12,0},{14,2},{1,5},{3,7},... | collective-permute-start | bytes 196616 | tf_op jit(solution)/shard_map/ppermute | solution.py:99
  29.4 1.1 %copy-start.2 = (f32[256]{0:T(256)S(1)}, f32[256]{0:T(256)}, u32[]{:S(2)}) copy-start(f32[256]{0:T(256)} %get-tuple-element.106) | copy-start | bytes 3076
  30.7 3.6 %collective-permute-start.6 = (f32[256]{0:T(256)S(1)}, f32[256]{0:T(256)S(1)}, u32[]{:S(2)}, u32[]{:S(2)}) collective-permute-start(f32[256]{0:T(256)S(1)} %fusion.4), channel_id=1, source_target_pairs={{0,4},{2,6},{4,0},{6,2},{8,12},{10,14},{12,8},{14,10},{1,5},{3,7},... | collective-permute-start | bytes 3080 | tf_op jit(solution)/shard_map/ppermute | solution.py:120
  32.1 7.2 %collective-permute-start.5 = (bf16[2,4,1,64,256]{4,3,1,2,0:T(8,128)(2,1)S(1)}, bf16[2,4,1,64,256]{4,3,1,2,0:T(8,128)(2,1)S(1)}, u32[]{:S(2)}, u32[]{:S(2)}) collective-permute-start(bf16[2,4,1,64,256]{4,3,1,2,0:T(8,128)(2,1)S(1)} %pad_maximum_fusion), channel_id=1, source_target_pairs={{0,1},{1,0},{2,3},{3,2},{4,5},{5,4},{6,7},{7,6},{8,9},{9,8},{10,11... | collective-permute-start | bytes 786440 | tf_op jit(solution)/shard_map/ppermute | solution.py:86
  34.3 4.5 %collective-permute-start.7 = (f32[256]{0:T(256)S(1)}, f32[256]{0:T(256)S(1)}, u32[]{:S(2)}, u32[]{:S(2)}) collective-permute-start(f32[256]{0:T(256)S(1)} %add.382), channel_id=1, source_target_pairs={{0,8},{2,10},{4,12},{6,14},{8,0},{10,2},{12,4},{14,6},{1,9},{3,11}... | collective-permute-start | bytes 3080 | tf_op jit(solution)/shard_map/ppermute | solution.py:120

commit v11 on v9

--- a/solution.py
+++ b/solution.py
@@ -125,28 +125,35 @@
         swap = [(i, i ^ 1) for i in range(blocks)]
         if lax.axis_size("chan") == 2:
             first = lax.axis_index("chan") == 0
-            got = lax.ppermute(jnp.where(first, frames_in, out_grad), "tm", swap)
-            traded = lax.ppermute(got, "chan", [(0, 1), (1, 0)])
-            other_frames = jnp.where(first, got, traded)
-            other_grad = jnp.where(first, traded, got)
+            both = ("tm", "chan")
+            got_frames = lax.ppermute(frames_in, both, [(2 * t, 2 * (t ^ 1)) for t in range(blocks)])
+            got_grad = lax.ppermute(out_grad, both, [(2 * t + 1, 2 * (t ^ 1) + 1) for t in range(blocks)])
+            traded_frames = lax.ppermute(got_frames, "chan", [(0, 1)])
+            traded_grad = lax.ppermute(got_grad, "chan", [(1, 0)])
+            other_frames = jnp.where(first, got_frames, traded_frames)
+            other_grad = jnp.where(first, traded_grad, got_grad)
         else:
             other_frames = lax.ppermute(frames_in, "tm", swap)
             other_grad = lax.ppermute(out_grad, "tm", swap)
-        frame_blocks = [jnp.where(upper, other_frames, frames_in), jnp.where(upper, frames_in, other_frames)]
-        grad_blocks = [jnp.where(upper, other_grad, out_grad), jnp.where(upper, out_grad, other_grad)]
+        own_order = [frames_in, other_frames]
+        grad_order = [out_grad, other_grad]
     else:
-        frame_blocks = [frames_in]
-        grad_blocks = [out_grad]
+        own_order = [frames_in]
+        grad_order = [out_grad]
     span = frame_count * width
     row_taps = row_taps_of(row_halo(frames_in), row_count)
     in_taps = prep_kernel(in_kernel, False, row_taps)
     adjoint_taps = prep_kernel(out_kernel, True, row_taps)
-    values = jnp.concatenate(
-        [conv_apply(block, row_halo(block), in_taps, row_taps) for block in frame_blocks]
-    )
-    adjoint_in = jnp.concatenate(
-        [conv_apply(block, row_halo(block), adjoint_taps, row_taps) for block in grad_blocks]
-    )
+
+    def in_clip_order(parts):
+        if width == 1:
+            return parts[0]
+        return jnp.concatenate(
+            [jnp.where(upper, parts[1], parts[0]), jnp.where(upper, parts[0], parts[1])]
+        )
+
+    values = in_clip_order([conv_apply(b, row_halo(b), in_taps, row_taps) for b in own_order])
+    adjoint_in = in_clip_order([conv_apply(b, row_halo(b), adjoint_taps, row_taps) for b in grad_order])
     input_gain = jnp.sqrt(1.0 - decay_rate * decay_rate)
     keep_padded = jnp.concatenate([frame_keep, jnp.zeros((1,), jnp.float32)])
     offset = group * span

time: 40.9 us -> 52.8 us (1.29)
  starting transfers between devices: 10.4 us -> 17.7 us
  matrix products: 5.41 us -> 10.6 us
  local copies, waits for them, and re-layouts: 3.47 us -> 7.64 us
  waiting for transfers between devices: 13.2 us -> 9.44 us
  other arithmetic: 6.98 us -> 5.9 us
    ppermute x2 -> x4, starting transfers between devices: 2.94 us -> 8.97 us  [the longest x1 4.85 us: local(): lax.ppermute(frames_in, both, [(2 * t, 2 * (t ^ 1)) for t in range(blocks)])]
    dot_general x24, matrix products: 5.41 us -> 10.6 us  [conv_apply(): jnp.dot(portion.reshape(-1, channels), taps[index, col_tap], preferred_el...]
    slice x4 -> x6, local copies, waits for them, and re-layouts: 0.54 us -> 4.07 us  [conv_apply(): padded[:, row_tap:row_tap + row_count, col_tap:col_tap + col_count, :]]
    ppermute x2 -> x4, waiting for transfers between devices: 4.04 us -> 1.1 us  [the longest x1 1.09 us: local(): traded_grad = lax.ppermute(got_grad, 'chan', [(1, 0)])]
    select_n x2 -> x1, other arithmetic: 2.89 us -> 1.08 us  [local(): other_grad = jnp.where(first, traded_grad, got_grad)]
    ppermute x3, waiting for transfers between devices: 5.38 us -> 4.04 us  [cyclic_carries(): received[step] = lax.ppermute(message, axis, route(step))]
    ppermute x2, starting transfers between devices: 1.93 us -> 2.91 us  [group_sum(): value = value + lax.ppermute(value, axis, route(step))]
    ppermute x3, starting transfers between devices: 4.93 us -> 5.63 us  [cyclic_carries(): received[step] = lax.ppermute(message, axis, route(step))]
  transfers between devices with their start and end apart: 9 -> 11, of which waited for: 7 -> 6; matrix products, arithmetic and copies ran while one was open for 18% -> 35% of each run, Pallas kernels for 0% -> 0%
where the time goes in v11:
time: 52.8 us; the launch traced here: 52.4 us
  starting transfers between devices  17.7 us (34%)
  matrix products  10.6 us (20%)
  waiting for transfers between devices  9.44 us (18%)
  local copies, waits for them, and re-layouts  7.64 us (14%)
  other arithmetic  5.9 us (11%)
  between operations  1.22 us (2%)
    dot_general x24, matrix products, conv_apply(): jnp.dot(portion.reshape(-1, channels), taps[index, col_tap], preferred_el...  10.6 us
    ppermute x3, starting transfers between devices, cyclic_carries(): received[step] = lax.ppermute(message, axis, route(step))  5.63 us
    ppermute x1, starting transfers between devices, local(): lax.ppermute(frames_in, both, [(2 * t, 2 * (t ^ 1)) for t in range(blocks)])  4.85 us
    ppermute x2, waiting for transfers between devices, group_sum(): value = value + lax.ppermute(value, axis, route(step))  4.3 us
    slice x6, local copies, waits for them, and re-layouts, conv_apply(): padded[:, row_tap:row_tap + row_count, col_tap:col_tap + col_count, :]  4.07 us
    ppermute x3, waiting for transfers between devices, cyclic_carries(): received[step] = lax.ppermute(message, axis, route(step))  4.04 us
    ppermute x2, starting transfers between devices, group_sum(): value = value + lax.ppermute(value, axis, route(step))  2.91 us
    ppermute x1, starting transfers between devices, local(): traded_frames = lax.ppermute(got_frames, 'chan', [(0, 1)])  1.47 us
  transfers between devices with their start and end apart: 11, of which 6 were waited for; matrix products, arithmetic and copies ran while one was open for 35% of the time, Pallas kernels for 0%

profile of v11, /device:TPU:0, one launch (start us, length us, event | category | flops | bytes accessed | tf_op | source)
XLA Modules:
  0.0 52.4 jit_solution(210106027873456209)
XLA Ops:
  0.6 4.8 %collective-permute-start = (bf16[4,1,64,512]{3,2,1,0:T(8,128)(2,1)}, bf16[4,1,64,512]{3,2,1,0:T(8,128)(2,1)}, u32[]{:S(2)}, u32[]{:S(2)}) collective-permute-start(bf16[4,1,64,512]{3,2,1,0:T(8,128)(2,1)} %param.6), channel_id=1, source_target_pairs={{0,2},{2,0},{4,6},{6,4},{8,10},{10,8},{12,14},{14,12},{16,18},{18,... | collective-permute-start | bytes 786440 | tf_op jit(solution)/shard_map/ppermute | solution.py:129
  5.5 1.4 %collective-permute-start.2 = (bf16[4,1,64,512]{3,2,1,0:T(8,128)(2,1)}, bf16[4,1,64,512]{3,2,1,0:T(8,128)(2,1)}, u32[]{:S(2)}, u32[]{:S(2)}) collective-permute-start(bf16[4,1,64,512]{3,2,1,0:T(8,128)(2,1)} %param.11), channel_id=1, source_target_pairs={{1,3},{3,1},{5,7},{7,5},{9,11},{11,9},{13,15},{15,13},{17,19},{19,... | collective-permute-start | bytes 786440 | tf_op jit(solution)/shard_map/ppermute | solution.py:130
  6.9 1.9 %pad_slice_fusion.5 = (bf16[4,1,64,512]{3,2,1,0:T(8,128)(2,1)}, bf16[4,1,64,512]{3,2,1,0:T(8,128)(2,1)S(1)}) fusion(bf16[4,1,64,512]{3,2,1,0:T(8,128)(2,1)} %param.6), kind=kLoop, calls=%fused_computation.23 | loop fusion | bytes 786432 | tf_op jit(solution)/shard_map/slice | solution.py:48
  8.7 1.9 %pad_slice_fusion.1 = (bf16[4,1,64,512]{3,2,1,0:T(8,128)(2,1)}, bf16[4,1,64,512]{3,2,1,0:T(8,128)(2,1)S(1)}) fusion(bf16[4,1,64,512]{3,2,1,0:T(8,128)(2,1)} %param.11), kind=kLoop, calls=%fused_computation.19 | loop fusion | bytes 786432 | tf_op jit(solution)/shard_map/slice | solution.py:48
  10.6 0.7 %mul.1561 = f32[4,8]{1,0:T(4,128)S(1)} reshape(f32[32]{0:T(128)} %param.10) | data formatting | bytes 256 | tf_op jit(solution)/shard_map/mul | solution.py:183
  12.9 1.2 %slice.320 = bf16[1,3,512,256]{3,2,1,0:T(8,128)(2,1)S(1)} slice(bf16[3,3,512,256]{3,2,1,0:T(8,128)(2,1)} %param.7), slice={[1:2], [0:3], [0:512], [0:256]} | slice | bytes 1572864 | tf_op jit(solution)/shard_map/slice | solution.py:31
  14.1 1.2 %slice.340 = bf16[1,3,256,512]{3,2,1,0:T(8,128)(2,1)S(1)} slice(bf16[3,3,256,512]{3,2,1,0:T(8,128)(2,1)} %param.8), slice={[1:2], [0:3], [0:256], [0:512]} | slice | bytes 1572864 | tf_op jit(solution)/shard_map/slice | solution.py:28
  16.3 1.9 %convolution_add_fusion.12 = f32[256,256]{1,0:T(8,128)} fusion(f32[256,256]{1,0:T(8,128)S(1)} %convolution_add_fusion.13, bf16[256,512]{1,0:T(8,128)(2,1)} %bitcast.362, bf16[1,3,512,256]{3,2,1,0:T(8,128)(2,1)S(1)} %slice.320), kind=kOutput, calls=%fused_computation.12 | convolution fusion | flops 67174400 | bytes 1048576 | tf_op jit(solution)/shard_map/dot_general | solution.py:49
  18.2 1.0 %fusion.9 = f32[256,256]{1,0:T(8,128)} fusion(bf16[256,512]{1,0:T(8,128)(2,1)S(1)} %bitcast.357, bf16[1,3,512,256]{2,3,1,0:T(8,128)(2,1)S(1)} %reverse_bitcast_fusion.1), kind=kOutput, calls=%fused_computation.52 | convolution fusion | flops 67108864 | bytes 786432 | tf_op jit(solution)/shard_map/dot_general | solution.py:49
  19.8 1.9 %convolution_add_fusion.9 = f32[256,256]{1,0:T(8,128)} fusion(f32[256,256]{1,0:T(8,128)} %fusion.9, bf16[256,512]{1,0:T(8,128)(2,1)S(1)} %bitcast.360, bf16[1,3,512,256]{2,3,1,0:T(8,128)(2,1)S(1)} %reverse_bitcast_fusion.1), kind=kOutput, calls=%fused_computation.9 | convolution fusion | flops 67174400 | bytes 1048576 | tf_op jit(solution)/shard_map/dot_general | solution.py:49
  21.8 1.5 %collective-permute-start.1 = (bf16[4,1,64,512]{3,2,1,0:T(8,128)(2,1)}, bf16[4,1,64,512]{3,2,1,0:T(8,128)(2,1)S(1)}, u32[]{:S(2)}, u32[]{:S(2)}) collective-permute-start(bf16[4,1,64,512]{3,2,1,0:T(8,128)(2,1)} %collective-permute-done), channel_id=1, source_target_pairs={{0,1},{2,3},{4,5},{6,7},{8,9},{10,11},{12,13},{14,15},{16,17},{18,... | collective-permute-start | bytes 786440 | tf_op jit(solution)/shard_map/ppermute | solution.py:131
  23.2 1.3 %collective-permute-start.3 = (bf16[4,1,64,512]{3,2,1,0:T(8,128)(2,1)}, bf16[4,1,64,512]{3,2,1,0:T(8,128)(2,1)}, u32[]{:S(2)}, u32[]{:S(2)}) collective-permute-start(bf16[4,1,64,512]{3,2,1,0:T(8,128)(2,1)} %collective-permute-done.2), channel_id=1, source_target_pairs={{1,0},{3,2},{5,4},{7,6},{9,8},{11,10},{13,12},{15,14},{17,16},{19,... | collective-permute-start | bytes 786440 | tf_op jit(solution)/shard_map/ppermute | solution.py:132
  24.6 1.3 %convolution_add_fusion.8 = f32[256,256]{1,0:T(8,128)S(1)} fusion(f32[256,256]{1,0:T(8,128)} %convolution_add_fusion.9, bf16[256,512]{1,0:T(8,128)(2,1)} %bitcast.361, bf16[1,3,512,256]{2,3,1,0:T(8,128)(2,1)S(1)} %reverse_bitcast_fusion.1), kind=kOutput, calls=%fused_computation.8 | convolution fusion | flops 67174400 | bytes 1048576 | tf_op jit(solution)/shard_map/dot_general | solution.py:49
  25.9 1.1 %collective-permute-done.3 = bf16[4,1,64,512]{3,2,1,0:T(8,128)(2,1)} collective-permute-done((bf16[4,1,64,512]{3,2,1,0:T(8,128)(2,1)}, bf16[4,1,64,512]{3,2,1,0:T(8,128)(2,1)}, u32[]{:S(2)}, u32[]{:S(2)}) %collective-permute-start.3) | collective-permute-done | bytes 262176 | tf_op jit(solution)/shard_map/ppermute | solution.py:132
  27.0 1.1 %broadcast_select_fusion = (bf16[4,1,64,512]{3,2,1,0:T(8,128)(2,1)S(1)}, bf16[4,1,64,512]{3,2,1,0:T(8,128)(2,1)S(1)}) fusion(bf16[4,1,64,512]{3,2,1,0:T(8,128)(2,1)} %collective-permute-done.3, bf16[4,1,64,512]{3,2,1,0:T(8,128)(2,1)} %collective-permute-done.2, pred[]{:T(512)S(6)} %eq.9, bf16[4,1,64,512]{3,2,1,0:T(8,128)(2,1)} %collective-permute-done, ...), kind=kLoop, calls=%fused_computation.48 | loop fusion | flops 262144 | bytes 1572865 | tf_op jit(solution)/shard_map/jit(_where)/select_n | solution.py:134
  30.0 1.6 %collective-permute-start.4 = (f32[1,64,256]{2,1,0:T(8,128)S(1)}, f32[1,64,256]{2,1,0:T(8,128)S(1)}, u32[]{:S(2)}, u32[]{:S(2)}) collective-permute-start(f32[1,64,256]{2,1,0:T(8,128)S(1)} %get-tuple-element.50), channel_id=1, source_target_pairs={{0,4},{2,6},{4,8},{6,10},{8,12},{10,14},{12,0},{14,2},{1,5},{3,7},... | collective-permute-start | bytes 196616 | tf_op jit(solution)/shard_map/ppermute | solution.py:90
  31.7 2.6 %collective-permute-start.5 = (f32[1,64,256]{2,1,0:T(8,128)S(1)}, f32[1,64,256]{2,1,0:T(8,128)S(1)}, u32[]{:S(2)}, u32[]{:S(2)}) collective-permute-start(f32[1,64,256]{2,1,0:T(8,128)S(1)} %get-tuple-element.77), channel_id=1, source_target_pairs={{0,8},{2,10},{4,12},{6,14},{8,0},{10,2},{12,4},{14,6},{1,9},{3,11}... | collective-permute-start | bytes 196616 | tf_op jit(solution)/shard_map/ppermute | solution.py:90
  34.3 1.3 %collective-permute-start.6 = (f32[1,64,256]{2,1,0:T(8,128)S(1)}, f32[1,64,256]{2,1,0:T(8,128)S(1)}, u32[]{:S(2)}, u32[]{:S(2)}) collective-permute-start(f32[1,64,256]{2,1,0:T(8,128)S(1)} %get-tuple-element.78), channel_id=1, source_target_pairs={{0,12},{2,14},{4,0},{6,2},{8,4},{10,6},{12,8},{14,10},{1,13},{3,15... | collective-permute-start | bytes 196616 | tf_op jit(solution)/shard_map/ppermute | solution.py:90
  35.7 1.0 %collective-permute-done.4 = f32[1,64,256]{2,1,0:T(8,128)S(1)} collective-permute-done((f32[1,64,256]{2,1,0:T(8,128)S(1)}, f32[1,64,256]{2,1,0:T(8,128)S(1)}, u32[]{:S(2)}, u32[]{:S(2)}) %collective-permute-start.4) | collective-permute-done | bytes 65568 | tf_op jit(solution)/shard_map/ppermute | solution.py:90
  36.6 2.8 %collective-permute-done.5 = f32[1,64,256]{2,1,0:T(8,128)S(1)} collective-permute-done((f32[1,64,256]{2,1,0:T(8,128)S(1)}, f32[1,64,256]{2,1,0:T(8,128)S(1)}, u32[]{:S(2)}, u32[]{:S(2)}) %collective-permute-start.5) | collective-permute-done | bytes 65568 | tf_op jit(solution)/shard_map/ppermute | solution.py:90
  42.4 1.7 %collective-permute-start.9 = (f32[256]{0:T(256)S(1)}, f32[256]{0:T(256)S(1)}, u32[]{:S(2)}, u32[]{:S(2)}) collective-permute-start(f32[256]{0:T(256)S(1)} %fusion.4), channel_id=1, source_target_pairs={{0,4},{2,6},{4,0},{6,2},{8,12},{10,14},{12,8},{14,10},{1,5},{3,7},... | collective-permute-start | bytes 3080 | tf_op jit(solution)/shard_map/ppermute | solution.py:111
  44.7 1.3 %collective-permute-done.9 = f32[256]{0:T(256)S(1)} collective-permute-done((f32[256]{0:T(256)S(1)}, f32[256]{0:T(256)S(1)}, u32[]{:S(2)}, u32[]{:S(2)}) %collective-permute-start.9) | collective-permute-done | bytes 1056 | tf_op jit(solution)/shard_map/ppermute | solution.py:111
  46.0 1.2 %collective-permute-start.10 = (f32[256]{0:T(256)S(1)}, f32[256]{0:T(256)S(1)}, u32[]{:S(2)}, u32[]{:S(2)}) collective-permute-start(f32[256]{0:T(256)S(1)} %add.758), channel_id=1, source_target_pairs={{0,8},{2,10},{4,12},{6,14},{8,0},{10,2},{12,4},{14,6},{1,9},{3,11}... | collective-permute-start | bytes 3080 | tf_op jit(solution)/shard_map/ppermute | solution.py:111
  47.5 3.0 %collective-permute-done.10 = f32[256]{0:T(256)S(1)} collective-permute-done((f32[256]{0:T(256)S(1)}, f32[256]{0:T(256)S(1)}, u32[]{:S(2)}, u32[]{:S(2)}) %collective-permute-start.10) | collective-permute-done | bytes 1056 | tf_op jit(solution)/shard_map/ppermute | solution.py:111
  (86 shorter events, 10.4 us)
Async XLA Ops:
  0.6 21.1 %collective-permute-start = (bf16[4,1,64,512]{3,2,1,0:T(8,128)(2,1)}, bf16[4,1,64,512]{3,2,1,0:T(8,128)(2,1)}, u32[]{:S(2)}, u32[]{:S(2)}) collective-permute-start(bf16[4,1,64,512]{3,2,1,0:T(8,128)(2,1)} %param.6), channel_id=1, source_target_pairs={{0,2},{2,0},{4,6},{6,4},{8,10},{10,8},{12,14},{14,12},{16,18},{18,... | collective-permute-start | bytes 786440 | tf_op jit(solution)/shard_map/ppermute | solution.py:129
  5.5 17.8 %collective-permute-start.2 = (bf16[4,1,64,512]{3,2,1,0:T(8,128)(2,1)}, bf16[4,1,64,512]{3,2,1,0:T(8,128)(2,1)}, u32[]{:S(2)}, u32[]{:S(2)}) collective-permute-start(bf16[4,1,64,512]{3,2,1,0:T(8,128)(2,1)} %param.11), channel_id=1, source_target_pairs={{1,3},{3,1},{5,7},{7,5},{9,11},{11,9},{13,15},{15,13},{17,19},{19,... | collective-permute-start | bytes 786440 | tf_op jit(solution)/shard_map/ppermute | solution.py:130
  12.9 2.6 %copy-start.3 = (f32[256]{0:T(256)S(1)}, f32[256]{0:T(256)}, u32[]{:S(2)}) copy-start(f32[256]{0:T(256)} %param.9) | copy-start | bytes 3076
  14.1 1.9 %copy-start = (bf16[4,1,64,512]{3,2,1,0:T(8,128)(2,1)S(1)}, bf16[4,1,64,512]{3,2,1,0:T(8,128)(2,1)}, u32[]{:S(2)}) copy-start(bf16[4,1,64,512]{3,2,1,0:T(8,128)(2,1)} %param.6) | copy-start | bytes 786436
  16.0 3.8 %copy-start.1 = (bf16[4,1,64,512]{3,2,1,0:T(8,128)(2,1)S(1)}, bf16[4,1,64,512]{3,2,1,0:T(8,128)(2,1)}, u32[]{:S(2)}) copy-start(bf16[4,1,64,512]{3,2,1,0:T(8,128)(2,1)} %param.11) | copy-start | bytes 786436
  21.8 4.2 %collective-permute-start.1 = (bf16[4,1,64,512]{3,2,1,0:T(8,128)(2,1)}, bf16[4,1,64,512]{3,2,1,0:T(8,128)(2,1)S(1)}, u32[]{:S(2)}, u32[]{:S(2)}) collective-permute-start(bf16[4,1,64,512]{3,2,1,0:T(8,128)(2,1)} %collective-permute-done), channel_id=1, source_target_pairs={{0,1},{2,3},{4,5},{6,7},{8,9},{10,11},{12,13},{14,15},{16,17},{18,... | collective-permute-start | bytes 786440 | tf_op jit(solution)/shard_map/ppermute | solution.py:131
  23.2 3.8 %collective-permute-start.3 = (bf16[4,1,64,512]{3,2,1,0:T(8,128)(2,1)}, bf16[4,1,64,512]{3,2,1,0:T(8,128)(2,1)}, u32[]{:S(2)}, u32[]{:S(2)}) collective-permute-start(bf16[4,1,64,512]{3,2,1,0:T(8,128)(2,1)} %collective-permute-done.2), channel_id=1, source_target_pairs={{1,0},{3,2},{5,4},{7,6},{9,8},{11,10},{13,12},{15,14},{17,16},{19,... | collective-permute-start | bytes 786440 | tf_op jit(solution)/shard_map/ppermute | solution.py:132
  28.2 1.1 %copy-start.2 = (f32[256,256]{1,0:T(8,128)S(1)}, f32[256,256]{1,0:T(8,128)}, u32[]{:S(2)}) copy-start(f32[256,256]{1,0:T(8,128)} %convolution_add_fusion.12) | copy-start | bytes 786436
  29.4 10.4 %copy-start.6 = (f32[256]{0:T(256)S(1)}, f32[256]{0:T(256)}, u32[]{:S(2)}) copy-start(f32[256]{0:T(256)} %get-tuple-element.36) | copy-start | bytes 3076
  29.6 10.2 %copy-start.5 = (f32[256]{0:T(256)S(1)}, f32[256]{0:T(256)}, u32[]{:S(2)}) copy-start(f32[256]{0:T(256)} %get-tuple-element.37) | copy-start | bytes 3076
  29.6 10.2 %copy-start.4 = (f32[256]{0:T(256)S(1)}, f32[256]{0:T(256)}, u32[]{:S(2)}) copy-start(f32[256]{0:T(256)} %get-tuple-element.38) | copy-start | bytes 3076
  30.0 6.6 %collective-permute-start.4 = (f32[1,64,256]{2,1,0:T(8,128)S(1)}, f32[1,64,256]{2,1,0:T(8,128)S(1)}, u32[]{:S(2)}, u32[]{:S(2)}) collective-permute-start(f32[1,64,256]{2,1,0:T(8,128)S(1)} %get-tuple-element.50), channel_id=1, source_target_pairs={{0,4},{2,6},{4,8},{6,10},{8,12},{10,14},{12,0},{14,2},{1,5},{3,7},... | collective-permute-start | bytes 196616 | tf_op jit(solution)/shard_map/ppermute | solution.py:90
  31.7 7.8 %collective-permute-start.5 = (f32[1,64,256]{2,1,0:T(8,128)S(1)}, f32[1,64,256]{2,1,0:T(8,128)S(1)}, u32[]{:S(2)}, u32[]{:S(2)}) collective-permute-start(f32[1,64,256]{2,1,0:T(8,128)S(1)} %get-tuple-element.77), channel_id=1, source_target_pairs={{0,8},{2,10},{4,12},{6,14},{8,0},{10,2},{12,4},{14,6},{1,9},{3,11}... | collective-permute-start | bytes 196616 | tf_op jit(solution)/shard_map/ppermute | solution.py:90
  34.3 5.4 %collective-permute-start.6 = (f32[1,64,256]{2,1,0:T(8,128)S(1)}, f32[1,64,256]{2,1,0:T(8,128)S(1)}, u32[]{:S(2)}, u32[]{:S(2)}) collective-permute-start(f32[1,64,256]{2,1,0:T(8,128)S(1)} %get-tuple-element.78), channel_id=1, source_target_pairs={{0,12},{2,14},{4,0},{6,2},{8,4},{10,6},{12,8},{14,10},{1,13},{3,15... | collective-permute-start | bytes 196616 | tf_op jit(solution)/shard_map/ppermute | solution.py:90
  42.2 8.9 %collective-permute-start.8 = (bf16[4,1,64,256]{3,2,1,0:T(8,128)(2,1)S(1)}, bf16[4,1,64,256]{3,2,1,0:T(8,128)(2,1)S(1)}, u32[]{:S(2)}, u32[]{:S(2)}) collective-permute-start(bf16[4,1,64,256]{3,2,1,0:T(8,128)(2,1)S(1)} %bitcast.369), channel_id=1, source_target_pairs={{0,1},{1,0},{2,3},{3,2},{4,5},{5,4},{6,7},{7,6},{8,9},{9,8},{10,11... | collective-permute-start | bytes 393224 | tf_op jit(solution)/shard_map/ppermute | solution.py:81
  42.4 3.6 %collective-permute-start.9 = (f32[256]{0:T(256)S(1)}, f32[256]{0:T(256)S(1)}, u32[]{:S(2)}, u32[]{:S(2)}) collective-permute-start(f32[256]{0:T(256)S(1)} %fusion.4), channel_id=1, source_target_pairs={{0,4},{2,6},{4,0},{6,2},{8,12},{10,14},{12,8},{14,10},{1,5},{3,7},... | collective-permute-start | bytes 3080 | tf_op jit(solution)/shard_map/ppermute | solution.py:111
  46.0 4.5 %collective-permute-start.10 = (f32[256]{0:T(256)S(1)}, f32[256]{0:T(256)S(1)}, u32[]{:S(2)}, u32[]{:S(2)}) collective-permute-start(f32[256]{0:T(256)S(1)} %add.758), channel_id=1, source_target_pairs={{0,8},{2,10},{4,12},{6,14},{8,0},{10,2},{12,4},{14,6},{1,9},{3,11}... | collective-permute-start | bytes 3080 | tf_op jit(solution)/shard_map/ppermute | solution.py:111
  47.4 4.3 %collective-permute-start.7 = (bf16[4,1,64,256]{3,2,1,0:T(8,128)(2,1)S(1)}, bf16[4,1,64,256]{3,2,1,0:T(8,128)(2,1)S(1)}, u32[]{:S(2)}, u32[]{:S(2)}) collective-permute-start(bf16[4,1,64,256]{3,2,1,0:T(8,128)(2,1)S(1)} %bitcast.370), channel_id=1, source_target_pairs={{0,1},{1,0},{2,3},{3,2},{4,5},{5,4},{6,7},{7,6},{8,9},{9,8},{10,11... | collective-permute-start | bytes 393224 | tf_op jit(solution)/shard_map/ppermute | solution.py:81

commit v12 on v9

--- a/solution.py
+++ b/solution.py
@@ -193,14 +193,29 @@
         local_states[-1], back_states[0], fwd_prod, bwd_prod, "tm", group, groups, route
     )
 
+    value_weight = decay_rate * decay_rate / input_gain
+    local_part = jnp.zeros(decay_rate.shape, jnp.float32)
+    state_weight = jnp.zeros_like(carry_in)
+    adjoint_weight = jnp.zeros_like(carry_in)
+    cross_weight = jnp.zeros(decay_rate.shape, jnp.float32)
+    for t in range(span):
+        earlier = local_states[t - 1] * decays[t] if t > 0 else 0.0
+        step_x = earlier - value_weight * values[t]
+        step_y = decays[t] * products[t - 1] if t > 0 else decays[t]
+        local_part = local_part + jnp.sum(back_states[t] * step_x, axis=(0, 1))
+        state_weight = state_weight + back_states[t] * step_y
+        adjoint_weight = adjoint_weight + back_products[t] * step_x
+        cross_weight = cross_weight + back_products[t] * step_y
+
     states = jnp.stack([local_states[t] + products[t] * carry_in for t in range(span)])
     adjoints = jnp.stack([back_states[t] + back_products[t] * carry_back for t in range(span)])
-    previous = jnp.concatenate([carry_in[None], states[:-1]], axis=0)
-    terms = adjoints * (
-        decays[:, None, None, :] * previous - decay_rate * decay_rate / input_gain * values
-    )
     total_count = frame_count * blocks * row_count * lax.axis_size("rows") * col_count
-    partial = jnp.sum(terms, axis=(0, 1, 2))
+    partial = (
+        local_part
+        + jnp.sum(carry_in * state_weight, axis=(0, 1))
+        + jnp.sum(carry_back * adjoint_weight, axis=(0, 1))
+        + cross_weight * jnp.sum(carry_back * carry_in, axis=(0, 1))
+    )
     summed = group_sum(partial, "tm", group, groups, lambda step: route(step, False))
     if summed is None:
         summed = lax.psum(partial, "tm") / width

time: 40.9 us -> 41.1 us (level)
  waiting for transfers between devices: 13.2 us -> 12.7 us
  local copies, waits for them, and re-layouts: 3.47 us -> 3.9 us
    mul x1, other arithmetic: 0.61 us -> 0.01 us  [local(): product = decays_next[t] if product is None else product * decays_next[t]]
    ppermute x1, waiting for transfers between devices: 1.85 us -> 1.26 us  [local(): traded = lax.ppermute(got, 'chan', [(0, 1), (1, 0)])]
    div x1 -> x0, other arithmetic: 0.58 us -> none  [local(): decay_rate * decay_rate / input_gain * values]
    sqrt x0 -> x1, other arithmetic: none -> 0.58 us  [local(): input_gain = jnp.sqrt(1.0 - decay_rate * decay_rate)]
    dynamic_slice x1, other arithmetic: 0.01 us -> 0.58 us  [cyclic_carries(): lax.dynamic_index_in_dim(bwd_prod, jnp.minimum(source, count - 1), 0, kee...]
    unnamed x22 -> x58, local copies, waits for them, and re-layouts: 0.05 us -> 0.5 us
where the time goes in v12:
time: 41.1 us; the launch traced here: 40.9 us
  waiting for transfers between devices  12.7 us (31%)
  starting transfers between devices  10.4 us (25%)
  other arithmetic  7.03 us (17%)
  matrix products  5.44 us (13%)
  local copies, waits for them, and re-layouts  3.9 us (9%)
  between operations  1.36 us (3%)
    dot_general x24, matrix products, conv_apply(): jnp.dot(portion.reshape(-1, channels), taps[index, col_tap], preferred_el...  5.44 us
    ppermute x3, waiting for transfers between devices, cyclic_carries(): received[step] = lax.ppermute(message, axis, route(step))  5.4 us
    ppermute x3, starting transfers between devices, cyclic_carries(): received[step] = lax.ppermute(message, axis, route(step))  4.93 us
    ppermute x2, waiting for transfers between devices, group_sum(): value = value + lax.ppermute(value, axis, route(step))  3.81 us
    ppermute x1, starting transfers between devices, local(): got = lax.ppermute(jnp.where(first, frames_in, out_grad), 'tm', swap)  2.94 us
    ppermute x1, waiting for transfers between devices, local(): got = lax.ppermute(jnp.where(first, frames_in, out_grad), 'tm', swap)  2.25 us
    ppermute x2, starting transfers between devices, group_sum(): value = value + lax.ppermute(value, axis, route(step))  1.9 us
    select_n x1, other arithmetic, local(): got = lax.ppermute(jnp.where(first, frames_in, out_grad), 'tm', swap)  1.7 us
  transfers between devices with their start and end apart: 9, of which 7 were waited for; matrix products, arithmetic and copies ran while one was open for 18% of the time, Pallas kernels for 0%

profile of v12, /device:TPU:0, one launch (start us, length us, event | category | flops | bytes accessed | tf_op | source)
XLA Modules:
  0.0 40.9 jit_solution(5090041685428015206)
XLA Ops:
  0.6 1.7 %broadcast_select_fusion.2 = bf16[4,1,64,512]{3,2,1,0:T(8,128)(2,1)} fusion(bf16[4,1,64,512]{3,2,1,0:T(8,128)(2,1)} %param.6, bf16[4,1,64,512]{3,2,1,0:T(8,128)(2,1)} %param.11, pred[]{:T(512)S(6)} %eq.9), kind=kLoop, calls=%fused_computation.46 | loop fusion | flops 131072 | bytes 786433 | tf_op jit(solution)/shard_map/jit(_where)/select_n | solution.py:128
  2.3 2.9 %collective-permute-start = (bf16[4,1,64,512]{3,2,1,0:T(8,128)(2,1)}, bf16[4,1,64,512]{3,2,1,0:T(8,128)(2,1)}, u32[]{:S(2)}, u32[]{:S(2)}) collective-permute-start(bf16[4,1,64,512]{3,2,1,0:T(8,128)(2,1)} %broadcast_select_fusion.2), channel_id=1, source_target_pairs={{0,2},{2,0},{4,6},{6,4},{8,10},{10,8},{12,14},{14,12},{1,3},{3,1},... | collective-permute-start | bytes 786440 | tf_op jit(solution)/shard_map/ppermute | solution.py:128
  5.3 1.2 %slice.341 = bf16[1,3,512,256]{3,2,1,0:T(8,128)(2,1)S(1)} slice(bf16[3,3,512,256]{3,2,1,0:T(8,128)(2,1)} %param.7), slice={[1:2], [0:3], [0:512], [0:256]} | slice | bytes 1572864 | tf_op jit(solution)/shard_map/slice | solution.py:31
  6.5 1.2 %slice.361 = bf16[1,3,256,512]{3,2,1,0:T(8,128)(2,1)S(1)} slice(bf16[3,3,256,512]{3,2,1,0:T(8,128)(2,1)} %param.8), slice={[1:2], [0:3], [0:256], [0:512]} | slice | bytes 1572864 | tf_op jit(solution)/shard_map/slice | solution.py:28
  8.0 0.6 %subtract_sqrt_fusion = (f32[256]{0:T(256)S(1)}, f32[256]{0:T(256)}) fusion(f32[256]{0:T(256)S(1)} %copy-done.10), kind=kLoop, calls=%fused_computation.184 | loop fusion | flops 768 | bytes 3072 | tf_op jit(solution)/shard_map/sqrt | solution.py:150
  9.1 0.3 copy-done.11
  9.7 2.2 %collective-permute-done = bf16[4,1,64,512]{3,2,1,0:T(8,128)(2,1)} collective-permute-done((bf16[4,1,64,512]{3,2,1,0:T(8,128)(2,1)}, bf16[4,1,64,512]{3,2,1,0:T(8,128)(2,1)}, u32[]{:S(2)}, u32[]{:S(2)}) %collective-permute-start) | collective-permute-done | bytes 262176 | tf_op jit(solution)/shard_map/ppermute | solution.py:128
  11.9 0.6 %constant_dynamic-slice_fusion.2 = (f32[1,1,256]{2,1,0:T(1,128)}, f32[1,1,256]{2,1,0:T(1,128)}, f32[1,1,256]{2,1,0:T(1,128)}) fusion(f32[4,1,256]{2,1,0:T(1,128)S(1)} %slice_multiply_fusion.1, s32[]{:T(128)S(6)} %select_n.215, s32[]{:T(128)S(6)} %select_n.218, s32[]{:T(128)S(6)} %select_n.221), kind=kLoop, calls=%fused_computation.158 | loop fusion | flops 256 | bytes 6156 | tf_op jit(solution)/shard_map/jit(dynamic_index_in_dim)/dynamic_slice | solution.py:99
  12.5 1.3 %collective-permute-done.1 = bf16[4,1,64,512]{3,2,1,0:T(8,128)(2,1)} collective-permute-done((bf16[4,1,64,512]{3,2,1,0:T(8,128)(2,1)}, bf16[4,1,64,512]{3,2,1,0:T(8,128)(2,1)}, u32[]{:S(2)}, u32[]{:S(2)}) %collective-permute-start.1) | collective-permute-done | bytes 262176 | tf_op jit(solution)/shard_map/ppermute | solution.py:129
  13.8 1.2 %broadcast_select_fusion.5 = (bf16[4,1,64,512]{3,2,1,0:T(8,128)(2,1)S(1)}, bf16[4,1,64,512]{3,2,1,0:T(8,128)(2,1)S(1)}, bf16[4,1,64,512]{3,2,1,0:T(8,128)(2,1)S(1)}, bf16[4,1,64,512]{3,2,1,0:T(8,128)(2,1)S(1)}) fusion(bf16[4,1,64,512]{3,2,1,0:T(8,128)(2,1)S(1)} %copy-done, pred[]{:T(512)S(6)} %eq.8, bf16[4,1,64,512]{3,2,1,0:T(8,128)(2,1)} %collective-permute-done, ...), kind=kLoop, calls=%fused_computation.49 | loop fusion | flops 786432 | bytes 2097154 | tf_op jit(solution)/shard_map/jit(_where)/select_n | solution.py:135
  17.2 0.3 convolution_add_fusion.8
  19.0 2.9 %collective-permute-start.3 = (f32[1,64,256]{2,1,0:T(8,128)S(1)}, f32[1,64,256]{2,1,0:T(8,128)S(1)}, u32[]{:S(2)}, u32[]{:S(2)}) collective-permute-start(f32[1,64,256]{2,1,0:T(8,128)S(1)} %get-tuple-element.64), channel_id=1, source_target_pairs={{0,8},{2,10},{4,12},{6,14},{8,0},{10,2},{12,4},{14,6},{1,9},{3,11}... | collective-permute-start | bytes 196616 | tf_op jit(solution)/shard_map/ppermute | solution.py:90
  21.9 1.4 %collective-permute-start.4 = (f32[1,64,256]{2,1,0:T(8,128)S(1)}, f32[1,64,256]{2,1,0:T(8,128)S(1)}, u32[]{:S(2)}, u32[]{:S(2)}) collective-permute-start(f32[1,64,256]{2,1,0:T(8,128)S(1)} %get-tuple-element.63), channel_id=1, source_target_pairs={{0,12},{2,14},{4,0},{6,2},{8,4},{10,6},{12,8},{14,10},{1,13},{3,15... | collective-permute-start | bytes 196616 | tf_op jit(solution)/shard_map/ppermute | solution.py:90
  23.2 0.7 %collective-permute-start.2 = (f32[1,64,256]{2,1,0:T(8,128)S(1)}, f32[1,64,256]{2,1,0:T(8,128)S(1)}, u32[]{:S(2)}, u32[]{:S(2)}) collective-permute-start(f32[1,64,256]{2,1,0:T(8,128)S(1)} %get-tuple-element.43), channel_id=1, source_target_pairs={{0,4},{2,6},{4,8},{6,10},{8,12},{10,14},{12,0},{14,2},{1,5},{3,7},... | collective-permute-start | bytes 196616 | tf_op jit(solution)/shard_map/ppermute | solution.py:90
  23.9 1.3 %collective-permute-done.3 = f32[1,64,256]{2,1,0:T(8,128)S(1)} collective-permute-done((f32[1,64,256]{2,1,0:T(8,128)S(1)}, f32[1,64,256]{2,1,0:T(8,128)S(1)}, u32[]{:S(2)}, u32[]{:S(2)}) %collective-permute-start.3) | collective-permute-done | bytes 65568 | tf_op jit(solution)/shard_map/ppermute | solution.py:90
  25.2 0.9 %collective-permute-done.4 = f32[1,64,256]{2,1,0:T(8,128)S(1)} collective-permute-done((f32[1,64,256]{2,1,0:T(8,128)S(1)}, f32[1,64,256]{2,1,0:T(8,128)S(1)}, u32[]{:S(2)}, u32[]{:S(2)}) %collective-permute-start.4) | collective-permute-done | bytes 65568 | tf_op jit(solution)/shard_map/ppermute | solution.py:90
  26.1 3.2 %collective-permute-done.2 = f32[1,64,256]{2,1,0:T(8,128)S(1)} collective-permute-done((f32[1,64,256]{2,1,0:T(8,128)S(1)}, f32[1,64,256]{2,1,0:T(8,128)S(1)}, u32[]{:S(2)}, u32[]{:S(2)}) %collective-permute-start.2) | collective-permute-done | bytes 65568 | tf_op jit(solution)/shard_map/ppermute | solution.py:90
  32.3 0.6 %collective-permute-start.5 = (bf16[4,1,64,256]{3,2,1,0:T(8,128)(2,1)S(1)}, bf16[4,1,64,256]{3,2,1,0:T(8,128)(2,1)S(1)}, u32[]{:S(2)}, u32[]{:S(2)}) collective-permute-start(bf16[4,1,64,256]{3,2,1,0:T(8,128)(2,1)S(1)} %bitcast.277), channel_id=1, source_target_pairs={{0,1},{1,0},{2,3},{3,2},{4,5},{5,4},{6,7},{7,6},{8,9},{9,8},{10,11... | collective-permute-start | bytes 393224 | tf_op jit(solution)/shard_map/ppermute | solution.py:81
  33.1 1.4 %collective-permute-done.7 = f32[256]{0:T(256)S(1)} collective-permute-done((f32[256]{0:T(256)S(1)}, f32[256]{0:T(256)S(1)}, u32[]{:S(2)}, u32[]{:S(2)}) %collective-permute-start.7) | collective-permute-done | bytes 1056 | tf_op jit(solution)/shard_map/ppermute | solution.py:111
  34.4 1.8 %collective-permute-start.8 = (f32[256]{0:T(256)S(1)}, f32[256]{0:T(256)S(1)}, u32[]{:S(2)}, u32[]{:S(2)}) collective-permute-start(f32[256]{0:T(256)S(1)} %add.510), channel_id=1, source_target_pairs={{0,8},{2,10},{4,12},{6,14},{8,0},{10,2},{12,4},{14,6},{1,9},{3,11}... | collective-permute-start | bytes 3080 | tf_op jit(solution)/shard_map/ppermute | solution.py:111
  36.5 2.4 %collective-permute-done.8 = f32[256]{0:T(256)S(1)} collective-permute-done((f32[256]{0:T(256)S(1)}, f32[256]{0:T(256)S(1)}, u32[]{:S(2)}, u32[]{:S(2)}) %collective-permute-start.8) | collective-permute-done | bytes 1056 | tf_op jit(solution)/shard_map/ppermute | solution.py:111
  38.9 0.6 %add_multiply_fusion = f32[256]{0:T(256)} fusion(f32[256]{0:T(256)S(1)} %add.510, f32[256]{0:T(256)S(1)} %collective-permute-done.8), kind=kLoop, calls=%fused_computation.182 | loop fusion | flops 512 | bytes 3072 | tf_op jit(solution)/shard_map/div | solution.py:222
  39.5 0.7 %add_convert_fusion = bf16[4,1,64,256]{3,2,1,0:T(8,128)(2,1)} fusion(f32[4,1,64,256]{3,2,1,0:T(8,128)S(1)} %bitcast.270, bf16[4,1,64,256]{3,2,1,0:T(8,128)(2,1)S(1)} %collective-permute-done.6), kind=kLoop, calls=%fused_computation.42 | loop fusion | flops 196608 | bytes 524288 | tf_op jit(solution)/shard_map/convert_element_type | solution.py:83
  40.2 0.7 %add_convert_fusion.1 = bf16[4,1,64,256]{3,2,1,0:T(8,128)(2,1)} fusion(f32[4,1,64,256]{3,2,1,0:T(8,128)S(1)} %bitcast.274, bf16[4,1,64,256]{3,2,1,0:T(8,128)(2,1)S(1)} %collective-permute-done.5), kind=kLoop, calls=%fused_computation.43 | loop fusion | flops 196608 | bytes 524288 | tf_op jit(solution)/shard_map/convert_element_type | solution.py:83
  (118 shorter events, 7.5 us)
Async XLA Ops:
  2.3 9.6 %collective-permute-start = (bf16[4,1,64,512]{3,2,1,0:T(8,128)(2,1)}, bf16[4,1,64,512]{3,2,1,0:T(8,128)(2,1)}, u32[]{:S(2)}, u32[]{:S(2)}) collective-permute-start(bf16[4,1,64,512]{3,2,1,0:T(8,128)(2,1)} %broadcast_select_fusion.2), channel_id=1, source_target_pairs={{0,2},{2,0},{4,6},{6,4},{8,10},{10,8},{12,14},{14,12},{1,3},{3,1},... | collective-permute-start | bytes 786440 | tf_op jit(solution)/shard_map/ppermute | solution.py:128
  5.3 2.5 %copy-start.28 = (f32[32]{0:T(128)S(1)}, f32[32]{0:T(128)}, u32[]{:S(2)}) copy-start(f32[32]{0:T(128)} %param.10) | copy-start | bytes 388
  5.3 2.7 %copy-start.10 = (f32[256]{0:T(256)S(1)}, f32[256]{0:T(256)}, u32[]{:S(2)}) copy-start(f32[256]{0:T(256)} %param.9) | copy-start | bytes 3076
  6.5 7.3 %copy-start = (bf16[4,1,64,512]{3,2,1,0:T(8,128)(2,1)S(1)}, bf16[4,1,64,512]{3,2,1,0:T(8,128)(2,1)}, u32[]{:S(2)}) copy-start(bf16[4,1,64,512]{3,2,1,0:T(8,128)(2,1)} %param.6) | copy-start | bytes 786436
  11.9 1.9 %collective-permute-start.1 = (bf16[4,1,64,512]{3,2,1,0:T(8,128)(2,1)}, bf16[4,1,64,512]{3,2,1,0:T(8,128)(2,1)}, u32[]{:S(2)}, u32[]{:S(2)}) collective-permute-start(bf16[4,1,64,512]{3,2,1,0:T(8,128)(2,1)} %collective-permute-done), channel_id=1, source_target_pairs={{0,1},{1,0},{2,3},{3,2},{4,5},{5,4},{6,7},{7,6},{8,9},{9,8},{10,11... | collective-permute-start | bytes 786440 | tf_op jit(solution)/shard_map/ppermute | solution.py:129
  17.4 1.2 %copy-start.4 = (f32[1,256]{1,0:T(1,128)S(1)}, f32[1,256]{1,0:T(1,128)}, u32[]{:S(2)}) copy-start(f32[1,256]{1,0:T(1,128)} %copy-done.3) | copy-start | bytes 3076
  17.4 1.2 %copy-start.6 = (f32[1,256]{1,0:T(1,128)S(1)}, f32[1,256]{1,0:T(1,128)}, u32[]{:S(2)}) copy-start(f32[1,256]{1,0:T(1,128)} %copy-done.5) | copy-start | bytes 3076
  17.5 1.2 %copy-start.9 = (f32[256]{0:T(256)S(1)}, f32[256]{0:T(256)}, u32[]{:S(2)}) copy-start(f32[256]{0:T(256)} %get-tuple-element.108) | copy-start | bytes 3076
  17.5 1.2 %copy-start.12 = (f32[1,256]{1,0:T(1,128)S(1)}, f32[1,256]{1,0:T(1,128)}, u32[]{:S(2)}) copy-start(f32[1,256]{1,0:T(1,128)} %copy-done.11) | copy-start | bytes 3076
  17.5 1.2 %copy-start.14 = (f32[1,256]{1,0:T(1,128)S(1)}, f32[1,256]{1,0:T(1,128)}, u32[]{:S(2)}) copy-start(f32[1,256]{1,0:T(1,128)} %copy-done.13) | copy-start | bytes 3076
  17.5 1.2 %copy-start.16 = (f32[1,256]{1,0:T(1,128)S(1)}, f32[1,256]{1,0:T(1,128)}, u32[]{:S(2)}) copy-start(f32[1,256]{1,0:T(1,128)} %copy-done.15) | copy-start | bytes 3076
  17.5 1.2 %copy-start.18 = (f32[1,256]{1,0:T(1,128)S(1)}, f32[1,256]{1,0:T(1,128)}, u32[]{:S(2)}) copy-start(f32[1,256]{1,0:T(1,128)} %copy-done.17) | copy-start | bytes 3076
  17.5 1.2 %copy-start.20 = (f32[1,256]{1,0:T(1,128)S(1)}, f32[1,256]{1,0:T(1,128)}, u32[]{:S(2)}) copy-start(f32[1,256]{1,0:T(1,128)} %copy-done.19) | copy-start | bytes 3076
  17.5 1.2 %copy-start.22 = (f32[1,256]{1,0:T(1,128)S(1)}, f32[1,256]{1,0:T(1,128)}, u32[]{:S(2)}) copy-start(f32[1,256]{1,0:T(1,128)} %copy-done.21) | copy-start | bytes 3076
  18.1 11.2 %copy-start.25 = (f32[1,1,256]{2,1,0:T(1,128)S(1)}, f32[1,1,256]{2,1,0:T(1,128)}, u32[]{:S(2)}) copy-start(f32[1,1,256]{2,1,0:T(1,128)} %get-tuple-element.100) | copy-start | bytes 3076
  18.1 11.2 %copy-start.26 = (f32[1,1,256]{2,1,0:T(1,128)S(1)}, f32[1,1,256]{2,1,0:T(1,128)}, u32[]{:S(2)}) copy-start(f32[1,1,256]{2,1,0:T(1,128)} %get-tuple-element.101) | copy-start | bytes 3076
  18.1 11.2 %copy-start.27 = (f32[1,1,256]{2,1,0:T(1,128)S(1)}, f32[1,1,256]{2,1,0:T(1,128)}, u32[]{:S(2)}) copy-start(f32[1,1,256]{2,1,0:T(1,128)} %get-tuple-element.102) | copy-start | bytes 3076
  19.0 6.2 %collective-permute-start.3 = (f32[1,64,256]{2,1,0:T(8,128)S(1)}, f32[1,64,256]{2,1,0:T(8,128)S(1)}, u32[]{:S(2)}, u32[]{:S(2)}) collective-permute-start(f32[1,64,256]{2,1,0:T(8,128)S(1)} %get-tuple-element.64), channel_id=1, source_target_pairs={{0,8},{2,10},{4,12},{6,14},{8,0},{10,2},{12,4},{14,6},{1,9},{3,11}... | collective-permute-start | bytes 196616 | tf_op jit(solution)/shard_map/ppermute | solution.py:90
  21.9 4.3 %collective-permute-start.4 = (f32[1,64,256]{2,1,0:T(8,128)S(1)}, f32[1,64,256]{2,1,0:T(8,128)S(1)}, u32[]{:S(2)}, u32[]{:S(2)}) collective-permute-start(f32[1,64,256]{2,1,0:T(8,128)S(1)} %get-tuple-element.63), channel_id=1, source_target_pairs={{0,12},{2,14},{4,0},{6,2},{8,4},{10,6},{12,8},{14,10},{1,13},{3,15... | collective-permute-start | bytes 196616 | tf_op jit(solution)/shard_map/ppermute | solution.py:90
  23.2 6.1 %collective-permute-start.2 = (f32[1,64,256]{2,1,0:T(8,128)S(1)}, f32[1,64,256]{2,1,0:T(8,128)S(1)}, u32[]{:S(2)}, u32[]{:S(2)}) collective-permute-start(f32[1,64,256]{2,1,0:T(8,128)S(1)} %get-tuple-element.43), channel_id=1, source_target_pairs={{0,4},{2,6},{4,8},{6,10},{8,12},{10,14},{12,0},{14,2},{1,5},{3,7},... | collective-permute-start | bytes 196616 | tf_op jit(solution)/shard_map/ppermute | solution.py:90
  30.8 3.6 %collective-permute-start.7 = (f32[256]{0:T(256)S(1)}, f32[256]{0:T(256)S(1)}, u32[]{:S(2)}, u32[]{:S(2)}) collective-permute-start(f32[256]{0:T(256)S(1)} %multiply_add_fusion.9), channel_id=1, source_target_pairs={{0,4},{2,6},{4,0},{6,2},{8,12},{10,14},{12,8},{14,10},{1,5},{3,7},... | collective-permute-start | bytes 3080 | tf_op jit(solution)/shard_map/ppermute | solution.py:111
  31.4 8.1 %collective-permute-start.6 = (bf16[4,1,64,256]{3,2,1,0:T(8,128)(2,1)S(1)}, bf16[4,1,64,256]{3,2,1,0:T(8,128)(2,1)S(1)}, u32[]{:S(2)}, u32[]{:S(2)}) collective-permute-start(bf16[4,1,64,256]{3,2,1,0:T(8,128)(2,1)S(1)} %bitcast.276), channel_id=1, source_target_pairs={{0,1},{1,0},{2,3},{3,2},{4,5},{5,4},{6,7},{7,6},{8,9},{9,8},{10,11... | collective-permute-start | bytes 393224 | tf_op jit(solution)/shard_map/ppermute | solution.py:81
  32.3 7.9 %collective-permute-start.5 = (bf16[4,1,64,256]{3,2,1,0:T(8,128)(2,1)S(1)}, bf16[4,1,64,256]{3,2,1,0:T(8,128)(2,1)S(1)}, u32[]{:S(2)}, u32[]{:S(2)}) collective-permute-start(bf16[4,1,64,256]{3,2,1,0:T(8,128)(2,1)S(1)} %bitcast.277), channel_id=1, source_target_pairs={{0,1},{1,0},{2,3},{3,2},{4,5},{5,4},{6,7},{7,6},{8,9},{9,8},{10,11... | collective-permute-start | bytes 393224 | tf_op jit(solution)/shard_map/ppermute | solution.py:81
  34.4 4.5 %collective-permute-start.8 = (f32[256]{0:T(256)S(1)}, f32[256]{0:T(256)S(1)}, u32[]{:S(2)}, u32[]{:S(2)}) collective-permute-start(f32[256]{0:T(256)S(1)} %add.510), channel_id=1, source_target_pairs={{0,8},{2,10},{4,12},{6,14},{8,0},{10,2},{12,4},{14,6},{1,9},{3,11}... | collective-permute-start | bytes 3080 | tf_op jit(solution)/shard_map/ppermute | solution.py:111
  (14 other events, 9.9 us)

commit v13 on v9

--- a/solution.py
+++ b/solution.py
@@ -125,7 +125,8 @@
         swap = [(i, i ^ 1) for i in range(blocks)]
         if lax.axis_size("chan") == 2:
             first = lax.axis_index("chan") == 0
-            got = lax.ppermute(jnp.where(first, frames_in, out_grad), "tm", swap)
+            outgoing = lax.cond(first, lambda: frames_in, lambda: out_grad)
+            got = lax.ppermute(outgoing, "tm", swap)
             traded = lax.ppermute(got, "chan", [(0, 1), (1, 0)])
             other_frames = jnp.where(first, got, traded)
             other_grad = jnp.where(first, traded, got)

time: 40.9 us -> 40.9 us (level)
  other arithmetic: 6.98 us -> 5.27 us
  local copies, waits for them, and re-layouts: 3.47 us -> 5.14 us
    select_n x1 -> x0, other arithmetic: 1.71 us -> none  [local(): got = lax.ppermute(jnp.where(first, frames_in, out_grad), 'tm', swap)]
    cond x0 -> x1, local copies, waits for them, and re-layouts: none -> 1.67 us
where the time goes in v13:
time: 40.9 us; the launch traced here: 40.7 us
  waiting for transfers between devices  13.2 us (32%)
  starting transfers between devices  10.4 us (25%)
  matrix products  5.41 us (13%)
  other arithmetic  5.27 us (13%)
  local copies, waits for them, and re-layouts  5.14 us (13%)
  between operations  1.2 us (3%)
    dot_general x24, matrix products, conv_apply(): jnp.dot(portion.reshape(-1, channels), taps[index, col_tap], preferred_el...  5.41 us
    ppermute x3, waiting for transfers between devices, cyclic_carries(): received[step] = lax.ppermute(message, axis, route(step))  5.38 us
    ppermute x3, starting transfers between devices, cyclic_carries(): received[step] = lax.ppermute(message, axis, route(step))  4.93 us
    ppermute x2, waiting for transfers between devices, group_sum(): value = value + lax.ppermute(value, axis, route(step))  3.81 us
    ppermute x1, starting transfers between devices, local(): got = lax.ppermute(outgoing, 'tm', swap)  2.94 us
    ppermute x1, waiting for transfers between devices, local(): got = lax.ppermute(outgoing, 'tm', swap)  2.17 us
    ppermute x2, starting transfers between devices, group_sum(): value = value + lax.ppermute(value, axis, route(step))  1.89 us
    ppermute x1, waiting for transfers between devices, local(): traded = lax.ppermute(got, 'chan', [(0, 1), (1, 0)])  1.85 us
  transfers between devices with their start and end apart: 9, of which 7 were waited for; matrix products, arithmetic and copies ran while one was open for 18% of the time, Pallas kernels for 0%

profile of v13, /device:TPU:0, one launch (start us, length us, event | category | flops | bytes accessed | tf_op | source)
XLA Modules:
  0.0 40.7 jit_solution(3414989318124377718)
XLA Ops:
  0.6 1.7 %conditional.1 = (bf16[4,1,64,512]{3,2,1,0:T(8,128)(2,1)}) conditional(s32[]{:T(128)} %convert_element_type.103, bf16[4,1,64,512]{3,2,1,0:T(8,128)(2,1)} %param.13, bf16[4,1,64,512]{3,2,1,0:T(8,128)(2,1)} %param.8), branch_computations={%region_0.1_spmd, %region_1.2_spmd} | conditional | bytes 524296 | solution.py:128
  0.7 1.7 %copy.16 = bf16[4,1,64,512]{3,2,1,0:T(8,128)(2,1)} copy(bf16[4,1,64,512]{3,2,1,0:T(8,128)(2,1)} %param.1) | data formatting | bytes 524288 | tf_op jit(solution)/shard_map/cond
  2.3 2.9 %collective-permute-start = (bf16[4,1,64,512]{3,2,1,0:T(8,128)(2,1)}, bf16[4,1,64,512]{3,2,1,0:T(8,128)(2,1)}, u32[]{:S(2)}, u32[]{:S(2)}) collective-permute-start(bf16[4,1,64,512]{3,2,1,0:T(8,128)(2,1)} %get-tuple-element.163), channel_id=1, source_target_pairs={{0,2},{2,0},{4,6},{6,4},{8,10},{10,8},{12,14},{14,12},{1,3},{3,1},... | collective-permute-start | bytes 786440 | tf_op jit(solution)/shard_map/ppermute | solution.py:129
  5.3 1.2 %slice.320 = bf16[1,3,512,256]{3,2,1,0:T(8,128)(2,1)S(1)} slice(bf16[3,3,512,256]{3,2,1,0:T(8,128)(2,1)} %param.9), slice={[1:2], [0:3], [0:512], [0:256]} | slice | bytes 1572864 | tf_op jit(solution)/shard_map/slice | solution.py:31
  6.5 1.2 %slice.340 = bf16[1,3,256,512]{3,2,1,0:T(8,128)(2,1)S(1)} slice(bf16[3,3,256,512]{3,2,1,0:T(8,128)(2,1)} %param.10), slice={[1:2], [0:3], [0:256], [0:512]} | slice | bytes 1572864 | tf_op jit(solution)/shard_map/slice | solution.py:28
  8.0 0.6 %multiply_divide_fusion = (f32[256]{0:T(256)}, f32[256]{0:T(256)S(1)}) fusion(f32[256]{0:T(256)S(1)} %copy-done.1), kind=kLoop, calls=%fused_computation.189 | loop fusion | flops 768 | bytes 3072 | tf_op jit(solution)/shard_map/div | solution.py:201
  9.0 0.6 %fusion.67 = (f32[256]{0:T(256)}, f32[256]{0:T(256)}, f32[256]{0:T(256)}, f32[256]{0:T(256)}, f32[256]{0:T(256)}, /*index=5*/f32[256]{0:T(256)}, f32[256]{0:T(256)}) fusion(f32[256]{0:T(256)S(1)} %bitcast.338, f32[256]{0:T(256)S(1)} %bitcast.325, f32[256]{0:T(256)S(1)} %bitcast.336, f32[256]{0:T(256)S(1)} %bitcast.322, f32[256]{0:T(256)S(1)} %bitcast.334, ...), kind=kLoop, calls=%fused_computation.191 | loop fusion | flops 1792 | bytes 15360 | tf_op jit(solution)/shard_map/mul | solution.py:173
  9.7 2.2 %collective-permute-done = bf16[4,1,64,512]{3,2,1,0:T(8,128)(2,1)} collective-permute-done((bf16[4,1,64,512]{3,2,1,0:T(8,128)(2,1)}, bf16[4,1,64,512]{3,2,1,0:T(8,128)(2,1)}, u32[]{:S(2)}, u32[]{:S(2)}) %collective-permute-start) | collective-permute-done | bytes 262176 | tf_op jit(solution)/shard_map/ppermute | solution.py:129
  11.9 1.9 %collective-permute-done.1 = bf16[4,1,64,512]{3,2,1,0:T(8,128)(2,1)} collective-permute-done((bf16[4,1,64,512]{3,2,1,0:T(8,128)(2,1)}, bf16[4,1,64,512]{3,2,1,0:T(8,128)(2,1)}, u32[]{:S(2)}, u32[]{:S(2)}) %collective-permute-start.1) | collective-permute-done | bytes 262176 | tf_op jit(solution)/shard_map/ppermute | solution.py:130
  13.8 1.2 %broadcast_select_fusion.5 = (bf16[4,1,64,512]{3,2,1,0:T(8,128)(2,1)S(1)}, bf16[4,1,64,512]{3,2,1,0:T(8,128)(2,1)S(1)}, bf16[4,1,64,512]{3,2,1,0:T(8,128)(2,1)S(1)}, bf16[4,1,64,512]{3,2,1,0:T(8,128)(2,1)S(1)}) fusion(bf16[4,1,64,512]{3,2,1,0:T(8,128)(2,1)S(1)} %copy-done, pred[]{:T(512)S(6)} %eq.8, bf16[4,1,64,512]{3,2,1,0:T(8,128)(2,1)} %collective-permute-done, ...), kind=kLoop, calls=%fused_computation.53 | loop fusion | flops 786432 | bytes 2097154 | tf_op jit(solution)/shard_map/jit(_where)/select_n | solution.py:136
  17.3 0.3 convolution_add_fusion.9
  18.6 2.9 %collective-permute-start.3 = (f32[1,64,256]{2,1,0:T(8,128)S(1)}, f32[1,64,256]{2,1,0:T(8,128)S(1)}, u32[]{:S(2)}, u32[]{:S(2)}) collective-permute-start(f32[1,64,256]{2,1,0:T(8,128)S(1)} %get-tuple-element.84), channel_id=1, source_target_pairs={{0,8},{2,10},{4,12},{6,14},{8,0},{10,2},{12,4},{14,6},{1,9},{3,11}... | collective-permute-start | bytes 196616 | tf_op jit(solution)/shard_map/ppermute | solution.py:90
  21.5 1.3 %collective-permute-start.4 = (f32[1,64,256]{2,1,0:T(8,128)S(1)}, f32[1,64,256]{2,1,0:T(8,128)S(1)}, u32[]{:S(2)}, u32[]{:S(2)}) collective-permute-start(f32[1,64,256]{2,1,0:T(8,128)S(1)} %get-tuple-element.85), channel_id=1, source_target_pairs={{0,12},{2,14},{4,0},{6,2},{8,4},{10,6},{12,8},{14,10},{1,13},{3,15... | collective-permute-start | bytes 196616 | tf_op jit(solution)/shard_map/ppermute | solution.py:90
  22.9 0.7 %collective-permute-start.2 = (f32[1,64,256]{2,1,0:T(8,128)S(1)}, f32[1,64,256]{2,1,0:T(8,128)S(1)}, u32[]{:S(2)}, u32[]{:S(2)}) collective-permute-start(f32[1,64,256]{2,1,0:T(8,128)S(1)} %get-tuple-element.55), channel_id=1, source_target_pairs={{0,4},{2,6},{4,8},{6,10},{8,12},{10,14},{12,0},{14,2},{1,5},{3,7},... | collective-permute-start | bytes 196616 | tf_op jit(solution)/shard_map/ppermute | solution.py:90
  23.5 1.3 %collective-permute-done.3 = f32[1,64,256]{2,1,0:T(8,128)S(1)} collective-permute-done((f32[1,64,256]{2,1,0:T(8,128)S(1)}, f32[1,64,256]{2,1,0:T(8,128)S(1)}, u32[]{:S(2)}, u32[]{:S(2)}) %collective-permute-start.3) | collective-permute-done | bytes 65568 | tf_op jit(solution)/shard_map/ppermute | solution.py:90
  24.8 0.9 %collective-permute-done.4 = f32[1,64,256]{2,1,0:T(8,128)S(1)} collective-permute-done((f32[1,64,256]{2,1,0:T(8,128)S(1)}, f32[1,64,256]{2,1,0:T(8,128)S(1)}, u32[]{:S(2)}, u32[]{:S(2)}) %collective-permute-start.4) | collective-permute-done | bytes 65568 | tf_op jit(solution)/shard_map/ppermute | solution.py:90
  25.8 3.1 %collective-permute-done.2 = f32[1,64,256]{2,1,0:T(8,128)S(1)} collective-permute-done((f32[1,64,256]{2,1,0:T(8,128)S(1)}, f32[1,64,256]{2,1,0:T(8,128)S(1)}, u32[]{:S(2)}, u32[]{:S(2)}) %collective-permute-start.2) | collective-permute-done | bytes 65568 | tf_op jit(solution)/shard_map/ppermute | solution.py:90
  32.1 0.6 %collective-permute-start.5 = (bf16[4,1,64,256]{3,2,1,0:T(8,128)(2,1)S(1)}, bf16[4,1,64,256]{3,2,1,0:T(8,128)(2,1)S(1)}, u32[]{:S(2)}, u32[]{:S(2)}) collective-permute-start(bf16[4,1,64,256]{3,2,1,0:T(8,128)(2,1)S(1)} %bitcast.309), channel_id=1, source_target_pairs={{0,1},{1,0},{2,3},{3,2},{4,5},{5,4},{6,7},{7,6},{8,9},{9,8},{10,11... | collective-permute-start | bytes 393224 | tf_op jit(solution)/shard_map/ppermute | solution.py:81
  32.9 1.4 %collective-permute-done.7 = f32[256]{0:T(256)S(1)} collective-permute-done((f32[256]{0:T(256)S(1)}, f32[256]{0:T(256)S(1)}, u32[]{:S(2)}, u32[]{:S(2)}) %collective-permute-start.7) | collective-permute-done | bytes 1056 | tf_op jit(solution)/shard_map/ppermute | solution.py:111
  34.3 1.8 %collective-permute-start.8 = (f32[256]{0:T(256)S(1)}, f32[256]{0:T(256)S(1)}, u32[]{:S(2)}, u32[]{:S(2)}) collective-permute-start(f32[256]{0:T(256)S(1)} %add.366), channel_id=1, source_target_pairs={{0,8},{2,10},{4,12},{6,14},{8,0},{10,2},{12,4},{14,6},{1,9},{3,11}... | collective-permute-start | bytes 3080 | tf_op jit(solution)/shard_map/ppermute | solution.py:111
  36.3 2.4 %collective-permute-done.8 = f32[256]{0:T(256)S(1)} collective-permute-done((f32[256]{0:T(256)S(1)}, f32[256]{0:T(256)S(1)}, u32[]{:S(2)}, u32[]{:S(2)}) %collective-permute-start.8) | collective-permute-done | bytes 1056 | tf_op jit(solution)/shard_map/ppermute | solution.py:111
  38.7 0.6 %add_multiply_fusion = f32[256]{0:T(256)} fusion(f32[256]{0:T(256)S(1)} %add.366, f32[256]{0:T(256)S(1)} %collective-permute-done.8), kind=kLoop, calls=%fused_computation.187 | loop fusion | flops 512 | bytes 3072 | tf_op jit(solution)/shard_map/div | solution.py:208
  39.3 0.7 %add_convert_fusion = bf16[4,1,64,256]{3,2,1,0:T(8,128)(2,1)} fusion(f32[4,1,64,256]{3,2,1,0:T(8,128)S(1)} %bitcast.298, bf16[4,1,64,256]{3,2,1,0:T(8,128)(2,1)S(1)} %collective-permute-done.6), kind=kLoop, calls=%fused_computation.46 | loop fusion | flops 196608 | bytes 524288 | tf_op jit(solution)/shard_map/convert_element_type | solution.py:83
  40.0 0.7 %add_convert_fusion.1 = bf16[4,1,64,256]{3,2,1,0:T(8,128)(2,1)} fusion(f32[4,1,64,256]{3,2,1,0:T(8,128)S(1)} %bitcast.299, bf16[4,1,64,256]{3,2,1,0:T(8,128)(2,1)S(1)} %collective-permute-done.5), kind=kLoop, calls=%fused_computation.47 | loop fusion | flops 196608 | bytes 524288 | tf_op jit(solution)/shard_map/convert_element_type | solution.py:83
  (90 shorter events, 7.3 us)
Async XLA Ops:
  2.3 9.5 %collective-permute-start = (bf16[4,1,64,512]{3,2,1,0:T(8,128)(2,1)}, bf16[4,1,64,512]{3,2,1,0:T(8,128)(2,1)}, u32[]{:S(2)}, u32[]{:S(2)}) collective-permute-start(bf16[4,1,64,512]{3,2,1,0:T(8,128)(2,1)} %get-tuple-element.163), channel_id=1, source_target_pairs={{0,2},{2,0},{4,6},{6,4},{8,10},{10,8},{12,14},{14,12},{1,3},{3,1},... | collective-permute-start | bytes 786440 | tf_op jit(solution)/shard_map/ppermute | solution.py:129
  5.3 2.5 %copy-start.10 = (f32[32]{0:T(128)S(1)}, f32[32]{0:T(128)}, u32[]{:S(2)}) copy-start(f32[32]{0:T(128)} %param.12) | copy-start | bytes 388
  5.3 2.7 %copy-start.1 = (f32[256]{0:T(256)S(1)}, f32[256]{0:T(256)}, u32[]{:S(2)}) copy-start(f32[256]{0:T(256)} %param.11) | copy-start | bytes 3076
  6.5 7.3 %copy-start = (bf16[4,1,64,512]{3,2,1,0:T(8,128)(2,1)S(1)}, bf16[4,1,64,512]{3,2,1,0:T(8,128)(2,1)}, u32[]{:S(2)}) copy-start(bf16[4,1,64,512]{3,2,1,0:T(8,128)(2,1)} %param.8) | copy-start | bytes 786436
  11.9 1.9 %collective-permute-start.1 = (bf16[4,1,64,512]{3,2,1,0:T(8,128)(2,1)}, bf16[4,1,64,512]{3,2,1,0:T(8,128)(2,1)}, u32[]{:S(2)}, u32[]{:S(2)}) collective-permute-start(bf16[4,1,64,512]{3,2,1,0:T(8,128)(2,1)} %collective-permute-done), channel_id=1, source_target_pairs={{0,1},{1,0},{2,3},{3,2},{4,5},{5,4},{6,7},{7,6},{8,9},{9,8},{10,11... | collective-permute-start | bytes 786440 | tf_op jit(solution)/shard_map/ppermute | solution.py:130
  17.6 11.3 %copy-start.9 = (f32[256]{0:T(256)S(1)}, f32[256]{0:T(256)}, u32[]{:S(2)}) copy-start(f32[256]{0:T(256)} %get-tuple-element.41) | copy-start | bytes 3076
  17.9 11.1 %copy-start.8 = (f32[256]{0:T(256)S(1)}, f32[256]{0:T(256)}, u32[]{:S(2)}) copy-start(f32[256]{0:T(256)} %get-tuple-element.42) | copy-start | bytes 3076
  17.9 11.1 %copy-start.7 = (f32[256]{0:T(256)S(1)}, f32[256]{0:T(256)}, u32[]{:S(2)}) copy-start(f32[256]{0:T(256)} %get-tuple-element.43) | copy-start | bytes 3076
  17.9 11.2 %copy-start.6 = (f32[256]{0:T(256)S(1)}, f32[256]{0:T(256)}, u32[]{:S(2)}) copy-start(f32[256]{0:T(256)} %get-tuple-element.44) | copy-start | bytes 3076
  18.2 10.9 %copy-start.5 = (f32[256]{0:T(256)S(1)}, f32[256]{0:T(256)}, u32[]{:S(2)}) copy-start(f32[256]{0:T(256)} %get-tuple-element.45) | copy-start | bytes 3076
  18.2 10.9 %copy-start.4 = (f32[256]{0:T(256)S(1)}, f32[256]{0:T(256)}, u32[]{:S(2)}) copy-start(f32[256]{0:T(256)} %get-tuple-element.46) | copy-start | bytes 3076
  18.2 11.0 %copy-start.3 = (f32[256]{0:T(256)S(1)}, f32[256]{0:T(256)}, u32[]{:S(2)}) copy-start(f32[256]{0:T(256)} %get-tuple-element.47) | copy-start | bytes 3076
  18.6 6.2 %collective-permute-start.3 = (f32[1,64,256]{2,1,0:T(8,128)S(1)}, f32[1,64,256]{2,1,0:T(8,128)S(1)}, u32[]{:S(2)}, u32[]{:S(2)}) collective-permute-start(f32[1,64,256]{2,1,0:T(8,128)S(1)} %get-tuple-element.84), channel_id=1, source_target_pairs={{0,8},{2,10},{4,12},{6,14},{8,0},{10,2},{12,4},{14,6},{1,9},{3,11}... | collective-permute-start | bytes 196616 | tf_op jit(solution)/shard_map/ppermute | solution.py:90
  21.5 4.3 %collective-permute-start.4 = (f32[1,64,256]{2,1,0:T(8,128)S(1)}, f32[1,64,256]{2,1,0:T(8,128)S(1)}, u32[]{:S(2)}, u32[]{:S(2)}) collective-permute-start(f32[1,64,256]{2,1,0:T(8,128)S(1)} %get-tuple-element.85), channel_id=1, source_target_pairs={{0,12},{2,14},{4,0},{6,2},{8,4},{10,6},{12,8},{14,10},{1,13},{3,15... | collective-permute-start | bytes 196616 | tf_op jit(solution)/shard_map/ppermute | solution.py:90
  22.9 6.1 %collective-permute-start.2 = (f32[1,64,256]{2,1,0:T(8,128)S(1)}, f32[1,64,256]{2,1,0:T(8,128)S(1)}, u32[]{:S(2)}, u32[]{:S(2)}) collective-permute-start(f32[1,64,256]{2,1,0:T(8,128)S(1)} %get-tuple-element.55), channel_id=1, source_target_pairs={{0,4},{2,6},{4,8},{6,10},{8,12},{10,14},{12,0},{14,2},{1,5},{3,7},... | collective-permute-start | bytes 196616 | tf_op jit(solution)/shard_map/ppermute | solution.py:90
  29.3 1.2 %copy-start.2 = (f32[256]{0:T(256)S(1)}, f32[256]{0:T(256)}, u32[]{:S(2)}) copy-start(f32[256]{0:T(256)} %get-tuple-element.108) | copy-start | bytes 3076
  30.6 3.6 %collective-permute-start.7 = (f32[256]{0:T(256)S(1)}, f32[256]{0:T(256)S(1)}, u32[]{:S(2)}, u32[]{:S(2)}) collective-permute-start(f32[256]{0:T(256)S(1)} %fusion.4), channel_id=1, source_target_pairs={{0,4},{2,6},{4,0},{6,2},{8,12},{10,14},{12,8},{14,10},{1,5},{3,7},... | collective-permute-start | bytes 3080 | tf_op jit(solution)/shard_map/ppermute | solution.py:111
  31.2 8.1 %collective-permute-start.6 = (bf16[4,1,64,256]{3,2,1,0:T(8,128)(2,1)S(1)}, bf16[4,1,64,256]{3,2,1,0:T(8,128)(2,1)S(1)}, u32[]{:S(2)}, u32[]{:S(2)}) collective-permute-start(bf16[4,1,64,256]{3,2,1,0:T(8,128)(2,1)S(1)} %bitcast.308), channel_id=1, source_target_pairs={{0,1},{1,0},{2,3},{3,2},{4,5},{5,4},{6,7},{7,6},{8,9},{9,8},{10,11... | collective-permute-start | bytes 393224 | tf_op jit(solution)/shard_map/ppermute | solution.py:81
  32.1 7.9 %collective-permute-start.5 = (bf16[4,1,64,256]{3,2,1,0:T(8,128)(2,1)S(1)}, bf16[4,1,64,256]{3,2,1,0:T(8,128)(2,1)S(1)}, u32[]{:S(2)}, u32[]{:S(2)}) collective-permute-start(bf16[4,1,64,256]{3,2,1,0:T(8,128)(2,1)S(1)} %bitcast.309), channel_id=1, source_target_pairs={{0,1},{1,0},{2,3},{3,2},{4,5},{5,4},{6,7},{7,6},{8,9},{9,8},{10,11... | collective-permute-start | bytes 393224 | tf_op jit(solution)/shard_map/ppermute | solution.py:81
  34.3 4.5 %collective-permute-start.8 = (f32[256]{0:T(256)S(1)}, f32[256]{0:T(256)S(1)}, u32[]{:S(2)}, u32[]{:S(2)}) collective-permute-start(f32[256]{0:T(256)S(1)} %add.366), channel_id=1, source_target_pairs={{0,8},{2,10},{4,12},{6,14},{8,0},{10,2},{12,4},{14,6},{1,9},{3,11}... | collective-permute-start | bytes 3080 | tf_op jit(solution)/shard_map/ppermute | solution.py:111

commit v14 on v9

--- a/solution.py
+++ b/solution.py
@@ -104,13 +104,12 @@
 def group_sum(value, axis, index, count, route):
     if count == 1:
         return value
-    if count & (count - 1):
-        return None
-    step = 1
-    while step < count:
-        value = value + lax.ppermute(value, axis, route(step))
-        step *= 2
-    return value
+    got = [value] + [lax.ppermute(value, axis, route(step)) for step in range(1, count)]
+    ordered = jnp.take(jnp.stack(got), (index - jnp.arange(count)) % count, axis=0)
+    total = ordered[0]
+    for position in range(1, count):
+        total = total + ordered[position]
+    return total
 
 
 def local(frames_in, in_kernel, out_kernel, decay_rate, frame_keep, out_grad):
@@ -201,7 +200,7 @@
     )
     total_count = frame_count * blocks * row_count * lax.axis_size("rows") * col_count
     partial = jnp.sum(terms, axis=(0, 1, 2))
-    summed = group_sum(partial, "tm", group, groups, lambda step: route(step, False))
+    summed = group_sum(partial, "tm", group, groups, route)
     if summed is None:
         summed = lax.psum(partial, "tm") / width
     grad_decay = all_sum(summed, "rows") / math.sqrt(total_count)

time: 40.9 us -> 40.5 us (level)
  starting transfers between devices: 10.4 us -> 13.3 us
  waiting for transfers between devices: 13.2 us -> 10.5 us
  other arithmetic: 6.98 us -> 5.91 us
  local copies, waits for them, and re-layouts: 3.47 us -> 3.99 us
    ppermute x2 -> x3, waiting for transfers between devices: 3.78 us -> 0.01 us  [group_sum(): lax.ppermute(value, axis, route(step))]
    ppermute x2 -> x3, starting transfers between devices: 1.93 us -> 4.8 us  [group_sum(): lax.ppermute(value, axis, route(step))]
    ppermute x1, waiting for transfers between devices: 2.18 us -> 3.27 us  [local(): got = lax.ppermute(jnp.where(first, frames_in, out_grad), 'tm', swap)]
    mul x1, other arithmetic: 0.61 us -> 0.01 us  [local(): product = decays_next[t] if product is None else product * decays_next[t]]
    div x1, other arithmetic: 0.58 us -> 0.01 us  [local(): decay_rate * decay_rate / input_gain * values]
    gather x0 -> x1, local copies, waits for them, and re-layouts: none -> 0.56 us  [group_sum(): jnp.take(jnp.stack(got), (index - jnp.arange(count)) % count, axis=0)]
  transfers between devices with their start and end apart: 9 -> 10, of which waited for: 7 -> 5; matrix products, arithmetic and copies ran while one was open for 18% -> 19% of each run, Pallas kernels for 0% -> 0%
where the time goes in v14:
time: 40.5 us; the launch traced here: 40.3 us
  starting transfers between devices  13.3 us (33%)
  waiting for transfers between devices  10.5 us (26%)
  other arithmetic  5.91 us (15%)
  matrix products  5.43 us (13%)
  local copies, waits for them, and re-layouts  3.99 us (10%)
  between operations  1.17 us (3%)
    dot_general x24, matrix products, conv_apply(): jnp.dot(portion.reshape(-1, channels), taps[index, col_tap], preferred_el...  5.43 us
    ppermute x3, waiting for transfers between devices, cyclic_carries(): received[step] = lax.ppermute(message, axis, route(step))  5.37 us
    ppermute x3, starting transfers between devices, cyclic_carries(): received[step] = lax.ppermute(message, axis, route(step))  4.93 us
    ppermute x3, starting transfers between devices, group_sum(): lax.ppermute(value, axis, route(step))  4.8 us
    ppermute x1, waiting for transfers between devices, local(): got = lax.ppermute(jnp.where(first, frames_in, out_grad), 'tm', swap)  3.27 us
    ppermute x1, starting transfers between devices, local(): got = lax.ppermute(jnp.where(first, frames_in, out_grad), 'tm', swap)  2.94 us
    ppermute x1, waiting for transfers between devices, local(): traded = lax.ppermute(got, 'chan', [(0, 1), (1, 0)])  1.85 us
    select_n x1, other arithmetic, local(): got = lax.ppermute(jnp.where(first, frames_in, out_grad), 'tm', swap)  1.68 us
  transfers between devices with their start and end apart: 10, of which 5 were waited for; matrix products, arithmetic and copies ran while one was open for 19% of the time, Pallas kernels for 0%

profile of v14, /device:TPU:0, one launch (start us, length us, event | category | flops | bytes accessed | tf_op | source)
XLA Modules:
  0.0 40.3 jit_solution(17293860808619626047)
XLA Ops:
  0.6 1.7 %broadcast_select_fusion.2 = bf16[4,1,64,512]{3,2,1,0:T(8,128)(2,1)} fusion(bf16[4,1,64,512]{3,2,1,0:T(8,128)(2,1)} %param.6, bf16[4,1,64,512]{3,2,1,0:T(8,128)(2,1)} %param.11, pred[]{:T(512)S(6)} %eq.11), kind=kLoop, calls=%fused_computation.51 | loop fusion | flops 131072 | bytes 786433 | tf_op jit(solution)/shard_map/jit(_where)/select_n | solution.py:127
  2.3 2.9 %collective-permute-start = (bf16[4,1,64,512]{3,2,1,0:T(8,128)(2,1)}, bf16[4,1,64,512]{3,2,1,0:T(8,128)(2,1)}, u32[]{:S(2)}, u32[]{:S(2)}) collective-permute-start(bf16[4,1,64,512]{3,2,1,0:T(8,128)(2,1)} %broadcast_select_fusion.2), channel_id=1, source_target_pairs={{0,2},{2,0},{4,6},{6,4},{8,10},{10,8},{12,14},{14,12},{1,3},{3,1},... | collective-permute-start | bytes 786440 | tf_op jit(solution)/shard_map/ppermute | solution.py:127
  5.3 1.2 %slice.332 = bf16[1,3,512,256]{3,2,1,0:T(8,128)(2,1)S(1)} slice(bf16[3,3,512,256]{3,2,1,0:T(8,128)(2,1)} %param.7), slice={[1:2], [0:3], [0:512], [0:256]} | slice | bytes 1572864 | tf_op jit(solution)/shard_map/slice | solution.py:31
  6.5 1.2 %slice.352 = bf16[1,3,256,512]{3,2,1,0:T(8,128)(2,1)S(1)} slice(bf16[3,3,256,512]{3,2,1,0:T(8,128)(2,1)} %param.8), slice={[1:2], [0:3], [0:256], [0:512]} | slice | bytes 1572864 | tf_op jit(solution)/shard_map/slice | solution.py:28
  8.6 3.3 %collective-permute-done = bf16[4,1,64,512]{3,2,1,0:T(8,128)(2,1)} collective-permute-done((bf16[4,1,64,512]{3,2,1,0:T(8,128)(2,1)}, bf16[4,1,64,512]{3,2,1,0:T(8,128)(2,1)}, u32[]{:S(2)}, u32[]{:S(2)}) %collective-permute-start) | collective-permute-done | bytes 262176 | tf_op jit(solution)/shard_map/ppermute | solution.py:127
  11.9 1.9 %collective-permute-done.1 = bf16[4,1,64,512]{3,2,1,0:T(8,128)(2,1)} collective-permute-done((bf16[4,1,64,512]{3,2,1,0:T(8,128)(2,1)}, bf16[4,1,64,512]{3,2,1,0:T(8,128)(2,1)}, u32[]{:S(2)}, u32[]{:S(2)}) %collective-permute-start.1) | collective-permute-done | bytes 262176 | tf_op jit(solution)/shard_map/ppermute | solution.py:128
  13.8 1.2 %broadcast_select_fusion.6 = (bf16[4,1,64,512]{3,2,1,0:T(8,128)(2,1)S(1)}, bf16[4,1,64,512]{3,2,1,0:T(8,128)(2,1)S(1)}, bf16[4,1,64,512]{3,2,1,0:T(8,128)(2,1)S(1)}, bf16[4,1,64,512]{3,2,1,0:T(8,128)(2,1)S(1)}) fusion(bf16[4,1,64,512]{3,2,1,0:T(8,128)(2,1)S(1)} %copy-done, pred[]{:T(512)S(6)} %eq.10, bf16[4,1,64,512]{3,2,1,0:T(8,128)(2,1)} %collective-permute-done, ...), kind=kLoop, calls=%fused_computation.55 | loop fusion | flops 786432 | bytes 2097154 | tf_op jit(solution)/shard_map/jit(_where)/select_n | solution.py:134
  17.3 0.3 convolution_add_fusion.9
  17.6 0.3 convolution_add_fusion.8
  17.9 0.3 convolution_add_fusion.11
  18.1 0.3 convolution_add_fusion.10
  18.5 2.9 %collective-permute-start.3 = (f32[1,64,256]{2,1,0:T(8,128)S(1)}, f32[1,64,256]{2,1,0:T(8,128)S(1)}, u32[]{:S(2)}, u32[]{:S(2)}) collective-permute-start(f32[1,64,256]{2,1,0:T(8,128)S(1)} %get-tuple-element.79), channel_id=1, source_target_pairs={{0,8},{2,10},{4,12},{6,14},{8,0},{10,2},{12,4},{14,6},{1,9},{3,11}... | collective-permute-start | bytes 196616 | tf_op jit(solution)/shard_map/ppermute | solution.py:90
  21.5 1.3 %collective-permute-start.4 = (f32[1,64,256]{2,1,0:T(8,128)S(1)}, f32[1,64,256]{2,1,0:T(8,128)S(1)}, u32[]{:S(2)}, u32[]{:S(2)}) collective-permute-start(f32[1,64,256]{2,1,0:T(8,128)S(1)} %get-tuple-element.80), channel_id=1, source_target_pairs={{0,12},{2,14},{4,0},{6,2},{8,4},{10,6},{12,8},{14,10},{1,13},{3,15... | collective-permute-start | bytes 196616 | tf_op jit(solution)/shard_map/ppermute | solution.py:90
  22.8 0.7 %collective-permute-start.2 = (f32[1,64,256]{2,1,0:T(8,128)S(1)}, f32[1,64,256]{2,1,0:T(8,128)S(1)}, u32[]{:S(2)}, u32[]{:S(2)}) collective-permute-start(f32[1,64,256]{2,1,0:T(8,128)S(1)} %get-tuple-element.50), channel_id=1, source_target_pairs={{0,4},{2,6},{4,8},{6,10},{8,12},{10,14},{12,0},{14,2},{1,5},{3,7},... | collective-permute-start | bytes 196616 | tf_op jit(solution)/shard_map/ppermute | solution.py:90
  23.5 1.3 %collective-permute-done.3 = f32[1,64,256]{2,1,0:T(8,128)S(1)} collective-permute-done((f32[1,64,256]{2,1,0:T(8,128)S(1)}, f32[1,64,256]{2,1,0:T(8,128)S(1)}, u32[]{:S(2)}, u32[]{:S(2)}) %collective-permute-start.3) | collective-permute-done | bytes 65568 | tf_op jit(solution)/shard_map/ppermute | solution.py:90
  24.8 0.9 %collective-permute-done.4 = f32[1,64,256]{2,1,0:T(8,128)S(1)} collective-permute-done((f32[1,64,256]{2,1,0:T(8,128)S(1)}, f32[1,64,256]{2,1,0:T(8,128)S(1)}, u32[]{:S(2)}, u32[]{:S(2)}) %collective-permute-start.4) | collective-permute-done | bytes 65568 | tf_op jit(solution)/shard_map/ppermute | solution.py:90
  25.7 3.1 %collective-permute-done.2 = f32[1,64,256]{2,1,0:T(8,128)S(1)} collective-permute-done((f32[1,64,256]{2,1,0:T(8,128)S(1)}, f32[1,64,256]{2,1,0:T(8,128)S(1)}, u32[]{:S(2)}, u32[]{:S(2)}) %collective-permute-start.2) | collective-permute-done | bytes 65568 | tf_op jit(solution)/shard_map/ppermute | solution.py:90
  29.5 2.3 %collective-permute-start.8 = (f32[256]{0:T(256)S(1)}, f32[256]{0:T(256)S(1)}, u32[]{:S(2)}, u32[]{:S(2)}) collective-permute-start(f32[256]{0:T(256)S(1)} %fusion.4), channel_id=1, source_target_pairs={{0,8},{2,10},{4,12},{6,14},{8,0},{10,2},{12,4},{14,6},{1,9},{3,11}... | collective-permute-start | bytes 3080 | tf_op jit(solution)/shard_map/ppermute | solution.py:107
  31.8 2.4 %collective-permute-start.9 = (f32[256]{0:T(256)S(1)}, f32[256]{0:T(256)S(1)}, u32[]{:S(2)}, u32[]{:S(2)}) collective-permute-start(f32[256]{0:T(256)S(1)} %fusion.4), channel_id=1, source_target_pairs={{0,12},{2,14},{4,0},{6,2},{8,4},{10,6},{12,8},{14,10},{1,13},{3,15... | collective-permute-start | bytes 3080 | tf_op jit(solution)/shard_map/ppermute | solution.py:107
  36.7 0.6 %collective-permute-start.5 = (bf16[4,1,64,256]{3,2,1,0:T(8,128)(2,1)S(1)}, bf16[4,1,64,256]{3,2,1,0:T(8,128)(2,1)S(1)}, u32[]{:S(2)}, u32[]{:S(2)}) collective-permute-start(bf16[4,1,64,256]{3,2,1,0:T(8,128)(2,1)S(1)} %bitcast.316), channel_id=1, source_target_pairs={{0,1},{1,0},{2,3},{3,2},{4,5},{5,4},{6,7},{7,6},{8,9},{9,8},{10,11... | collective-permute-start | bytes 393224 | tf_op jit(solution)/shard_map/ppermute | solution.py:81
  37.7 0.6 %gather_fusion = f32[4,256]{1,0:T(4,128)S(1)} fusion(f32[4,256]{1,0:T(4,128)S(1)} %pad_maximum_fusion, s32[1024]{0:T(1024)S(1)} %pad_clamp_fusion), kind=kCustom, calls=%fused_computation | custom fusion | bytes 8208 | tf_op jit(solution)/shard_map/jit(_take)/gather | solution.py:108
  38.4 0.6 %fusion.52 = f32[1,256]{1,0:T(1,128)} fusion(f32[4,256]{1,0:T(4,128)S(1)} %broadcast_select_fusion.7), kind=kLoop, calls=%fused_computation.202 | loop fusion | flops 1024 | bytes 5120 | tf_op jit(solution)/shard_map/div | solution.py:206
  38.9 0.7 %add_convert_fusion = bf16[4,1,64,256]{3,2,1,0:T(8,128)(2,1)} fusion(f32[4,1,64,256]{3,2,1,0:T(8,128)S(1)} %bitcast.305, bf16[4,1,64,256]{3,2,1,0:T(8,128)(2,1)S(1)} %collective-permute-done.6), kind=kLoop, calls=%fused_computation.47 | loop fusion | flops 196608 | bytes 524288 | tf_op jit(solution)/shard_map/convert_element_type | solution.py:83
  39.6 0.7 %add_convert_fusion.1 = bf16[4,1,64,256]{3,2,1,0:T(8,128)(2,1)} fusion(f32[4,1,64,256]{3,2,1,0:T(8,128)S(1)} %bitcast.306, bf16[4,1,64,256]{3,2,1,0:T(8,128)(2,1)S(1)} %collective-permute-done.5), kind=kLoop, calls=%fused_computation.48 | loop fusion | flops 196608 | bytes 524288 | tf_op jit(solution)/shard_map/convert_element_type | solution.py:83
  (80 shorter events, 6.6 us)
Async XLA Ops:
  2.3 9.6 %collective-permute-start = (bf16[4,1,64,512]{3,2,1,0:T(8,128)(2,1)}, bf16[4,1,64,512]{3,2,1,0:T(8,128)(2,1)}, u32[]{:S(2)}, u32[]{:S(2)}) collective-permute-start(bf16[4,1,64,512]{3,2,1,0:T(8,128)(2,1)} %broadcast_select_fusion.2), channel_id=1, source_target_pairs={{0,2},{2,0},{4,6},{6,4},{8,10},{10,8},{12,14},{14,12},{1,3},{3,1},... | collective-permute-start | bytes 786440 | tf_op jit(solution)/shard_map/ppermute | solution.py:127
  5.3 2.5 %copy-start.2 = (f32[32]{0:T(128)S(1)}, f32[32]{0:T(128)}, u32[]{:S(2)}) copy-start(f32[32]{0:T(128)} %param.10) | copy-start | bytes 388
  5.3 2.7 %copy-start.1 = (f32[256]{0:T(256)S(1)}, f32[256]{0:T(256)}, u32[]{:S(2)}) copy-start(f32[256]{0:T(256)} %param.9) | copy-start | bytes 3076
  6.5 7.3 %copy-start = (bf16[4,1,64,512]{3,2,1,0:T(8,128)(2,1)S(1)}, bf16[4,1,64,512]{3,2,1,0:T(8,128)(2,1)}, u32[]{:S(2)}) copy-start(bf16[4,1,64,512]{3,2,1,0:T(8,128)(2,1)} %param.6) | copy-start | bytes 786436
  11.9 1.9 %collective-permute-start.1 = (bf16[4,1,64,512]{3,2,1,0:T(8,128)(2,1)}, bf16[4,1,64,512]{3,2,1,0:T(8,128)(2,1)}, u32[]{:S(2)}, u32[]{:S(2)}) collective-permute-start(bf16[4,1,64,512]{3,2,1,0:T(8,128)(2,1)} %collective-permute-done), channel_id=1, source_target_pairs={{0,1},{1,0},{2,3},{3,2},{4,5},{5,4},{6,7},{7,6},{8,9},{9,8},{10,11... | collective-permute-start | bytes 786440 | tf_op jit(solution)/shard_map/ppermute | solution.py:128
  18.5 6.2 %collective-permute-start.3 = (f32[1,64,256]{2,1,0:T(8,128)S(1)}, f32[1,64,256]{2,1,0:T(8,128)S(1)}, u32[]{:S(2)}, u32[]{:S(2)}) collective-permute-start(f32[1,64,256]{2,1,0:T(8,128)S(1)} %get-tuple-element.79), channel_id=1, source_target_pairs={{0,8},{2,10},{4,12},{6,14},{8,0},{10,2},{12,4},{14,6},{1,9},{3,11}... | collective-permute-start | bytes 196616 | tf_op jit(solution)/shard_map/ppermute | solution.py:90
  21.5 4.3 %collective-permute-start.4 = (f32[1,64,256]{2,1,0:T(8,128)S(1)}, f32[1,64,256]{2,1,0:T(8,128)S(1)}, u32[]{:S(2)}, u32[]{:S(2)}) collective-permute-start(f32[1,64,256]{2,1,0:T(8,128)S(1)} %get-tuple-element.80), channel_id=1, source_target_pairs={{0,12},{2,14},{4,0},{6,2},{8,4},{10,6},{12,8},{14,10},{1,13},{3,15... | collective-permute-start | bytes 196616 | tf_op jit(solution)/shard_map/ppermute | solution.py:90
  22.8 6.1 %collective-permute-start.2 = (f32[1,64,256]{2,1,0:T(8,128)S(1)}, f32[1,64,256]{2,1,0:T(8,128)S(1)}, u32[]{:S(2)}, u32[]{:S(2)}) collective-permute-start(f32[1,64,256]{2,1,0:T(8,128)S(1)} %get-tuple-element.50), channel_id=1, source_target_pairs={{0,4},{2,6},{4,8},{6,10},{8,12},{10,14},{12,0},{14,2},{1,5},{3,7},... | collective-permute-start | bytes 196616 | tf_op jit(solution)/shard_map/ppermute | solution.py:90
  29.4 8.3 %collective-permute-start.7 = (f32[256]{0:T(256)S(1)}, f32[256]{0:T(256)S(1)}, u32[]{:S(2)}, u32[]{:S(2)}) collective-permute-start(f32[256]{0:T(256)S(1)} %fusion.4), channel_id=1, source_target_pairs={{0,4},{2,6},{4,8},{6,10},{8,12},{10,14},{12,0},{14,2},{1,5},{3,7},... | collective-permute-start | bytes 3080 | tf_op jit(solution)/shard_map/ppermute | solution.py:107
  29.5 8.2 %collective-permute-start.8 = (f32[256]{0:T(256)S(1)}, f32[256]{0:T(256)S(1)}, u32[]{:S(2)}, u32[]{:S(2)}) collective-permute-start(f32[256]{0:T(256)S(1)} %fusion.4), channel_id=1, source_target_pairs={{0,8},{2,10},{4,12},{6,14},{8,0},{10,2},{12,4},{14,6},{1,9},{3,11}... | collective-permute-start | bytes 3080 | tf_op jit(solution)/shard_map/ppermute | solution.py:107
  31.8 5.9 %collective-permute-start.9 = (f32[256]{0:T(256)S(1)}, f32[256]{0:T(256)S(1)}, u32[]{:S(2)}, u32[]{:S(2)}) collective-permute-start(f32[256]{0:T(256)S(1)} %fusion.4), channel_id=1, source_target_pairs={{0,12},{2,14},{4,0},{6,2},{8,4},{10,6},{12,8},{14,10},{1,13},{3,15... | collective-permute-start | bytes 3080 | tf_op jit(solution)/shard_map/ppermute | solution.py:107
  35.8 3.2 %collective-permute-start.6 = (bf16[4,1,64,256]{3,2,1,0:T(8,128)(2,1)S(1)}, bf16[4,1,64,256]{3,2,1,0:T(8,128)(2,1)S(1)}, u32[]{:S(2)}, u32[]{:S(2)}) collective-permute-start(bf16[4,1,64,256]{3,2,1,0:T(8,128)(2,1)S(1)} %bitcast.315), channel_id=1, source_target_pairs={{0,1},{1,0},{2,3},{3,2},{4,5},{5,4},{6,7},{7,6},{8,9},{9,8},{10,11... | collective-permute-start | bytes 393224 | tf_op jit(solution)/shard_map/ppermute | solution.py:81
  36.7 2.9 %collective-permute-start.5 = (bf16[4,1,64,256]{3,2,1,0:T(8,128)(2,1)S(1)}, bf16[4,1,64,256]{3,2,1,0:T(8,128)(2,1)S(1)}, u32[]{:S(2)}, u32[]{:S(2)}) collective-permute-start(bf16[4,1,64,256]{3,2,1,0:T(8,128)(2,1)S(1)} %bitcast.316), channel_id=1, source_target_pairs={{0,1},{1,0},{2,3},{3,2},{4,5},{5,4},{6,7},{7,6},{8,9},{9,8},{10,11... | collective-permute-start | bytes 393224 | tf_op jit(solution)/shard_map/ppermute | solution.py:81

commit v15 on v10

--- a/solution.py
+++ b/solution.py
@@ -113,13 +113,12 @@
 def group_sum(value, axis, index, count, route):
     if count == 1:
         return value
-    if count & (count - 1):
-        return None
-    step = 1
-    while step < count:
-        value = value + lax.ppermute(value, axis, route(step))
-        step *= 2
-    return value
+    got = [value] + [lax.ppermute(value, axis, route(step)) for step in range(1, count)]
+    ordered = jnp.take(jnp.stack(got), (index - jnp.arange(count)) % count, axis=0)
+    total = ordered[0]
+    for position in range(1, count):
+        total = total + ordered[position]
+    return total
 
 
 def local(frames_in, in_kernel, out_kernel, decay_rate, frame_keep, out_grad):
@@ -210,7 +209,7 @@
     )
     total_count = frame_count * blocks * row_count * lax.axis_size("rows") * col_count
     partial = jnp.sum(terms, axis=(0, 1, 2))
-    summed = group_sum(partial, "tm", group, groups, lambda step: route(step, False))
+    summed = group_sum(partial, "tm", group, groups, route)
     if summed is None:
         summed = lax.psum(partial, "tm") / width
     grad_decay = all_sum(summed, "rows") / math.sqrt(total_count)

time: 40.9 us -> 40 us (0.978)
  waiting for transfers between devices: 13.8 us -> 10.5 us
  starting transfers between devices: 9.82 us -> 12.7 us
  other arithmetic: 6.99 us -> 5.92 us
  local copies, waits for them, and re-layouts: 3.47 us -> 3.99 us
    ppermute x2 -> x3, waiting for transfers between devices: 4.34 us -> 0.01 us  [group_sum(): lax.ppermute(value, axis, route(step))]
    ppermute x2 -> x3, starting transfers between devices: 1.88 us -> 4.79 us  [group_sum(): lax.ppermute(value, axis, route(step))]
    ppermute x1, waiting for transfers between devices: 2.19 us -> 3.27 us  [local(): got = lax.ppermute(jnp.where(first, frames_in, out_grad), 'tm', swap)]
    mul x1, other arithmetic: 0.6 us -> 0.01 us  [local(): product = decays_next[t] if product is None else product * decays_next[t]]
    div x1, other arithmetic: 0.58 us -> 0.01 us  [local(): decay_rate * decay_rate / input_gain * values]
    gather x0 -> x1, local copies, waits for them, and re-layouts: none -> 0.56 us  [group_sum(): jnp.take(jnp.stack(got), (index - jnp.arange(count)) % count, axis=0)]
  transfers between devices with their start and end apart: 8 -> 9, of which waited for: 7 -> 5; matrix products, arithmetic and copies ran while one was open for 16% -> 18% of each run, Pallas kernels for 0% -> 0%
where the time goes in v15:
time: 40 us; the launch traced here: 39.8 us
  starting transfers between devices  12.7 us (32%)
  waiting for transfers between devices  10.5 us (26%)
  other arithmetic  5.92 us (15%)
  matrix products  5.45 us (14%)
  local copies, waits for them, and re-layouts  3.99 us (10%)
  between operations  1.18 us (3%)
    dot_general x24, matrix products, conv_apply(): jnp.dot(portion.reshape(-1, channels), taps[index, col_tap], preferred_el...  5.45 us
    ppermute x3, waiting for transfers between devices, cyclic_carries(): received[step] = lax.ppermute(message, axis, route(step))  5.37 us
    ppermute x3, starting transfers between devices, cyclic_carries(): received[step] = lax.ppermute(message, axis, route(step))  4.93 us
    ppermute x3, starting transfers between devices, group_sum(): lax.ppermute(value, axis, route(step))  4.79 us
    ppermute x1, waiting for transfers between devices, local(): got = lax.ppermute(jnp.where(first, frames_in, out_grad), 'tm', swap)  3.27 us
    ppermute x1, starting transfers between devices, local(): got = lax.ppermute(jnp.where(first, frames_in, out_grad), 'tm', swap)  2.94 us
    ppermute x1, waiting for transfers between devices, local(): traded = lax.ppermute(got, 'chan', [(0, 1), (1, 0)])  1.85 us
    select_n x1, other arithmetic, local(): got = lax.ppermute(jnp.where(first, frames_in, out_grad), 'tm', swap)  1.68 us
  transfers between devices with their start and end apart: 9, of which 5 were waited for; matrix products, arithmetic and copies ran while one was open for 18% of the time, Pallas kernels for 0%

profile of v15, /device:TPU:0, one launch (start us, length us, event | category | flops | bytes accessed | tf_op | source)
XLA Modules:
  0.0 39.8 jit_solution(15060677868261565396)
XLA Ops:
  0.6 1.7 %broadcast_select_fusion.2 = bf16[4,1,64,512]{3,2,1,0:T(8,128)(2,1)} fusion(bf16[4,1,64,512]{3,2,1,0:T(8,128)(2,1)} %param.6, bf16[4,1,64,512]{3,2,1,0:T(8,128)(2,1)} %param.11, pred[]{:T(512)S(6)} %eq.11), kind=kLoop, calls=%fused_computation.54 | loop fusion | flops 131072 | bytes 786433 | tf_op jit(solution)/shard_map/jit(_where)/select_n | solution.py:136
  2.3 2.9 %collective-permute-start = (bf16[4,1,64,512]{3,2,1,0:T(8,128)(2,1)}, bf16[4,1,64,512]{3,2,1,0:T(8,128)(2,1)}, u32[]{:S(2)}, u32[]{:S(2)}) collective-permute-start(bf16[4,1,64,512]{3,2,1,0:T(8,128)(2,1)} %broadcast_select_fusion.2), channel_id=1, source_target_pairs={{0,2},{2,0},{4,6},{6,4},{8,10},{10,8},{12,14},{14,12},{1,3},{3,1},... | collective-permute-start | bytes 786440 | tf_op jit(solution)/shard_map/ppermute | solution.py:136
  5.3 1.2 %slice.338 = bf16[1,3,512,256]{3,2,1,0:T(8,128)(2,1)S(1)} slice(bf16[3,3,512,256]{3,2,1,0:T(8,128)(2,1)} %param.7), slice={[1:2], [0:3], [0:512], [0:256]} | slice | bytes 1572864 | tf_op jit(solution)/shard_map/slice | solution.py:31
  6.5 1.2 %slice.358 = bf16[1,3,256,512]{3,2,1,0:T(8,128)(2,1)S(1)} slice(bf16[3,3,256,512]{3,2,1,0:T(8,128)(2,1)} %param.8), slice={[1:2], [0:3], [0:256], [0:512]} | slice | bytes 1572864 | tf_op jit(solution)/shard_map/slice | solution.py:28
  8.6 3.3 %collective-permute-done = bf16[4,1,64,512]{3,2,1,0:T(8,128)(2,1)} collective-permute-done((bf16[4,1,64,512]{3,2,1,0:T(8,128)(2,1)}, bf16[4,1,64,512]{3,2,1,0:T(8,128)(2,1)}, u32[]{:S(2)}, u32[]{:S(2)}) %collective-permute-start) | collective-permute-done | bytes 262176 | tf_op jit(solution)/shard_map/ppermute | solution.py:136
  11.9 1.9 %collective-permute-done.1 = bf16[4,1,64,512]{3,2,1,0:T(8,128)(2,1)} collective-permute-done((bf16[4,1,64,512]{3,2,1,0:T(8,128)(2,1)}, bf16[4,1,64,512]{3,2,1,0:T(8,128)(2,1)}, u32[]{:S(2)}, u32[]{:S(2)}) %collective-permute-start.1) | collective-permute-done | bytes 262176 | tf_op jit(solution)/shard_map/ppermute | solution.py:137
  13.8 1.2 %broadcast_select_fusion.6 = (bf16[4,1,64,512]{3,2,1,0:T(8,128)(2,1)S(1)}, bf16[4,1,64,512]{3,2,1,0:T(8,128)(2,1)S(1)}, bf16[4,1,64,512]{3,2,1,0:T(8,128)(2,1)S(1)}, bf16[4,1,64,512]{3,2,1,0:T(8,128)(2,1)S(1)}) fusion(bf16[4,1,64,512]{3,2,1,0:T(8,128)(2,1)S(1)} %copy-done, pred[]{:T(512)S(6)} %eq.10, bf16[4,1,64,512]{3,2,1,0:T(8,128)(2,1)} %collective-permute-done, ...), kind=kLoop, calls=%fused_computation.58 | loop fusion | flops 786432 | bytes 2097154 | tf_op jit(solution)/shard_map/jit(_where)/select_n | solution.py:143
  15.9 0.3 fusion.11
  17.3 0.3 convolution_add_fusion.9
  17.6 0.3 convolution_add_fusion.8
  17.9 0.3 convolution_add_fusion.11
  18.1 0.3 convolution_add_fusion.10
  18.5 2.9 %collective-permute-start.3 = (f32[1,64,256]{2,1,0:T(8,128)S(1)}, f32[1,64,256]{2,1,0:T(8,128)S(1)}, u32[]{:S(2)}, u32[]{:S(2)}) collective-permute-start(f32[1,64,256]{2,1,0:T(8,128)S(1)} %get-tuple-element.82), channel_id=1, source_target_pairs={{0,8},{2,10},{4,12},{6,14},{8,0},{10,2},{12,4},{14,6},{1,9},{3,11}... | collective-permute-start | bytes 196616 | tf_op jit(solution)/shard_map/ppermute | solution.py:99
  21.5 1.3 %collective-permute-start.4 = (f32[1,64,256]{2,1,0:T(8,128)S(1)}, f32[1,64,256]{2,1,0:T(8,128)S(1)}, u32[]{:S(2)}, u32[]{:S(2)}) collective-permute-start(f32[1,64,256]{2,1,0:T(8,128)S(1)} %get-tuple-element.83), channel_id=1, source_target_pairs={{0,12},{2,14},{4,0},{6,2},{8,4},{10,6},{12,8},{14,10},{1,13},{3,15... | collective-permute-start | bytes 196616 | tf_op jit(solution)/shard_map/ppermute | solution.py:99
  22.8 0.7 %collective-permute-start.2 = (f32[1,64,256]{2,1,0:T(8,128)S(1)}, f32[1,64,256]{2,1,0:T(8,128)S(1)}, u32[]{:S(2)}, u32[]{:S(2)}) collective-permute-start(f32[1,64,256]{2,1,0:T(8,128)S(1)} %get-tuple-element.53), channel_id=1, source_target_pairs={{0,4},{2,6},{4,8},{6,10},{8,12},{10,14},{12,0},{14,2},{1,5},{3,7},... | collective-permute-start | bytes 196616 | tf_op jit(solution)/shard_map/ppermute | solution.py:99
  23.5 1.3 %collective-permute-done.3 = f32[1,64,256]{2,1,0:T(8,128)S(1)} collective-permute-done((f32[1,64,256]{2,1,0:T(8,128)S(1)}, f32[1,64,256]{2,1,0:T(8,128)S(1)}, u32[]{:S(2)}, u32[]{:S(2)}) %collective-permute-start.3) | collective-permute-done | bytes 65568 | tf_op jit(solution)/shard_map/ppermute | solution.py:99
  24.8 0.9 %collective-permute-done.4 = f32[1,64,256]{2,1,0:T(8,128)S(1)} collective-permute-done((f32[1,64,256]{2,1,0:T(8,128)S(1)}, f32[1,64,256]{2,1,0:T(8,128)S(1)}, u32[]{:S(2)}, u32[]{:S(2)}) %collective-permute-start.4) | collective-permute-done | bytes 65568 | tf_op jit(solution)/shard_map/ppermute | solution.py:99
  25.7 3.1 %collective-permute-done.2 = f32[1,64,256]{2,1,0:T(8,128)S(1)} collective-permute-done((f32[1,64,256]{2,1,0:T(8,128)S(1)}, f32[1,64,256]{2,1,0:T(8,128)S(1)}, u32[]{:S(2)}, u32[]{:S(2)}) %collective-permute-start.2) | collective-permute-done | bytes 65568 | tf_op jit(solution)/shard_map/ppermute | solution.py:99
  29.5 2.3 %collective-permute-start.7 = (f32[256]{0:T(256)S(1)}, f32[256]{0:T(256)S(1)}, u32[]{:S(2)}, u32[]{:S(2)}) collective-permute-start(f32[256]{0:T(256)S(1)} %fusion.4), channel_id=1, source_target_pairs={{0,8},{2,10},{4,12},{6,14},{8,0},{10,2},{12,4},{14,6},{1,9},{3,11}... | collective-permute-start | bytes 3080 | tf_op jit(solution)/shard_map/ppermute | solution.py:116
  31.8 2.4 %collective-permute-start.8 = (f32[256]{0:T(256)S(1)}, f32[256]{0:T(256)S(1)}, u32[]{:S(2)}, u32[]{:S(2)}) collective-permute-start(f32[256]{0:T(256)S(1)} %fusion.4), channel_id=1, source_target_pairs={{0,12},{2,14},{4,0},{6,2},{8,4},{10,6},{12,8},{14,10},{1,13},{3,15... | collective-permute-start | bytes 3080 | tf_op jit(solution)/shard_map/ppermute | solution.py:116
  37.2 0.6 %gather_fusion = f32[4,256]{1,0:T(4,128)S(1)} fusion(f32[4,256]{1,0:T(4,128)S(1)} %pad_maximum_fusion.1, s32[1024]{0:T(1024)S(1)} %pad_clamp_fusion), kind=kCustom, calls=%fused_computation | custom fusion | bytes 8208 | tf_op jit(solution)/shard_map/jit(_take)/gather | solution.py:117
  37.8 0.6 %fusion.55 = f32[1,256]{1,0:T(1,128)} fusion(f32[4,256]{1,0:T(4,128)S(1)} %broadcast_select_fusion.7), kind=kLoop, calls=%fused_computation.208 | loop fusion | flops 1024 | bytes 5120 | tf_op jit(solution)/shard_map/div | solution.py:215
  38.4 0.7 %fusion.7 = bf16[4,1,64,256]{3,2,1,0:T(8,128)(2,1)} fusion(f32[4,1,64,256]{3,2,1,0:T(8,128)S(1)} %bitcast.311, bf16[2,4,1,64,256]{4,3,1,2,0:T(8,128)(2,1)S(1)} %collective-permute-done.5), kind=kLoop, calls=%fused_computation.49 | loop fusion | flops 196608 | bytes 524288 | tf_op jit(solution)/shard_map/convert_element_type | solution.py:91
  39.1 0.7 %fusion.13 = bf16[4,1,64,256]{3,2,1,0:T(8,128)(2,1)} fusion(f32[4,1,64,256]{3,2,0,1:T(8,128)S(1)} %bitcast.312, bf16[2,4,1,64,256]{4,3,1,2,0:T(8,128)(2,1)S(1)} %collective-permute-done.5), kind=kLoop, calls=%fused_computation.63 | loop fusion | flops 196608 | bytes 524288
  (79 shorter events, 6.4 us)
Async XLA Ops:
  2.3 9.6 %collective-permute-start = (bf16[4,1,64,512]{3,2,1,0:T(8,128)(2,1)}, bf16[4,1,64,512]{3,2,1,0:T(8,128)(2,1)}, u32[]{:S(2)}, u32[]{:S(2)}) collective-permute-start(bf16[4,1,64,512]{3,2,1,0:T(8,128)(2,1)} %broadcast_select_fusion.2), channel_id=1, source_target_pairs={{0,2},{2,0},{4,6},{6,4},{8,10},{10,8},{12,14},{14,12},{1,3},{3,1},... | collective-permute-start | bytes 786440 | tf_op jit(solution)/shard_map/ppermute | solution.py:136
  5.3 2.5 %copy-start.2 = (f32[32]{0:T(128)S(1)}, f32[32]{0:T(128)}, u32[]{:S(2)}) copy-start(f32[32]{0:T(128)} %param.10) | copy-start | bytes 388
  5.3 2.7 %copy-start.1 = (f32[256]{0:T(256)S(1)}, f32[256]{0:T(256)}, u32[]{:S(2)}) copy-start(f32[256]{0:T(256)} %param.9) | copy-start | bytes 3076
  6.5 7.3 %copy-start = (bf16[4,1,64,512]{3,2,1,0:T(8,128)(2,1)S(1)}, bf16[4,1,64,512]{3,2,1,0:T(8,128)(2,1)}, u32[]{:S(2)}) copy-start(bf16[4,1,64,512]{3,2,1,0:T(8,128)(2,1)} %param.6) | copy-start | bytes 786436
  11.9 1.9 %collective-permute-start.1 = (bf16[4,1,64,512]{3,2,1,0:T(8,128)(2,1)}, bf16[4,1,64,512]{3,2,1,0:T(8,128)(2,1)}, u32[]{:S(2)}, u32[]{:S(2)}) collective-permute-start(bf16[4,1,64,512]{3,2,1,0:T(8,128)(2,1)} %collective-permute-done), channel_id=1, source_target_pairs={{0,1},{1,0},{2,3},{3,2},{4,5},{5,4},{6,7},{7,6},{8,9},{9,8},{10,11... | collective-permute-start | bytes 786440 | tf_op jit(solution)/shard_map/ppermute | solution.py:137
  18.5 6.2 %collective-permute-start.3 = (f32[1,64,256]{2,1,0:T(8,128)S(1)}, f32[1,64,256]{2,1,0:T(8,128)S(1)}, u32[]{:S(2)}, u32[]{:S(2)}) collective-permute-start(f32[1,64,256]{2,1,0:T(8,128)S(1)} %get-tuple-element.82), channel_id=1, source_target_pairs={{0,8},{2,10},{4,12},{6,14},{8,0},{10,2},{12,4},{14,6},{1,9},{3,11}... | collective-permute-start | bytes 196616 | tf_op jit(solution)/shard_map/ppermute | solution.py:99
  21.5 4.3 %collective-permute-start.4 = (f32[1,64,256]{2,1,0:T(8,128)S(1)}, f32[1,64,256]{2,1,0:T(8,128)S(1)}, u32[]{:S(2)}, u32[]{:S(2)}) collective-permute-start(f32[1,64,256]{2,1,0:T(8,128)S(1)} %get-tuple-element.83), channel_id=1, source_target_pairs={{0,12},{2,14},{4,0},{6,2},{8,4},{10,6},{12,8},{14,10},{1,13},{3,15... | collective-permute-start | bytes 196616 | tf_op jit(solution)/shard_map/ppermute | solution.py:99
  22.8 6.1 %collective-permute-start.2 = (f32[1,64,256]{2,1,0:T(8,128)S(1)}, f32[1,64,256]{2,1,0:T(8,128)S(1)}, u32[]{:S(2)}, u32[]{:S(2)}) collective-permute-start(f32[1,64,256]{2,1,0:T(8,128)S(1)} %get-tuple-element.53), channel_id=1, source_target_pairs={{0,4},{2,6},{4,8},{6,10},{8,12},{10,14},{12,0},{14,2},{1,5},{3,7},... | collective-permute-start | bytes 196616 | tf_op jit(solution)/shard_map/ppermute | solution.py:99
  29.4 7.8 %collective-permute-start.6 = (f32[256]{0:T(256)S(1)}, f32[256]{0:T(256)S(1)}, u32[]{:S(2)}, u32[]{:S(2)}) collective-permute-start(f32[256]{0:T(256)S(1)} %fusion.4), channel_id=1, source_target_pairs={{0,4},{2,6},{4,8},{6,10},{8,12},{10,14},{12,0},{14,2},{1,5},{3,7},... | collective-permute-start | bytes 3080 | tf_op jit(solution)/shard_map/ppermute | solution.py:116
  29.5 7.7 %collective-permute-start.7 = (f32[256]{0:T(256)S(1)}, f32[256]{0:T(256)S(1)}, u32[]{:S(2)}, u32[]{:S(2)}) collective-permute-start(f32[256]{0:T(256)S(1)} %fusion.4), channel_id=1, source_target_pairs={{0,8},{2,10},{4,12},{6,14},{8,0},{10,2},{12,4},{14,6},{1,9},{3,11}... | collective-permute-start | bytes 3080 | tf_op jit(solution)/shard_map/ppermute | solution.py:116
  31.8 5.4 %collective-permute-start.8 = (f32[256]{0:T(256)S(1)}, f32[256]{0:T(256)S(1)}, u32[]{:S(2)}, u32[]{:S(2)}) collective-permute-start(f32[256]{0:T(256)S(1)} %fusion.4), channel_id=1, source_target_pairs={{0,12},{2,14},{4,0},{6,2},{8,4},{10,6},{12,8},{14,10},{1,13},{3,15... | collective-permute-start | bytes 3080 | tf_op jit(solution)/shard_map/ppermute | solution.py:116
  36.7 1.8 %collective-permute-start.5 = (bf16[2,4,1,64,256]{4,3,1,2,0:T(8,128)(2,1)S(1)}, bf16[2,4,1,64,256]{4,3,1,2,0:T(8,128)(2,1)S(1)}, u32[]{:S(2)}, u32[]{:S(2)}) collective-permute-start(bf16[2,4,1,64,256]{4,3,1,2,0:T(8,128)(2,1)S(1)} %pad_maximum_fusion), channel_id=1, source_target_pairs={{0,1},{1,0},{2,3},{3,2},{4,5},{5,4},{6,7},{7,6},{8,9},{9,8},{10,11... | collective-permute-start | bytes 786440 | tf_op jit(solution)/shard_map/ppermute | solution.py:86

commit v16 on v15

--- a/solution.py
+++ b/solution.py
@@ -114,10 +114,17 @@
     if count == 1:
         return value
     got = [value] + [lax.ppermute(value, axis, route(step)) for step in range(1, count)]
-    ordered = jnp.take(jnp.stack(got), (index - jnp.arange(count)) % count, axis=0)
-    total = ordered[0]
+
+    def of_group(position):
+        step = (index - position) % count
+        picked = got[0]
+        for candidate in range(1, count):
+            picked = jnp.where(step == candidate, got[candidate], picked)
+        return picked
+
+    total = of_group(0)
     for position in range(1, count):
-        total = total + ordered[position]
+        total = total + of_group(position)
     return total
 
 

time: 40 us -> 39.1 us (0.978)
  other arithmetic: 5.92 us -> 6.99 us
  starting transfers between devices: 12.7 us -> 11.9 us
  waiting for transfers between devices: 10.5 us -> 9.94 us
  local copies, waits for them, and re-layouts: 3.99 us -> 3.47 us
    ppermute x1, waiting for transfers between devices: 3.27 us -> 2.18 us  [local(): got = lax.ppermute(jnp.where(first, frames_in, out_grad), 'tm', swap)]
    ppermute x3, starting transfers between devices: 4.79 us -> 3.91 us  [group_sum(): lax.ppermute(value, axis, route(step))]
    mul x1, other arithmetic: 0.01 us -> 0.61 us  [local(): product = decays_next[t] if product is None else product * decays_next[t]]
    div x1, other arithmetic: 0.01 us -> 0.58 us  [local(): decay_rate * decay_rate / input_gain * values]
    gather x1 -> x0, local copies, waits for them, and re-layouts: 0.56 us -> none  [group_sum(): jnp.take(jnp.stack(got), (index - jnp.arange(count)) % count, axis=0)]
    ppermute x3, waiting for transfers between devices: 0.01 us -> 0.46 us  [group_sum(): lax.ppermute(value, axis, route(step))]
  transfers between devices with their start and end apart: 9 -> 9, of which waited for: 5 -> 7; matrix products, arithmetic and copies ran while one was open for 18% -> 20% of each run, Pallas kernels for 0% -> 0%
where the time goes in v16:
time: 39.1 us; the launch traced here: 38.9 us
  starting transfers between devices  11.9 us (30%)
  waiting for transfers between devices  9.94 us (25%)
  other arithmetic  6.99 us (18%)
  matrix products  5.42 us (14%)
  local copies, waits for them, and re-layouts  3.47 us (9%)
  between operations  1.23 us (3%)
    dot_general x24, matrix products, conv_apply(): jnp.dot(portion.reshape(-1, channels), taps[index, col_tap], preferred_el...  5.42 us
    ppermute x3, waiting for transfers between devices, cyclic_carries(): received[step] = lax.ppermute(message, axis, route(step))  5.38 us
    ppermute x3, starting transfers between devices, cyclic_carries(): received[step] = lax.ppermute(message, axis, route(step))  4.93 us
    ppermute x3, starting transfers between devices, group_sum(): lax.ppermute(value, axis, route(step))  3.91 us
    ppermute x1, starting transfers between devices, local(): got = lax.ppermute(jnp.where(first, frames_in, out_grad), 'tm', swap)  2.94 us
    ppermute x1, waiting for transfers between devices, local(): got = lax.ppermute(jnp.where(first, frames_in, out_grad), 'tm', swap)  2.18 us
    ppermute x1, waiting for transfers between devices, local(): traded = lax.ppermute(got, 'chan', [(0, 1), (1, 0)])  1.85 us
    select_n x1, other arithmetic, local(): got = lax.ppermute(jnp.where(first, frames_in, out_grad), 'tm', swap)  1.71 us
  transfers between devices with their start and end apart: 9, of which 7 were waited for; matrix products, arithmetic and copies ran while one was open for 20% of the time, Pallas kernels for 0%

profile of v16, /device:TPU:0, one launch (start us, length us, event | category | flops | bytes accessed | tf_op | source)
XLA Modules:
  0.0 38.9 jit_solution(7005878245418143718)
XLA Ops:
  0.6 1.7 %broadcast_select_fusion.2 = bf16[4,1,64,512]{3,2,1,0:T(8,128)(2,1)} fusion(bf16[4,1,64,512]{3,2,1,0:T(8,128)(2,1)} %param.6, bf16[4,1,64,512]{3,2,1,0:T(8,128)(2,1)} %param.11, pred[]{:T(512)S(6)} %eq.49), kind=kLoop, calls=%fused_computation.53 | loop fusion | flops 131072 | bytes 786433 | tf_op jit(solution)/shard_map/jit(_where)/select_n | solution.py:143
  2.3 2.9 %collective-permute-start = (bf16[4,1,64,512]{3,2,1,0:T(8,128)(2,1)}, bf16[4,1,64,512]{3,2,1,0:T(8,128)(2,1)}, u32[]{:S(2)}, u32[]{:S(2)}) collective-permute-start(bf16[4,1,64,512]{3,2,1,0:T(8,128)(2,1)} %broadcast_select_fusion.2), channel_id=1, source_target_pairs={{0,2},{2,0},{4,6},{6,4},{8,10},{10,8},{12,14},{14,12},{1,3},{3,1},... | collective-permute-start | bytes 786440 | tf_op jit(solution)/shard_map/ppermute | solution.py:143
  5.3 1.2 %slice.326 = bf16[1,3,512,256]{3,2,1,0:T(8,128)(2,1)S(1)} slice(bf16[3,3,512,256]{3,2,1,0:T(8,128)(2,1)} %param.7), slice={[1:2], [0:3], [0:512], [0:256]} | slice | bytes 1572864 | tf_op jit(solution)/shard_map/slice | solution.py:31
  6.5 1.2 %slice.346 = bf16[1,3,256,512]{3,2,1,0:T(8,128)(2,1)S(1)} slice(bf16[3,3,256,512]{3,2,1,0:T(8,128)(2,1)} %param.8), slice={[1:2], [0:3], [0:256], [0:512]} | slice | bytes 1572864 | tf_op jit(solution)/shard_map/slice | solution.py:28
  8.0 0.6 %multiply_divide_fusion = (f32[256]{0:T(256)}, f32[256]{0:T(256)S(1)}) fusion(f32[256]{0:T(256)S(1)} %copy-done.1), kind=kLoop, calls=%fused_computation.196 | loop fusion | flops 768 | bytes 3072 | tf_op jit(solution)/shard_map/div | solution.py:215
  9.0 0.6 %fusion.70 = (f32[256]{0:T(256)}, f32[256]{0:T(256)}, f32[256]{0:T(256)}, f32[256]{0:T(256)}, f32[256]{0:T(256)}, /*index=5*/f32[256]{0:T(256)}, f32[256]{0:T(256)}) fusion(f32[256]{0:T(256)S(1)} %bitcast.344, f32[256]{0:T(256)S(1)} %bitcast.331, f32[256]{0:T(256)S(1)} %bitcast.342, f32[256]{0:T(256)S(1)} %bitcast.328, f32[256]{0:T(256)S(1)} %bitcast.340, ...), kind=kLoop, calls=%fused_computation.198 | loop fusion | flops 1792 | bytes 15360 | tf_op jit(solution)/shard_map/mul | solution.py:187
  9.7 2.2 %collective-permute-done = bf16[4,1,64,512]{3,2,1,0:T(8,128)(2,1)} collective-permute-done((bf16[4,1,64,512]{3,2,1,0:T(8,128)(2,1)}, bf16[4,1,64,512]{3,2,1,0:T(8,128)(2,1)}, u32[]{:S(2)}, u32[]{:S(2)}) %collective-permute-start) | collective-permute-done | bytes 262176 | tf_op jit(solution)/shard_map/ppermute | solution.py:143
  11.9 1.9 %collective-permute-done.1 = bf16[4,1,64,512]{3,2,1,0:T(8,128)(2,1)} collective-permute-done((bf16[4,1,64,512]{3,2,1,0:T(8,128)(2,1)}, bf16[4,1,64,512]{3,2,1,0:T(8,128)(2,1)}, u32[]{:S(2)}, u32[]{:S(2)}) %collective-permute-start.1) | collective-permute-done | bytes 262176 | tf_op jit(solution)/shard_map/ppermute | solution.py:144
  13.8 1.2 %broadcast_select_fusion.6 = (bf16[4,1,64,512]{3,2,1,0:T(8,128)(2,1)S(1)}, bf16[4,1,64,512]{3,2,1,0:T(8,128)(2,1)S(1)}, bf16[4,1,64,512]{3,2,1,0:T(8,128)(2,1)S(1)}, bf16[4,1,64,512]{3,2,1,0:T(8,128)(2,1)S(1)}) fusion(bf16[4,1,64,512]{3,2,1,0:T(8,128)(2,1)S(1)} %copy-done, pred[]{:T(512)S(6)} %eq.48, bf16[4,1,64,512]{3,2,1,0:T(8,128)(2,1)} %collective-permute-done, ...), kind=kLoop, calls=%fused_computation.57 | loop fusion | flops 786432 | bytes 2097154 | tf_op jit(solution)/shard_map/jit(_where)/select_n | solution.py:150
  17.4 0.3 convolution_add_fusion.9
  17.9 0.3 convolution_add_fusion.11
  18.2 0.3 convolution_add_fusion.10
  18.6 2.9 %collective-permute-start.3 = (f32[1,64,256]{2,1,0:T(8,128)S(1)}, f32[1,64,256]{2,1,0:T(8,128)S(1)}, u32[]{:S(2)}, u32[]{:S(2)}) collective-permute-start(f32[1,64,256]{2,1,0:T(8,128)S(1)} %get-tuple-element.82), channel_id=1, source_target_pairs={{0,8},{2,10},{4,12},{6,14},{8,0},{10,2},{12,4},{14,6},{1,9},{3,11}... | collective-permute-start | bytes 196616 | tf_op jit(solution)/shard_map/ppermute | solution.py:99
  21.5 1.3 %collective-permute-start.4 = (f32[1,64,256]{2,1,0:T(8,128)S(1)}, f32[1,64,256]{2,1,0:T(8,128)S(1)}, u32[]{:S(2)}, u32[]{:S(2)}) collective-permute-start(f32[1,64,256]{2,1,0:T(8,128)S(1)} %get-tuple-element.83), channel_id=1, source_target_pairs={{0,12},{2,14},{4,0},{6,2},{8,4},{10,6},{12,8},{14,10},{1,13},{3,15... | collective-permute-start | bytes 196616 | tf_op jit(solution)/shard_map/ppermute | solution.py:99
  22.9 0.7 %collective-permute-start.2 = (f32[1,64,256]{2,1,0:T(8,128)S(1)}, f32[1,64,256]{2,1,0:T(8,128)S(1)}, u32[]{:S(2)}, u32[]{:S(2)}) collective-permute-start(f32[1,64,256]{2,1,0:T(8,128)S(1)} %get-tuple-element.53), channel_id=1, source_target_pairs={{0,4},{2,6},{4,8},{6,10},{8,12},{10,14},{12,0},{14,2},{1,5},{3,7},... | collective-permute-start | bytes 196616 | tf_op jit(solution)/shard_map/ppermute | solution.py:99
  23.6 1.3 %collective-permute-done.3 = f32[1,64,256]{2,1,0:T(8,128)S(1)} collective-permute-done((f32[1,64,256]{2,1,0:T(8,128)S(1)}, f32[1,64,256]{2,1,0:T(8,128)S(1)}, u32[]{:S(2)}, u32[]{:S(2)}) %collective-permute-start.3) | collective-permute-done | bytes 65568 | tf_op jit(solution)/shard_map/ppermute | solution.py:99
  24.9 0.9 %collective-permute-done.4 = f32[1,64,256]{2,1,0:T(8,128)S(1)} collective-permute-done((f32[1,64,256]{2,1,0:T(8,128)S(1)}, f32[1,64,256]{2,1,0:T(8,128)S(1)}, u32[]{:S(2)}, u32[]{:S(2)}) %collective-permute-start.4) | collective-permute-done | bytes 65568 | tf_op jit(solution)/shard_map/ppermute | solution.py:99
  25.8 3.1 %collective-permute-done.2 = f32[1,64,256]{2,1,0:T(8,128)S(1)} collective-permute-done((f32[1,64,256]{2,1,0:T(8,128)S(1)}, f32[1,64,256]{2,1,0:T(8,128)S(1)}, u32[]{:S(2)}, u32[]{:S(2)}) %collective-permute-start.2) | collective-permute-done | bytes 65568 | tf_op jit(solution)/shard_map/ppermute | solution.py:99
  29.6 1.9 %collective-permute-start.6 = (f32[256]{0:T(256)S(1)}, f32[256]{0:T(256)S(1)}, u32[]{:S(2)}, u32[]{:S(2)}) collective-permute-start(f32[256]{0:T(256)S(1)} %fusion.4), channel_id=1, source_target_pairs={{0,12},{2,14},{4,0},{6,2},{8,4},{10,6},{12,8},{14,10},{1,13},{3,15... | collective-permute-start | bytes 3080 | tf_op jit(solution)/shard_map/ppermute | solution.py:116
  31.5 1.9 %collective-permute-start.8 = (f32[256]{0:T(256)S(1)}, f32[256]{0:T(256)S(1)}, u32[]{:S(2)}, u32[]{:S(2)}) collective-permute-start(f32[256]{0:T(256)S(1)} %fusion.4), channel_id=1, source_target_pairs={{0,4},{2,6},{4,8},{6,10},{8,12},{10,14},{12,0},{14,2},{1,5},{3,7},... | collective-permute-start | bytes 3080 | tf_op jit(solution)/shard_map/ppermute | solution.py:116
  36.4 0.5 %collective-permute-done.8 = f32[256]{0:T(256)S(1)} collective-permute-done((f32[256]{0:T(256)S(1)}, f32[256]{0:T(256)S(1)}, u32[]{:S(2)}, u32[]{:S(2)}) %collective-permute-start.8) | collective-permute-done | bytes 1056 | tf_op jit(solution)/shard_map/ppermute | solution.py:116
  36.9 0.6 %add_multiply_fusion = f32[256]{0:T(256)} fusion(f32[256]{0:T(256)S(1)} %collective-permute-done.6, f32[256]{0:T(256)S(1)} %collective-permute-done.7, f32[256]{0:T(256)S(1)} %collective-permute-done.8, f32[256]{0:T(256)S(1)} %fusion.4, pred[]{:T(512)S(6)} %eq.61, pred[]{:T(512)S(6)} %eq.60, pred[]{:T(512)S(6)} %eq.59, pred[]{:T(512)S(6)} %eq.58, ...), kind=kLoop, calls=%fused_computation.194 | loop fusion | flops 4096 | bytes 5132 | tf_op jit(solution)/shard_map/div | solution.py:222
  37.5 0.7 %fusion.7 = bf16[4,1,64,256]{3,2,1,0:T(8,128)(2,1)} fusion(f32[4,1,64,256]{3,2,1,0:T(8,128)S(1)} %bitcast.304, bf16[2,4,1,64,256]{4,3,1,2,0:T(8,128)(2,1)S(1)} %collective-permute-done.5), kind=kLoop, calls=%fused_computation.48 | loop fusion | flops 196608 | bytes 524288 | tf_op jit(solution)/shard_map/convert_element_type | solution.py:91
  38.2 0.7 %fusion.13 = bf16[4,1,64,256]{3,2,1,0:T(8,128)(2,1)} fusion(f32[4,1,64,256]{3,2,0,1:T(8,128)S(1)} %bitcast.305, bf16[2,4,1,64,256]{4,3,1,2,0:T(8,128)(2,1)S(1)} %collective-permute-done.5), kind=kLoop, calls=%fused_computation.62 | loop fusion | flops 196608 | bytes 524288
  (89 shorter events, 6.9 us)
Async XLA Ops:
  2.3 9.6 %collective-permute-start = (bf16[4,1,64,512]{3,2,1,0:T(8,128)(2,1)}, bf16[4,1,64,512]{3,2,1,0:T(8,128)(2,1)}, u32[]{:S(2)}, u32[]{:S(2)}) collective-permute-start(bf16[4,1,64,512]{3,2,1,0:T(8,128)(2,1)} %broadcast_select_fusion.2), channel_id=1, source_target_pairs={{0,2},{2,0},{4,6},{6,4},{8,10},{10,8},{12,14},{14,12},{1,3},{3,1},... | collective-permute-start | bytes 786440 | tf_op jit(solution)/shard_map/ppermute | solution.py:143
  5.3 2.5 %copy-start.10 = (f32[32]{0:T(128)S(1)}, f32[32]{0:T(128)}, u32[]{:S(2)}) copy-start(f32[32]{0:T(128)} %param.10) | copy-start | bytes 388
  5.3 2.7 %copy-start.1 = (f32[256]{0:T(256)S(1)}, f32[256]{0:T(256)}, u32[]{:S(2)}) copy-start(f32[256]{0:T(256)} %param.9) | copy-start | bytes 3076
  6.5 7.3 %copy-start = (bf16[4,1,64,512]{3,2,1,0:T(8,128)(2,1)S(1)}, bf16[4,1,64,512]{3,2,1,0:T(8,128)(2,1)}, u32[]{:S(2)}) copy-start(bf16[4,1,64,512]{3,2,1,0:T(8,128)(2,1)} %param.6) | copy-start | bytes 786436
  11.9 1.9 %collective-permute-start.1 = (bf16[4,1,64,512]{3,2,1,0:T(8,128)(2,1)}, bf16[4,1,64,512]{3,2,1,0:T(8,128)(2,1)}, u32[]{:S(2)}, u32[]{:S(2)}) collective-permute-start(bf16[4,1,64,512]{3,2,1,0:T(8,128)(2,1)} %collective-permute-done), channel_id=1, source_target_pairs={{0,1},{1,0},{2,3},{3,2},{4,5},{5,4},{6,7},{7,6},{8,9},{9,8},{10,11... | collective-permute-start | bytes 786440 | tf_op jit(solution)/shard_map/ppermute | solution.py:144
  17.6 11.3 %copy-start.9 = (f32[256]{0:T(256)S(1)}, f32[256]{0:T(256)}, u32[]{:S(2)}) copy-start(f32[256]{0:T(256)} %get-tuple-element.39) | copy-start | bytes 3076
  17.9 11.1 %copy-start.8 = (f32[256]{0:T(256)S(1)}, f32[256]{0:T(256)}, u32[]{:S(2)}) copy-start(f32[256]{0:T(256)} %get-tuple-element.40) | copy-start | bytes 3076
  17.9 11.1 %copy-start.7 = (f32[256]{0:T(256)S(1)}, f32[256]{0:T(256)}, u32[]{:S(2)}) copy-start(f32[256]{0:T(256)} %get-tuple-element.41) | copy-start | bytes 3076
  17.9 11.2 %copy-start.6 = (f32[256]{0:T(256)S(1)}, f32[256]{0:T(256)}, u32[]{:S(2)}) copy-start(f32[256]{0:T(256)} %get-tuple-element.42) | copy-start | bytes 3076
  18.2 10.9 %copy-start.5 = (f32[256]{0:T(256)S(1)}, f32[256]{0:T(256)}, u32[]{:S(2)}) copy-start(f32[256]{0:T(256)} %get-tuple-element.43) | copy-start | bytes 3076
  18.2 10.9 %copy-start.4 = (f32[256]{0:T(256)S(1)}, f32[256]{0:T(256)}, u32[]{:S(2)}) copy-start(f32[256]{0:T(256)} %get-tuple-element.44) | copy-start | bytes 3076
  18.2 11.0 %copy-start.3 = (f32[256]{0:T(256)S(1)}, f32[256]{0:T(256)}, u32[]{:S(2)}) copy-start(f32[256]{0:T(256)} %get-tuple-element.45) | copy-start | bytes 3076
  18.6 10.8 %copy-start.2 = (f32[256]{0:T(256)S(1)}, f32[256]{0:T(256)}, u32[]{:S(2)}) copy-start(f32[256]{0:T(256)} %get-tuple-element.106) | copy-start | bytes 3076
  18.6 6.2 %collective-permute-start.3 = (f32[1,64,256]{2,1,0:T(8,128)S(1)}, f32[1,64,256]{2,1,0:T(8,128)S(1)}, u32[]{:S(2)}, u32[]{:S(2)}) collective-permute-start(f32[1,64,256]{2,1,0:T(8,128)S(1)} %get-tuple-element.82), channel_id=1, source_target_pairs={{0,8},{2,10},{4,12},{6,14},{8,0},{10,2},{12,4},{14,6},{1,9},{3,11}... | collective-permute-start | bytes 196616 | tf_op jit(solution)/shard_map/ppermute | solution.py:99
  21.5 4.3 %collective-permute-start.4 = (f32[1,64,256]{2,1,0:T(8,128)S(1)}, f32[1,64,256]{2,1,0:T(8,128)S(1)}, u32[]{:S(2)}, u32[]{:S(2)}) collective-permute-start(f32[1,64,256]{2,1,0:T(8,128)S(1)} %get-tuple-element.83), channel_id=1, source_target_pairs={{0,12},{2,14},{4,0},{6,2},{8,4},{10,6},{12,8},{14,10},{1,13},{3,15... | collective-permute-start | bytes 196616 | tf_op jit(solution)/shard_map/ppermute | solution.py:99
  22.9 6.1 %collective-permute-start.2 = (f32[1,64,256]{2,1,0:T(8,128)S(1)}, f32[1,64,256]{2,1,0:T(8,128)S(1)}, u32[]{:S(2)}, u32[]{:S(2)}) collective-permute-start(f32[1,64,256]{2,1,0:T(8,128)S(1)} %get-tuple-element.53), channel_id=1, source_target_pairs={{0,4},{2,6},{4,8},{6,10},{8,12},{10,14},{12,0},{14,2},{1,5},{3,7},... | collective-permute-start | bytes 196616 | tf_op jit(solution)/shard_map/ppermute | solution.py:99
  29.6 6.9 %collective-permute-start.6 = (f32[256]{0:T(256)S(1)}, f32[256]{0:T(256)S(1)}, u32[]{:S(2)}, u32[]{:S(2)}) collective-permute-start(f32[256]{0:T(256)S(1)} %fusion.4), channel_id=1, source_target_pairs={{0,12},{2,14},{4,0},{6,2},{8,4},{10,6},{12,8},{14,10},{1,13},{3,15... | collective-permute-start | bytes 3080 | tf_op jit(solution)/shard_map/ppermute | solution.py:116
  31.4 5.0 %collective-permute-start.7 = (f32[256]{0:T(256)S(1)}, f32[256]{0:T(256)S(1)}, u32[]{:S(2)}, u32[]{:S(2)}) collective-permute-start(f32[256]{0:T(256)S(1)} %fusion.4), channel_id=1, source_target_pairs={{0,8},{2,10},{4,12},{6,14},{8,0},{10,2},{12,4},{14,6},{1,9},{3,11}... | collective-permute-start | bytes 3080 | tf_op jit(solution)/shard_map/ppermute | solution.py:116
  31.5 5.4 %collective-permute-start.8 = (f32[256]{0:T(256)S(1)}, f32[256]{0:T(256)S(1)}, u32[]{:S(2)}, u32[]{:S(2)}) collective-permute-start(f32[256]{0:T(256)S(1)} %fusion.4), channel_id=1, source_target_pairs={{0,4},{2,6},{4,8},{6,10},{8,12},{10,14},{12,0},{14,2},{1,5},{3,7},... | collective-permute-start | bytes 3080 | tf_op jit(solution)/shard_map/ppermute | solution.py:116
  35.9 1.6 %collective-permute-start.5 = (bf16[2,4,1,64,256]{4,3,1,2,0:T(8,128)(2,1)S(1)}, bf16[2,4,1,64,256]{4,3,1,2,0:T(8,128)(2,1)S(1)}, u32[]{:S(2)}, u32[]{:S(2)}) collective-permute-start(bf16[2,4,1,64,256]{4,3,1,2,0:T(8,128)(2,1)S(1)} %pad_maximum_fusion), channel_id=1, source_target_pairs={{0,1},{1,0},{2,3},{3,2},{4,5},{5,4},{6,7},{7,6},{8,9},{9,8},{10,11... | collective-permute-start | bytes 786440 | tf_op jit(solution)/shard_map/ppermute | solution.py:86

commit v17 on v16

--- a/solution.py
+++ b/solution.py
@@ -140,8 +140,13 @@
         swap = [(i, i ^ 1) for i in range(blocks)]
         if lax.axis_size("chan") == 2:
             first = lax.axis_index("chan") == 0
-            got = lax.ppermute(jnp.where(first, frames_in, out_grad), "tm", swap)
-            traded = lax.ppermute(got, "chan", [(0, 1), (1, 0)])
+            outgoing = jnp.where(first, frames_in, out_grad)
+            cut = frame_count // 2 if frame_count > 1 else frame_count
+            pieces = [outgoing[:cut], outgoing[cut:]] if cut < frame_count else [outgoing]
+            arrived = [lax.ppermute(piece, "tm", swap) for piece in pieces]
+            handed = [lax.ppermute(piece, "chan", [(0, 1), (1, 0)]) for piece in arrived]
+            got = jnp.concatenate(arrived)
+            traded = jnp.concatenate(handed)
             other_frames = jnp.where(first, got, traded)
             other_grad = jnp.where(first, traded, got)
         else:

time: 39.1 us -> 42.1 us (1.077)
  waiting for transfers between devices: 9.94 us -> 7.48 us
  local copies, waits for them, and re-layouts: 3.47 us -> 5.27 us
  other arithmetic: 6.99 us -> 8.65 us
  starting transfers between devices: 11.9 us -> 13.1 us
  between operations: 1.23 us -> 1.86 us
    ppermute x2 -> x4, waiting for transfers between devices: 4.04 us -> 0.97 us  [the longest x2 0.96 us: local(): lax.ppermute(piece, 'chan', [(0, 1), (1, 0)])]
    dynamic_slice x1, other arithmetic: 0.01 us -> 1.28 us  [cyclic_carries(): lax.dynamic_index_in_dim(bwd_prod, jnp.minimum(source, count - 1), 0, kee...]
    unnamed x22 -> x106, local copies, waits for them, and re-layouts: 0.05 us -> 1.15 us
    select_n x1, other arithmetic: 1.71 us -> 0.99 us  [local(): outgoing = jnp.where(first, frames_in, out_grad)]
    slice x0 -> x1, local copies, waits for them, and re-layouts: none -> 0.72 us  [local(): outgoing[cut:]]
    ppermute x3, waiting for transfers between devices: 0.46 us -> 1.16 us  [group_sum(): lax.ppermute(value, axis, route(step))]
    mul x1, other arithmetic: 0.01 us -> 0.62 us  [local(): product = decays[t] if product is None else product * decays[t]]
    ppermute x2 -> x4, starting transfers between devices: 2.94 us -> 3.55 us  [the longest x2 2.97 us: local(): arrived = [lax.ppermute(piece, 'tm', swap) for piece in pieces]]
  transfers between devices with their start and end apart: 9 -> 11, of which waited for: 7 -> 5; matrix products, arithmetic and copies ran while one was open for 20% -> 26% of each run, Pallas kernels for 0% -> 0%
where the time goes in v17:
time: 42.1 us; the launch traced here: 41.8 us
  starting transfers between devices  13.1 us (31%)
  other arithmetic  8.65 us (21%)
  waiting for transfers between devices  7.48 us (18%)
  matrix products  5.45 us (13%)
  local copies, waits for them, and re-layouts  5.27 us (13%)
  between operations  1.86 us (4%)
    dot_general x24, matrix products, conv_apply(): jnp.dot(portion.reshape(-1, channels), taps[index, col_tap], preferred_el...  5.45 us
    ppermute x3, waiting for transfers between devices, cyclic_carries(): received[step] = lax.ppermute(message, axis, route(step))  5.35 us
    ppermute x3, starting transfers between devices, cyclic_carries(): received[step] = lax.ppermute(message, axis, route(step))  5.29 us
    ppermute x3, starting transfers between devices, group_sum(): lax.ppermute(value, axis, route(step))  4.2 us
    ppermute x2, starting transfers between devices, local(): arrived = [lax.ppermute(piece, 'tm', swap) for piece in pieces]  2.97 us
    dynamic_slice x1, other arithmetic, cyclic_carries(): lax.dynamic_index_in_dim(bwd_prod, jnp.minimum(source, count - 1), 0, kee...  1.28 us
    slice x1, local copies, waits for them, and re-layouts, prep_kernel(): taps = jnp.stack([kernel[a] for a in row_taps])  1.21 us
    slice x1, local copies, waits for them, and re-layouts, prep_kernel(): taps = jnp.stack([flipped[a] for a in row_taps])  1.19 us
  transfers between devices with their start and end apart: 11, of which 5 were waited for; matrix products, arithmetic and copies ran while one was open for 26% of the time, Pallas kernels for 0%

profile of v17, /device:TPU:0, one launch (start us, length us, event | category | flops | bytes accessed | tf_op | source)
XLA Modules:
  0.0 41.8 jit_solution(5703030571362267826)
XLA Ops:
  0.6 1.0 %broadcast_select_fusion.2 = bf16[4,1,64,512]{3,2,1,0:T(8,128)(2,1)S(1)} fusion(bf16[4,1,64,512]{3,2,1,0:T(8,128)(2,1)} %param.6, bf16[4,1,64,512]{3,2,1,0:T(8,128)(2,1)} %param.11, pred[]{:T(512)S(6)} %eq.49), kind=kLoop, calls=%fused_computation.53 | loop fusion | flops 131072 | bytes 786433 | tf_op jit(solution)/shard_map/jit(_where)/select_n | solution.py:143
  1.6 0.7 %fusion.76 = (bf16[2,1,64,512]{3,2,1,0:T(8,128)(2,1)}, bf16[2,1,64,512]{3,2,1,0:T(8,128)(2,1)}) fusion(bf16[4,1,64,512]{3,2,1,0:T(8,128)(2,1)S(1)} %broadcast_select_fusion.2), kind=kLoop, calls=%fused_computation.204 | loop fusion | bytes 524288 | tf_op jit(solution)/shard_map/slice | solution.py:145
  2.3 2.9 %collective-permute-start = (bf16[2,1,64,512]{3,2,1,0:T(8,128)(2,1)}, bf16[2,1,64,512]{3,2,1,0:T(8,128)(2,1)}, u32[]{:S(2)}, u32[]{:S(2)}) collective-permute-start(bf16[2,1,64,512]{3,2,1,0:T(8,128)(2,1)} %get-tuple-element.77), channel_id=1, source_target_pairs={{0,2},{2,0},{4,6},{6,4},{8,10},{10,8},{12,14},{14,12},{1,3},{3,1},... | collective-permute-start | bytes 393224 | tf_op jit(solution)/shard_map/ppermute | solution.py:146
  5.3 1.2 %slice.334 = bf16[1,3,512,256]{3,2,1,0:T(8,128)(2,1)S(1)} slice(bf16[3,3,512,256]{3,2,1,0:T(8,128)(2,1)} %param.7), slice={[1:2], [0:3], [0:512], [0:256]} | slice | bytes 1572864 | tf_op jit(solution)/shard_map/slice | solution.py:31
  6.5 1.2 %slice.354 = bf16[1,3,256,512]{3,2,1,0:T(8,128)(2,1)S(1)} slice(bf16[3,3,256,512]{3,2,1,0:T(8,128)(2,1)} %param.8), slice={[1:2], [0:3], [0:256], [0:512]} | slice | bytes 1572864 | tf_op jit(solution)/shard_map/slice | solution.py:28
  8.0 0.6 %multiply_divide_fusion = (f32[256]{0:T(256)}, f32[256]{0:T(256)S(1)}) fusion(f32[256]{0:T(256)S(1)} %copy-done.12), kind=kLoop, calls=%fused_computation.200 | loop fusion | flops 768 | bytes 3072 | tf_op jit(solution)/shard_map/div | solution.py:220
  9.1 0.7 %slice_multiply_fusion.8 = (f32[4,1,256]{2,1,0:T(1,128)}, f32[4,1,256]{2,1,0:T(1,128)}) fusion(f32[4,8,256]{2,1,0:T(8,128)S(1)} %get-tuple-element.110, f32[4,8,256]{2,1,0:T(8,128)S(1)} %get-tuple-element.111), kind=kLoop, calls=%fused_computation.180 | loop fusion | flops 14336 | bytes 73728 | tf_op jit(solution)/shard_map/mul | solution.py:203
  9.8 0.6 %fusion.70 = (f32[256]{0:T(256)}, f32[256]{0:T(256)}, f32[256]{0:T(256)}, f32[256]{0:T(256)}, f32[256]{0:T(256)}, /*index=5*/f32[256]{0:T(256)}, f32[256]{0:T(256)}) fusion(f32[256]{0:T(256)S(1)} %bitcast.344, f32[256]{0:T(256)S(1)} %bitcast.331, f32[256]{0:T(256)S(1)} %bitcast.342, f32[256]{0:T(256)S(1)} %bitcast.328, f32[256]{0:T(256)S(1)} %bitcast.340, ...), kind=kLoop, calls=%fused_computation.202 | loop fusion | flops 1792 | bytes 15360 | tf_op jit(solution)/shard_map/mul | solution.py:192
  10.5 0.6 %fusion.71 = (f32[256]{0:T(256)}, f32[256]{0:T(256)}, f32[256]{0:T(256)}, f32[256]{0:T(256)}, f32[256]{0:T(256)}, /*index=5*/f32[256]{0:T(256)}, f32[256]{0:T(256)}) fusion(f32[256]{0:T(256)S(1)} %bitcast.350, f32[256]{0:T(256)S(1)} %bitcast.316, f32[256]{0:T(256)S(1)} %bitcast.352, f32[256]{0:T(256)S(1)} %bitcast.319, f32[256]{0:T(256)S(1)} %bitcast.346, ...), kind=kLoop, calls=%fused_computation.203 | loop fusion | flops 1792 | bytes 15360 | tf_op jit(solution)/shard_map/mul | solution.py:184
  11.2 1.3 %constant_dynamic-slice_fusion.2 = (f32[1,1,256]{2,1,0:T(1,128)}, f32[1,1,256]{2,1,0:T(1,128)}, f32[1,1,256]{2,1,0:T(1,128)}) fusion(f32[4,1,256]{2,1,0:T(1,128)} %get-tuple-element.128, s32[]{:T(128)S(6)} %select_n.321, s32[]{:T(128)S(6)} %select_n.324, s32[]{:T(128)S(6)} %select_n.327), kind=kLoop, calls=%fused_computation.174 | loop fusion | flops 256 | bytes 6156 | tf_op jit(solution)/shard_map/jit(dynamic_index_in_dim)/dynamic_slice | solution.py:108
  12.5 0.9 %constant_dynamic-update-slice_fusion.1 = bf16[4,1,64,512]{3,2,1,0:T(8,128)(2,1)S(1)} fusion(bf16[2,1,64,512]{3,2,1,0:T(8,128)(2,1)} %collective-permute-done), kind=kLoop, calls=%fused_computation.142 | loop fusion | bytes 262144
  13.4 0.6 %collective-permute-start.3 = (bf16[2,1,64,512]{3,2,1,0:T(8,128)(2,1)S(1)}, bf16[2,1,64,512]{3,2,1,0:T(8,128)(2,1)S(1)}, u32[]{:S(2)}, u32[]{:S(2)}) collective-permute-start(bf16[2,1,64,512]{3,2,1,0:T(8,128)(2,1)S(1)} %collective-permute-done.1), channel_id=1, source_target_pairs={{0,1},{1,0},{2,3},{3,2},{4,5},{5,4},{6,7},{7,6},{8,9},{9,8},{10,11... | collective-permute-start | bytes 393224 | tf_op jit(solution)/shard_map/ppermute | solution.py:147
  14.1 0.9 %collective-permute-done.3 = bf16[2,1,64,512]{3,2,1,0:T(8,128)(2,1)S(1)} collective-permute-done((bf16[2,1,64,512]{3,2,1,0:T(8,128)(2,1)S(1)}, bf16[2,1,64,512]{3,2,1,0:T(8,128)(2,1)S(1)}, u32[]{:S(2)}, u32[]{:S(2)}) %collective-permute-start.3) | collective-permute-done | bytes 131104 | tf_op jit(solution)/shard_map/ppermute | solution.py:147
  15.0 1.0 %broadcast_select_fusion.6 = (bf16[4,1,64,512]{3,2,1,0:T(8,128)(2,1)S(1)}, bf16[4,1,64,512]{3,2,1,0:T(8,128)(2,1)S(1)}, bf16[4,1,64,512]{3,2,1,0:T(8,128)(2,1)S(1)}, bf16[4,1,64,512]{3,2,1,0:T(8,128)(2,1)S(1)}) fusion(bf16[4,1,64,512]{3,2,1,0:T(8,128)(2,1)S(1)} %copy-done, pred[]{:T(512)S(6)} %eq.48, ...), kind=kLoop, calls=%fused_computation.57 | loop fusion | flops 786432 | bytes 2097154 | tf_op jit(solution)/shard_map/jit(_where)/select_n | solution.py:155
  20.1 3.3 %collective-permute-start.5 = (f32[1,64,256]{2,1,0:T(8,128)S(1)}, f32[1,64,256]{2,1,0:T(8,128)S(1)}, u32[]{:S(2)}, u32[]{:S(2)}) collective-permute-start(f32[1,64,256]{2,1,0:T(8,128)S(1)} %get-tuple-element.84), channel_id=1, source_target_pairs={{0,8},{2,10},{4,12},{6,14},{8,0},{10,2},{12,4},{14,6},{1,9},{3,11}... | collective-permute-start | bytes 196616 | tf_op jit(solution)/shard_map/ppermute | solution.py:99
  23.4 1.3 %collective-permute-start.6 = (f32[1,64,256]{2,1,0:T(8,128)S(1)}, f32[1,64,256]{2,1,0:T(8,128)S(1)}, u32[]{:S(2)}, u32[]{:S(2)}) collective-permute-start(f32[1,64,256]{2,1,0:T(8,128)S(1)} %get-tuple-element.85), channel_id=1, source_target_pairs={{0,12},{2,14},{4,0},{6,2},{8,4},{10,6},{12,8},{14,10},{1,13},{3,15... | collective-permute-start | bytes 196616 | tf_op jit(solution)/shard_map/ppermute | solution.py:99
  24.7 0.7 %collective-permute-start.4 = (f32[1,64,256]{2,1,0:T(8,128)S(1)}, f32[1,64,256]{2,1,0:T(8,128)S(1)}, u32[]{:S(2)}, u32[]{:S(2)}) collective-permute-start(f32[1,64,256]{2,1,0:T(8,128)S(1)} %get-tuple-element.53), channel_id=1, source_target_pairs={{0,4},{2,6},{4,8},{6,10},{8,12},{10,14},{12,0},{14,2},{1,5},{3,7},... | collective-permute-start | bytes 196616 | tf_op jit(solution)/shard_map/ppermute | solution.py:99
  25.4 1.8 %collective-permute-done.5 = f32[1,64,256]{2,1,0:T(8,128)S(1)} collective-permute-done((f32[1,64,256]{2,1,0:T(8,128)S(1)}, f32[1,64,256]{2,1,0:T(8,128)S(1)}, u32[]{:S(2)}, u32[]{:S(2)}) %collective-permute-start.5) | collective-permute-done | bytes 65568 | tf_op jit(solution)/shard_map/ppermute | solution.py:99
  27.8 3.0 %collective-permute-done.4 = f32[1,64,256]{2,1,0:T(8,128)S(1)} collective-permute-done((f32[1,64,256]{2,1,0:T(8,128)S(1)}, f32[1,64,256]{2,1,0:T(8,128)S(1)}, u32[]{:S(2)}, u32[]{:S(2)}) %collective-permute-start.4) | collective-permute-done | bytes 65568 | tf_op jit(solution)/shard_map/ppermute | solution.py:99
  31.8 3.6 %collective-permute-start.8 = (f32[256]{0:T(256)S(1)}, f32[256]{0:T(256)S(1)}, u32[]{:S(2)}, u32[]{:S(2)}) collective-permute-start(f32[256]{0:T(256)S(1)} %fusion.4), channel_id=1, source_target_pairs={{0,12},{2,14},{4,0},{6,2},{8,4},{10,6},{12,8},{14,10},{1,13},{3,15... | collective-permute-start | bytes 3080 | tf_op jit(solution)/shard_map/ppermute | solution.py:116
  38.7 1.2 %collective-permute-done.9 = f32[256]{0:T(256)S(1)} collective-permute-done((f32[256]{0:T(256)S(1)}, f32[256]{0:T(256)S(1)}, u32[]{:S(2)}, u32[]{:S(2)}) %collective-permute-start.9) | collective-permute-done | bytes 1056 | tf_op jit(solution)/shard_map/ppermute | solution.py:116
  39.9 0.6 %add_multiply_fusion = f32[256]{0:T(256)} fusion(f32[256]{0:T(256)S(1)} %collective-permute-done.8, f32[256]{0:T(256)S(1)} %collective-permute-done.9, f32[256]{0:T(256)S(1)} %collective-permute-done.10, f32[256]{0:T(256)S(1)} %fusion.4, pred[]{:T(512)S(6)} %eq.61, pred[]{:T(512)S(6)} %eq.60, pred[]{:T(512)S(6)} %eq.59, pred[]{:T(512)S(6)} %eq.58, ...), kind=kLoop, calls=%fused_computation.198 | loop fusion | flops 4096 | bytes 5132 | tf_op jit(solution)/shard_map/div | solution.py:227
  40.4 0.7 %fusion.7 = bf16[4,1,64,256]{3,2,1,0:T(8,128)(2,1)} fusion(f32[4,1,64,256]{3,2,1,0:T(8,128)S(1)} %bitcast.304, bf16[2,4,1,64,256]{4,3,1,2,0:T(8,128)(2,1)S(1)} %collective-permute-done.7), kind=kLoop, calls=%fused_computation.48 | loop fusion | flops 196608 | bytes 524288 | tf_op jit(solution)/shard_map/convert_element_type | solution.py:91
  41.1 0.7 %fusion.13 = bf16[4,1,64,256]{3,2,1,0:T(8,128)(2,1)} fusion(f32[4,1,64,256]{3,2,0,1:T(8,128)S(1)} %bitcast.305, bf16[2,4,1,64,256]{4,3,1,2,0:T(8,128)(2,1)S(1)} %collective-permute-done.7), kind=kLoop, calls=%fused_computation.62 | loop fusion | flops 196608 | bytes 524288
  (180 shorter events, 8.9 us)
Async XLA Ops:
  2.3 10.2 %collective-permute-start = (bf16[2,1,64,512]{3,2,1,0:T(8,128)(2,1)}, bf16[2,1,64,512]{3,2,1,0:T(8,128)(2,1)}, u32[]{:S(2)}, u32[]{:S(2)}) collective-permute-start(bf16[2,1,64,512]{3,2,1,0:T(8,128)(2,1)} %get-tuple-element.77), channel_id=1, source_target_pairs={{0,2},{2,0},{4,6},{6,4},{8,10},{10,8},{12,14},{14,12},{1,3},{3,1},... | collective-permute-start | bytes 393224 | tf_op jit(solution)/shard_map/ppermute | solution.py:146
  5.3 8.2 %collective-permute-start.1 = (bf16[2,1,64,512]{3,2,1,0:T(8,128)(2,1)}, bf16[2,1,64,512]{3,2,1,0:T(8,128)(2,1)S(1)}, u32[]{:S(2)}, u32[]{:S(2)}) collective-permute-start(bf16[2,1,64,512]{3,2,1,0:T(8,128)(2,1)} %get-tuple-element.76), channel_id=1, source_target_pairs={{0,2},{2,0},{4,6},{6,4},{8,10},{10,8},{12,14},{14,12},{1,3},{3,1},... | collective-permute-start | bytes 393224 | tf_op jit(solution)/shard_map/ppermute | solution.py:146
  12.5 1.6 %collective-permute-start.2 = (bf16[2,1,64,512]{3,2,1,0:T(8,128)(2,1)}, bf16[2,1,64,512]{3,2,1,0:T(8,128)(2,1)S(1)}, u32[]{:S(2)}, u32[]{:S(2)}) collective-permute-start(bf16[2,1,64,512]{3,2,1,0:T(8,128)(2,1)} %collective-permute-done), channel_id=1, source_target_pairs={{0,1},{1,0},{2,3},{3,2},{4,5},{5,4},{6,7},{7,6},{8,9},{9,8},{10,11... | collective-permute-start | bytes 393224 | tf_op jit(solution)/shard_map/ppermute | solution.py:147
  13.4 1.6 %collective-permute-start.3 = (bf16[2,1,64,512]{3,2,1,0:T(8,128)(2,1)S(1)}, bf16[2,1,64,512]{3,2,1,0:T(8,128)(2,1)S(1)}, u32[]{:S(2)}, u32[]{:S(2)}) collective-permute-start(bf16[2,1,64,512]{3,2,1,0:T(8,128)(2,1)S(1)} %collective-permute-done.1), channel_id=1, source_target_pairs={{0,1},{1,0},{2,3},{3,2},{4,5},{5,4},{6,7},{7,6},{8,9},{9,8},{10,11... | collective-permute-start | bytes 393224 | tf_op jit(solution)/shard_map/ppermute | solution.py:147
  18.9 11.9 %copy-start.34 = (f32[1,1,256]{2,1,0:T(1,128)S(1)}, f32[1,1,256]{2,1,0:T(1,128)}, u32[]{:S(2)}) copy-start(f32[1,1,256]{2,1,0:T(1,128)} %get-tuple-element.102) | copy-start | bytes 3076
  18.9 11.9 %copy-start.35 = (f32[1,1,256]{2,1,0:T(1,128)S(1)}, f32[1,1,256]{2,1,0:T(1,128)}, u32[]{:S(2)}) copy-start(f32[1,1,256]{2,1,0:T(1,128)} %get-tuple-element.103) | copy-start | bytes 3076
  18.9 11.9 %copy-start.36 = (f32[1,1,256]{2,1,0:T(1,128)S(1)}, f32[1,1,256]{2,1,0:T(1,128)}, u32[]{:S(2)}) copy-start(f32[1,1,256]{2,1,0:T(1,128)} %get-tuple-element.104) | copy-start | bytes 3076
  18.9 11.9 %copy-start.50 = (f32[256]{0:T(256)S(1)}, f32[256]{0:T(256)}, u32[]{:S(2)}) copy-start(f32[256]{0:T(256)} %get-tuple-element.39) | copy-start | bytes 3076
  19.2 11.7 %copy-start.49 = (f32[256]{0:T(256)S(1)}, f32[256]{0:T(256)}, u32[]{:S(2)}) copy-start(f32[256]{0:T(256)} %get-tuple-element.40) | copy-start | bytes 3076
  19.2 11.7 %copy-start.48 = (f32[256]{0:T(256)S(1)}, f32[256]{0:T(256)}, u32[]{:S(2)}) copy-start(f32[256]{0:T(256)} %get-tuple-element.41) | copy-start | bytes 3076
  19.2 11.7 %copy-start.47 = (f32[256]{0:T(256)S(1)}, f32[256]{0:T(256)}, u32[]{:S(2)}) copy-start(f32[256]{0:T(256)} %get-tuple-element.42) | copy-start | bytes 3076
  19.5 11.5 %copy-start.46 = (f32[256]{0:T(256)S(1)}, f32[256]{0:T(256)}, u32[]{:S(2)}) copy-start(f32[256]{0:T(256)} %get-tuple-element.43) | copy-start | bytes 3076
  19.5 11.5 %copy-start.45 = (f32[256]{0:T(256)S(1)}, f32[256]{0:T(256)}, u32[]{:S(2)}) copy-start(f32[256]{0:T(256)} %get-tuple-element.44) | copy-start | bytes 3076
  19.5 11.6 %copy-start.44 = (f32[256]{0:T(256)S(1)}, f32[256]{0:T(256)}, u32[]{:S(2)}) copy-start(f32[256]{0:T(256)} %get-tuple-element.45) | copy-start | bytes 3076
  19.5 11.6 %copy-start.16 = (f32[1,256]{1,0:T(1,128)S(1)}, f32[1,256]{1,0:T(1,128)}, u32[]{:S(2)}) copy-start(f32[1,256]{1,0:T(1,128)} %copy-done.15) | copy-start | bytes 3076
  19.8 11.3 %copy-start.14 = (f32[1,256]{1,0:T(1,128)S(1)}, f32[1,256]{1,0:T(1,128)}, u32[]{:S(2)}) copy-start(f32[1,256]{1,0:T(1,128)} %copy-done.13) | copy-start | bytes 3076
  19.8 11.4 %copy-start.43 = (f32[256]{0:T(256)S(1)}, f32[256]{0:T(256)}, u32[]{:S(2)}) copy-start(f32[256]{0:T(256)} %get-tuple-element.52) | copy-start | bytes 3076
  20.1 7.1 %collective-permute-start.5 = (f32[1,64,256]{2,1,0:T(8,128)S(1)}, f32[1,64,256]{2,1,0:T(8,128)S(1)}, u32[]{:S(2)}, u32[]{:S(2)}) collective-permute-start(f32[1,64,256]{2,1,0:T(8,128)S(1)} %get-tuple-element.84), channel_id=1, source_target_pairs={{0,8},{2,10},{4,12},{6,14},{8,0},{10,2},{12,4},{14,6},{1,9},{3,11}... | collective-permute-start | bytes 196616 | tf_op jit(solution)/shard_map/ppermute | solution.py:99
  23.4 4.4 %collective-permute-start.6 = (f32[1,64,256]{2,1,0:T(8,128)S(1)}, f32[1,64,256]{2,1,0:T(8,128)S(1)}, u32[]{:S(2)}, u32[]{:S(2)}) collective-permute-start(f32[1,64,256]{2,1,0:T(8,128)S(1)} %get-tuple-element.85), channel_id=1, source_target_pairs={{0,12},{2,14},{4,0},{6,2},{8,4},{10,6},{12,8},{14,10},{1,13},{3,15... | collective-permute-start | bytes 196616 | tf_op jit(solution)/shard_map/ppermute | solution.py:99
  24.7 6.1 %collective-permute-start.4 = (f32[1,64,256]{2,1,0:T(8,128)S(1)}, f32[1,64,256]{2,1,0:T(8,128)S(1)}, u32[]{:S(2)}, u32[]{:S(2)}) collective-permute-start(f32[1,64,256]{2,1,0:T(8,128)S(1)} %get-tuple-element.53), channel_id=1, source_target_pairs={{0,4},{2,6},{4,8},{6,10},{8,12},{10,14},{12,0},{14,2},{1,5},{3,7},... | collective-permute-start | bytes 196616 | tf_op jit(solution)/shard_map/ppermute | solution.py:99
  31.5 7.2 %collective-permute-start.10 = (f32[256]{0:T(256)S(1)}, f32[256]{0:T(256)S(1)}, u32[]{:S(2)}, u32[]{:S(2)}) collective-permute-start(f32[256]{0:T(256)S(1)} %fusion.4), channel_id=1, source_target_pairs={{0,4},{2,6},{4,8},{6,10},{8,12},{10,14},{12,0},{14,2},{1,5},{3,7},... | collective-permute-start | bytes 3080 | tf_op jit(solution)/shard_map/ppermute | solution.py:116
  31.8 6.9 %collective-permute-start.8 = (f32[256]{0:T(256)S(1)}, f32[256]{0:T(256)S(1)}, u32[]{:S(2)}, u32[]{:S(2)}) collective-permute-start(f32[256]{0:T(256)S(1)} %fusion.4), channel_id=1, source_target_pairs={{0,12},{2,14},{4,0},{6,2},{8,4},{10,6},{12,8},{14,10},{1,13},{3,15... | collective-permute-start | bytes 3080 | tf_op jit(solution)/shard_map/ppermute | solution.py:116
  35.4 4.5 %collective-permute-start.9 = (f32[256]{0:T(256)S(1)}, f32[256]{0:T(256)S(1)}, u32[]{:S(2)}, u32[]{:S(2)}) collective-permute-start(f32[256]{0:T(256)S(1)} %fusion.4), channel_id=1, source_target_pairs={{0,8},{2,10},{4,12},{6,14},{8,0},{10,2},{12,4},{14,6},{1,9},{3,11}... | collective-permute-start | bytes 3080 | tf_op jit(solution)/shard_map/ppermute | solution.py:116
  38.2 2.2 %collective-permute-start.7 = (bf16[2,4,1,64,256]{4,3,1,2,0:T(8,128)(2,1)S(1)}, bf16[2,4,1,64,256]{4,3,1,2,0:T(8,128)(2,1)S(1)}, u32[]{:S(2)}, u32[]{:S(2)}) collective-permute-start(bf16[2,4,1,64,256]{4,3,1,2,0:T(8,128)(2,1)S(1)} %pad_maximum_fusion), channel_id=1, source_target_pairs={{0,1},{1,0},{2,3},{3,2},{4,5},{5,4},{6,7},{7,6},{8,9},{9,8},{10,11... | collective-permute-start | bytes 786440 | tf_op jit(solution)/shard_map/ppermute | solution.py:86
  (39 other events, 130.9 us)

commit v18 on v16

--- a/solution.py
+++ b/solution.py
@@ -92,7 +92,7 @@
     return results
 
 
-def cyclic_carries(fwd_end, bwd_start, fwd_prod, bwd_prod, axis, index, count, route):
+def shifted_carries(fwd_end, bwd_start, fwd_prod, bwd_prod, axis, index, count, route):
     received = {}
     for step in range(1, count):
         message = jnp.where(index + step < count, fwd_end, bwd_start)
@@ -107,6 +107,32 @@
         source = index + step
         factor = lax.dynamic_index_in_dim(bwd_prod, jnp.minimum(source, count - 1), 0, keepdims=False)
         carry_back = jnp.where(source < count, received[count - step], 0.0) + factor * carry_back
+    return carry_in, carry_back
+
+
+def cyclic_carries(fwd_end, bwd_start, fwd_prod, bwd_prod, axis, index, count, route, partner=None):
+    if partner is None or count & (count - 1):
+        return shifted_carries(fwd_end, bwd_start, fwd_prod, bwd_prod, axis, index, count, route)
+    received = {}
+    for step in range(1, count):
+        message = jnp.where((index ^ step) > index, fwd_end, bwd_start)
+        received[step] = lax.ppermute(message, axis, partner(step))
+
+    def from_group(other):
+        step = index ^ other
+        picked = received[1]
+        for candidate in range(2, count):
+            picked = jnp.where(step == candidate, received[candidate], picked)
+        return picked
+
+    carry_in = jnp.zeros_like(fwd_end)
+    for other in range(count - 1):
+        factor = lax.dynamic_index_in_dim(fwd_prod, other, 0, keepdims=False)
+        carry_in = jnp.where(other < index, from_group(other) + factor * carry_in, carry_in)
+    carry_back = jnp.zeros_like(bwd_start)
+    for other in reversed(range(1, count)):
+        factor = lax.dynamic_index_in_dim(bwd_prod, other, 0, keepdims=False)
+        carry_back = jnp.where(other > index, from_group(other) + factor * carry_back, carry_back)
     return carry_in, carry_back
 
 
@@ -205,7 +231,8 @@
         ]
 
     carry_in, carry_back = cyclic_carries(
-        local_states[-1], back_states[0], fwd_prod, bwd_prod, "tm", group, groups, route
+        local_states[-1], back_states[0], fwd_prod, bwd_prod, "tm", group, groups, route,
+        lambda step: route(step, False),
     )
 
     states = jnp.stack([local_states[t] + products[t] * carry_in for t in range(span)])

time: 39.1 us -> 53.7 us (1.37); the launches traced: 38.9 us -> 52.8 us
  other arithmetic: 6.99 us -> 23.4 us
  waiting for transfers between devices: 9.94 us -> 7.36 us
  starting transfers between devices: 11.9 us -> 10.7 us
  local copies, waits for them, and re-layouts: 3.47 us -> 4.23 us
    unnamed x14 -> x15, other arithmetic: 0.95 us -> 11.6 us
    ppermute x1, waiting for transfers between devices: 2.18 us -> 0.01 us  [local(): got = lax.ppermute(jnp.where(first, frames_in, out_grad), 'tm', swap)]
    ppermute x1, waiting for transfers between devices: 1.85 us -> 0.01 us  [local(): traded = lax.ppermute(got, 'chan', [(0, 1), (1, 0)])]
    ppermute x3, waiting for transfers between devices: 0.46 us -> 1.93 us  [group_sum(): lax.ppermute(value, axis, route(step))]
    select_n x2, other arithmetic: 0.12 us -> 1.47 us  [cyclic_carries(): message = jnp.where(index ^ step > index, fwd_end, bwd_start)]
    dynamic_slice x2, other arithmetic: 0.01 us -> 1.19 us  [the longest x1 0.6 us: cyclic_carries(): factor = lax.dynamic_index_in_dim(bwd_prod, other, 0, keepdims=False)]
    select_n x1, other arithmetic: 1.71 us -> 0.99 us  [local(): got = lax.ppermute(jnp.where(first, frames_in, out_grad), 'tm', swap)]
    ppermute x3, starting transfers between devices: 3.91 us -> 3.2 us  [group_sum(): lax.ppermute(value, axis, route(step))]
  transfers between devices with their start and end apart: 9 -> 9, of which waited for: 7 -> 4; matrix products, arithmetic and copies ran while one was open for 20% -> 24% of each run, Pallas kernels for 0% -> 0%
where the time goes in v18:
time: 53.7 us; the launch traced here: 52.8 us
  other arithmetic  23.4 us (44%)
  starting transfers between devices  10.7 us (20%)
  waiting for transfers between devices  7.36 us (14%)
  matrix products  5.44 us (10%)
  local copies, waits for them, and re-layouts  4.23 us (8%)
  between operations  1.7 us (3%)
    unnamed x15, other arithmetic  11.6 us
    dot_general x24, matrix products, conv_apply(): jnp.dot(portion.reshape(-1, channels), taps[index, col_tap], preferred_el...  5.44 us
    ppermute x3, waiting for transfers between devices, cyclic_carries(): received[step] = lax.ppermute(message, axis, partner(step))  5.43 us
    ppermute x3, starting transfers between devices, cyclic_carries(): received[step] = lax.ppermute(message, axis, partner(step))  4.39 us
    ppermute x3, starting transfers between devices, group_sum(): lax.ppermute(value, axis, route(step))  3.2 us
    ppermute x1, starting transfers between devices, local(): got = lax.ppermute(jnp.where(first, frames_in, out_grad), 'tm', swap)  3 us
    ppermute x3, waiting for transfers between devices, group_sum(): lax.ppermute(value, axis, route(step))  1.93 us
    select_n x2, other arithmetic, cyclic_carries(): message = jnp.where(index ^ step > index, fwd_end, bwd_start)  1.47 us
  transfers between devices with their start and end apart: 9, of which 4 were waited for; matrix products, arithmetic and copies ran while one was open for 24% of the time, Pallas kernels for 0%

profile of v18, /device:TPU:0, one launch (start us, length us, event | category | flops | bytes accessed | tf_op | source)
XLA Modules:
  0.0 52.8 jit_solution(10004327525910190832)
XLA Ops:
  0.6 1.0 %broadcast_select_fusion.2 = bf16[4,1,64,512]{3,2,1,0:T(8,128)(2,1)S(1)} fusion(bf16[4,1,64,512]{3,2,1,0:T(8,128)(2,1)} %param.6, bf16[4,1,64,512]{3,2,1,0:T(8,128)(2,1)} %param.11, pred[]{:T(512)S(6)} %eq.77), kind=kLoop, calls=%fused_computation.53 | loop fusion | flops 131072 | bytes 786433 | tf_op jit(solution)/shard_map/jit(_where)/select_n | solution.py:169
  1.6 3.0 %collective-permute-start = (bf16[4,1,64,512]{3,2,1,0:T(8,128)(2,1)S(1)}, bf16[4,1,64,512]{3,2,1,0:T(8,128)(2,1)S(1)}, u32[]{:S(2)}, u32[]{:S(2)}) collective-permute-start(bf16[4,1,64,512]{3,2,1,0:T(8,128)(2,1)S(1)} %broadcast_select_fusion.2), channel_id=1, source_target_pairs={{0,2},{2,0},{4,6},{6,4},{8,10},{10,8},{12,14},{14,12},{1,3},{3,1},... | collective-permute-start | bytes 786440 | tf_op jit(solution)/shard_map/ppermute | solution.py:169
  6.3 0.8 %broadcast_multiply_fusion = (f32[4,8,256]{2,1,0:T(8,128)S(1)}, f32[4,8,256]{2,1,0:T(8,128)S(1)}) fusion(f32[4,8]{1,0:T(4,128)S(1)} %mul.911, f32[256]{0:T(256)} %param.9, f32[4,8]{1,0:T(4,128)S(1)} %mul.865), kind=kLoop, calls=%fused_computation.158 | loop fusion | flops 16384 | bytes 66816 | tf_op jit(solution)/shard_map/mul | solution.py:218
  9.3 1.3 %multiply_divide_fusion = (f32[256]{0:T(256)}, f32[256]{0:T(256)S(1)}) fusion(f32[256]{0:T(256)} %param.9), kind=kLoop, calls=%fused_computation.192 | loop fusion | flops 768 | bytes 3072 | tf_op jit(solution)/shard_map/div | solution.py:242
  10.5 1.2 %slice.352 = bf16[1,3,256,512]{3,2,1,0:T(8,128)(2,1)S(1)} slice(bf16[3,3,256,512]{3,2,1,0:T(8,128)(2,1)} %param.8), slice={[1:2], [0:3], [0:256], [0:512]} | slice | bytes 1572864 | tf_op jit(solution)/shard_map/slice | solution.py:28
  12.7 1.2 %slice.332 = bf16[1,3,512,256]{3,2,1,0:T(8,128)(2,1)S(1)} slice(bf16[3,3,512,256]{3,2,1,0:T(8,128)(2,1)} %param.7), slice={[1:2], [0:3], [0:512], [0:256]} | slice | bytes 1572864 | tf_op jit(solution)/shard_map/slice | solution.py:31
  14.6 1.1 %broadcast_select_fusion.6 = (bf16[4,1,64,512]{3,2,1,0:T(8,128)(2,1)S(1)}, bf16[4,1,64,512]{3,2,1,0:T(8,128)(2,1)S(1)}, bf16[4,1,64,512]{3,2,1,0:T(8,128)(2,1)S(1)}, bf16[4,1,64,512]{3,2,1,0:T(8,128)(2,1)S(1)}) fusion(bf16[4,1,64,512]{3,2,1,0:T(8,128)(2,1)S(1)} %copy-done, pred[]{:T(512)S(6)} %eq.76, bf16[4,1,64,512]{3,2,1,0:T(8,128)(2,1)} %copy-done.5, ...), kind=kLoop, calls=%fused_computation.57 | loop fusion | flops 786432 | bytes 2097154 | tf_op jit(solution)/shard_map/jit(_where)/select_n | solution.py:176
  20.9 3.6 %collective-permute-start.2 = (f32[1,64,256]{2,1,0:T(8,128)}, f32[1,64,256]{2,1,0:T(8,128)}, u32[]{:S(2)}, u32[]{:S(2)}) collective-permute-start(f32[1,64,256]{2,1,0:T(8,128)} %get-tuple-element.81), channel_id=1, source_target_pairs={{0,12},{2,14},{4,8},{6,10},{8,4},{10,6},{12,0},{14,2},{1,13},{3,15... | collective-permute-start | bytes 196616 | tf_op jit(solution)/shard_map/ppermute | solution.py:119
  24.5 0.8 %collective-permute-start.4 = (f32[1,64,256]{2,1,0:T(8,128)}, f32[1,64,256]{2,1,0:T(8,128)}, u32[]{:S(2)}, u32[]{:S(2)}) collective-permute-start(f32[1,64,256]{2,1,0:T(8,128)} %get-tuple-element.53), channel_id=1, source_target_pairs={{0,4},{2,6},{4,0},{6,2},{8,12},{10,14},{12,8},{14,10},{1,5},{3,7},... | collective-permute-start | bytes 196616 | tf_op jit(solution)/shard_map/ppermute | solution.py:119
  25.5 2.3 %collective-permute-done.2 = f32[1,64,256]{2,1,0:T(8,128)} collective-permute-done((f32[1,64,256]{2,1,0:T(8,128)}, f32[1,64,256]{2,1,0:T(8,128)}, u32[]{:S(2)}, u32[]{:S(2)}) %collective-permute-start.2) | collective-permute-done | bytes 65568 | tf_op jit(solution)/shard_map/ppermute | solution.py:119
  27.8 3.2 %collective-permute-done.3 = f32[1,64,256]{2,1,0:T(8,128)} collective-permute-done((f32[1,64,256]{2,1,0:T(8,128)}, f32[1,64,256]{2,1,0:T(8,128)}, u32[]{:S(2)}, u32[]{:S(2)}) %collective-permute-start.3) | collective-permute-done | bytes 65568 | tf_op jit(solution)/shard_map/ppermute | solution.py:119
  30.9 1.0 %constant_dynamic-update-slice_fusion.7 = (f32[8,1,64,256]{3,2,1,0:T(8,128)S(1)}, bf16[1,1,64,256]{3,2,1,0:T(8,128)(2,1)S(1)}, f32[1,64,256]{2,1,0:T(8,128)S(1)}) fusion(f32[256]{0:T(256)} %get-tuple-element.39, f32[64,256]{1,0:T(8,128)} %copy-done.4, f32[256]{0:T(256)} %bitcast.359, f32[1,64,256]{2,1,0:T(8,128)} %collective-permute-done.2, ...), kind=kLoop, calls=%fused_computation.150 | loop fusion | flops 278527 | bytes 430089
  31.9 0.9 %constant_dynamic-update-slice_fusion.6 = (f32[8,1,64,256]{3,2,1,0:T(8,128)S(1)}, bf16[1,1,64,256]{3,2,1,0:T(8,128)(2,1)S(1)}) fusion(f32[8,1,64,256]{3,2,1,0:T(8,128)S(1)} %get-tuple-element.36, f32[1,64,256]{2,1,0:T(8,128)S(1)} %get-tuple-element.38, f32[256]{0:T(256)} %get-tuple-element.40, f32[64,256]{1,0:T(8,128)} %get-tuple-element.55, ...), kind=kLoop, calls=%fused_computation.149 | loop fusion | flops 81920 | bytes 296960
  32.8 0.9 %constant_dynamic-update-slice_fusion.5 = (f32[8,1,64,256]{3,2,1,0:T(8,128)S(1)}, bf16[1,1,64,256]{3,2,1,0:T(8,128)(2,1)S(1)}) fusion(f32[8,1,64,256]{3,2,1,0:T(8,128)S(1)} %get-tuple-element.34, f32[1,64,256]{2,1,0:T(8,128)S(1)} %get-tuple-element.38, f32[256]{0:T(256)} %get-tuple-element.41, f32[64,256]{1,0:T(8,128)} %get-tuple-element.55), kind=kLoop, calls=%fused_computation.148 | loop fusion | flops 49152 | bytes 230400
  33.6 0.9 %constant_dynamic-update-slice_fusion.4 = (f32[8,1,64,256]{3,2,1,0:T(8,128)S(1)}, bf16[1,1,64,256]{3,2,1,0:T(8,128)(2,1)S(1)}) fusion(f32[8,1,64,256]{3,2,1,0:T(8,128)S(1)} %get-tuple-element.32, f32[1,64,256]{2,1,0:T(8,128)S(1)} %get-tuple-element.38, f32[256]{0:T(256)} %get-tuple-element.42, f32[64,256]{1,0:T(8,128)} %get-tuple-element.56, ...), kind=kLoop, calls=%fused_computation.147 | loop fusion | flops 81920 | bytes 296960
  34.5 0.9 %constant_dynamic-update-slice_fusion.3 = (f32[8,1,64,256]{3,2,1,0:T(8,128)S(1)}, bf16[1,1,64,256]{3,2,1,0:T(8,128)(2,1)S(1)}) fusion(f32[8,1,64,256]{3,2,1,0:T(8,128)S(1)} %get-tuple-element.30, f32[1,64,256]{2,1,0:T(8,128)S(1)} %get-tuple-element.38, f32[256]{0:T(256)} %get-tuple-element.43, f32[64,256]{1,0:T(8,128)} %get-tuple-element.56), kind=kLoop, calls=%fused_computation.146 | loop fusion | flops 49152 | bytes 230400
  35.4 0.9 %constant_dynamic-update-slice_fusion.2 = (f32[8,1,64,256]{3,2,1,0:T(8,128)S(1)}, bf16[1,1,64,256]{3,2,1,0:T(8,128)(2,1)S(1)}) fusion(f32[8,1,64,256]{3,2,1,0:T(8,128)S(1)} %get-tuple-element.28, f32[1,64,256]{2,1,0:T(8,128)S(1)} %get-tuple-element.38, f32[256]{0:T(256)} %get-tuple-element.44, f32[64,256]{1,0:T(8,128)} %get-tuple-element.57, ...), kind=kLoop, calls=%fused_computation.145 | loop fusion | flops 81920 | bytes 296960
  36.2 0.9 %constant_dynamic-update-slice_fusion.1 = (f32[8,1,64,256]{3,2,1,0:T(8,128)S(1)}, bf16[1,1,64,256]{3,2,1,0:T(8,128)(2,1)S(1)}) fusion(f32[8,1,64,256]{3,2,1,0:T(8,128)S(1)} %get-tuple-element.26, f32[1,64,256]{2,1,0:T(8,128)S(1)} %get-tuple-element.38, f32[256]{0:T(256)} %get-tuple-element.45, f32[64,256]{1,0:T(8,128)} %get-tuple-element.57), kind=kLoop, calls=%fused_computation.144 | loop fusion | flops 49152 | bytes 230400
  37.8 1.0 %bitcast_dynamic-update-slice_fusion = (f32[8,1,64,256]{3,2,1,0:T(8,128)S(1)}, f32[1,64,256]{2,1,0:T(8,128)S(1)}) fusion(f32[256]{0:T(256)} %bitcast.356, f32[1,64,256]{2,1,0:T(8,128)} %collective-permute-done.2, f32[1,64,256]{2,1,0:T(8,128)} %collective-permute-done.3, f32[1,64,256]{2,1,0:T(8,128)} %collective-permute-done.4, pred[]{:T(512)S(6)} %eq.83, ...), kind=kLoop, calls=%fused_computation.103 | loop fusion | flops 229375 | bytes 330761
  39.5 0.9 %constant_dynamic-update-slice_fusion.13 = (f32[8,1,64,256]{3,2,1,0:T(8,128)S(1)}, bf16[1,1,64,256]{3,2,1,0:T(8,128)(2,1)S(1)}) fusion(f32[8,1,64,256]{3,2,1,0:T(8,128)S(1)} %get-tuple-element.18, f32[1,64,256]{2,1,0:T(8,128)S(1)} %get-tuple-element.21, f32[256]{0:T(256)} %get-tuple-element.52, f32[64,256]{1,0:T(8,128)} %get-tuple-element.61), kind=kLoop, calls=%fused_computation.156 | loop fusion | flops 49152 | bytes 230400
  40.3 0.9 %constant_dynamic-update-slice_fusion.12 = (f32[8,1,64,256]{3,2,1,0:T(8,128)S(1)}, bf16[1,1,64,256]{3,2,1,0:T(8,128)(2,1)S(1)}) fusion(f32[8,1,64,256]{3,2,1,0:T(8,128)S(1)} %get-tuple-element.16, f32[1,64,256]{2,1,0:T(8,128)S(1)} %get-tuple-element.21, f32[256]{0:T(256)} %get-tuple-element.51, f32[256,256]{1,0:T(8,128)S(1)} %convolution_add_fusion.14, ...), kind=kLoop, calls=%fused_computation.155 | loop fusion | flops 98304 | bytes 297984
  42.8 2.5 %collective-permute-start.6 = (f32[256]{0:T(256)S(1)}, f32[256]{0:T(256)S(1)}, u32[]{:S(2)}, u32[]{:S(2)}) collective-permute-start(f32[256]{0:T(256)S(1)} %fusion.4), channel_id=1, source_target_pairs={{0,12},{2,14},{4,0},{6,2},{8,4},{10,6},{12,8},{14,10},{1,13},{3,15... | collective-permute-start | bytes 3080 | tf_op jit(solution)/shard_map/ppermute | solution.py:142
  49.0 0.8 %collective-permute-done.7 = f32[256]{0:T(256)S(1)} collective-permute-done((f32[256]{0:T(256)S(1)}, f32[256]{0:T(256)S(1)}, u32[]{:S(2)}, u32[]{:S(2)}) %collective-permute-start.7) | collective-permute-done | bytes 1056 | tf_op jit(solution)/shard_map/ppermute | solution.py:142
  49.8 1.1 %collective-permute-done.8 = f32[256]{0:T(256)S(1)} collective-permute-done((f32[256]{0:T(256)S(1)}, f32[256]{0:T(256)S(1)}, u32[]{:S(2)}, u32[]{:S(2)}) %collective-permute-start.8) | collective-permute-done | bytes 1056 | tf_op jit(solution)/shard_map/ppermute | solution.py:142
  (144 shorter events, 18.5 us)
Async XLA Ops:
  1.6 10.8 %collective-permute-start = (bf16[4,1,64,512]{3,2,1,0:T(8,128)(2,1)S(1)}, bf16[4,1,64,512]{3,2,1,0:T(8,128)(2,1)S(1)}, u32[]{:S(2)}, u32[]{:S(2)}) collective-permute-start(bf16[4,1,64,512]{3,2,1,0:T(8,128)(2,1)S(1)} %broadcast_select_fusion.2), channel_id=1, source_target_pairs={{0,2},{2,0},{4,6},{6,4},{8,10},{10,8},{12,14},{14,12},{1,3},{3,1},... | collective-permute-start | bytes 786440 | tf_op jit(solution)/shard_map/ppermute | solution.py:169
  9.2 4.7 %copy-start.6 = (f32[1,256]{1,0:T(1,128)}, f32[1,256]{1,0:T(1,128)S(1)}, u32[]{:S(2)}) copy-start(f32[1,256]{1,0:T(1,128)S(1)} %get-tuple-element.112) | copy-start | bytes 3076
  9.2 4.7 %copy-start.8 = (f32[1,256]{1,0:T(1,128)}, f32[1,256]{1,0:T(1,128)S(1)}, u32[]{:S(2)}) copy-start(f32[1,256]{1,0:T(1,128)S(1)} %get-tuple-element.114) | copy-start | bytes 3076
  9.2 4.7 %copy-start.16 = (f32[1,256]{1,0:T(1,128)}, f32[1,256]{1,0:T(1,128)S(1)}, u32[]{:S(2)}) copy-start(f32[1,256]{1,0:T(1,128)S(1)} %get-tuple-element.119) | copy-start | bytes 3076
  9.2 4.7 %copy-start.26 = (f32[1,256]{1,0:T(1,128)}, f32[1,256]{1,0:T(1,128)S(1)}, u32[]{:S(2)}) copy-start(f32[1,256]{1,0:T(1,128)S(1)} %get-tuple-element.113) | copy-start | bytes 3076
  9.2 4.7 %copy-start.28 = (f32[1,256]{1,0:T(1,128)}, f32[1,256]{1,0:T(1,128)S(1)}, u32[]{:S(2)}) copy-start(f32[1,256]{1,0:T(1,128)S(1)} %get-tuple-element.115) | copy-start | bytes 3076
  9.2 4.7 %copy-start.30 = (f32[1,256]{1,0:T(1,128)}, f32[1,256]{1,0:T(1,128)S(1)}, u32[]{:S(2)}) copy-start(f32[1,256]{1,0:T(1,128)S(1)} %get-tuple-element.116) | copy-start | bytes 3076
  9.3 4.7 %copy-start.32 = (f32[1,256]{1,0:T(1,128)}, f32[1,256]{1,0:T(1,128)S(1)}, u32[]{:S(2)}) copy-start(f32[1,256]{1,0:T(1,128)S(1)} %get-tuple-element.118) | copy-start | bytes 3076
  10.5 4.0 %copy-start.1 = (bf16[4,1,64,512]{3,2,1,0:T(8,128)(2,1)S(1)}, bf16[4,1,64,512]{3,2,1,0:T(8,128)(2,1)}, u32[]{:S(2)}) copy-start(bf16[4,1,64,512]{3,2,1,0:T(8,128)(2,1)} %param.11) | copy-start | bytes 786436
  12.5 2.1 %collective-permute-start.1 = (bf16[4,1,64,512]{3,2,1,0:T(8,128)(2,1)S(1)}, bf16[4,1,64,512]{3,2,1,0:T(8,128)(2,1)}, u32[]{:S(2)}, u32[]{:S(2)}) collective-permute-start(bf16[4,1,64,512]{3,2,1,0:T(8,128)(2,1)S(1)} %collective-permute-done), channel_id=1, source_target_pairs={{0,1},{1,0},{2,3},{3,2},{4,5},{5,4},{6,7},{7,6},{8,9},{9,8},{10,11... | collective-permute-start | bytes 786440 | tf_op jit(solution)/shard_map/ppermute | solution.py:170
  20.2 4.3 %copy-start.2 = (f32[64,256]{1,0:T(8,128)}, f32[64,256]{1,0:T(8,128)S(1)}, u32[]{:S(2)}) copy-start(f32[64,256]{1,0:T(8,128)S(1)} %get-tuple-element.58) | copy-start | bytes 196612
  20.2 5.1 %copy-start.4 = (f32[64,256]{1,0:T(8,128)}, f32[64,256]{1,0:T(8,128)S(1)}, u32[]{:S(2)}) copy-start(f32[64,256]{1,0:T(8,128)S(1)} %get-tuple-element.54) | copy-start | bytes 196612
  20.9 6.9 %collective-permute-start.2 = (f32[1,64,256]{2,1,0:T(8,128)}, f32[1,64,256]{2,1,0:T(8,128)}, u32[]{:S(2)}, u32[]{:S(2)}) collective-permute-start(f32[1,64,256]{2,1,0:T(8,128)} %get-tuple-element.81), channel_id=1, source_target_pairs={{0,12},{2,14},{4,8},{6,10},{8,4},{10,6},{12,0},{14,2},{1,13},{3,15... | collective-permute-start | bytes 196616 | tf_op jit(solution)/shard_map/ppermute | solution.py:119
  24.5 6.4 %collective-permute-start.3 = (f32[1,64,256]{2,1,0:T(8,128)}, f32[1,64,256]{2,1,0:T(8,128)}, u32[]{:S(2)}, u32[]{:S(2)}) collective-permute-start(f32[1,64,256]{2,1,0:T(8,128)} %get-tuple-element.80), channel_id=1, source_target_pairs={{0,8},{2,10},{4,12},{6,14},{8,0},{10,2},{12,4},{14,6},{1,9},{3,11}... | collective-permute-start | bytes 196616 | tf_op jit(solution)/shard_map/ppermute | solution.py:119
  24.5 6.4 %collective-permute-start.4 = (f32[1,64,256]{2,1,0:T(8,128)}, f32[1,64,256]{2,1,0:T(8,128)}, u32[]{:S(2)}, u32[]{:S(2)}) collective-permute-start(f32[1,64,256]{2,1,0:T(8,128)} %get-tuple-element.53), channel_id=1, source_target_pairs={{0,4},{2,6},{4,0},{6,2},{8,12},{10,14},{12,8},{14,10},{1,5},{3,7},... | collective-permute-start | bytes 196616 | tf_op jit(solution)/shard_map/ppermute | solution.py:119
  25.3 17.2 %copy-start.37 = (f32[256]{0:T(256)S(1)}, f32[256]{0:T(256)}, u32[]{:S(2)}) copy-start(f32[256]{0:T(256)} %get-tuple-element.48) | copy-start | bytes 3076
  25.3 17.3 %copy-start.36 = (f32[256]{0:T(256)S(1)}, f32[256]{0:T(256)}, u32[]{:S(2)}) copy-start(f32[256]{0:T(256)} %get-tuple-element.47) | copy-start | bytes 3076
  25.4 17.3 %copy-start.34 = (f32[256]{0:T(256)S(1)}, f32[256]{0:T(256)}, u32[]{:S(2)}) copy-start(f32[256]{0:T(256)} %get-tuple-element.104) | copy-start | bytes 3076
  37.1 9.0 %copy-start.3 = (f32[64,256]{1,0:T(8,128)S(1)}, f32[64,256]{1,0:T(8,128)}, u32[]{:S(2)}) copy-start(f32[64,256]{1,0:T(8,128)} %copy-done.2) | copy-start | bytes 196612
  37.1 9.0 %copy-start.35 = (f32[256]{0:T(256)S(1)}, f32[256]{0:T(256)}, u32[]{:S(2)}) copy-start(f32[256]{0:T(256)} %get-tuple-element.46) | copy-start | bytes 3076
  42.8 6.2 %collective-permute-start.6 = (f32[256]{0:T(256)S(1)}, f32[256]{0:T(256)S(1)}, u32[]{:S(2)}, u32[]{:S(2)}) collective-permute-start(f32[256]{0:T(256)S(1)} %fusion.4), channel_id=1, source_target_pairs={{0,12},{2,14},{4,0},{6,2},{8,4},{10,6},{12,8},{14,10},{1,13},{3,15... | collective-permute-start | bytes 3080 | tf_op jit(solution)/shard_map/ppermute | solution.py:142
  45.3 4.5 %collective-permute-start.7 = (f32[256]{0:T(256)S(1)}, f32[256]{0:T(256)S(1)}, u32[]{:S(2)}, u32[]{:S(2)}) collective-permute-start(f32[256]{0:T(256)S(1)} %fusion.4), channel_id=1, source_target_pairs={{0,8},{2,10},{4,12},{6,14},{8,0},{10,2},{12,4},{14,6},{1,9},{3,11}... | collective-permute-start | bytes 3080 | tf_op jit(solution)/shard_map/ppermute | solution.py:142
  45.5 5.4 %collective-permute-start.8 = (f32[256]{0:T(256)S(1)}, f32[256]{0:T(256)S(1)}, u32[]{:S(2)}, u32[]{:S(2)}) collective-permute-start(f32[256]{0:T(256)S(1)} %fusion.4), channel_id=1, source_target_pairs={{0,4},{2,6},{4,8},{6,10},{8,12},{10,14},{12,0},{14,2},{1,5},{3,7},... | collective-permute-start | bytes 3080 | tf_op jit(solution)/shard_map/ppermute | solution.py:142
  48.5 3.0 %collective-permute-start.5 = (bf16[2,4,1,64,256]{4,3,1,2,0:T(8,128)(2,1)S(1)}, bf16[2,4,1,64,256]{4,3,1,2,0:T(8,128)(2,1)S(1)}, u32[]{:S(2)}, u32[]{:S(2)}) collective-permute-start(bf16[2,4,1,64,256]{4,3,1,2,0:T(8,128)(2,1)S(1)} %pad_maximum_fusion), channel_id=1, source_target_pairs={{0,1},{1,0},{2,3},{3,2},{4,5},{5,4},{6,7},{7,6},{8,9},{9,8},{10,11... | collective-permute-start | bytes 786440 | tf_op jit(solution)/shard_map/ppermute | solution.py:86
  (23 other events, 48.2 us)

commit v19 on v16

--- a/solution.py
+++ b/solution.py
@@ -147,8 +147,8 @@
         else:
             other_frames = lax.ppermute(frames_in, "tm", swap)
             other_grad = lax.ppermute(out_grad, "tm", swap)
-        frame_blocks = [jnp.where(upper, other_frames, frames_in), jnp.where(upper, frames_in, other_frames)]
-        grad_blocks = [jnp.where(upper, other_grad, out_grad), jnp.where(upper, out_grad, other_grad)]
+        frame_blocks = [frames_in, other_frames]
+        grad_blocks = [out_grad, other_grad]
     else:
         frame_blocks = [frames_in]
         grad_blocks = [out_grad]
@@ -156,12 +156,16 @@
     row_taps = row_taps_of(row_halo(frames_in), row_count)
     in_taps = prep_kernel(in_kernel, False, row_taps)
     adjoint_taps = prep_kernel(out_kernel, True, row_taps)
-    values = jnp.concatenate(
-        [conv_apply(block, row_halo(block), in_taps, row_taps) for block in frame_blocks]
-    )
-    adjoint_in = jnp.concatenate(
-        [conv_apply(block, row_halo(block), adjoint_taps, row_taps) for block in grad_blocks]
-    )
+
+    def in_clip_order(parts):
+        if width == 1:
+            return parts[0]
+        return jnp.concatenate(
+            [jnp.where(upper, parts[1], parts[0]), jnp.where(upper, parts[0], parts[1])]
+        )
+
+    values = in_clip_order([conv_apply(b, row_halo(b), in_taps, row_taps) for b in frame_blocks])
+    adjoint_in = in_clip_order([conv_apply(b, row_halo(b), adjoint_taps, row_taps) for b in grad_blocks])
     input_gain = jnp.sqrt(1.0 - decay_rate * decay_rate)
     keep_padded = jnp.concatenate([frame_keep, jnp.zeros((1,), jnp.float32)])
     offset = group * span

time: 39.1 us -> 40.3 us (1.031)
  waiting for transfers between devices: 9.94 us -> 6.42 us
  matrix products: 5.42 us -> 8.87 us
  other arithmetic: 6.99 us -> 7.92 us
  local copies, waits for them, and re-layouts: 3.47 us -> 3.88 us
    dot_general x24, matrix products: 5.42 us -> 8.87 us  [conv_apply(): jnp.dot(portion.reshape(-1, channels), taps[index, col_tap], preferred_el...]
    slice x0 -> x1, other arithmetic: none -> 2.69 us  [conv_apply(): padded[:, row_tap:row_tap + row_count, col_tap:col_tap + col_count, :]]
    ppermute x1, waiting for transfers between devices: 2.18 us -> 0.01 us  [local(): got = lax.ppermute(jnp.where(first, frames_in, out_grad), 'tm', swap)]
    select_n x2 -> x1, other arithmetic: 2.89 us -> 1.07 us  [local(): other_frames = jnp.where(first, got, traded)]
    ppermute x1, waiting for transfers between devices: 1.85 us -> 0.51 us  [local(): traded = lax.ppermute(got, 'chan', [(0, 1), (1, 0)])]
    concatenate x1, other arithmetic: 0.07 us -> 0.73 us  [local(): keep_padded = jnp.concatenate([frame_keep, jnp.zeros((1,), jnp.float32)])]
    mul x1, local copies, waits for them, and re-layouts: 0.08 us -> 0.74 us  [local(): frame_keep[:, None] * decay_rate[None, :]]
    div x1, other arithmetic: 0.58 us -> 0.01 us  [local(): decay_rate * decay_rate / input_gain * values]
  transfers between devices with their start and end apart: 9 -> 9, of which waited for: 7 -> 6; matrix products, arithmetic and copies ran while one was open for 20% -> 32% of each run, Pallas kernels for 0% -> 0%
where the time goes in v19:
time: 40.3 us; the launch traced here: 40 us
  starting transfers between devices  11.6 us (29%)
  matrix products  8.87 us (22%)
  other arithmetic  7.92 us (20%)
  waiting for transfers between devices  6.42 us (16%)
  local copies, waits for them, and re-layouts  3.88 us (10%)
  between operations  1.3 us (3%)
    dot_general x24, matrix products, conv_apply(): jnp.dot(portion.reshape(-1, channels), taps[index, col_tap], preferred_el...  8.87 us
    ppermute x3, waiting for transfers between devices, cyclic_carries(): received[step] = lax.ppermute(message, axis, route(step))  5.38 us
    ppermute x3, starting transfers between devices, cyclic_carries(): received[step] = lax.ppermute(message, axis, route(step))  4.67 us
    ppermute x3, starting transfers between devices, group_sum(): lax.ppermute(value, axis, route(step))  3.91 us
    ppermute x1, starting transfers between devices, local(): got = lax.ppermute(jnp.where(first, frames_in, out_grad), 'tm', swap)  2.94 us
    slice x1, other arithmetic, conv_apply(): padded[:, row_tap:row_tap + row_count, col_tap:col_tap + col_count, :]  2.69 us
    slice x1, local copies, waits for them, and re-layouts, prep_kernel(): taps = jnp.stack([flipped[a] for a in row_taps])  1.23 us
    slice x1, local copies, waits for them, and re-layouts, prep_kernel(): taps = jnp.stack([kernel[a] for a in row_taps])  1.2 us
  transfers between devices with their start and end apart: 9, of which 6 were waited for; matrix products, arithmetic and copies ran while one was open for 32% of the time, Pallas kernels for 0%

profile of v19, /device:TPU:0, one launch (start us, length us, event | category | flops | bytes accessed | tf_op | source)
XLA Modules:
  0.0 40.0 jit_solution(9442273292887400389)
XLA Ops:
  0.6 2.7 %pad_slice_fusion.5 = (bf16[4,1,64,512]{3,2,1,0:T(8,128)(2,1)}, bf16[4,1,64,512]{3,2,1,0:T(8,128)(2,1)S(1)}, bf16[4,1,64,512]{3,2,1,0:T(8,128)(2,1)}, bf16[4,1,6...) fusion(bf16[4,1,64,512]{3,2,1,0:T(8,128)(2,1)} %param.6, bf16[4,1,64,512]{3,2,1,0:T(8,128)(2,1)} %param.11, pred[]{:T(512)S(6)} %eq.49), kind=kLoop, calls=%fused_computation.23 | loop fusion | flops 131072 | bytes 1835009 | tf_op jit(solution)/shard_map/slice | solution.py:48
  3.3 2.9 %collective-permute-start = (bf16[4,1,64,512]{3,2,1,0:T(8,128)(2,1)}, bf16[4,1,64,512]{3,2,1,0:T(8,128)(2,1)}, u32[]{:S(2)}, u32[]{:S(2)}) collective-permute-start(bf16[4,1,64,512]{3,2,1,0:T(8,128)(2,1)} %get-tuple-element.72), channel_id=1, source_target_pairs={{0,2},{2,0},{4,6},{6,4},{8,10},{10,8},{12,14},{14,12},{1,3},{3,1},... | collective-permute-start | bytes 786440 | tf_op jit(solution)/shard_map/ppermute | solution.py:143
  6.3 0.7 %mul.1561 = f32[4,8]{1,0:T(4,128)S(1)} reshape(f32[32]{0:T(128)} %param.10) | data formatting | bytes 256 | tf_op jit(solution)/shard_map/mul | solution.py:195
  7.0 0.7 %pad_maximum_fusion.1 = f32[33]{0:T(128)S(1)} fusion(f32[1]{0:T(128)} %constant.86.clone.1, f32[32]{0:T(128)} %param.10), kind=kLoop, calls=%fused_computation.197 | loop fusion | flops 33 | bytes 264 | tf_op jit(solution)/shard_map/concatenate | solution.py:170
  7.7 1.2 %slice.326 = bf16[1,3,512,256]{3,2,1,0:T(8,128)(2,1)S(1)} slice(bf16[3,3,512,256]{3,2,1,0:T(8,128)(2,1)} %param.7), slice={[1:2], [0:3], [0:512], [0:256]} | slice | bytes 1572864 | tf_op jit(solution)/shard_map/slice | solution.py:31
  9.0 1.2 %slice.346 = bf16[1,3,256,512]{3,2,1,0:T(8,128)(2,1)S(1)} slice(bf16[3,3,256,512]{3,2,1,0:T(8,128)(2,1)} %param.8), slice={[1:2], [0:3], [0:256], [0:512]} | slice | bytes 1572864 | tf_op jit(solution)/shard_map/slice | solution.py:28
  10.8 0.9 %convolution_add_fusion.13 = f32[256,256]{1,0:T(8,128)} fusion(f32[256,256]{1,0:T(8,128)S(1)} %fusion.9, bf16[256,512]{1,0:T(8,128)(2,1)S(1)} %bitcast.367, bf16[1,3,512,256]{3,2,1,0:T(8,128)(2,1)S(1)} %slice.326), kind=kOutput, calls=%fused_computation.13 | convolution fusion | flops 67174400 | bytes 1048576 | tf_op jit(solution)/shard_map/dot_general | solution.py:49
  12.2 0.6 %fusion.54 = (f32[256]{0:T(256)}, f32[256]{0:T(256)}, f32[256]{0:T(256)}, f32[256]{0:T(256)S(1)}, f32[256]{0:T(256)S(1)}, /*index=5*/f32[256]{0:T(256)S(1)}, f32[256]{0:T(256)S(1)}) fusion(f32[256]{0:T(256)S(1)} %bitcast.405, f32[256]{0:T(256)S(1)} %bitcast.392, f32[256]{0:T(256)S(1)} %bitcast.403, f32[256]{0:T(256)S(1)} %bitcast.389, f32[256]{0:T(256)S(1)} %bitcast.401, ...), kind=kLoop, calls=%fused_computation.198 | loop fusion | flops 1792 | bytes 15360 | tf_op jit(solution)/shard_map/mul | solution.py:191
  12.9 2.0 %convolution_add_fusion.12 = f32[256,256]{1,0:T(8,128)} fusion(f32[256,256]{1,0:T(8,128)} %convolution_add_fusion.13, bf16[256,512]{1,0:T(8,128)(2,1)} %bitcast.370, bf16[1,3,512,256]{3,2,1,0:T(8,128)(2,1)S(1)} %slice.326), kind=kOutput, calls=%fused_computation.12 | convolution fusion | flops 67174400 | bytes 1048576 | tf_op jit(solution)/shard_map/dot_general | solution.py:49
  15.0 1.2 %convolution_add_fusion.9 = f32[256,256]{1,0:T(8,128)S(1)} fusion(f32[256,256]{1,0:T(8,128)S(1)} %fusion.11, bf16[256,512]{1,0:T(8,128)(2,1)} %bitcast.368, bf16[1,3,512,256]{2,3,1,0:T(8,128)(2,1)S(1)} %reverse_bitcast_fusion.1), kind=kOutput, calls=%fused_computation.9 | convolution fusion | flops 67174400 | bytes 1048576 | tf_op jit(solution)/shard_map/dot_general | solution.py:49
  16.2 0.5 %collective-permute-done.1 = bf16[4,1,64,512]{3,2,1,0:T(8,128)(2,1)} collective-permute-done((bf16[4,1,64,512]{3,2,1,0:T(8,128)(2,1)}, bf16[4,1,64,512]{3,2,1,0:T(8,128)(2,1)}, u32[]{:S(2)}, u32[]{:S(2)}) %collective-permute-start.1) | collective-permute-done | bytes 262176 | tf_op jit(solution)/shard_map/ppermute | solution.py:144
  16.7 1.1 %broadcast_select_fusion.1 = (bf16[4,1,64,512]{3,2,1,0:T(8,128)(2,1)S(1)}, bf16[4,1,64,512]{3,2,1,0:T(8,128)(2,1)S(1)}) fusion(bf16[4,1,64,512]{3,2,1,0:T(8,128)(2,1)} %collective-permute-done, bf16[4,1,64,512]{3,2,1,0:T(8,128)(2,1)} %collective-permute-done.1, pred[]{:T(512)S(6)} %eq.49), kind=kLoop, calls=%fused_computation.52 | loop fusion | flops 262144 | bytes 1048577 | tf_op jit(solution)/shard_map/jit(_where)/select_n | solution.py:145
  20.0 2.6 %collective-permute-start.3 = (f32[1,64,256]{2,1,0:T(8,128)S(1)}, f32[1,64,256]{2,1,0:T(8,128)S(1)}, u32[]{:S(2)}, u32[]{:S(2)}) collective-permute-start(f32[1,64,256]{2,1,0:T(8,128)S(1)} %get-tuple-element.83), channel_id=1, source_target_pairs={{0,8},{2,10},{4,12},{6,14},{8,0},{10,2},{12,4},{14,6},{1,9},{3,11}... | collective-permute-start | bytes 196616 | tf_op jit(solution)/shard_map/ppermute | solution.py:99
  22.7 1.3 %collective-permute-start.4 = (f32[1,64,256]{2,1,0:T(8,128)S(1)}, f32[1,64,256]{2,1,0:T(8,128)S(1)}, u32[]{:S(2)}, u32[]{:S(2)}) collective-permute-start(f32[1,64,256]{2,1,0:T(8,128)S(1)} %get-tuple-element.84), channel_id=1, source_target_pairs={{0,12},{2,14},{4,0},{6,2},{8,4},{10,6},{12,8},{14,10},{1,13},{3,15... | collective-permute-start | bytes 196616 | tf_op jit(solution)/shard_map/ppermute | solution.py:99
  24.0 0.7 %collective-permute-start.2 = (f32[1,64,256]{2,1,0:T(8,128)S(1)}, f32[1,64,256]{2,1,0:T(8,128)S(1)}, u32[]{:S(2)}, u32[]{:S(2)}) collective-permute-start(f32[1,64,256]{2,1,0:T(8,128)S(1)} %get-tuple-element.53), channel_id=1, source_target_pairs={{0,4},{2,6},{4,8},{6,10},{8,12},{10,14},{12,0},{14,2},{1,5},{3,7},... | collective-permute-start | bytes 196616 | tf_op jit(solution)/shard_map/ppermute | solution.py:99
  24.7 1.8 %collective-permute-done.3 = f32[1,64,256]{2,1,0:T(8,128)S(1)} collective-permute-done((f32[1,64,256]{2,1,0:T(8,128)S(1)}, f32[1,64,256]{2,1,0:T(8,128)S(1)}, u32[]{:S(2)}, u32[]{:S(2)}) %collective-permute-start.3) | collective-permute-done | bytes 65568 | tf_op jit(solution)/shard_map/ppermute | solution.py:99
  26.5 0.5 %collective-permute-done.4 = f32[1,64,256]{2,1,0:T(8,128)S(1)} collective-permute-done((f32[1,64,256]{2,1,0:T(8,128)S(1)}, f32[1,64,256]{2,1,0:T(8,128)S(1)}, u32[]{:S(2)}, u32[]{:S(2)}) %collective-permute-start.4) | collective-permute-done | bytes 65568 | tf_op jit(solution)/shard_map/ppermute | solution.py:99
  27.0 3.1 %collective-permute-done.2 = f32[1,64,256]{2,1,0:T(8,128)S(1)} collective-permute-done((f32[1,64,256]{2,1,0:T(8,128)S(1)}, f32[1,64,256]{2,1,0:T(8,128)S(1)}, u32[]{:S(2)}, u32[]{:S(2)}) %collective-permute-start.2) | collective-permute-done | bytes 65568 | tf_op jit(solution)/shard_map/ppermute | solution.py:99
  30.6 1.9 %collective-permute-start.6 = (f32[256]{0:T(256)S(1)}, f32[256]{0:T(256)S(1)}, u32[]{:S(2)}, u32[]{:S(2)}) collective-permute-start(f32[256]{0:T(256)S(1)} %fusion.4), channel_id=1, source_target_pairs={{0,12},{2,14},{4,0},{6,2},{8,4},{10,6},{12,8},{14,10},{1,13},{3,15... | collective-permute-start | bytes 3080 | tf_op jit(solution)/shard_map/ppermute | solution.py:116
  32.6 1.9 %collective-permute-start.8 = (f32[256]{0:T(256)S(1)}, f32[256]{0:T(256)S(1)}, u32[]{:S(2)}, u32[]{:S(2)}) collective-permute-start(f32[256]{0:T(256)S(1)} %fusion.4), channel_id=1, source_target_pairs={{0,4},{2,6},{4,8},{6,10},{8,12},{10,14},{12,0},{14,2},{1,5},{3,7},... | collective-permute-start | bytes 3080 | tf_op jit(solution)/shard_map/ppermute | solution.py:116
  37.5 0.5 %collective-permute-done.8 = f32[256]{0:T(256)S(1)} collective-permute-done((f32[256]{0:T(256)S(1)}, f32[256]{0:T(256)S(1)}, u32[]{:S(2)}, u32[]{:S(2)}) %collective-permute-start.8) | collective-permute-done | bytes 1056 | tf_op jit(solution)/shard_map/ppermute | solution.py:116
  38.0 0.6 %add_multiply_fusion = f32[256]{0:T(256)} fusion(f32[256]{0:T(256)S(1)} %collective-permute-done.6, f32[256]{0:T(256)S(1)} %collective-permute-done.7, f32[256]{0:T(256)S(1)} %collective-permute-done.8, f32[256]{0:T(256)S(1)} %fusion.4, pred[]{:T(512)S(6)} %eq.61, pred[]{:T(512)S(6)} %eq.60, pred[]{:T(512)S(6)} %eq.59, pred[]{:T(512)S(6)} %eq.58, ...), kind=kLoop, calls=%fused_computation.194 | loop fusion | flops 4096 | bytes 5132 | tf_op jit(solution)/shard_map/div | solution.py:226
  38.6 0.7 %fusion.7 = bf16[4,1,64,256]{3,2,1,0:T(8,128)(2,1)} fusion(f32[4,1,64,256]{3,2,1,0:T(8,128)S(1)} %bitcast.365, bf16[2,4,1,64,256]{4,3,1,2,0:T(8,128)(2,1)S(1)} %collective-permute-done.5), kind=kLoop, calls=%fused_computation.48 | loop fusion | flops 196608 | bytes 524288 | tf_op jit(solution)/shard_map/convert_element_type | solution.py:91
  39.3 0.7 %fusion.13 = bf16[4,1,64,256]{3,2,1,0:T(8,128)(2,1)} fusion(f32[4,1,64,256]{3,2,0,1:T(8,128)S(1)} %bitcast.366, bf16[2,4,1,64,256]{4,3,1,2,0:T(8,128)(2,1)S(1)} %collective-permute-done.5), kind=kLoop, calls=%fused_computation.58 | loop fusion | flops 196608 | bytes 524288
  (80 shorter events, 6.6 us)
Async XLA Ops:
  3.3 11.5 %collective-permute-start = (bf16[4,1,64,512]{3,2,1,0:T(8,128)(2,1)}, bf16[4,1,64,512]{3,2,1,0:T(8,128)(2,1)}, u32[]{:S(2)}, u32[]{:S(2)}) collective-permute-start(bf16[4,1,64,512]{3,2,1,0:T(8,128)(2,1)} %get-tuple-element.72), channel_id=1, source_target_pairs={{0,2},{2,0},{4,6},{6,4},{8,10},{10,8},{12,14},{14,12},{1,3},{3,1},... | collective-permute-start | bytes 786440 | tf_op jit(solution)/shard_map/ppermute | solution.py:143
  7.7 2.5 %copy-start.3 = (f32[256]{0:T(256)S(1)}, f32[256]{0:T(256)}, u32[]{:S(2)}) copy-start(f32[256]{0:T(256)} %param.9) | copy-start | bytes 3076
  8.9 1.9 %copy-start = (bf16[4,1,64,512]{3,2,1,0:T(8,128)(2,1)S(1)}, bf16[4,1,64,512]{3,2,1,0:T(8,128)(2,1)}, u32[]{:S(2)}) copy-start(bf16[4,1,64,512]{3,2,1,0:T(8,128)(2,1)} %param.6) | copy-start | bytes 786436
  14.8 1.9 %collective-permute-start.1 = (bf16[4,1,64,512]{3,2,1,0:T(8,128)(2,1)}, bf16[4,1,64,512]{3,2,1,0:T(8,128)(2,1)}, u32[]{:S(2)}, u32[]{:S(2)}) collective-permute-start(bf16[4,1,64,512]{3,2,1,0:T(8,128)(2,1)} %collective-permute-done), channel_id=1, source_target_pairs={{0,1},{1,0},{2,3},{3,2},{4,5},{5,4},{6,7},{7,6},{8,9},{9,8},{10,11... | collective-permute-start | bytes 786440 | tf_op jit(solution)/shard_map/ppermute | solution.py:144
  18.0 1.3 %copy-start.2 = (f32[256,256]{1,0:T(8,128)S(1)}, f32[256,256]{1,0:T(8,128)}, u32[]{:S(2)}) copy-start(f32[256,256]{1,0:T(8,128)} %convolution_add_fusion.12) | copy-start | bytes 786436
  18.5 1.1 %copy-start.1 = (bf16[4,1,64,512]{3,2,1,0:T(8,128)(2,1)S(1)}, bf16[4,1,64,512]{3,2,1,0:T(8,128)(2,1)}, u32[]{:S(2)}) copy-start(bf16[4,1,64,512]{3,2,1,0:T(8,128)(2,1)} %get-tuple-element.73) | copy-start | bytes 786436
  19.3 10.8 %copy-start.6 = (f32[256]{0:T(256)S(1)}, f32[256]{0:T(256)}, u32[]{:S(2)}) copy-start(f32[256]{0:T(256)} %get-tuple-element.39) | copy-start | bytes 3076
  19.6 10.6 %copy-start.5 = (f32[256]{0:T(256)S(1)}, f32[256]{0:T(256)}, u32[]{:S(2)}) copy-start(f32[256]{0:T(256)} %get-tuple-element.40) | copy-start | bytes 3076
  19.6 10.6 %copy-start.4 = (f32[256]{0:T(256)S(1)}, f32[256]{0:T(256)}, u32[]{:S(2)}) copy-start(f32[256]{0:T(256)} %get-tuple-element.41) | copy-start | bytes 3076
  20.0 6.5 %collective-permute-start.3 = (f32[1,64,256]{2,1,0:T(8,128)S(1)}, f32[1,64,256]{2,1,0:T(8,128)S(1)}, u32[]{:S(2)}, u32[]{:S(2)}) collective-permute-start(f32[1,64,256]{2,1,0:T(8,128)S(1)} %get-tuple-element.83), channel_id=1, source_target_pairs={{0,8},{2,10},{4,12},{6,14},{8,0},{10,2},{12,4},{14,6},{1,9},{3,11}... | collective-permute-start | bytes 196616 | tf_op jit(solution)/shard_map/ppermute | solution.py:99
  22.7 4.3 %collective-permute-start.4 = (f32[1,64,256]{2,1,0:T(8,128)S(1)}, f32[1,64,256]{2,1,0:T(8,128)S(1)}, u32[]{:S(2)}, u32[]{:S(2)}) collective-permute-start(f32[1,64,256]{2,1,0:T(8,128)S(1)} %get-tuple-element.84), channel_id=1, source_target_pairs={{0,12},{2,14},{4,0},{6,2},{8,4},{10,6},{12,8},{14,10},{1,13},{3,15... | collective-permute-start | bytes 196616 | tf_op jit(solution)/shard_map/ppermute | solution.py:99
  24.0 6.1 %collective-permute-start.2 = (f32[1,64,256]{2,1,0:T(8,128)S(1)}, f32[1,64,256]{2,1,0:T(8,128)S(1)}, u32[]{:S(2)}, u32[]{:S(2)}) collective-permute-start(f32[1,64,256]{2,1,0:T(8,128)S(1)} %get-tuple-element.53), channel_id=1, source_target_pairs={{0,4},{2,6},{4,8},{6,10},{8,12},{10,14},{12,0},{14,2},{1,5},{3,7},... | collective-permute-start | bytes 196616 | tf_op jit(solution)/shard_map/ppermute | solution.py:99
  30.6 6.9 %collective-permute-start.6 = (f32[256]{0:T(256)S(1)}, f32[256]{0:T(256)S(1)}, u32[]{:S(2)}, u32[]{:S(2)}) collective-permute-start(f32[256]{0:T(256)S(1)} %fusion.4), channel_id=1, source_target_pairs={{0,12},{2,14},{4,0},{6,2},{8,4},{10,6},{12,8},{14,10},{1,13},{3,15... | collective-permute-start | bytes 3080 | tf_op jit(solution)/shard_map/ppermute | solution.py:116
  32.5 5.0 %collective-permute-start.7 = (f32[256]{0:T(256)S(1)}, f32[256]{0:T(256)S(1)}, u32[]{:S(2)}, u32[]{:S(2)}) collective-permute-start(f32[256]{0:T(256)S(1)} %fusion.4), channel_id=1, source_target_pairs={{0,8},{2,10},{4,12},{6,14},{8,0},{10,2},{12,4},{14,6},{1,9},{3,11}... | collective-permute-start | bytes 3080 | tf_op jit(solution)/shard_map/ppermute | solution.py:116
  32.6 5.4 %collective-permute-start.8 = (f32[256]{0:T(256)S(1)}, f32[256]{0:T(256)S(1)}, u32[]{:S(2)}, u32[]{:S(2)}) collective-permute-start(f32[256]{0:T(256)S(1)} %fusion.4), channel_id=1, source_target_pairs={{0,4},{2,6},{4,8},{6,10},{8,12},{10,14},{12,0},{14,2},{1,5},{3,7},... | collective-permute-start | bytes 3080 | tf_op jit(solution)/shard_map/ppermute | solution.py:116
  37.0 1.6 %collective-permute-start.5 = (bf16[2,4,1,64,256]{4,3,1,2,0:T(8,128)(2,1)S(1)}, bf16[2,4,1,64,256]{4,3,1,2,0:T(8,128)(2,1)S(1)}, u32[]{:S(2)}, u32[]{:S(2)}) collective-permute-start(bf16[2,4,1,64,256]{4,3,1,2,0:T(8,128)(2,1)S(1)} %pad_maximum_fusion), channel_id=1, source_target_pairs={{0,1},{1,0},{2,3},{3,2},{4,5},{5,4},{6,7},{7,6},{8,9},{9,8},{10,11... | collective-permute-start | bytes 786440 | tf_op jit(solution)/shard_map/ppermute | solution.py:86

commit v20 on v16

--- a/solution.py
+++ b/solution.py
@@ -79,15 +79,12 @@
             for job in jobs
         ]
     width = jobs[0][2].shape[3] // count
-    others = []
-    for cells, halo, taps, row_taps in jobs:
-        other_taps = lax.dynamic_slice_in_dim(taps, (1 - mine) * width, width, axis=3)
-        others.append(conv_apply(cells, halo, other_taps, row_taps).astype(jnp.bfloat16))
-    got = lax.ppermute(jnp.stack(others), "chan", [(0, 1), (1, 0)])
+    full = [conv_apply(*job) for job in jobs]
+    others = [lax.dynamic_slice_in_dim(part, (1 - mine) * width, width, axis=3) for part in full]
+    got = lax.ppermute(jnp.stack(others).astype(jnp.bfloat16), "chan", [(0, 1), (1, 0)])
     results = []
-    for index, (cells, halo, taps, row_taps) in enumerate(jobs):
-        own_taps = lax.dynamic_slice_in_dim(taps, mine * width, width, axis=3)
-        own = conv_apply(cells, halo, own_taps, row_taps)
+    for index, part in enumerate(full):
+        own = lax.dynamic_slice_in_dim(part, mine * width, width, axis=3)
         results.append((own + got[index].astype(jnp.float32)).astype(jnp.bfloat16))
     return results
 

time: 39.1 us -> 41 us (1.049)
  waiting for transfers between devices: 9.94 us -> 12.8 us
  matrix products: 5.42 us -> 4.37 us
    ppermute x3, waiting for transfers between devices: 0.46 us -> 3.42 us  [group_sum(): lax.ppermute(value, axis, route(step))]
    dot_general x24 -> x18, matrix products: 5.42 us -> 4.37 us  [conv_apply(): jnp.dot(portion.reshape(-1, channels), taps[index, col_tap], preferred_el...]
  transfers between devices with their start and end apart: 9 -> 9, of which waited for: 7 -> 7; matrix products, arithmetic and copies ran while one was open for 20% -> 12% of each run, Pallas kernels for 0% -> 0%
where the time goes in v20:
time: 41 us; the launch traced here: 40.8 us
  waiting for transfers between devices  12.8 us (31%)
  starting transfers between devices  11.9 us (29%)
  other arithmetic  7.03 us (17%)
  matrix products  4.37 us (11%)
  local copies, waits for them, and re-layouts  3.53 us (9%)
  between operations  1.17 us (3%)
    ppermute x3, waiting for transfers between devices, cyclic_carries(): received[step] = lax.ppermute(message, axis, route(step))  5.38 us
    ppermute x3, starting transfers between devices, cyclic_carries(): received[step] = lax.ppermute(message, axis, route(step))  4.93 us
    dot_general x18, matrix products, conv_apply(): jnp.dot(portion.reshape(-1, channels), taps[index, col_tap], preferred_el...  4.37 us
    ppermute x3, starting transfers between devices, group_sum(): lax.ppermute(value, axis, route(step))  3.93 us
    ppermute x3, waiting for transfers between devices, group_sum(): lax.ppermute(value, axis, route(step))  3.42 us
    ppermute x1, starting transfers between devices, local(): got = lax.ppermute(jnp.where(first, frames_in, out_grad), 'tm', swap)  2.94 us
    ppermute x1, waiting for transfers between devices, local(): got = lax.ppermute(jnp.where(first, frames_in, out_grad), 'tm', swap)  2.18 us
    ppermute x1, waiting for transfers between devices, local(): traded = lax.ppermute(got, 'chan', [(0, 1), (1, 0)])  1.85 us
  transfers between devices with their start and end apart: 9, of which 7 were waited for; matrix products, arithmetic and copies ran while one was open for 12% of the time, Pallas kernels for 0%

profile of v20, /device:TPU:0, one launch (start us, length us, event | category | flops | bytes accessed | tf_op | source)
XLA Modules:
  0.0 40.8 jit_solution(18048370418860624254)
XLA Ops:
  0.6 1.7 %broadcast_select_fusion.2 = bf16[4,1,64,512]{3,2,1,0:T(8,128)(2,1)} fusion(bf16[4,1,64,512]{3,2,1,0:T(8,128)(2,1)} %param.6, bf16[4,1,64,512]{3,2,1,0:T(8,128)(2,1)} %param.11, pred[]{:T(512)S(6)} %eq.49), kind=kLoop, calls=%fused_computation.57 | loop fusion | flops 131072 | bytes 786433 | tf_op jit(solution)/shard_map/jit(_where)/select_n | solution.py:140
  2.3 2.9 %collective-permute-start = (bf16[4,1,64,512]{3,2,1,0:T(8,128)(2,1)}, bf16[4,1,64,512]{3,2,1,0:T(8,128)(2,1)}, u32[]{:S(2)}, u32[]{:S(2)}) collective-permute-start(bf16[4,1,64,512]{3,2,1,0:T(8,128)(2,1)} %broadcast_select_fusion.2), channel_id=1, source_target_pairs={{0,2},{2,0},{4,6},{6,4},{8,10},{10,8},{12,14},{14,12},{1,3},{3,1},... | collective-permute-start | bytes 786440 | tf_op jit(solution)/shard_map/ppermute | solution.py:140
  5.3 1.2 %slice.302 = bf16[1,3,512,256]{3,2,1,0:T(8,128)(2,1)S(1)} slice(bf16[3,3,512,256]{3,2,1,0:T(8,128)(2,1)} %param.7), slice={[1:2], [0:3], [0:512], [0:256]} | slice | bytes 1572864 | tf_op jit(solution)/shard_map/slice | solution.py:31
  6.5 1.2 %slice.322 = bf16[1,3,256,512]{3,2,1,0:T(8,128)(2,1)S(1)} slice(bf16[3,3,256,512]{3,2,1,0:T(8,128)(2,1)} %param.8), slice={[1:2], [0:3], [0:256], [0:512]} | slice | bytes 1572864 | tf_op jit(solution)/shard_map/slice | solution.py:28
  8.0 0.6 %multiply_divide_fusion = (f32[256]{0:T(256)}, f32[256]{0:T(256)S(1)}) fusion(f32[256]{0:T(256)S(1)} %copy-done.1), kind=kLoop, calls=%fused_computation.174 | loop fusion | flops 768 | bytes 3072 | tf_op jit(solution)/shard_map/div | solution.py:212
  9.0 0.6 %fusion.56 = (f32[256]{0:T(256)}, f32[256]{0:T(256)}, f32[256]{0:T(256)}, f32[256]{0:T(256)}, f32[256]{0:T(256)}, /*index=5*/f32[256]{0:T(256)}, f32[256]{0:T(256)}) fusion(f32[256]{0:T(256)S(1)} %bitcast.316, f32[256]{0:T(256)S(1)} %bitcast.303, f32[256]{0:T(256)S(1)} %bitcast.314, f32[256]{0:T(256)S(1)} %bitcast.300, f32[256]{0:T(256)S(1)} %bitcast.312, ...), kind=kLoop, calls=%fused_computation.176 | loop fusion | flops 1792 | bytes 15360 | tf_op jit(solution)/shard_map/mul | solution.py:184
  9.7 2.2 %collective-permute-done = bf16[4,1,64,512]{3,2,1,0:T(8,128)(2,1)} collective-permute-done((bf16[4,1,64,512]{3,2,1,0:T(8,128)(2,1)}, bf16[4,1,64,512]{3,2,1,0:T(8,128)(2,1)}, u32[]{:S(2)}, u32[]{:S(2)}) %collective-permute-start) | collective-permute-done | bytes 262176 | tf_op jit(solution)/shard_map/ppermute | solution.py:140
  11.9 1.9 %collective-permute-done.1 = bf16[4,1,64,512]{3,2,1,0:T(8,128)(2,1)} collective-permute-done((bf16[4,1,64,512]{3,2,1,0:T(8,128)(2,1)}, bf16[4,1,64,512]{3,2,1,0:T(8,128)(2,1)}, u32[]{:S(2)}, u32[]{:S(2)}) %collective-permute-start.1) | collective-permute-done | bytes 262176 | tf_op jit(solution)/shard_map/ppermute | solution.py:141
  13.8 1.2 %broadcast_select_fusion.6 = (bf16[4,1,64,512]{3,2,1,0:T(8,128)(2,1)S(1)}, bf16[4,1,64,512]{3,2,1,0:T(8,128)(2,1)S(1)}, bf16[4,1,64,512]{3,2,1,0:T(8,128)(2,1)S(1)}, bf16[4,1,64,512]{3,2,1,0:T(8,128)(2,1)S(1)}) fusion(bf16[4,1,64,512]{3,2,1,0:T(8,128)(2,1)S(1)} %copy-done, pred[]{:T(512)S(6)} %eq.48, bf16[4,1,64,512]{3,2,1,0:T(8,128)(2,1)} %collective-permute-done, ...), kind=kLoop, calls=%fused_computation.61 | loop fusion | flops 786432 | bytes 2097154 | tf_op jit(solution)/shard_map/jit(_where)/select_n | solution.py:147
  18.6 2.9 %collective-permute-start.3 = (f32[1,64,256]{2,1,0:T(8,128)S(1)}, f32[1,64,256]{2,1,0:T(8,128)S(1)}, u32[]{:S(2)}, u32[]{:S(2)}) collective-permute-start(f32[1,64,256]{2,1,0:T(8,128)S(1)} %get-tuple-element.82), channel_id=1, source_target_pairs={{0,8},{2,10},{4,12},{6,14},{8,0},{10,2},{12,4},{14,6},{1,9},{3,11}... | collective-permute-start | bytes 196616 | tf_op jit(solution)/shard_map/ppermute | solution.py:96
  21.5 1.3 %collective-permute-start.4 = (f32[1,64,256]{2,1,0:T(8,128)S(1)}, f32[1,64,256]{2,1,0:T(8,128)S(1)}, u32[]{:S(2)}, u32[]{:S(2)}) collective-permute-start(f32[1,64,256]{2,1,0:T(8,128)S(1)} %get-tuple-element.83), channel_id=1, source_target_pairs={{0,12},{2,14},{4,0},{6,2},{8,4},{10,6},{12,8},{14,10},{1,13},{3,15... | collective-permute-start | bytes 196616 | tf_op jit(solution)/shard_map/ppermute | solution.py:96
  22.9 0.7 %collective-permute-start.2 = (f32[1,64,256]{2,1,0:T(8,128)S(1)}, f32[1,64,256]{2,1,0:T(8,128)S(1)}, u32[]{:S(2)}, u32[]{:S(2)}) collective-permute-start(f32[1,64,256]{2,1,0:T(8,128)S(1)} %get-tuple-element.53), channel_id=1, source_target_pairs={{0,4},{2,6},{4,8},{6,10},{8,12},{10,14},{12,0},{14,2},{1,5},{3,7},... | collective-permute-start | bytes 196616 | tf_op jit(solution)/shard_map/ppermute | solution.py:96
  23.6 1.4 %collective-permute-done.3 = f32[1,64,256]{2,1,0:T(8,128)S(1)} collective-permute-done((f32[1,64,256]{2,1,0:T(8,128)S(1)}, f32[1,64,256]{2,1,0:T(8,128)S(1)}, u32[]{:S(2)}, u32[]{:S(2)}) %collective-permute-start.3) | collective-permute-done | bytes 65568 | tf_op jit(solution)/shard_map/ppermute | solution.py:96
  24.9 0.9 %collective-permute-done.4 = f32[1,64,256]{2,1,0:T(8,128)S(1)} collective-permute-done((f32[1,64,256]{2,1,0:T(8,128)S(1)}, f32[1,64,256]{2,1,0:T(8,128)S(1)}, u32[]{:S(2)}, u32[]{:S(2)}) %collective-permute-start.4) | collective-permute-done | bytes 65568 | tf_op jit(solution)/shard_map/ppermute | solution.py:96
  25.8 3.1 %collective-permute-done.2 = f32[1,64,256]{2,1,0:T(8,128)S(1)} collective-permute-done((f32[1,64,256]{2,1,0:T(8,128)S(1)}, f32[1,64,256]{2,1,0:T(8,128)S(1)}, u32[]{:S(2)}, u32[]{:S(2)}) %collective-permute-start.2) | collective-permute-done | bytes 65568 | tf_op jit(solution)/shard_map/ppermute | solution.py:96
  29.9 0.3 convolution_add_fusion.1
  30.2 0.3 convolution_add_fusion
  31.5 1.9 %collective-permute-start.6 = (f32[256]{0:T(256)S(1)}, f32[256]{0:T(256)S(1)}, u32[]{:S(2)}, u32[]{:S(2)}) collective-permute-start(f32[256]{0:T(256)S(1)} %fusion.2), channel_id=1, source_target_pairs={{0,12},{2,14},{4,0},{6,2},{8,4},{10,6},{12,8},{14,10},{1,13},{3,15... | collective-permute-start | bytes 3080 | tf_op jit(solution)/shard_map/ppermute | solution.py:113
  33.5 1.9 %collective-permute-start.8 = (f32[256]{0:T(256)S(1)}, f32[256]{0:T(256)S(1)}, u32[]{:S(2)}, u32[]{:S(2)}) collective-permute-start(f32[256]{0:T(256)S(1)} %fusion.2), channel_id=1, source_target_pairs={{0,4},{2,6},{4,8},{6,10},{8,12},{10,14},{12,0},{14,2},{1,5},{3,7},... | collective-permute-start | bytes 3080 | tf_op jit(solution)/shard_map/ppermute | solution.py:113
  35.4 2.4 %collective-permute-done.7 = f32[256]{0:T(256)S(1)} collective-permute-done((f32[256]{0:T(256)S(1)}, f32[256]{0:T(256)S(1)}, u32[]{:S(2)}, u32[]{:S(2)}) %collective-permute-start.7) | collective-permute-done | bytes 1056 | tf_op jit(solution)/shard_map/ppermute | solution.py:113
  37.8 1.0 %collective-permute-done.8 = f32[256]{0:T(256)S(1)} collective-permute-done((f32[256]{0:T(256)S(1)}, f32[256]{0:T(256)S(1)}, u32[]{:S(2)}, u32[]{:S(2)}) %collective-permute-start.8) | collective-permute-done | bytes 1056 | tf_op jit(solution)/shard_map/ppermute | solution.py:113
  38.9 0.6 %add_multiply_fusion = f32[256]{0:T(256)} fusion(f32[256]{0:T(256)S(1)} %collective-permute-done.6, f32[256]{0:T(256)S(1)} %collective-permute-done.7, f32[256]{0:T(256)S(1)} %collective-permute-done.8, f32[256]{0:T(256)S(1)} %fusion.2, pred[]{:T(512)S(6)} %eq.61, pred[]{:T(512)S(6)} %eq.60, pred[]{:T(512)S(6)} %eq.59, pred[]{:T(512)S(6)} %eq.58, ...), kind=kLoop, calls=%fused_computation.172 | loop fusion | flops 4096 | bytes 5132 | tf_op jit(solution)/shard_map/div | solution.py:219
  39.4 0.7 %fusion.7 = bf16[4,1,64,256]{3,2,1,0:T(8,128)(2,1)} fusion(f32[4,1,64,512]{3,2,0,1:T(8,128)S(1)} %bitcast.271, s32[]{:T(128)S(6)} %select_n.295, bf16[2,4,1,64,256]{4,3,1,2,0:T(8,128)(2,1)S(1)} %collective-permute-done.5), kind=kLoop, calls=%fused_computation.50 | loop fusion | flops 196608 | bytes 524292 | tf_op jit(solution)/shard_map/convert_element_type | solution.py:88
  40.1 0.7 %fusion.15 = bf16[4,1,64,256]{3,2,1,0:T(8,128)(2,1)} fusion(f32[4,1,64,512]{3,2,0,1:T(8,128)S(1)} %bitcast.273, s32[]{:T(128)S(6)} %select_n.295, bf16[2,4,1,64,256]{4,3,1,2,0:T(8,128)(2,1)S(1)} %collective-permute-done.5), kind=kLoop, calls=%fused_computation.68 | loop fusion | flops 196608 | bytes 524292
  (85 shorter events, 6.1 us)
Async XLA Ops:
  2.3 9.6 %collective-permute-start = (bf16[4,1,64,512]{3,2,1,0:T(8,128)(2,1)}, bf16[4,1,64,512]{3,2,1,0:T(8,128)(2,1)}, u32[]{:S(2)}, u32[]{:S(2)}) collective-permute-start(bf16[4,1,64,512]{3,2,1,0:T(8,128)(2,1)} %broadcast_select_fusion.2), channel_id=1, source_target_pairs={{0,2},{2,0},{4,6},{6,4},{8,10},{10,8},{12,14},{14,12},{1,3},{3,1},... | collective-permute-start | bytes 786440 | tf_op jit(solution)/shard_map/ppermute | solution.py:140
  5.3 2.5 %copy-start.10 = (f32[32]{0:T(128)S(1)}, f32[32]{0:T(128)}, u32[]{:S(2)}) copy-start(f32[32]{0:T(128)} %param.10) | copy-start | bytes 388
  5.3 2.7 %copy-start.1 = (f32[256]{0:T(256)S(1)}, f32[256]{0:T(256)}, u32[]{:S(2)}) copy-start(f32[256]{0:T(256)} %param.9) | copy-start | bytes 3076
  6.5 7.3 %copy-start = (bf16[4,1,64,512]{3,2,1,0:T(8,128)(2,1)S(1)}, bf16[4,1,64,512]{3,2,1,0:T(8,128)(2,1)}, u32[]{:S(2)}) copy-start(bf16[4,1,64,512]{3,2,1,0:T(8,128)(2,1)} %param.6) | copy-start | bytes 786436
  11.9 1.9 %collective-permute-start.1 = (bf16[4,1,64,512]{3,2,1,0:T(8,128)(2,1)}, bf16[4,1,64,512]{3,2,1,0:T(8,128)(2,1)}, u32[]{:S(2)}, u32[]{:S(2)}) collective-permute-start(bf16[4,1,64,512]{3,2,1,0:T(8,128)(2,1)} %collective-permute-done), channel_id=1, source_target_pairs={{0,1},{1,0},{2,3},{3,2},{4,5},{5,4},{6,7},{7,6},{8,9},{9,8},{10,11... | collective-permute-start | bytes 786440 | tf_op jit(solution)/shard_map/ppermute | solution.py:141
  17.6 11.3 %copy-start.9 = (f32[256]{0:T(256)S(1)}, f32[256]{0:T(256)}, u32[]{:S(2)}) copy-start(f32[256]{0:T(256)} %get-tuple-element.39) | copy-start | bytes 3076
  17.9 11.1 %copy-start.8 = (f32[256]{0:T(256)S(1)}, f32[256]{0:T(256)}, u32[]{:S(2)}) copy-start(f32[256]{0:T(256)} %get-tuple-element.40) | copy-start | bytes 3076
  17.9 11.1 %copy-start.7 = (f32[256]{0:T(256)S(1)}, f32[256]{0:T(256)}, u32[]{:S(2)}) copy-start(f32[256]{0:T(256)} %get-tuple-element.41) | copy-start | bytes 3076
  17.9 11.2 %copy-start.6 = (f32[256]{0:T(256)S(1)}, f32[256]{0:T(256)}, u32[]{:S(2)}) copy-start(f32[256]{0:T(256)} %get-tuple-element.42) | copy-start | bytes 3076
  18.2 10.9 %copy-start.5 = (f32[256]{0:T(256)S(1)}, f32[256]{0:T(256)}, u32[]{:S(2)}) copy-start(f32[256]{0:T(256)} %get-tuple-element.43) | copy-start | bytes 3076
  18.2 10.9 %copy-start.4 = (f32[256]{0:T(256)S(1)}, f32[256]{0:T(256)}, u32[]{:S(2)}) copy-start(f32[256]{0:T(256)} %get-tuple-element.44) | copy-start | bytes 3076
  18.2 11.0 %copy-start.3 = (f32[256]{0:T(256)S(1)}, f32[256]{0:T(256)}, u32[]{:S(2)}) copy-start(f32[256]{0:T(256)} %get-tuple-element.45) | copy-start | bytes 3076
  18.6 6.3 %collective-permute-start.3 = (f32[1,64,256]{2,1,0:T(8,128)S(1)}, f32[1,64,256]{2,1,0:T(8,128)S(1)}, u32[]{:S(2)}, u32[]{:S(2)}) collective-permute-start(f32[1,64,256]{2,1,0:T(8,128)S(1)} %get-tuple-element.82), channel_id=1, source_target_pairs={{0,8},{2,10},{4,12},{6,14},{8,0},{10,2},{12,4},{14,6},{1,9},{3,11}... | collective-permute-start | bytes 196616 | tf_op jit(solution)/shard_map/ppermute | solution.py:96
  21.5 4.3 %collective-permute-start.4 = (f32[1,64,256]{2,1,0:T(8,128)S(1)}, f32[1,64,256]{2,1,0:T(8,128)S(1)}, u32[]{:S(2)}, u32[]{:S(2)}) collective-permute-start(f32[1,64,256]{2,1,0:T(8,128)S(1)} %get-tuple-element.83), channel_id=1, source_target_pairs={{0,12},{2,14},{4,0},{6,2},{8,4},{10,6},{12,8},{14,10},{1,13},{3,15... | collective-permute-start | bytes 196616 | tf_op jit(solution)/shard_map/ppermute | solution.py:96
  22.9 6.1 %collective-permute-start.2 = (f32[1,64,256]{2,1,0:T(8,128)S(1)}, f32[1,64,256]{2,1,0:T(8,128)S(1)}, u32[]{:S(2)}, u32[]{:S(2)}) collective-permute-start(f32[1,64,256]{2,1,0:T(8,128)S(1)} %get-tuple-element.53), channel_id=1, source_target_pairs={{0,4},{2,6},{4,8},{6,10},{8,12},{10,14},{12,0},{14,2},{1,5},{3,7},... | collective-permute-start | bytes 196616 | tf_op jit(solution)/shard_map/ppermute | solution.py:96
  30.5 0.9 %copy-start.2 = (f32[256]{0:T(256)S(1)}, f32[256]{0:T(256)}, u32[]{:S(2)}) copy-start(f32[256]{0:T(256)} %get-tuple-element.106) | copy-start | bytes 3076
  31.3 8.2 %collective-permute-start.5 = (bf16[2,4,1,64,256]{4,3,1,2,0:T(8,128)(2,1)S(1)}, bf16[2,4,1,64,256]{4,3,1,2,0:T(8,128)(2,1)S(1)}, u32[]{:S(2)}, u32[]{:S(2)}) collective-permute-start(bf16[2,4,1,64,256]{4,3,1,2,0:T(8,128)(2,1)S(1)} %pad_maximum_fusion), channel_id=1, source_target_pairs={{0,1},{1,0},{2,3},{3,2},{4,5},{5,4},{6,7},{7,6},{8,9},{9,8},{10,11... | collective-permute-start | bytes 786440 | tf_op jit(solution)/shard_map/ppermute | solution.py:84
  31.5 3.9 %collective-permute-start.6 = (f32[256]{0:T(256)S(1)}, f32[256]{0:T(256)S(1)}, u32[]{:S(2)}, u32[]{:S(2)}) collective-permute-start(f32[256]{0:T(256)S(1)} %fusion.2), channel_id=1, source_target_pairs={{0,12},{2,14},{4,0},{6,2},{8,4},{10,6},{12,8},{14,10},{1,13},{3,15... | collective-permute-start | bytes 3080 | tf_op jit(solution)/shard_map/ppermute | solution.py:113
  33.4 4.5 %collective-permute-start.7 = (f32[256]{0:T(256)S(1)}, f32[256]{0:T(256)S(1)}, u32[]{:S(2)}, u32[]{:S(2)}) collective-permute-start(f32[256]{0:T(256)S(1)} %fusion.2), channel_id=1, source_target_pairs={{0,8},{2,10},{4,12},{6,14},{8,0},{10,2},{12,4},{14,6},{1,9},{3,11}... | collective-permute-start | bytes 3080 | tf_op jit(solution)/shard_map/ppermute | solution.py:113
  33.5 5.4 %collective-permute-start.8 = (f32[256]{0:T(256)S(1)}, f32[256]{0:T(256)S(1)}, u32[]{:S(2)}, u32[]{:S(2)}) collective-permute-start(f32[256]{0:T(256)S(1)} %fusion.2), channel_id=1, source_target_pairs={{0,4},{2,6},{4,8},{6,10},{8,12},{10,14},{12,0},{14,2},{1,5},{3,7},... | collective-permute-start | bytes 3080 | tf_op jit(solution)/shard_map/ppermute | solution.py:113
